TPU v7x, 128 devices: a whole 4x4x4 slice. The times are simulated.
128 devices in a mesh: dp: 32 (over y, z, x_hi), mp: 4 (over x_lo, core).
Axes of the slice: x: 4 (x_hi: 2, x_lo: 2; x = x_hi * 2 + x_lo), y: 4, z: 4, core: 2. Of those that a mesh axis runs over, the one named last changes fastest.
Arguments:
- tokens: bfloat16 [8192, 2048], P('dp'), may hold values from -6 to 6
- lengths: int32 [4], replicated, may hold values from 1 to 4096, 8192 in all
- w_query: float32 [2048, 2048], P('dp', 'mp')
- w_key: float32 [2048, 2048], P('dp', 'mp')
- w_value: float32 [2048, 2048], P('dp', 'mp'), may hold values from -0.125 to 0.125
- w_out: float32 [2048, 2048], P('dp', 'mp'), may hold values from -0.125 to 0.125
- w_gate: float32 [2048, 4096], P('dp', 'mp'), may hold values from -0.125 to 0.125
- w_up: float32 [2048, 4096], P('dp', 'mp'), may hold values from -0.125 to 0.125
- w_down: float32 [4096, 2048], P('dp', 'mp'), may hold values from -0.09375 to 0.09375
Outputs:
- layer_out: bfloat16 [8192, 2048], P(('dp', 'mp'))
Inputs may be any that keep to these rules, and one draw needn't show every extreme that they name: Every prompt is 1 to 4096 tokens long and one is exactly 4096; the lengths sum to 8192.
All inputs are finite; a program needn't handle non-finite values.
Results may differ from a plain program's by a relative error of at most 0.02.
The roundings to bfloat16 on the way count: a program that leaves them out, or rounds other values in their place, can miss the bound.
Values may be sent and summed in bfloat16 or wider, within the bound.
No kernel may reach another device: no remote copies, remote signals or barrier semaphores. Data moves between devices by JAX's collectives and lax.ppermute only.
A program may use at most 128 MiB of HBM per device.

v0:
```python
import jax
import jax.numpy as jnp
from jax import lax
from jax.sharding import PartitionSpec as P

HEAD = 128


epsilon = 1e-05
theta_base = 10000.0


def passed_along(value, axis, steps):
    count = lax.axis_size(axis)
    initial, last = (max(0, -steps), min(count, count - steps))
    return lax.ppermute(value, axis, [(source, source + steps) for source in range(initial, last)])


def layer_norm(rows):
    values = rows.astype(jnp.float32)
    centre = jnp.mean(values, axis=-1, keepdims=True)
    spread = jnp.mean(jnp.square(values - centre), axis=-1, keepdims=True)
    return (values - centre) * lax.rsqrt(spread + epsilon)


def prompt_coords(first, count, lengths):
    where = first + jnp.arange(count)
    ends = jnp.cumsum(lengths)
    passed = (ends[None, :] <= where[:, None]).astype(jnp.int32)
    prompt = jnp.sum(passed, axis=1)
    offset = where - jnp.sum(passed * lengths[None, :], axis=1)
    prompt = jnp.where(where < 0, -1, prompt)
    return (prompt, offset, where)


def rotate(values, offset):
    half = values.shape[-1] // 2
    freqs = jnp.power(theta_base, -jnp.arange(half, dtype=jnp.float32) * 2.0 / values.shape[-1])
    angles = offset.astype(jnp.float32)[:, None] * freqs[None, :]
    cosine = jnp.cos(angles)[:, None, :]
    sine = jnp.sin(angles)[:, None, :]
    first_half = values[..., :half]
    second_half = values[..., half:]
    return jnp.concatenate(
        [first_half * cosine - second_half * sine, second_half * cosine + first_half * sine],
        axis=-1,
    )


def row_product(left, pieces):
    block = jnp.concatenate(pieces, axis=1)
    return jnp.dot(left, block, preferred_element_type=jnp.float32)


def on_device(tokens, lengths, w_query, w_key, w_value, w_out, w_gate, w_up, w_down):
    half_type = jnp.bfloat16
    rows = tokens.shape[0]
    narrow = w_query.shape[1]
    heads_dev = narrow // HEAD
    dp_index = lax.axis_index("dp")
    mp_index = lax.axis_index("mp")
    reach = lax.axis_size("dp") // 2
    normed = layer_norm(tokens).astype(half_type)
    joined = row_product(
        normed,
        (
            lax.all_gather(w_query.astype(half_type), "dp", axis=0, tiled=True),
            lax.all_gather(w_key.astype(half_type), "dp", axis=0, tiled=True),
            lax.all_gather(w_value.astype(half_type), "dp", axis=0, tiled=True),
        ),
    )
    q_prompt, q_offset, q_where = prompt_coords(dp_index * rows, rows, lengths)
    shaped = joined.reshape(rows, 3, heads_dev, HEAD)
    query = rotate(shaped[:, 0], q_offset).astype(half_type)
    keys = rotate(shaped[:, 1], q_offset).astype(half_type)
    values = shaped[:, 2].astype(half_type)
    own_first = dp_index * rows
    own_pair = jnp.stack((keys, values))
    scale = 1.0 / HEAD**0.5

    def online_step(state, pair, first):
        accum, total, top = state
        k_prompt, k_offset, k_where = prompt_coords(first, rows, lengths)
        scores = (
            jnp.einsum("qhd,khd->hqk", query, pair[0], preferred_element_type=jnp.float32) * scale
        )
        allowed = (q_prompt[:, None] == k_prompt[None, :]) & (k_where[None, :] <= q_where[:, None])
        scores = jnp.where(allowed[None], scores, -jnp.inf)
        new_top = jnp.maximum(top, jnp.max(scores, axis=-1, keepdims=True))
        fade = jnp.exp(top - new_top)
        weights = jnp.exp(scores - new_top)
        probs = weights.astype(half_type)
        product = jnp.einsum("hqk,khd->qhd", probs, pair[1], preferred_element_type=jnp.float32)
        accum = accum * jnp.transpose(fade, (1, 0, 2)) + product
        total = total * fade + jnp.sum(weights, axis=-1, keepdims=True)
        return (accum, total, new_top)

    start_state = (
        jnp.zeros((rows, heads_dev, HEAD), jnp.float32),
        jnp.zeros((heads_dev, rows, 1), jnp.float32),
        jnp.full((heads_dev, rows, 1), -jnp.inf, jnp.float32),
    )
    state = online_step(start_state, own_pair, own_first)

    def relay_step(hop, carry):
        carried, running = carry
        carried = passed_along(carried, "dp", 1)
        first = own_first - (hop + 1) * rows
        return (carried, online_step(running, carried, first))

    unused, state = lax.fori_loop(0, reach, relay_step, (own_pair, state))
    accum, total, top = state
    context = (accum / jnp.transpose(total, (1, 0, 2))).astype(half_type).reshape(rows, narrow)
    by_rows = lax.all_gather(w_out.astype(half_type), "dp", axis=0, tiled=True)
    server_out = lax.all_to_all(by_rows, "mp", split_axis=0, concat_axis=1, tiled=True)
    partial_out = jnp.dot(context, server_out, preferred_element_type=jnp.float32)
    attended = lax.psum(partial_out.astype(jnp.bfloat16), "mp").astype(jnp.float32)
    mixed = (tokens.astype(jnp.float32) + attended).astype(half_type)
    normed_two = layer_norm(mixed).astype(half_type)
    units = w_gate.shape[1]
    gate_up = row_product(
        normed_two,
        (
            lax.all_gather(w_gate.astype(half_type), "dp", axis=0, tiled=True),
            lax.all_gather(w_up.astype(half_type), "dp", axis=0, tiled=True),
        ),
    )
    hidden = (jax.nn.silu(gate_up[:, :units]) * gate_up[:, units:]).astype(half_type)
    gathered_down = lax.all_gather(w_down.astype(half_type), "dp", axis=0, tiled=True)
    slab = rows // lax.axis_size("mp")
    server_down = lax.all_to_all(gathered_down, "mp", split_axis=0, concat_axis=1, tiled=True)
    share = lax.psum_scatter(
        jnp.dot(hidden, server_down, preferred_element_type=jnp.float32).astype(jnp.bfloat16),
        "mp",
        scatter_dimension=0,
        tiled=True,
    ).astype(jnp.float32)
    own_rows = lax.dynamic_slice_in_dim(mixed, mp_index * slab, slab, 0)
    return (own_rows.astype(jnp.float32) + share).astype(half_type)


def solution(mesh):
    in_specs = (
        P("dp", None),
        P(),
        P("dp", "mp"),
        P("dp", "mp"),
        P("dp", "mp"),
        P("dp", "mp"),
        P("dp", "mp"),
        P("dp", "mp"),
        P("dp", "mp"),
    )
    out_specs = P(("dp", "mp"), None)
    return jax.shard_map(
        on_device, mesh=mesh, in_specs=in_specs, out_specs=out_specs, check_vma=False
    )
```

profile of v0, /device:TPU:4, one launch (start us, length us, event | category | flops | bytes accessed | tf_op | source)
XLA Modules:
  0.0 903.4 jit_solution(11053108783286988303)
XLA Ops:
  17.0 64.1 %all-gather.10.cloned.1.call-done = bf16[2048,512]{1,0:T(8,128)(2,1)} async-done(((bf16[64,512]{1,0:T(8,128)(2,1)}), bf16[2048,512]{1,0:T(8,128)(2,1)}) %all-gather.10.cloned.1.call-update) | async-done | bytes 2097168 | tf_op jit(solution)/shard_map/all_gather | solution.py:68
  81.2 72.1 %all-gather.12.cloned.1.call-done = bf16[2048,512]{1,0:T(8,128)(2,1)} async-done(((bf16[64,512]{1,0:T(8,128)(2,1)}), bf16[2048,512]{1,0:T(8,128)(2,1)}) %all-gather.12.cloned.1.call-update) | async-done | bytes 2097168 | tf_op jit(solution)/shard_map/all_gather | solution.py:69
  153.3 72.1 %all-gather.8.cloned.1.call-done = bf16[2048,512]{1,0:T(8,128)(2,1)} async-done(((bf16[64,512]{1,0:T(8,128)(2,1)}), bf16[2048,512]{1,0:T(8,128)(2,1)}) %all-gather.8.cloned.1.call-update) | async-done | bytes 2097168 | tf_op jit(solution)/shard_map/all_gather | solution.py:67
  225.4 5.2 fusion.13
  234.6 62.8 %all-gather.14.cloned.1.call-done = bf16[2048,512]{1,0:T(8,128)(2,1)} async-done(((bf16[64,512]{1,0:T(8,128)(2,1)}), bf16[2048,512]{1,0:T(8,128)(2,1)}) %all-gather.14.cloned.1.call-update) | async-done | bytes 2097168 | tf_op jit(solution)/shard_map/all_gather | solution.py:114
  297.3 4.5 all-to-all-start
  302.0 300.7 %while.23 = (s32[]{:T(128)}, bf16[2,256,4,128]{3,1,2,0:T(8,128)(2,1)S(1)}, f32[256,4,128]{2,0,1:T(8,128)S(1)}, f32[4,256,1]{1,0,2:T(4,128)S(1)}, f32[4,256,1]{1,...) while((s32[]{:T(128)}, ...), condition=%wide.region_11.12_spmd.clone.clone, body=%wide.region_7.11_spmd.clone.clone.sunk | while | flops 136518656 | bytes 8333513 | solution.py:111
  302.0 5.2 collective-permute-start
  307.5 37.1 %collective-permute-done = bf16[2,256,4,128]{3,1,2,0:T(8,128)(2,1)S(1)} collective-permute-done((bf16[2,256,4,128]{3,1,2,0:T(8,128)(2,1)S(1)}, bf16[2,256,4,128]{3,1,2,0:T(8,128)(2,1)S(1)}, u32[]{:S(2)}, u32[]{:S(2)}) %collective-permute-start) | collective-permute-done | bytes 524320 | tf_op jit(solution)/shard_map/while/body/eval_jaxpr/ppermute | solution.py:16
  345.7 3.4 collective-permute-start
  349.4 19.8 %collective-permute-done = bf16[2,256,4,128]{3,1,2,0:T(8,128)(2,1)S(1)} collective-permute-done((bf16[2,256,4,128]{3,1,2,0:T(8,128)(2,1)S(1)}, bf16[2,256,4,128]{3,1,2,0:T(8,128)(2,1)S(1)}, u32[]{:S(2)}, u32[]{:S(2)}) %collective-permute-start) | collective-permute-done | bytes 524320 | tf_op jit(solution)/shard_map/while/body/eval_jaxpr/ppermute | solution.py:16
  370.2 2.6 collective-permute-start
  373.1 16.1 %collective-permute-done = bf16[2,256,4,128]{3,1,2,0:T(8,128)(2,1)S(1)} collective-permute-done((bf16[2,256,4,128]{3,1,2,0:T(8,128)(2,1)S(1)}, bf16[2,256,4,128]{3,1,2,0:T(8,128)(2,1)S(1)}, u32[]{:S(2)}, u32[]{:S(2)}) %collective-permute-start) | collective-permute-done | bytes 524320 | tf_op jit(solution)/shard_map/while/body/eval_jaxpr/ppermute | solution.py:16
  390.2 4.3 collective-permute-start
  394.8 11.5 %collective-permute-done = bf16[2,256,4,128]{3,1,2,0:T(8,128)(2,1)S(1)} collective-permute-done((bf16[2,256,4,128]{3,1,2,0:T(8,128)(2,1)S(1)}, bf16[2,256,4,128]{3,1,2,0:T(8,128)(2,1)S(1)}, u32[]{:S(2)}, u32[]{:S(2)}) %collective-permute-start) | collective-permute-done | bytes 524320 | tf_op jit(solution)/shard_map/while/body/eval_jaxpr/ppermute | solution.py:16
  407.4 4.9 collective-permute-start
  412.6 10.0 %collective-permute-done = bf16[2,256,4,128]{3,1,2,0:T(8,128)(2,1)S(1)} collective-permute-done((bf16[2,256,4,128]{3,1,2,0:T(8,128)(2,1)S(1)}, bf16[2,256,4,128]{3,1,2,0:T(8,128)(2,1)S(1)}, u32[]{:S(2)}, u32[]{:S(2)}) %collective-permute-start) | collective-permute-done | bytes 524320 | tf_op jit(solution)/shard_map/while/body/eval_jaxpr/ppermute | solution.py:16
  423.6 5.5 collective-permute-start
  429.4 8.5 collective-permute-done
  438.9 6.1 collective-permute-start
  445.3 6.9 collective-permute-done
  453.3 6.8 collective-permute-start
  460.3 6.4 collective-permute-done
  467.8 6.8 collective-permute-start
  474.9 6.4 collective-permute-done
  482.3 6.8 collective-permute-start
  489.4 6.9 collective-permute-done
  497.4 6.8 collective-permute-start
  504.5 8.0 collective-permute-done
  513.5 6.8 collective-permute-start
  520.6 9.1 %collective-permute-done = bf16[2,256,4,128]{3,1,2,0:T(8,128)(2,1)S(1)} collective-permute-done((bf16[2,256,4,128]{3,1,2,0:T(8,128)(2,1)S(1)}, bf16[2,256,4,128]{3,1,2,0:T(8,128)(2,1)S(1)}, u32[]{:S(2)}, u32[]{:S(2)}) %collective-permute-start) | collective-permute-done | bytes 524320 | tf_op jit(solution)/shard_map/while/body/eval_jaxpr/ppermute | solution.py:16
  530.8 6.8 collective-permute-start
  537.8 10.2 %collective-permute-done = bf16[2,256,4,128]{3,1,2,0:T(8,128)(2,1)S(1)} collective-permute-done((bf16[2,256,4,128]{3,1,2,0:T(8,128)(2,1)S(1)}, bf16[2,256,4,128]{3,1,2,0:T(8,128)(2,1)S(1)}, u32[]{:S(2)}, u32[]{:S(2)}) %collective-permute-start) | collective-permute-done | bytes 524320 | tf_op jit(solution)/shard_map/while/body/eval_jaxpr/ppermute | solution.py:16
  549.1 6.8 collective-permute-start
  556.1 11.4 %collective-permute-done = bf16[2,256,4,128]{3,1,2,0:T(8,128)(2,1)S(1)} collective-permute-done((bf16[2,256,4,128]{3,1,2,0:T(8,128)(2,1)S(1)}, bf16[2,256,4,128]{3,1,2,0:T(8,128)(2,1)S(1)}, u32[]{:S(2)}, u32[]{:S(2)}) %collective-permute-start) | collective-permute-done | bytes 524320 | tf_op jit(solution)/shard_map/while/body/eval_jaxpr/ppermute | solution.py:16
  568.6 6.8 collective-permute-start
  575.6 11.5 %collective-permute-done = bf16[2,256,4,128]{3,1,2,0:T(8,128)(2,1)S(1)} collective-permute-done((bf16[2,256,4,128]{3,1,2,0:T(8,128)(2,1)S(1)}, bf16[2,256,4,128]{3,1,2,0:T(8,128)(2,1)S(1)}, u32[]{:S(2)}, u32[]{:S(2)}) %collective-permute-start) | collective-permute-done | bytes 524320 | tf_op jit(solution)/shard_map/while/body/eval_jaxpr/ppermute | solution.py:16
  588.2 6.8 collective-permute-start
  595.3 6.4 collective-permute-done
  603.0 2.8 copy.43
  611.0 4.9 all-to-all-start.1
  616.1 65.2 %all-reduce.2.cloned.1.call-done = bf16[256,2048]{1,0:T(8,128)(2,1)} async-done(((bf16[256,2048]{1,0:T(8,128)(2,1)}), bf16[256,2048]{1,0:T(8,128)(2,1)}) %all-reduce.2.cloned.1.call-update) | async-done | bytes 1048592 | tf_op jit(solution)/shard_map/psum | solution.py:117
  683.3 88.9 %all-gather.16.cloned.1.call-done = bf16[2048,1024]{1,0:T(8,128)(2,1)} async-done(((bf16[64,1024]{1,0:T(8,128)(2,1)}), bf16[2048,1024]{1,0:T(8,128)(2,1)}) %all-gather.16.cloned.1.call-update) | async-done | bytes 4194320 | tf_op jit(solution)/shard_map/all_gather | solution.py:124
  772.2 82.9 %all-gather.18.cloned.1.call-done = bf16[2048,1024]{1,0:T(8,128)(2,1)} async-done(((bf16[64,1024]{1,0:T(8,128)(2,1)}), bf16[2048,1024]{1,0:T(8,128)(2,1)}) %all-gather.18.cloned.1.call-update) | async-done | bytes 4194320 | tf_op jit(solution)/shard_map/all_gather | solution.py:125
  855.1 7.2 fusion.9
  862.3 6.3 copy.44
  868.6 5.1 convolution_convert_fusion.1
  873.7 21.5 %reduce-scatter.2.cloned.1.call-done = bf16[64,2048]{1,0:T(8,128)(2,1)} async-done(((bf16[256,2048]{1,0:T(8,128)(2,1)}), bf16[64,2048]{1,0:T(8,128)(2,1)}) %reduce-scatter.2.cloned.1.call-update) | async-done | bytes 262160 | tf_op jit(solution)/shard_map/reduce_scatter | solution.py:132
  (240 shorter events, 43.5 us)
Async XLA Ops:
  6.5 9.7 %copy-start.1 = (s32[4]{0:T(128)S(1)}, s32[4]{0:T(128)}, u32[]{:S(2)}) copy-start(s32[4]{0:T(128)} %param.12) | copy-start | bytes 52
  6.5 9.0 %copy-start = (bf16[256,2048]{1,0:T(8,128)(2,1)S(1)}, bf16[256,2048]{1,0:T(8,128)(2,1)}, u32[]{:S(2)}) copy-start(bf16[256,2048]{1,0:T(8,128)(2,1)} %param.11) | copy-start | bytes 3145732
  6.5 74.6 %all-gather.10.cloned.1.call-start = ((), (), s32[]{:S(2)}) async-start(), calls=%async_computation.4 | async-start | bytes 2162688 | tf_op jit(solution)/shard_map/all_gather | solution.py:68
  8.2 145.1 %all-gather.12.cloned.1.call-start = ((), (), s32[]{:S(2)}) async-start(), calls=%async_computation.5 | async-start | bytes 2162688 | tf_op jit(solution)/shard_map/all_gather | solution.py:69
  9.8 215.6 %all-gather.8.cloned.1.call-start = ((), (), s32[]{:S(2)}) async-start(), calls=%async_computation.3 | async-start | bytes 2162688 | tf_op jit(solution)/shard_map/all_gather | solution.py:67
  11.4 285.9 %all-gather.14.cloned.1.call-start = ((), (), s32[]{:S(2)}) async-start(), calls=%async_computation.6 | async-start | bytes 2162688 | tf_op jit(solution)/shard_map/all_gather | solution.py:114
  13.0 598.0 %all-gather.20.cloned.1.call-start = ((), (), s32[]{:S(2)}) async-start(), calls=%async_computation.10 | async-start | bytes 4325376 | tf_op jit(solution)/shard_map/all_gather | solution.py:129
  297.3 305.6 %all-to-all-start = ((bf16[4,512,512]{2,1,0:T(8,128)(2,1)}), bf16[4,512,512]{2,1,0:T(8,128)(2,1)}, u32[]{:S(2)}, u32[]{:S(2)}) async-start(bf16[4,512,512]{2,1,0:T(8,128)(2,1)} %bitcast.88), calls=%async_computation | async-start | bytes 4194304 | tf_op jit(solution)/shard_map/all_to_all | solution.py:115
  301.8 379.4 %all-reduce.2.cloned.1.call-start = ((), (), s32[]{:S(2)}) async-start(), calls=%async_computation.7 | async-start | bytes 2097152 | tf_op jit(solution)/shard_map/psum | solution.py:117
  302.0 42.6 %collective-permute-start = (bf16[2,256,4,128]{3,1,2,0:T(8,128)(2,1)S(1)}, bf16[2,256,4,128]{3,1,2,0:T(8,128)(2,1)S(1)}, u32[]{:S(2)}, u32[]{:S(2)}) collective-permute-start(bf16[2,256,4,128]{3,1,2,0:T(8,128)(2,1)S(1)} %get-tuple-element.447), channel_id=1, source_target_pairs={{0,4},{4,8},{8,12},{12,16},{16,20},{20,24},{24,28},{28,32},{32,36}... | collective-permute-start | bytes 1572872 | tf_op jit(solution)/shard_map/while/body/eval_jaxpr/ppermute | solution.py:16
  345.7 23.5 %collective-permute-start = (bf16[2,256,4,128]{3,1,2,0:T(8,128)(2,1)S(1)}, bf16[2,256,4,128]{3,1,2,0:T(8,128)(2,1)S(1)}, u32[]{:S(2)}, u32[]{:S(2)}) collective-permute-start(bf16[2,256,4,128]{3,1,2,0:T(8,128)(2,1)S(1)} %get-tuple-element.447), channel_id=1, source_target_pairs={{0,4},{4,8},{8,12},{12,16},{16,20},{20,24},{24,28},{28,32},{32,36}... | collective-permute-start | bytes 1572872 | tf_op jit(solution)/shard_map/while/body/eval_jaxpr/ppermute | solution.py:16
  370.2 19.0 %collective-permute-start = (bf16[2,256,4,128]{3,1,2,0:T(8,128)(2,1)S(1)}, bf16[2,256,4,128]{3,1,2,0:T(8,128)(2,1)S(1)}, u32[]{:S(2)}, u32[]{:S(2)}) collective-permute-start(bf16[2,256,4,128]{3,1,2,0:T(8,128)(2,1)S(1)} %get-tuple-element.447), channel_id=1, source_target_pairs={{0,4},{4,8},{8,12},{12,16},{16,20},{20,24},{24,28},{28,32},{32,36}... | collective-permute-start | bytes 1572872 | tf_op jit(solution)/shard_map/while/body/eval_jaxpr/ppermute | solution.py:16
  390.2 16.1 %collective-permute-start = (bf16[2,256,4,128]{3,1,2,0:T(8,128)(2,1)S(1)}, bf16[2,256,4,128]{3,1,2,0:T(8,128)(2,1)S(1)}, u32[]{:S(2)}, u32[]{:S(2)}) collective-permute-start(bf16[2,256,4,128]{3,1,2,0:T(8,128)(2,1)S(1)} %get-tuple-element.447), channel_id=1, source_target_pairs={{0,4},{4,8},{8,12},{12,16},{16,20},{20,24},{24,28},{28,32},{32,36}... | collective-permute-start | bytes 1572872 | tf_op jit(solution)/shard_map/while/body/eval_jaxpr/ppermute | solution.py:16
  407.4 15.2 %collective-permute-start = (bf16[2,256,4,128]{3,1,2,0:T(8,128)(2,1)S(1)}, bf16[2,256,4,128]{3,1,2,0:T(8,128)(2,1)S(1)}, u32[]{:S(2)}, u32[]{:S(2)}) collective-permute-start(bf16[2,256,4,128]{3,1,2,0:T(8,128)(2,1)S(1)} %get-tuple-element.447), channel_id=1, source_target_pairs={{0,4},{4,8},{8,12},{12,16},{16,20},{20,24},{24,28},{28,32},{32,36}... | collective-permute-start | bytes 1572872 | tf_op jit(solution)/shard_map/while/body/eval_jaxpr/ppermute | solution.py:16
  423.6 14.3 %collective-permute-start = (bf16[2,256,4,128]{3,1,2,0:T(8,128)(2,1)S(1)}, bf16[2,256,4,128]{3,1,2,0:T(8,128)(2,1)S(1)}, u32[]{:S(2)}, u32[]{:S(2)}) collective-permute-start(bf16[2,256,4,128]{3,1,2,0:T(8,128)(2,1)S(1)} %get-tuple-element.447), channel_id=1, source_target_pairs={{0,4},{4,8},{8,12},{12,16},{16,20},{20,24},{24,28},{28,32},{32,36}... | collective-permute-start | bytes 1572872 | tf_op jit(solution)/shard_map/while/body/eval_jaxpr/ppermute | solution.py:16
  438.9 13.3 %collective-permute-start = (bf16[2,256,4,128]{3,1,2,0:T(8,128)(2,1)S(1)}, bf16[2,256,4,128]{3,1,2,0:T(8,128)(2,1)S(1)}, u32[]{:S(2)}, u32[]{:S(2)}) collective-permute-start(bf16[2,256,4,128]{3,1,2,0:T(8,128)(2,1)S(1)} %get-tuple-element.447), channel_id=1, source_target_pairs={{0,4},{4,8},{8,12},{12,16},{16,20},{20,24},{24,28},{28,32},{32,36}... | collective-permute-start | bytes 1572872 | tf_op jit(solution)/shard_map/while/body/eval_jaxpr/ppermute | solution.py:16
  453.3 13.4 %collective-permute-start = (bf16[2,256,4,128]{3,1,2,0:T(8,128)(2,1)S(1)}, bf16[2,256,4,128]{3,1,2,0:T(8,128)(2,1)S(1)}, u32[]{:S(2)}, u32[]{:S(2)}) collective-permute-start(bf16[2,256,4,128]{3,1,2,0:T(8,128)(2,1)S(1)} %get-tuple-element.447), channel_id=1, source_target_pairs={{0,4},{4,8},{8,12},{12,16},{16,20},{20,24},{24,28},{28,32},{32,36}... | collective-permute-start | bytes 1572872 | tf_op jit(solution)/shard_map/while/body/eval_jaxpr/ppermute | solution.py:16
  467.8 13.5 %collective-permute-start = (bf16[2,256,4,128]{3,1,2,0:T(8,128)(2,1)S(1)}, bf16[2,256,4,128]{3,1,2,0:T(8,128)(2,1)S(1)}, u32[]{:S(2)}, u32[]{:S(2)}) collective-permute-start(bf16[2,256,4,128]{3,1,2,0:T(8,128)(2,1)S(1)} %get-tuple-element.447), channel_id=1, source_target_pairs={{0,4},{4,8},{8,12},{12,16},{16,20},{20,24},{24,28},{28,32},{32,36}... | collective-permute-start | bytes 1572872 | tf_op jit(solution)/shard_map/while/body/eval_jaxpr/ppermute | solution.py:16
  482.3 14.0 %collective-permute-start = (bf16[2,256,4,128]{3,1,2,0:T(8,128)(2,1)S(1)}, bf16[2,256,4,128]{3,1,2,0:T(8,128)(2,1)S(1)}, u32[]{:S(2)}, u32[]{:S(2)}) collective-permute-start(bf16[2,256,4,128]{3,1,2,0:T(8,128)(2,1)S(1)} %get-tuple-element.447), channel_id=1, source_target_pairs={{0,4},{4,8},{8,12},{12,16},{16,20},{20,24},{24,28},{28,32},{32,36}... | collective-permute-start | bytes 1572872 | tf_op jit(solution)/shard_map/while/body/eval_jaxpr/ppermute | solution.py:16
  497.4 15.1 %collective-permute-start = (bf16[2,256,4,128]{3,1,2,0:T(8,128)(2,1)S(1)}, bf16[2,256,4,128]{3,1,2,0:T(8,128)(2,1)S(1)}, u32[]{:S(2)}, u32[]{:S(2)}) collective-permute-start(bf16[2,256,4,128]{3,1,2,0:T(8,128)(2,1)S(1)} %get-tuple-element.447), channel_id=1, source_target_pairs={{0,4},{4,8},{8,12},{12,16},{16,20},{20,24},{24,28},{28,32},{32,36}... | collective-permute-start | bytes 1572872 | tf_op jit(solution)/shard_map/while/body/eval_jaxpr/ppermute | solution.py:16
  513.5 16.2 %collective-permute-start = (bf16[2,256,4,128]{3,1,2,0:T(8,128)(2,1)S(1)}, bf16[2,256,4,128]{3,1,2,0:T(8,128)(2,1)S(1)}, u32[]{:S(2)}, u32[]{:S(2)}) collective-permute-start(bf16[2,256,4,128]{3,1,2,0:T(8,128)(2,1)S(1)} %get-tuple-element.447), channel_id=1, source_target_pairs={{0,4},{4,8},{8,12},{12,16},{16,20},{20,24},{24,28},{28,32},{32,36}... | collective-permute-start | bytes 1572872 | tf_op jit(solution)/shard_map/while/body/eval_jaxpr/ppermute | solution.py:16
  530.8 17.3 %collective-permute-start = (bf16[2,256,4,128]{3,1,2,0:T(8,128)(2,1)S(1)}, bf16[2,256,4,128]{3,1,2,0:T(8,128)(2,1)S(1)}, u32[]{:S(2)}, u32[]{:S(2)}) collective-permute-start(bf16[2,256,4,128]{3,1,2,0:T(8,128)(2,1)S(1)} %get-tuple-element.447), channel_id=1, source_target_pairs={{0,4},{4,8},{8,12},{12,16},{16,20},{20,24},{24,28},{28,32},{32,36}... | collective-permute-start | bytes 1572872 | tf_op jit(solution)/shard_map/while/body/eval_jaxpr/ppermute | solution.py:16
  549.1 18.5 %collective-permute-start = (bf16[2,256,4,128]{3,1,2,0:T(8,128)(2,1)S(1)}, bf16[2,256,4,128]{3,1,2,0:T(8,128)(2,1)S(1)}, u32[]{:S(2)}, u32[]{:S(2)}) collective-permute-start(bf16[2,256,4,128]{3,1,2,0:T(8,128)(2,1)S(1)} %get-tuple-element.447), channel_id=1, source_target_pairs={{0,4},{4,8},{8,12},{12,16},{16,20},{20,24},{24,28},{28,32},{32,36}... | collective-permute-start | bytes 1572872 | tf_op jit(solution)/shard_map/while/body/eval_jaxpr/ppermute | solution.py:16
  568.6 18.6 %collective-permute-start = (bf16[2,256,4,128]{3,1,2,0:T(8,128)(2,1)S(1)}, bf16[2,256,4,128]{3,1,2,0:T(8,128)(2,1)S(1)}, u32[]{:S(2)}, u32[]{:S(2)}) collective-permute-start(bf16[2,256,4,128]{3,1,2,0:T(8,128)(2,1)S(1)} %get-tuple-element.447), channel_id=1, source_target_pairs={{0,4},{4,8},{8,12},{12,16},{16,20},{20,24},{24,28},{28,32},{32,36}... | collective-permute-start | bytes 1572872 | tf_op jit(solution)/shard_map/while/body/eval_jaxpr/ppermute | solution.py:16
  588.2 13.5 %collective-permute-start = (bf16[2,256,4,128]{3,1,2,0:T(8,128)(2,1)S(1)}, bf16[2,256,4,128]{3,1,2,0:T(8,128)(2,1)S(1)}, u32[]{:S(2)}, u32[]{:S(2)}) collective-permute-start(bf16[2,256,4,128]{3,1,2,0:T(8,128)(2,1)S(1)} %get-tuple-element.447), channel_id=1, source_target_pairs={{0,4},{4,8},{8,12},{12,16},{16,20},{20,24},{24,28},{28,32},{32,36}... | collective-permute-start | bytes 1572872 | tf_op jit(solution)/shard_map/while/body/eval_jaxpr/ppermute | solution.py:16
  607.6 164.6 %all-gather.16.cloned.1.call-start = ((), (), s32[]{:S(2)}) async-start(), calls=%async_computation.8 | async-start | bytes 4325376 | tf_op jit(solution)/shard_map/all_gather | solution.py:124
  609.3 245.8 %all-gather.18.cloned.1.call-start = ((), (), s32[]{:S(2)}) async-start(), calls=%async_computation.9 | async-start | bytes 4325376 | tf_op jit(solution)/shard_map/all_gather | solution.py:125
  611.0 251.3 %all-to-all-start.1 = ((bf16[4,1024,512]{2,1,0:T(8,128)(2,1)}), bf16[4,1024,512]{2,1,0:T(8,128)(2,1)}, u32[]{:S(2)}, u32[]{:S(2)}) async-start(bf16[4,1024,512]{2,1,0:T(8,128)(2,1)} %bitcast.82), calls=%async_computation.1 | async-start | bytes 8388608 | tf_op jit(solution)/shard_map/all_to_all | solution.py:131
  615.9 279.3 %reduce-scatter.2.cloned.1.call-start = ((), (), s32[]{:S(2)}) async-start(), calls=%async_computation.11 | async-start | bytes 1310720 | tf_op jit(solution)/shard_map/reduce_scatter | solution.py:132
Sparse Core Ops, SparseCore 0:
  10.5 70.6 all-gather.9
  84.3 68.9 all-gather.11
  156.4 68.9 all-gather.7
  228.4 68.9 all-gather.13
  300.3 90.5 all-gather.19
  607.7 73.4 all-reduce.1
  684.8 87.3 all-gather.15
  775.7 79.3 all-gather.17
  873.8 21.3 reduce-scatter.1
where the time goes:
time: 906 us; the launch traced here: 903 us
  waiting for transfers between devices  716 us (79%)
  starting transfers between devices  103 us (11%)
  matrix products  32.3 us (4%)
  other arithmetic  24.8 us (3%)
  between operations  13.4 us (1%)
  local copies, waits for them, and re-layouts  12.3 us (1%)
    ppermute x16, waiting for transfers between devices, passed_along(): lax.ppermute(value, axis, [(source, source + steps) for source in range(i...  186 us
    ppermute x16, starting transfers between devices, passed_along(): lax.ppermute(value, axis, [(source, source + steps) for source in range(i...  93.3 us
    all_gather x1, waiting for transfers between devices, on_device(): lax.all_gather(w_gate.astype(half_type), 'dp', axis=0, tiled=True)  88.9 us
    all_gather x1, waiting for transfers between devices, on_device(): lax.all_gather(w_up.astype(half_type), 'dp', axis=0, tiled=True)  82.9 us
    all_gather x1, waiting for transfers between devices, on_device(): lax.all_gather(w_query.astype(half_type), 'dp', axis=0, tiled=True)  72.1 us
    all_gather x1, waiting for transfers between devices, on_device(): lax.all_gather(w_value.astype(half_type), 'dp', axis=0, tiled=True)  72.1 us
    psum x1, waiting for transfers between devices, on_device(): lax.psum(partial_out.astype(jnp.bfloat16), 'mp').astype(jnp.float32)  65.2 us
    all_gather x1, waiting for transfers between devices, on_device(): lax.all_gather(w_key.astype(half_type), 'dp', axis=0, tiled=True)  64.1 us
  transfers between devices with their start and end apart: 27, of which 24 were waited for; matrix products, arithmetic and copies ran while one was open for 6% of the time, Pallas kernels for 0%

commit v1 on v0

v1 whole, which is shorter than its diff:
```python
import jax
import jax.numpy as jnp
from jax import lax
from jax.sharding import PartitionSpec as P

HEAD = 128


epsilon = 1e-05
theta_base = 10000.0


def shifted(value, axis, steps):
    count = lax.axis_size(axis)
    return lax.ppermute(value, axis, [(source, source + steps) for source in range(count - steps)])


def gather_by_exchange(value, axis):
    count = lax.axis_size(axis)
    copies = jnp.broadcast_to(value[None], (count,) + value.shape)
    got = lax.all_to_all(copies, axis, 0, 0, tiled=True)
    return got.reshape((count * value.shape[0],) + value.shape[1:])


def scatter_sum(value, axis):
    count = lax.axis_size(axis)
    pieces = value.reshape((count, value.shape[0] // count) + value.shape[1:])
    got = lax.all_to_all(pieces, axis, 0, 0, tiled=True)
    return jnp.sum(got.astype(jnp.float32), axis=0)


def layer_norm(rows):
    values = rows.astype(jnp.float32)
    centre = jnp.mean(values, axis=-1, keepdims=True)
    spread = jnp.mean(jnp.square(values - centre), axis=-1, keepdims=True)
    return (values - centre) * lax.rsqrt(spread + epsilon)


def prompt_coords(first, count, lengths):
    where = first + jnp.arange(count)
    ends = jnp.cumsum(lengths)
    passed = (ends[None, :] <= where[:, None]).astype(jnp.int32)
    prompt = jnp.sum(passed, axis=1)
    offset = where - jnp.sum(passed * lengths[None, :], axis=1)
    prompt = jnp.where(where < 0, -1, prompt)
    return (prompt, offset, where)


def rotate(values, offset):
    half = values.shape[-1] // 2
    freqs = jnp.power(theta_base, -jnp.arange(half, dtype=jnp.float32) * 2.0 / values.shape[-1])
    angles = offset.astype(jnp.float32)[:, None] * freqs[None, :]
    cosine = jnp.cos(angles)[:, None, :]
    sine = jnp.sin(angles)[:, None, :]
    first_half = values[..., :half]
    second_half = values[..., half:]
    return jnp.concatenate(
        [first_half * cosine - second_half * sine, second_half * cosine + first_half * sine],
        axis=-1,
    )


def on_device(tokens, lengths, w_query, w_key, w_value, w_out, w_gate, w_up, w_down):
    half_type = jnp.bfloat16
    rows = tokens.shape[0]
    narrow = w_query.shape[1]
    units = w_gate.shape[1]
    shard_rows = w_query.shape[0]
    heads_dev = narrow // HEAD
    dp_index = lax.axis_index("dp")
    mp_index = lax.axis_index("mp")
    mp_size = lax.axis_size("mp")
    reach = lax.axis_size("dp") // 2

    qkv_shard = jnp.concatenate(
        [w.astype(half_type) for w in (w_query, w_key, w_value)], axis=1
    )
    rest_shard = jnp.concatenate(
        [
            w_out.astype(half_type),
            w_gate.astype(half_type),
            w_up.astype(half_type),
            w_down.astype(half_type).reshape(shard_rows, -1),
        ],
        axis=1,
    )
    qkv_full = gather_by_exchange(qkv_shard, "dp")
    rest_full = lax.all_gather(rest_shard, "dp", axis=0, tiled=True)

    normed = layer_norm(tokens).astype(half_type)
    joined = jnp.dot(normed, qkv_full, preferred_element_type=jnp.float32)
    q_prompt, q_offset, q_where = prompt_coords(dp_index * rows, rows, lengths)
    shaped = joined.reshape(rows, 3, heads_dev, HEAD)
    query = rotate(shaped[:, 0], q_offset).astype(half_type)
    keys = rotate(shaped[:, 1], q_offset).astype(half_type)
    values = shaped[:, 2].astype(half_type)
    own_first = dp_index * rows
    scale = 1.0 / HEAD**0.5

    def online_step(state, pair, first):
        accum, total, top = state
        k_prompt, k_offset, k_where = prompt_coords(first, rows, lengths)
        scores = (
            jnp.einsum("qhd,khd->hqk", query, pair[0], preferred_element_type=jnp.float32) * scale
        )
        allowed = (q_prompt[:, None] == k_prompt[None, :]) & (k_where[None, :] <= q_where[:, None])
        scores = jnp.where(allowed[None], scores, -jnp.inf)
        new_top = jnp.maximum(top, jnp.max(scores, axis=-1, keepdims=True))
        fade = jnp.exp(top - new_top)
        weights = jnp.exp(scores - new_top)
        probs = weights.astype(half_type)
        product = jnp.einsum("hqk,khd->qhd", probs, pair[1], preferred_element_type=jnp.float32)
        accum = accum * jnp.transpose(fade, (1, 0, 2)) + product
        total = total * fade + jnp.sum(weights, axis=-1, keepdims=True)
        return (accum, total, new_top)

    state = (
        jnp.zeros((rows, heads_dev, HEAD), jnp.float32),
        jnp.zeros((heads_dev, rows, 1), jnp.float32),
        jnp.full((heads_dev, rows, 1), -jnp.inf, jnp.float32),
    )
    held = jnp.stack((keys, values))[None]
    farthest = shifted(held, "dp", reach)
    state = online_step(state, held[0], own_first)
    done = 1
    span = 1
    while span < reach:
        arrived = shifted(held, "dp", span)
        for slot in range(arrived.shape[0]):
            state = online_step(state, arrived[slot], own_first - (done + slot) * rows)
        done += arrived.shape[0]
        held = jnp.concatenate([held, arrived], axis=0)
        span *= 2
    state = online_step(state, farthest[0], own_first - reach * rows)
    accum, total, top = state
    context = (accum / jnp.transpose(total, (1, 0, 2))).astype(half_type).reshape(rows, narrow)

    out_cols = rest_full[:, :narrow]
    server_out = lax.all_to_all(out_cols, "mp", split_axis=0, concat_axis=1, tiled=True)
    partial_out = jnp.dot(context, server_out, preferred_element_type=jnp.float32)
    attended = scatter_sum(partial_out.astype(half_type), "mp")
    slab = rows // mp_size
    own_tokens = lax.dynamic_slice_in_dim(tokens, mp_index * slab, slab, 0)
    mixed = (own_tokens.astype(jnp.float32) + attended).astype(half_type)
    normed_own = layer_norm(mixed).astype(half_type)
    normed_two = gather_by_exchange(normed_own, "mp")

    gate = jnp.dot(normed_two, rest_full[:, narrow : narrow + units], preferred_element_type=jnp.float32)
    upper = jnp.dot(
        normed_two, rest_full[:, narrow + units : narrow + 2 * units], preferred_element_type=jnp.float32
    )
    hidden = (jax.nn.silu(gate) * upper).astype(half_type)
    down_cols = rest_full[:, narrow + 2 * units :].reshape(-1, narrow)
    server_down = lax.all_to_all(down_cols, "mp", split_axis=0, concat_axis=1, tiled=True)
    partial_down = jnp.dot(hidden, server_down, preferred_element_type=jnp.float32)
    share = scatter_sum(partial_down.astype(half_type), "mp")
    return (mixed.astype(jnp.float32) + share).astype(half_type)


def solution(mesh):
    in_specs = (
        P("dp", None),
        P(),
        P("dp", "mp"),
        P("dp", "mp"),
        P("dp", "mp"),
        P("dp", "mp"),
        P("dp", "mp"),
        P("dp", "mp"),
        P("dp", "mp"),
    )
    out_specs = P(("dp", "mp"), None)
    return jax.shard_map(
        on_device, mesh=mesh, in_specs=in_specs, out_specs=out_specs, check_vma=False
    )
```

time: 906 us -> 566 us (0.62)
  waiting for transfers between devices: 716 us -> 347 us
  local copies, waits for them, and re-layouts: 12.3 us -> 37 us
  starting transfers between devices: 103 us -> 82.4 us
  blocking collectives: 0 us -> 16.9 us
  matrix products: 32.3 us -> 46.3 us
    all_gather x7 -> x1, waiting for transfers between devices: 443 us -> 0.01 us  [on_device(): rest_full = lax.all_gather(rest_shard, 'dp', axis=0, tiled=True)]
    all_to_all x2 -> x5, waiting for transfers between devices: 0.01 us -> 157 us  [the longest x2 91.8 us: gather_by_exchange(): got = lax.all_to_all(copies, axis, 0, 0, tiled=True)]
    psum x1 -> x0, waiting for transfers between devices: 65.2 us -> none  [on_device(): lax.psum(partial_out.astype(jnp.bfloat16), 'mp').astype(jnp.float32)]
    ppermute x16 -> x5, starting transfers between devices: 93.3 us -> 41.9 us  [shifted(): lax.ppermute(value, axis, [(source, source + steps) for source in range(c...]
    all_to_all x2 -> x5, starting transfers between devices: 9.31 us -> 40.5 us  [the longest x1 17.4 us: on_device(): lax.all_to_all(out_cols, 'mp', split_axis=0, concat_axis=1, tiled=True)]
    reduce_scatter x1 -> x0, waiting for transfers between devices: 21.5 us -> none  [on_device(): lax.psum_scatter(jnp.dot(hidden, server_down, preferred_element_type=jnp....]
    all_to_all x0 -> x1, blocking collectives: none -> 16.9 us  [scatter_sum(): got = lax.all_to_all(pieces, axis, 0, 0, tiled=True)]
    dot_general x17, matrix products: 7.65 us -> 21.6 us  [online_step(): jnp.einsum('hqk,khd->qhd', probs, pair[1], preferred_element_type=jnp.flo...]
  transfers between devices with their start and end apart: 27 -> 11, of which waited for: 24 -> 9; matrix products, arithmetic and copies ran while one was open for 6% -> 12% of each run, Pallas kernels for 0% -> 0%
where the time goes in v1:
time: 566 us; the launch traced here: 563 us
  waiting for transfers between devices  347 us (61%)
  starting transfers between devices  82.4 us (15%)
  matrix products  46.3 us (8%)
  local copies, waits for them, and re-layouts  37 us (7%)
  other arithmetic  18.4 us (3%)
  blocking collectives  16.9 us (3%)
  between operations  14.2 us (3%)
    ppermute x5, waiting for transfers between devices, shifted(): lax.ppermute(value, axis, [(source, source + steps) for source in range(c...  190 us
    all_to_all x2, waiting for transfers between devices, gather_by_exchange(): got = lax.all_to_all(copies, axis, 0, 0, tiled=True)  91.8 us
    all_to_all x1, waiting for transfers between devices, on_device(): lax.all_to_all(down_cols, 'mp', split_axis=0, concat_axis=1, tiled=True)  46.5 us
    ppermute x5, starting transfers between devices, shifted(): lax.ppermute(value, axis, [(source, source + steps) for source in range(c...  41.9 us
    dot_general x17, matrix products, online_step(): jnp.einsum('hqk,khd->qhd', probs, pair[1], preferred_element_type=jnp.flo...  21.6 us
    all_to_all x1, starting transfers between devices, on_device(): lax.all_to_all(out_cols, 'mp', split_axis=0, concat_axis=1, tiled=True)  17.4 us
    all_to_all x1, blocking collectives, scatter_sum(): got = lax.all_to_all(pieces, axis, 0, 0, tiled=True)  16.9 us
    all_to_all x1, waiting for transfers between devices, on_device(): lax.all_to_all(out_cols, 'mp', split_axis=0, concat_axis=1, tiled=True)  16.3 us
  transfers between devices with their start and end apart: 11, of which 9 were waited for; matrix products, arithmetic and copies ran while one was open for 12% of the time, Pallas kernels for 0%

profile of v1, /device:TPU:4, one launch (start us, length us, event | category | flops | bytes accessed | tf_op | source)
XLA Modules:
  0.0 562.5 jit_solution(8692699569046391821)
XLA Ops:
  14.0 3.4 broadcast_in_dim.142
  17.4 11.2 %all-to-all-start = ((bf16[32,64,1536]{2,1,0:T(8,128)(2,1)}), bf16[32,64,1536]{2,1,0:T(8,128)(2,1)}, u32[]{:S(2)}, u32[]{:S(2)}) async-start(bf16[32,64,1536]{2,1,0:T(8,128)(2,1)} %broadcast_in_dim.142), calls=%async_computation | async-start | bytes 12582912 | tf_op jit(solution)/shard_map/all_to_all | solution.py:21
  30.3 83.7 %all-to-all-done = bf16[32,64,1536]{2,1,0:T(8,128)(2,1)} async-done(((bf16[32,64,1536]{2,1,0:T(8,128)(2,1)}), bf16[32,64,1536]{2,1,0:T(8,128)(2,1)}, u32[]{:S(2)}, u32[]{:S(2)}) %all-to-all-start) | async-done | bytes 6291488 | tf_op jit(solution)/shard_map/all_to_all | solution.py:21
  114.0 8.8 %copy.168 = bf16[1536,2048]{1,0:T(8,128)(2,1)} copy(bf16[1536,2048]{0,1:T(8,128)(2,1)} %bitcast.5) | data formatting | bytes 12582912 | tf_op jit(solution)/shard_map/dot_general | solution.py:91
  122.8 4.8 fusion.67
  127.9 18.5 %collective-permute-start = (bf16[1,2,256,4,128]{2,4,3,1,0:T(8,128)(2,1)S(1)}, bf16[1,2,256,4,128]{2,4,3,1,0:T(8,128)(2,1)S(1)}, u32[]{:S(2)}, u32[]{:S(2)}) collective-permute-start(bf16[1,2,256,4,128]{2,4,3,1,0:T(8,128)(2,1)S(1)} %maximum_bitcast_fusion), channel_id=1, source_target_pairs={{0,4},{4,8},{8,12},{12,16},{16,20},{20,24},{24,28},{28,32},{32,36}... | collective-permute-start | bytes 1572872 | tf_op jit(solution)/shard_map/ppermute | solution.py:15
  146.4 11.6 %collective-permute-done = bf16[1,2,256,4,128]{2,4,3,1,0:T(8,128)(2,1)S(1)} collective-permute-done((bf16[1,2,256,4,128]{2,4,3,1,0:T(8,128)(2,1)S(1)}, bf16[1,2,256,4,128]{2,4,3,1,0:T(8,128)(2,1)S(1)}, u32[]{:S(2)}, u32[]{:S(2)}) %collective-permute-start) | collective-permute-done | bytes 524320 | tf_op jit(solution)/shard_map/ppermute | solution.py:15
  158.1 1.4 collective-permute-start.1
  159.4 41.6 %collective-permute-done.1 = bf16[2,2,256,4,128]{2,4,3,1,0:T(8,128)(2,1)S(1)} collective-permute-done((bf16[2,2,256,4,128]{2,4,3,1,0:T(8,128)(2,1)S(1)}, bf16[2,2,256,4,128]{2,4,3,1,0:T(8,128)(2,1)S(1)}, u32[]{:S(2)}, u32[]{:S(2)}) %collective-permute-start.1) | collective-permute-done | bytes 1048608 | tf_op jit(solution)/shard_map/ppermute | solution.py:15
  201.2 6.1 %collective-permute-start.2 = (bf16[4,2,256,4,128]{2,4,3,1,0:T(8,128)(2,1)S(1)}, bf16[4,2,256,4,128]{2,4,3,1,0:T(8,128)(2,1)S(1)}, u32[]{:S(2)}, u32[]{:S(2)}) collective-permute-start(bf16[4,2,256,4,128]{2,4,3,1,0:T(8,128)(2,1)S(1)} %pad_maximum_fusion.1), channel_id=1, source_target_pairs={{0,16},{4,20},{8,24},{12,28},{16,32},{20,36},{24,40},{28,44},{32,4... | collective-permute-start | bytes 6291464 | tf_op jit(solution)/shard_map/ppermute | solution.py:15
  207.4 52.1 %collective-permute-done.2 = bf16[4,2,256,4,128]{2,4,3,1,0:T(8,128)(2,1)S(1)} collective-permute-done((bf16[4,2,256,4,128]{2,4,3,1,0:T(8,128)(2,1)S(1)}, bf16[4,2,256,4,128]{2,4,3,1,0:T(8,128)(2,1)S(1)}, u32[]{:S(2)}, u32[]{:S(2)}) %collective-permute-start.2) | collective-permute-done | bytes 2097184 | tf_op jit(solution)/shard_map/ppermute | solution.py:15
  259.9 10.2 %collective-permute-start.3 = (bf16[8,2,256,4,128]{2,4,3,1,0:T(8,128)(2,1)S(1)}, bf16[8,2,256,4,128]{2,4,3,1,0:T(8,128)(2,1)S(1)}, u32[]{:S(2)}, u32[]{:S(2)}) collective-permute-start(bf16[8,2,256,4,128]{2,4,3,1,0:T(8,128)(2,1)S(1)} %pad_maximum_fusion), channel_id=1, source_target_pairs={{0,32},{4,36},{8,40},{12,44},{16,48},{20,52},{24,56},{28,60},{32,6... | collective-permute-start | bytes 12582920 | tf_op jit(solution)/shard_map/ppermute | solution.py:15
  271.8 5.7 %collective-permute-start.4 = (bf16[1,2,256,4,128]{2,4,3,1,0:T(8,128)(2,1)S(1)}, bf16[1,2,256,4,128]{2,4,3,1,0:T(8,128)(2,1)S(1)}, u32[]{:S(2)}, u32[]{:S(2)}) collective-permute-start(bf16[1,2,256,4,128]{2,4,3,1,0:T(8,128)(2,1)S(1)} %maximum_bitcast_fusion), channel_id=1, source_target_pairs={{0,64},{4,68},{8,72},{12,76},{16,80},{20,84},{24,88},{28,92},{32,9... | collective-permute-start | bytes 1572872 | tf_op jit(solution)/shard_map/ppermute | solution.py:15
  278.4 84.8 %collective-permute-done.4 = bf16[1,2,256,4,128]{2,4,3,1,0:T(8,128)(2,1)S(1)} collective-permute-done((bf16[1,2,256,4,128]{2,4,3,1,0:T(8,128)(2,1)S(1)}, bf16[1,2,256,4,128]{2,4,3,1,0:T(8,128)(2,1)S(1)}, u32[]{:S(2)}, u32[]{:S(2)}) %collective-permute-start.4) | collective-permute-done | bytes 524320 | tf_op jit(solution)/shard_map/ppermute | solution.py:15
  363.3 1.4 fusion.195
  365.4 1.2 fusion.32
  374.1 1.1 convolution_bitcast_fusion.13
  375.2 1.1 convolution_bitcast_fusion.12
  377.4 1.2 convolution_bitcast_fusion.10
  378.6 1.1 convolution_bitcast_fusion.9
  379.8 1.1 convolution_bitcast_fusion.8
  382.0 1.1 convolution_bitcast_fusion.6
  383.1 1.2 convolution_bitcast_fusion.5
  385.4 1.1 convolution_bitcast_fusion.3
  386.5 3.0 slice.285
  389.5 17.4 %all-to-all-start.1 = ((bf16[4,512,512]{2,1,0:T(8,128)(2,1)}), bf16[4,512,512]{2,1,0:T(8,128)(2,1)S(1)}, u32[]{:S(2)}, u32[]{:S(2)}) async-start(bf16[4,512,512]{2,1,0:T(8,128)(2,1)} %bitcast.604), calls=%async_computation.1 | async-start | bytes 4194304 | tf_op jit(solution)/shard_map/all_to_all | solution.py:139
  407.0 1.5 fusion.105
  408.6 2.1 convolution_bitcast_fusion.2
  410.8 1.6 convolution_bitcast_fusion.1
  412.4 1.3 convolution_bitcast_fusion
  413.8 2.6 fusion.65
  416.4 16.3 %all-to-all-done.1 = bf16[4,512,512]{2,1,0:T(8,128)(2,1)S(1)} async-done(((bf16[4,512,512]{2,1,0:T(8,128)(2,1)}), bf16[4,512,512]{2,1,0:T(8,128)(2,1)S(1)}, u32[]{:S(2)}, u32[]{:S(2)}) %all-to-all-start.1) | async-done | bytes 2097184 | tf_op jit(solution)/shard_map/all_to_all | solution.py:139
  432.7 2.4 copy.220
  435.0 3.4 convolution_convert_fusion
  438.4 3.5 all-to-all-start.2
  441.9 4.6 slice.288
  446.5 7.1 %all_to_all.47 = bf16[4,1024,512]{2,1,0:T(8,128)(2,1)} reshape(bf16[2048,1024]{1,0:T(8,128)(2,1)} %slice.288) | data formatting | bytes 8388608 | tf_op jit(solution)/shard_map/all_to_all | solution.py:154
  453.6 2.7 all-to-all-done.2
  456.3 4.8 all-to-all-start.4
  461.4 1.1 convert_reduce_fusion.3
  462.9 46.5 %all-to-all-done.4 = bf16[4,1024,512]{2,1,0:T(8,128)(2,1)} async-done(((bf16[4,1024,512]{2,1,0:T(8,128)(2,1)}), bf16[4,1024,512]{2,1,0:T(8,128)(2,1)}, u32[]{:S(2)}, u32[]{:S(2)}) %all-to-all-start.4) | async-done | bytes 4194336 | tf_op jit(solution)/shard_map/all_to_all | solution.py:154
  509.4 1.1 broadcast_in_dim.162
  510.6 3.5 all-to-all-start.3
  514.1 6.3 %copy.221 = bf16[1024,4,512]{0,2,1:T(8,128)(2,1)} copy(bf16[1024,4,512]{2,0,1:T(8,128)(2,1)} %bitcast.139) | data formatting | bytes 8388608 | tf_op jit(solution)/shard_map/all_to_all | solution.py:154
  520.4 8.1 %all-to-all-done.3 = bf16[4,64,2048]{2,1,0:T(8,128)(2,1)S(1)} async-done(((bf16[4,64,2048]{2,1,0:T(8,128)(2,1)}), bf16[4,64,2048]{2,1,0:T(8,128)(2,1)S(1)}, u32[]{:S(2)}, u32[]{:S(2)}) %all-to-all-start.3) | async-done | bytes 1048608 | tf_op jit(solution)/shard_map/all_to_all | solution.py:21
  528.5 3.4 fusion.2
  531.9 5.9 %convolution_convert_fusion.1 = bf16[256,2048]{1,0:T(8,128)(2,1)S(1)} fusion(bf16[1024,2048]{0,1:T(8,128)(2,1)} %bitcast.607, bf16[256,2048]{1,0:T(8,128)(2,1)S(1)} %bitcast.609, bf16[2048,3584]{1,0:T(8,128)(2,1)} %all-gather.2.cloned.1.call-done, f32[256,1024]{1,0:T(8,128)S(1)} %fusion.2), kind=kOutput, calls=%fused_computation.8 | convolution fusion | flops 2149580800 | bytes 11534336 | tf_op jit(solution)/shard_map/dot_general | solution.py:155
  537.9 16.9 %all_to_all.58 = bf16[4,64,2048]{2,1,0:T(8,128)(2,1)S(1)} all-to-all(bf16[4,64,2048]{2,1,0:T(8,128)(2,1)S(1)} %bitcast.610), channel_id=1, replica_groups=mesh['dp'=32,'mp'=4] {'mp'}, dimensions={0} | all-to-all | bytes 2097152 | tf_op jit(solution)/shard_map/all_to_all | solution.py:28
  (143 shorter events, 25.5 us)
Async XLA Ops:
  6.5 380.0 %all-gather.2.cloned.1.call-start = ((), (), s32[]{:S(2)}) async-start(), calls=%async_computation.6 | async-start | bytes 15138816 | tf_op jit(solution)/shard_map/all_gather | solution.py:88
  17.4 11.3 %copy-start.16 = (s32[4]{0:T(128)S(1)}, s32[4]{0:T(128)}, u32[]{:S(2)}) copy-start(s32[4]{0:T(128)} %param.10) | copy-start | bytes 52
  17.4 11.8 %copy-start = (bf16[256,2048]{1,0:T(8,128)(2,1)S(1)}, bf16[256,2048]{1,0:T(8,128)(2,1)}, u32[]{:S(2)}) copy-start(bf16[256,2048]{1,0:T(8,128)(2,1)} %param.9) | copy-start | bytes 3145732
  17.4 96.5 %all-to-all-start = ((bf16[32,64,1536]{2,1,0:T(8,128)(2,1)}), bf16[32,64,1536]{2,1,0:T(8,128)(2,1)}, u32[]{:S(2)}, u32[]{:S(2)}) async-start(bf16[32,64,1536]{2,1,0:T(8,128)(2,1)} %broadcast_in_dim.142), calls=%async_computation | async-start | bytes 12582912 | tf_op jit(solution)/shard_map/all_to_all | solution.py:21
  127.9 30.1 %collective-permute-start = (bf16[1,2,256,4,128]{2,4,3,1,0:T(8,128)(2,1)S(1)}, bf16[1,2,256,4,128]{2,4,3,1,0:T(8,128)(2,1)S(1)}, u32[]{:S(2)}, u32[]{:S(2)}) collective-permute-start(bf16[1,2,256,4,128]{2,4,3,1,0:T(8,128)(2,1)S(1)} %maximum_bitcast_fusion), channel_id=1, source_target_pairs={{0,4},{4,8},{8,12},{12,16},{16,20},{20,24},{24,28},{28,32},{32,36}... | collective-permute-start | bytes 1572872 | tf_op jit(solution)/shard_map/ppermute | solution.py:15
  158.1 42.9 %collective-permute-start.1 = (bf16[2,2,256,4,128]{2,4,3,1,0:T(8,128)(2,1)S(1)}, bf16[2,2,256,4,128]{2,4,3,1,0:T(8,128)(2,1)S(1)}, u32[]{:S(2)}, u32[]{:S(2)}) collective-permute-start(bf16[2,2,256,4,128]{2,4,3,1,0:T(8,128)(2,1)S(1)} %pad_maximum_fusion.2), channel_id=1, source_target_pairs={{0,8},{4,12},{8,16},{12,20},{16,24},{20,28},{24,32},{28,36},{32,40... | collective-permute-start | bytes 3145736 | tf_op jit(solution)/shard_map/ppermute | solution.py:15
  201.2 58.3 %collective-permute-start.2 = (bf16[4,2,256,4,128]{2,4,3,1,0:T(8,128)(2,1)S(1)}, bf16[4,2,256,4,128]{2,4,3,1,0:T(8,128)(2,1)S(1)}, u32[]{:S(2)}, u32[]{:S(2)}) collective-permute-start(bf16[4,2,256,4,128]{2,4,3,1,0:T(8,128)(2,1)S(1)} %pad_maximum_fusion.1), channel_id=1, source_target_pairs={{0,16},{4,20},{8,24},{12,28},{16,32},{20,36},{24,40},{28,44},{32,4... | collective-permute-start | bytes 6291464 | tf_op jit(solution)/shard_map/ppermute | solution.py:15
  259.9 108.2 %collective-permute-start.3 = (bf16[8,2,256,4,128]{2,4,3,1,0:T(8,128)(2,1)S(1)}, bf16[8,2,256,4,128]{2,4,3,1,0:T(8,128)(2,1)S(1)}, u32[]{:S(2)}, u32[]{:S(2)}) collective-permute-start(bf16[8,2,256,4,128]{2,4,3,1,0:T(8,128)(2,1)S(1)} %pad_maximum_fusion), channel_id=1, source_target_pairs={{0,32},{4,36},{8,40},{12,44},{16,48},{20,52},{24,56},{28,60},{32,6... | collective-permute-start | bytes 12582920 | tf_op jit(solution)/shard_map/ppermute | solution.py:15
  271.8 91.4 %collective-permute-start.4 = (bf16[1,2,256,4,128]{2,4,3,1,0:T(8,128)(2,1)S(1)}, bf16[1,2,256,4,128]{2,4,3,1,0:T(8,128)(2,1)S(1)}, u32[]{:S(2)}, u32[]{:S(2)}) collective-permute-start(bf16[1,2,256,4,128]{2,4,3,1,0:T(8,128)(2,1)S(1)} %maximum_bitcast_fusion), channel_id=1, source_target_pairs={{0,64},{4,68},{8,72},{12,76},{16,80},{20,84},{24,88},{28,92},{32,9... | collective-permute-start | bytes 1572872 | tf_op jit(solution)/shard_map/ppermute | solution.py:15
  278.4 92.7 %copy-start.1 = (f32[4,256,256]{1,2,0:T(8,128)}, f32[4,256,256]{1,2,0:T(8,128)S(1)}, u32[]{:S(2)}) copy-start(f32[4,256,256]{1,2,0:T(8,128)S(1)} %get-tuple-element.126) | copy-start | bytes 3145732
  363.3 3.7 copy-start.15
  368.1 17.3 %copy-start.14 = (bf16[8,2,256,4,128]{2,4,3,1,0:T(8,128)(2,1)}, bf16[8,2,256,4,128]{2,4,3,1,0:T(8,128)(2,1)S(1)}, u32[]{:S(2)}) copy-start(bf16[8,2,256,4,128]{2,4,3,1,0:T(8,128)(2,1)S(1)} %collective-permute-done.3) | copy-start | bytes 12582916
  370.7 2.6 copy-start.4
  371.1 2.4 copy-start.5
  389.5 43.1 %all-to-all-start.1 = ((bf16[4,512,512]{2,1,0:T(8,128)(2,1)}), bf16[4,512,512]{2,1,0:T(8,128)(2,1)S(1)}, u32[]{:S(2)}, u32[]{:S(2)}) async-start(bf16[4,512,512]{2,1,0:T(8,128)(2,1)} %bitcast.604), calls=%async_computation.1 | async-start | bytes 4194304 | tf_op jit(solution)/shard_map/all_to_all | solution.py:139
  407.0 5.5 copy-start.3
  407.0 6.8 %copy-start.2 = (f32[4,256,256]{1,2,0:T(8,128)S(1)}, f32[4,256,256]{1,2,0:T(8,128)}, u32[]{:S(2)}) copy-start(f32[4,256,256]{1,2,0:T(8,128)} %copy-done.1) | copy-start | bytes 3145732
  407.0 6.8 %copy-start.6 = (f32[256,4,128]{0,2,1:T(8,128)S(1)}, f32[256,4,128]{0,2,1:T(8,128)}, u32[]{:S(2)}) copy-start(f32[256,4,128]{0,2,1:T(8,128)} %convolution_bitcast_fusion.13) | copy-start | bytes 1572868
  407.0 6.8 %copy-start.7 = (f32[256,4,128]{0,2,1:T(8,128)S(1)}, f32[256,4,128]{0,2,1:T(8,128)}, u32[]{:S(2)}) copy-start(f32[256,4,128]{0,2,1:T(8,128)} %convolution_bitcast_fusion.12) | copy-start | bytes 1572868
  407.0 6.8 %copy-start.8 = (f32[256,4,128]{0,2,1:T(8,128)S(1)}, f32[256,4,128]{0,2,1:T(8,128)}, u32[]{:S(2)}) copy-start(f32[256,4,128]{0,2,1:T(8,128)} %convolution_bitcast_fusion.11) | copy-start | bytes 1572868
  407.0 6.8 %copy-start.9 = (f32[256,4,128]{0,2,1:T(8,128)S(1)}, f32[256,4,128]{0,2,1:T(8,128)}, u32[]{:S(2)}) copy-start(f32[256,4,128]{0,2,1:T(8,128)} %convolution_bitcast_fusion.10) | copy-start | bytes 1572868
  407.0 6.8 %copy-start.10 = (f32[256,4,128]{0,2,1:T(8,128)S(1)}, f32[256,4,128]{0,2,1:T(8,128)}, u32[]{:S(2)}) copy-start(f32[256,4,128]{0,2,1:T(8,128)} %convolution_bitcast_fusion.9) | copy-start | bytes 1572868
  407.0 6.8 %copy-start.11 = (f32[256,4,128]{0,2,1:T(8,128)S(1)}, f32[256,4,128]{0,2,1:T(8,128)}, u32[]{:S(2)}) copy-start(f32[256,4,128]{0,2,1:T(8,128)} %convolution_bitcast_fusion.8) | copy-start | bytes 1572868
  407.0 6.8 %copy-start.12 = (f32[256,4,128]{0,2,1:T(8,128)S(1)}, f32[256,4,128]{0,2,1:T(8,128)}, u32[]{:S(2)}) copy-start(f32[256,4,128]{0,2,1:T(8,128)} %convolution_bitcast_fusion.7) | copy-start | bytes 1572868
  407.0 6.8 %copy-start.13 = (f32[256,4,128]{0,2,1:T(8,128)S(1)}, f32[256,4,128]{0,2,1:T(8,128)}, u32[]{:S(2)}) copy-start(f32[256,4,128]{0,2,1:T(8,128)} %convolution_bitcast_fusion.6) | copy-start | bytes 1572868
  438.4 18.0 %all-to-all-start.2 = ((bf16[4,64,2048]{2,1,0:T(8,128)(2,1)}), bf16[4,64,2048]{2,1,0:T(8,128)(2,1)S(1)}, u32[]{:S(2)}, u32[]{:S(2)}) async-start(bf16[4,64,2048]{2,1,0:T(8,128)(2,1)} %bitcast.137), calls=%async_computation.2 | async-start | bytes 2097152 | tf_op jit(solution)/shard_map/all_to_all | solution.py:28
  456.3 53.1 %all-to-all-start.4 = ((bf16[4,1024,512]{2,1,0:T(8,128)(2,1)}), bf16[4,1024,512]{2,1,0:T(8,128)(2,1)}, u32[]{:S(2)}, u32[]{:S(2)}) async-start(bf16[4,1024,512]{2,1,0:T(8,128)(2,1)} %all_to_all.47), calls=%async_computation.4 | async-start | bytes 8388608 | tf_op jit(solution)/shard_map/all_to_all | solution.py:154
  510.6 18.0 %all-to-all-start.3 = ((bf16[4,64,2048]{2,1,0:T(8,128)(2,1)}), bf16[4,64,2048]{2,1,0:T(8,128)(2,1)S(1)}, u32[]{:S(2)}, u32[]{:S(2)}) async-start(bf16[4,64,2048]{2,1,0:T(8,128)(2,1)} %broadcast_in_dim.162), calls=%async_computation.3 | async-start | bytes 2097152 | tf_op jit(solution)/shard_map/all_to_all | solution.py:21
Sparse Core Ops, SparseCore 0:
  11.4 224.9 all-gather.1

commit v2 on v1

--- a/solution.py
+++ b/solution.py
@@ -1,7 +1,7 @@
 import jax
 import jax.numpy as jnp
 from jax import lax
-from jax.sharding import PartitionSpec as P
+from jax.sharding import Mesh, PartitionSpec as P
 
 HEAD = 128
 
@@ -62,38 +62,62 @@
 
 def on_device(tokens, lengths, w_query, w_key, w_value, w_out, w_gate, w_up, w_down):
     half_type = jnp.bfloat16
+    dp = ("y", "r")
+    mp = "mp"
     rows = tokens.shape[0]
     narrow = w_query.shape[1]
-    units = w_gate.shape[1]
     shard_rows = w_query.shape[0]
     heads_dev = narrow // HEAD
-    dp_index = lax.axis_index("dp")
-    mp_index = lax.axis_index("mp")
-    mp_size = lax.axis_size("mp")
-    reach = lax.axis_size("dp") // 2
-
-    qkv_shard = jnp.concatenate(
-        [w.astype(half_type) for w in (w_query, w_key, w_value)], axis=1
-    )
+    dp_index = lax.axis_index(dp)
+    mp_index = lax.axis_index(mp)
+    mp_size = lax.axis_size(mp)
+    y_size = lax.axis_size("y")
+    r_size = lax.axis_size("r")
+    reach = lax.axis_size(dp) // 2
+
+    down_rows = w_down.shape[0]
+    per_mp = down_rows // mp_size
+    down_shard = lax.all_to_all(
+        w_down.astype(half_type).reshape(mp_size, per_mp, narrow), mp, 0, 0, tiled=True
+    )
+    down_shard = jnp.transpose(down_shard, (1, 0, 2)).reshape(per_mp, mp_size * narrow)
+    units_shard = w_gate.shape[1]
+    blocks = units_shard // down_rows
+
+    def unit_columns(w):
+        pieces = w.astype(half_type).reshape(shard_rows, blocks, mp_size, per_mp)
+        pieces = jnp.transpose(pieces, (2, 0, 1, 3))
+        got = lax.all_to_all(pieces, mp, 0, 0, tiled=True)
+        return jnp.transpose(got, (1, 0, 2, 3)).reshape(shard_rows, mp_size * blocks * per_mp)
+
+    gate_shard = unit_columns(w_gate)
+    up_shard = unit_columns(w_up)
+    units = gate_shard.shape[1]
     rest_shard = jnp.concatenate(
-        [
-            w_out.astype(half_type),
-            w_gate.astype(half_type),
-            w_up.astype(half_type),
-            w_down.astype(half_type).reshape(shard_rows, -1),
-        ],
-        axis=1,
-    )
-    qkv_full = gather_by_exchange(qkv_shard, "dp")
-    rest_full = lax.all_gather(rest_shard, "dp", axis=0, tiled=True)
+        [gate_shard, up_shard, down_shard.reshape(shard_rows, -1)], axis=1
+    )
+
+    out_full_rows = gather_by_exchange(jnp.transpose(w_out.astype(half_type)), mp)
+    out_full_rows = jnp.transpose(out_full_rows)
+    swap = [(a * mp_size + b, b * mp_size + a) for a in range(y_size) for b in range(mp_size)]
+    out_swapped = lax.ppermute(out_full_rows, ("y", mp), swap)
+    server_out = gather_by_exchange(out_swapped, "r")
+
+    kv_shard = jnp.concatenate([w.astype(half_type) for w in (w_key, w_value)], axis=1)
+    kv_full = gather_by_exchange(kv_shard, dp)
+    q_full = lax.all_gather(w_query.astype(half_type), dp, axis=0, tiled=True)
+    rest_full = lax.all_gather(rest_shard, dp, axis=0, tiled=True)
 
     normed = layer_norm(tokens).astype(half_type)
-    joined = jnp.dot(normed, qkv_full, preferred_element_type=jnp.float32)
+    joined_kv = jnp.dot(normed, kv_full, preferred_element_type=jnp.float32)
     q_prompt, q_offset, q_where = prompt_coords(dp_index * rows, rows, lengths)
-    shaped = joined.reshape(rows, 3, heads_dev, HEAD)
-    query = rotate(shaped[:, 0], q_offset).astype(half_type)
-    keys = rotate(shaped[:, 1], q_offset).astype(half_type)
-    values = shaped[:, 2].astype(half_type)
+    shaped = joined_kv.reshape(rows, 2, heads_dev, HEAD)
+    keys = rotate(shaped[:, 0], q_offset).astype(half_type)
+    values = shaped[:, 1].astype(half_type)
+    held = jnp.stack((keys, values))[None]
+    farthest = shifted(held, dp, reach)
+    joined_q = jnp.dot(normed, q_full, preferred_element_type=jnp.float32)
+    query = rotate(joined_q.reshape(rows, heads_dev, HEAD), q_offset).astype(half_type)
     own_first = dp_index * rows
     scale = 1.0 / HEAD**0.5
 
@@ -119,15 +143,19 @@
         jnp.zeros((heads_dev, rows, 1), jnp.float32),
         jnp.full((heads_dev, rows, 1), -jnp.inf, jnp.float32),
     )
-    held = jnp.stack((keys, values))[None]
-    farthest = shifted(held, "dp", reach)
     state = online_step(state, held[0], own_first)
     done = 1
     span = 1
     while span < reach:
-        arrived = shifted(held, "dp", span)
-        for slot in range(arrived.shape[0]):
-            state = online_step(state, arrived[slot], own_first - (done + slot) * rows)
+        arrived = shifted(held, dp, span)
+        if arrived.shape[0] < 4:
+            for slot in range(arrived.shape[0]):
+                state = online_step(state, arrived[slot], own_first - (done + slot) * rows)
+        else:
+            def slot_step(slot, state, arrived=arrived, done=done):
+                return online_step(state, arrived[slot], own_first - (done + slot) * rows)
+
+            state = lax.fori_loop(0, arrived.shape[0], slot_step, state)
         done += arrived.shape[0]
         held = jnp.concatenate([held, arrived], axis=0)
         span *= 2
@@ -135,41 +163,40 @@
     accum, total, top = state
     context = (accum / jnp.transpose(total, (1, 0, 2))).astype(half_type).reshape(rows, narrow)
 
-    out_cols = rest_full[:, :narrow]
-    server_out = lax.all_to_all(out_cols, "mp", split_axis=0, concat_axis=1, tiled=True)
     partial_out = jnp.dot(context, server_out, preferred_element_type=jnp.float32)
-    attended = scatter_sum(partial_out.astype(half_type), "mp")
+    attended = scatter_sum(partial_out.astype(half_type), mp)
     slab = rows // mp_size
     own_tokens = lax.dynamic_slice_in_dim(tokens, mp_index * slab, slab, 0)
     mixed = (own_tokens.astype(jnp.float32) + attended).astype(half_type)
     normed_own = layer_norm(mixed).astype(half_type)
-    normed_two = gather_by_exchange(normed_own, "mp")
-
-    gate = jnp.dot(normed_two, rest_full[:, narrow : narrow + units], preferred_element_type=jnp.float32)
-    upper = jnp.dot(
-        normed_two, rest_full[:, narrow + units : narrow + 2 * units], preferred_element_type=jnp.float32
-    )
+    normed_two = gather_by_exchange(normed_own, mp)
+
+    gate = jnp.dot(normed_two, rest_full[:, :units], preferred_element_type=jnp.float32)
+    upper = jnp.dot(normed_two, rest_full[:, units : 2 * units], preferred_element_type=jnp.float32)
     hidden = (jax.nn.silu(gate) * upper).astype(half_type)
-    down_cols = rest_full[:, narrow + 2 * units :].reshape(-1, narrow)
-    server_down = lax.all_to_all(down_cols, "mp", split_axis=0, concat_axis=1, tiled=True)
+    server_down = rest_full[:, 2 * units :].reshape(units, -1)
     partial_down = jnp.dot(hidden, server_down, preferred_element_type=jnp.float32)
-    share = scatter_sum(partial_down.astype(half_type), "mp")
+    share = scatter_sum(partial_down.astype(half_type), mp)
     return (mixed.astype(jnp.float32) + share).astype(half_type)
 
 
 def solution(mesh):
+    dp_size, mp_size = mesh.devices.shape
+    y_size = mesh.devices.shape[0] // 8 if dp_size % 8 == 0 else 1
+    fine = Mesh(mesh.devices.reshape(y_size, dp_size // y_size, mp_size), ("y", "r", "mp"))
+    dp = ("y", "r")
     in_specs = (
-        P("dp", None),
+        P(dp, None),
         P(),
-        P("dp", "mp"),
-        P("dp", "mp"),
-        P("dp", "mp"),
-        P("dp", "mp"),
-        P("dp", "mp"),
-        P("dp", "mp"),
-        P("dp", "mp"),
-    )
-    out_specs = P(("dp", "mp"), None)
+        P(dp, "mp"),
+        P(dp, "mp"),
+        P(dp, "mp"),
+        P(dp, "mp"),
+        P(dp, "mp"),
+        P(dp, "mp"),
+        P(dp, "mp"),
+    )
+    out_specs = P(("y", "r", "mp"), None)
     return jax.shard_map(
-        on_device, mesh=mesh, in_specs=in_specs, out_specs=out_specs, check_vma=False
-    )
+        on_device, mesh=fine, in_specs=in_specs, out_specs=out_specs, check_vma=False
+    )

time: 566 us -> 531 us (0.938)
  waiting for transfers between devices: 347 us -> 305 us
  matrix products: 46.3 us -> 58.6 us
  starting transfers between devices: 82.4 us -> 71.7 us
    all_gather x1 -> x2, waiting for transfers between devices: 0.01 us -> 92.4 us  [the longest x1 92.4 us: on_device(): q_full = lax.all_gather(w_query.astype(half_type), dp, axis=0, tiled=True)]
    all_to_all x2 -> x4, waiting for transfers between devices: 91.8 us -> 6 us  [gather_by_exchange(): got = lax.all_to_all(copies, axis, 0, 0, tiled=True)]
    all_to_all x2 -> x3, waiting for transfers between devices: 62.8 us -> 15.9 us  [the longest x2 11.4 us: unit_columns(): got = lax.all_to_all(pieces, mp, 0, 0, tiled=True)]
    all_to_all x3 -> x0, local copies, waits for them, and re-layouts: 15.8 us -> none  [the longest x2 13.4 us: on_device(): lax.all_to_all(down_cols, 'mp', split_axis=0, concat_axis=1, tiled=True)]
    ppermute x5, waiting for transfers between devices: 190 us -> 177 us  [shifted(): lax.ppermute(value, axis, [(source, source + steps) for source in range(c...]
    dot_general x17, matrix products: 7.26 us -> 20.5 us  [online_step(): jnp.einsum('qhd,khd->hqk', query, pair[0], preferred_element_type=jnp.flo...]
    ppermute x5, starting transfers between devices: 41.9 us -> 29.2 us  [shifted(): lax.ppermute(value, axis, [(source, source + steps) for source in range(c...]
    all_to_all x2 -> x3, starting transfers between devices: 22.3 us -> 10.5 us  [the longest x2 7.22 us: unit_columns(): got = lax.all_to_all(pieces, mp, 0, 0, tiled=True)]
  transfers between devices with their start and end apart: 11 -> 16, of which waited for: 9 -> 10; matrix products, arithmetic and copies ran while one was open for 12% -> 19% of each run, Pallas kernels for 0% -> 0%
where the time goes in v2:
time: 531 us; the launch traced here: 522 us
  waiting for transfers between devices  305 us (57%)
  starting transfers between devices  71.7 us (14%)
  matrix products  58.6 us (11%)
  local copies, waits for them, and re-layouts  32.6 us (6%)
  other arithmetic  22.2 us (4%)
  blocking collectives  16.9 us (3%)
  between operations  14 us (3%)
    ppermute x5, waiting for transfers between devices, shifted(): lax.ppermute(value, axis, [(source, source + steps) for source in range(c...  177 us
    all_gather x1, waiting for transfers between devices, on_device(): q_full = lax.all_gather(w_query.astype(half_type), dp, axis=0, tiled=True)  92.4 us
    ppermute x5, starting transfers between devices, shifted(): lax.ppermute(value, axis, [(source, source + steps) for source in range(c...  29.2 us
    all_to_all x4, starting transfers between devices, gather_by_exchange(): got = lax.all_to_all(copies, axis, 0, 0, tiled=True)  24.8 us
    dot_general x17, matrix products, online_step(): jnp.einsum('qhd,khd->hqk', query, pair[0], preferred_element_type=jnp.flo...  20.5 us
    dot_general x17, matrix products, online_step(): jnp.einsum('hqk,khd->qhd', probs, pair[1], preferred_element_type=jnp.flo...  19.2 us
    all_to_all x1, blocking collectives, scatter_sum(): got = lax.all_to_all(pieces, axis, 0, 0, tiled=True)  16.9 us
    all_to_all x1, waiting for transfers between devices, scatter_sum(): got = lax.all_to_all(pieces, axis, 0, 0, tiled=True)  14.4 us
  transfers between devices with their start and end apart: 16, of which 10 were waited for; matrix products, arithmetic and copies ran while one was open for 19% of the time, Pallas kernels for 0%

profile of v2, /device:TPU:4, one launch (start us, length us, event | category | flops | bytes accessed | tf_op | source)
XLA Modules:
  0.0 522.0 jit_solution(16162897478976833873)
XLA Ops:
  6.5 1.5 convert_element_type.165
  10.0 2.5 broadcast_in_dim.293
  12.5 11.2 %all-to-all-start = ((bf16[32,64,1024]{2,1,0:T(8,128)(2,1)}), bf16[32,64,1024]{2,1,0:T(8,128)(2,1)}, u32[]{:S(2)}, u32[]{:S(2)}) async-start(bf16[32,64,1024]{2,1,0:T(8,128)(2,1)} %broadcast_in_dim.293), calls=%async_computation | async-start | bytes 8388608 | tf_op jit(solution)/shard_map/all_to_all | solution.py:21
  27.4 92.4 %all-gather.3.cloned.1.call-done = bf16[2048,512]{1,0:T(8,128)(2,1)} async-done(((bf16[64,512]{1,0:T(8,128)(2,1)}), bf16[2048,512]{1,0:T(8,128)(2,1)}) %all-gather.3.cloned.1.call-update) | async-done | bytes 2097168 | tf_op jit(solution)/shard_map/all_gather | solution.py:108
  119.8 2.6 fusion.105
  122.4 3.4 all-to-all-start.5
  125.8 6.5 %copy.181 = bf16[1024,2048]{1,0:T(8,128)(2,1)} copy(bf16[1024,2048]{0,1:T(8,128)(2,1)} %bitcast.5) | data formatting | bytes 8388608 | tf_op jit(solution)/shard_map/dot_general | solution.py:112
  132.3 3.6 fusion.50
  137.5 5.2 %collective-permute-start = (bf16[1,2,256,4,128]{2,4,3,1,0:T(8,128)(2,1)S(1)}, bf16[1,2,256,4,128]{2,4,3,1,0:T(8,128)(2,1)S(1)}, u32[]{:S(2)}, u32[]{:S(2)}) collective-permute-start(bf16[1,2,256,4,128]{2,4,3,1,0:T(8,128)(2,1)S(1)} %maximum_bitcast_fusion), channel_id=1, source_target_pairs={{0,4},{4,8},{8,12},{12,16},{16,20},{20,24},{24,28},{28,32},{32,36}... | collective-permute-start | bytes 1572872 | tf_op jit(solution)/shard_map/ppermute | solution.py:15
  142.7 3.9 all-to-all-start.6
  147.3 11.4 %all-to-all-done.6 = bf16[4,2,8192]{2,1,0:T(2,128)(2,1)S(1)} async-done(((bf16[4,2,8192]{2,1,0:T(2,128)(2,1)}), bf16[4,2,8192]{2,1,0:T(2,128)(2,1)S(1)}, u32[]{:S(2)}, u32[]{:S(2)}) %all-to-all-start.6) | async-done | bytes 131104 | tf_op jit(solution)/shard_map/all_to_all | solution.py:90
  158.6 3.3 all-to-all-start.7
  162.0 4.6 all-to-all-done.7
  167.3 3.4 all-to-all-start.1
  173.4 3.2 all-to-all-done.1
  177.4 3.6 collective-permute-start.5
  182.2 3.5 collective-permute-start.1
  186.9 2.5 broadcast_in_dim.304
  189.4 6.7 %all-to-all-start.2 = ((bf16[8,64,2048]{2,1,0:T(8,128)(2,1)}), bf16[8,64,2048]{2,1,0:T(8,128)(2,1)}, u32[]{:S(2)}, u32[]{:S(2)}) async-start(bf16[8,64,2048]{2,1,0:T(8,128)(2,1)} %broadcast_in_dim.304), calls=%async_computation.2 | async-start | bytes 4194304 | tf_op jit(solution)/shard_map/all_to_all | solution.py:21
  196.1 8.9 %collective-permute-start.4 = (bf16[1,2,256,4,128]{2,4,3,1,0:T(8,128)(2,1)S(1)}, bf16[1,2,256,4,128]{2,4,3,1,0:T(8,128)(2,1)}, u32[]{:S(2)}, u32[]{:S(2)}) collective-permute-start(bf16[1,2,256,4,128]{2,4,3,1,0:T(8,128)(2,1)S(1)} %maximum_bitcast_fusion), channel_id=1, source_target_pairs={{0,64},{4,68},{8,72},{12,76},{16,80},{20,84},{24,88},{28,92},{32,9... | collective-permute-start | bytes 1572872 | tf_op jit(solution)/shard_map/ppermute | solution.py:15
  206.6 1.4 fusion.54
  208.3 5.9 %collective-permute-done.4 = bf16[1,2,256,4,128]{2,4,3,1,0:T(8,128)(2,1)} collective-permute-done((bf16[1,2,256,4,128]{2,4,3,1,0:T(8,128)(2,1)S(1)}, bf16[1,2,256,4,128]{2,4,3,1,0:T(8,128)(2,1)}, u32[]{:S(2)}, u32[]{:S(2)}) %collective-permute-start.4) | collective-permute-done | bytes 524320 | tf_op jit(solution)/shard_map/ppermute | solution.py:15
  214.2 2.3 fusion.114
  216.5 7.4 %collective-permute-done.1 = bf16[2,2,256,4,128]{2,4,3,1,0:T(8,128)(2,1)S(1)} collective-permute-done((bf16[2,2,256,4,128]{2,4,3,1,0:T(8,128)(2,1)}, bf16[2,2,256,4,128]{2,4,3,1,0:T(8,128)(2,1)S(1)}, u32[]{:S(2)}, u32[]{:S(2)}) %collective-permute-start.1) | collective-permute-done | bytes 1048608 | tf_op jit(solution)/shard_map/ppermute | solution.py:15
  224.1 7.0 %collective-permute-start.2 = (bf16[4,2,256,4,128]{2,4,3,1,0:T(8,128)(2,1)S(1)}, bf16[4,2,256,4,128]{2,4,3,1,0:T(8,128)(2,1)S(1)}, u32[]{:S(2)}, u32[]{:S(2)}) collective-permute-start(bf16[4,2,256,4,128]{2,4,3,1,0:T(8,128)(2,1)S(1)} %pad_maximum_fusion.1), channel_id=1, source_target_pairs={{0,16},{4,20},{8,24},{12,28},{16,32},{20,36},{24,40},{28,44},{32,4... | collective-permute-start | bytes 6291464 | tf_op jit(solution)/shard_map/ppermute | solution.py:15
  234.6 45.1 %collective-permute-done.2 = bf16[4,2,256,4,128]{2,4,3,1,0:T(8,128)(2,1)S(1)} collective-permute-done((bf16[4,2,256,4,128]{2,4,3,1,0:T(8,128)(2,1)S(1)}, bf16[4,2,256,4,128]{2,4,3,1,0:T(8,128)(2,1)S(1)}, u32[]{:S(2)}, u32[]{:S(2)}) %collective-permute-start.2) | collective-permute-done | bytes 2097184 | tf_op jit(solution)/shard_map/ppermute | solution.py:15
  279.7 2.3 pad_maximum_fusion
  282.2 4.6 collective-permute-start.3
  286.8 12.6 %while.42 = (s32[]{:T(128)}, f32[256,4,128]{0,2,1:T(8,128)S(1)}, f32[4,256,1]{1,0,2:T(4,128)S(1)}, f32[4,256,1]{1,0,2:T(4,128)S(1)}, s32[256]{0:T(256)S(1)}, /*i...) while((s32[]{:T(128)}, f32[256,4,128]{0,2,1:T(8,128)S(1)}, ...), condition=%wide.region_20.21_spmd.clone.clone, body=%wide.region_16.20_spmd.clone.clone.sunk | while | flops 136518656 | bytes 5188821 | solution.py:158
  294.9 1.4 fusion.140
  298.0 1.4 fusion.140
  299.4 118.2 %collective-permute-done.3 = bf16[8,2,256,4,128]{2,4,3,1,0:T(8,128)(2,1)} collective-permute-done((bf16[8,2,256,4,128]{2,4,3,1,0:T(8,128)(2,1)}, bf16[8,2,256,4,128]{2,4,3,1,0:T(8,128)(2,1)}, u32[]{:S(2)}, u32[]{:S(2)}) %collective-permute-start.3) | collective-permute-done | bytes 4194336 | tf_op jit(solution)/shard_map/ppermute | solution.py:15
  417.6 25.3 %while.43 = (s32[]{:T(128)}, f32[256,4,128]{0,2,1:T(8,128)S(1)}, f32[4,256,1]{1,0,2:T(4,128)S(1)}, f32[4,256,1]{1,0,2:T(4,128)S(1)}, s32[256]{0:T(256)S(1)}, /*i...) while((s32[]{:T(128)}, f32[256,4,128]{0,2,1:T(8,128)S(1)}, ...), condition=%wide.region_25.26_spmd.clone.clone, body=%wide.region_21.25_spmd.clone.clone.sunk | while | flops 136518656 | bytes 5188821 | solution.py:158
  419.4 1.4 fusion.146
  422.5 1.4 fusion.146
  425.7 1.4 fusion.146
  442.9 1.4 fusion.62
  444.3 1.6 divide_convert_fusion
  446.0 3.4 convolution_convert_fusion
  449.3 3.5 all-to-all-start.3
  452.9 14.4 %all-to-all-done.3 = bf16[4,64,2048]{2,1,0:T(8,128)(2,1)S(1)} async-done(((bf16[4,64,2048]{2,1,0:T(8,128)(2,1)}), bf16[4,64,2048]{2,1,0:T(8,128)(2,1)S(1)}, u32[]{:S(2)}, u32[]{:S(2)}) %all-to-all-start.3) | async-done | bytes 1048608 | tf_op jit(solution)/shard_map/all_to_all | solution.py:28
  470.1 3.5 all-to-all-start.4
  473.6 4.6 slice.146
  478.2 7.1 %reshape.917 = bf16[1024,2048]{1,0:T(8,128)(2,1)} reshape(bf16[2048,1024]{1,0:T(8,128)(2,1)} %slice.146) | data formatting | bytes 8388608 | tf_op jit(solution)/shard_map/reshape | solution.py:177
  485.3 2.7 all-to-all-done.4
  488.0 3.4 fusion.26
  491.5 5.9 %convolution_convert_fusion.1 = bf16[256,2048]{1,0:T(8,128)(2,1)S(1)} fusion(bf16[1024,2048]{1,0:T(8,128)(2,1)} %reshape.917, bf16[256,2048]{1,0:T(8,128)(2,1)S(1)} %bitcast.341, bf16[2048,3072]{1,0:T(8,128)(2,1)} %all-gather.5.cloned.1.call-done, f32[256,1024]{1,0:T(8,128)S(1)} %fusion.26), kind=kOutput, calls=%fused_computation.54 | convolution fusion | flops 2149580800 | bytes 11534336 | tf_op jit(solution)/shard_map/dot_general | solution.py:178
  497.4 16.9 %all_to_all.45 = bf16[4,64,2048]{2,1,0:T(8,128)(2,1)S(1)} all-to-all(bf16[4,64,2048]{2,1,0:T(8,128)(2,1)S(1)} %bitcast.342), channel_id=1, replica_groups=mesh['y'=4,'r'=8,'mp'=4] {'mp'}, dimensions={0} | all-to-all | bytes 2097152 | tf_op jit(solution)/shard_map/all_to_all | solution.py:28
  (237 shorter events, 54.0 us)
Async XLA Ops:
  6.5 113.2 %all-gather.3.cloned.1.call-start = ((), (), s32[]{:S(2)}) async-start(), calls=%async_computation.9 | async-start | bytes 2162688 | tf_op jit(solution)/shard_map/all_gather | solution.py:108
  12.5 11.3 %copy-start.12 = (f32[64,1024]{1,0:T(8,128)S(1)}, f32[64,1024]{1,0:T(8,128)}, u32[]{:S(2)}) copy-start(f32[64,1024]{1,0:T(8,128)} %param.19) | copy-start | bytes 786436
  12.5 12.4 %copy-start.13 = (f32[64,1024]{1,0:T(8,128)S(1)}, f32[64,1024]{1,0:T(8,128)}, u32[]{:S(2)}) copy-start(f32[64,1024]{1,0:T(8,128)} %param.20) | copy-start | bytes 786436
  12.5 109.9 %all-to-all-start = ((bf16[32,64,1024]{2,1,0:T(8,128)(2,1)}), bf16[32,64,1024]{2,1,0:T(8,128)(2,1)}, u32[]{:S(2)}, u32[]{:S(2)}) async-start(bf16[32,64,1024]{2,1,0:T(8,128)(2,1)} %broadcast_in_dim.293), calls=%async_computation | async-start | bytes 8388608 | tf_op jit(solution)/shard_map/all_to_all | solution.py:21
  23.7 2.3 copy-start.20
  23.7 2.6 copy-start.1
  24.0 3.4 copy-start.14
  122.4 20.3 %all-to-all-start.5 = ((bf16[4,2,8192]{2,1,0:T(2,128)(2,1)}), bf16[4,2,8192]{2,1,0:T(2,128)(2,1)S(1)}, u32[]{:S(2)}, u32[]{:S(2)}) async-start(bf16[4,2,8192]{2,1,0:T(2,128)(2,1)} %reshape.922), calls=%async_computation.5 | async-start | bytes 262144 | tf_op jit(solution)/shard_map/all_to_all | solution.py:90
  135.8 1.6 copy-start.3
  135.9 10.7 %copy-start.11 = (f32[128,512]{1,0:T(8,128)S(1)}, f32[128,512]{1,0:T(8,128)}, u32[]{:S(2)}) copy-start(f32[128,512]{1,0:T(8,128)} %param.21) | copy-start | bytes 786436
  136.7 0.7 copy-start.7
  136.7 0.7 copy-start.9
  137.5 43.5 %collective-permute-start = (bf16[1,2,256,4,128]{2,4,3,1,0:T(8,128)(2,1)S(1)}, bf16[1,2,256,4,128]{2,4,3,1,0:T(8,128)(2,1)S(1)}, u32[]{:S(2)}, u32[]{:S(2)}) collective-permute-start(bf16[1,2,256,4,128]{2,4,3,1,0:T(8,128)(2,1)S(1)} %maximum_bitcast_fusion), channel_id=1, source_target_pairs={{0,4},{4,8},{8,12},{12,16},{16,20},{20,24},{24,28},{28,32},{32,36}... | collective-permute-start | bytes 1572872 | tf_op jit(solution)/shard_map/ppermute | solution.py:15
  142.7 15.9 %all-to-all-start.6 = ((bf16[4,2,8192]{2,1,0:T(2,128)(2,1)}), bf16[4,2,8192]{2,1,0:T(2,128)(2,1)S(1)}, u32[]{:S(2)}, u32[]{:S(2)}) async-start(bf16[4,2,8192]{2,1,0:T(2,128)(2,1)} %reshape.920), calls=%async_computation.6 | async-start | bytes 262144 | tf_op jit(solution)/shard_map/all_to_all | solution.py:90
  158.6 7.9 %all-to-all-start.7 = ((bf16[4,32,512]{2,1,0:T(8,128)(2,1)}), bf16[4,32,512]{2,1,0:T(8,128)(2,1)S(1)}, u32[]{:S(2)}, u32[]{:S(2)}) async-start(bf16[4,32,512]{2,1,0:T(8,128)(2,1)} %bitcast.63), calls=%async_computation.7 | async-start | bytes 262144 | tf_op jit(solution)/shard_map/all_to_all | solution.py:80
  167.3 9.4 %all-to-all-start.1 = ((bf16[4,512,64]{1,2,0:T(8,128)(2,1)}), bf16[4,512,64]{1,2,0:T(8,128)(2,1)S(1)}, u32[]{:S(2)}, u32[]{:S(2)}) async-start(bf16[4,512,64]{1,2,0:T(8,128)(2,1)} %broadcast_in_dim.303), calls=%async_computation.1 | async-start | bytes 524288 | tf_op jit(solution)/shard_map/all_to_all | solution.py:21
  170.7 302.9 %all-gather.5.cloned.1.call-start = ((), (), s32[]{:S(2)}) async-start(), calls=%async_computation.10 | async-start | bytes 12976128 | tf_op jit(solution)/shard_map/all_gather | solution.py:109
  176.7 9.0 %copy-start.5 = (bf16[4,8,32,64]{3,2,1,0:T(8,128)(2,1)S(1)}, bf16[4,8,32,64]{3,2,1,0:T(8,128)(2,1)}, u32[]{:S(2)}) copy-start(bf16[4,8,32,64]{3,2,1,0:T(8,128)(2,1)} %reshape.921) | copy-start | bytes 393220
  177.4 9.5 %collective-permute-start.5 = (bf16[64,2048]{1,0:T(8,128)(2,1)}, bf16[64,2048]{1,0:T(8,128)(2,1)}, u32[]{:S(2)}, u32[]{:S(2)}) collective-permute-start(bf16[64,2048]{1,0:T(8,128)(2,1)} %bitcast.51), channel_id=1, source_target_pairs={{0,0},{1,32},{2,64},{3,96},{32,1},{33,33},{34,65},{35,97},{64,2},{... | collective-permute-start | bytes 786440 | tf_op jit(solution)/shard_map/ppermute | solution.py:103
  182.2 41.7 %collective-permute-start.1 = (bf16[2,2,256,4,128]{2,4,3,1,0:T(8,128)(2,1)}, bf16[2,2,256,4,128]{2,4,3,1,0:T(8,128)(2,1)S(1)}, u32[]{:S(2)}, u32[]{:S(2)}) collective-permute-start(bf16[2,2,256,4,128]{2,4,3,1,0:T(8,128)(2,1)} %pad_maximum_fusion.2), channel_id=1, source_target_pairs={{0,8},{4,12},{8,16},{12,20},{16,24},{20,28},{24,32},{28,36},{32,40... | collective-permute-start | bytes 3145736 | tf_op jit(solution)/shard_map/ppermute | solution.py:15
  189.4 15.6 %copy-start.6 = (bf16[256,4,64]{0,2,1:T(8,128)(2,1)S(1)}, bf16[256,4,64]{0,2,1:T(8,128)(2,1)}, u32[]{:S(2)}) copy-start(bf16[256,4,64]{0,2,1:T(8,128)(2,1)} %get-tuple-element.741) | copy-start | bytes 393220
  189.4 15.6 %copy-start.8 = (bf16[256,4,64]{0,2,1:T(8,128)(2,1)S(1)}, bf16[256,4,64]{0,2,1:T(8,128)(2,1)}, u32[]{:S(2)}) copy-start(bf16[256,4,64]{0,2,1:T(8,128)(2,1)} %copy-done.7) | copy-start | bytes 393220
  189.4 15.6 %copy-start.10 = (bf16[256,4,64]{0,2,1:T(8,128)(2,1)S(1)}, bf16[256,4,64]{0,2,1:T(8,128)(2,1)}, u32[]{:S(2)}) copy-start(bf16[256,4,64]{0,2,1:T(8,128)(2,1)} %copy-done.9) | copy-start | bytes 393220
  189.4 15.6 %copy-start.19 = (pred[256,256]{0,1:T(8,128)(4,1)S(1)}, pred[256,256]{0,1:T(8,128)(4,1)}, u32[]{:S(2)}) copy-start(pred[256,256]{0,1:T(8,128)(4,1)} %get-tuple-element.755) | copy-start | bytes 196612
  189.4 256.5 %all-to-all-start.2 = ((bf16[8,64,2048]{2,1,0:T(8,128)(2,1)}), bf16[8,64,2048]{2,1,0:T(8,128)(2,1)}, u32[]{:S(2)}, u32[]{:S(2)}) async-start(bf16[8,64,2048]{2,1,0:T(8,128)(2,1)} %broadcast_in_dim.304), calls=%async_computation.2 | async-start | bytes 4194304 | tf_op jit(solution)/shard_map/all_to_all | solution.py:21
  196.1 11.8 %copy-start.18 = (pred[256,256]{0,1:T(8,128)(4,1)S(1)}, pred[256,256]{0,1:T(8,128)(4,1)}, u32[]{:S(2)}) copy-start(pred[256,256]{0,1:T(8,128)(4,1)} %get-tuple-element.756) | copy-start | bytes 196612
  196.1 18.1 %collective-permute-start.4 = (bf16[1,2,256,4,128]{2,4,3,1,0:T(8,128)(2,1)S(1)}, bf16[1,2,256,4,128]{2,4,3,1,0:T(8,128)(2,1)}, u32[]{:S(2)}, u32[]{:S(2)}) collective-permute-start(bf16[1,2,256,4,128]{2,4,3,1,0:T(8,128)(2,1)S(1)} %maximum_bitcast_fusion), channel_id=1, source_target_pairs={{0,64},{4,68},{8,72},{12,76},{16,80},{20,84},{24,88},{28,92},{32,9... | collective-permute-start | bytes 1572872 | tf_op jit(solution)/shard_map/ppermute | solution.py:15
  206.4 7.9 %copy-start.17 = (pred[256,256]{0,1:T(8,128)(4,1)S(1)}, pred[256,256]{0,1:T(8,128)(4,1)}, u32[]{:S(2)}) copy-start(pred[256,256]{0,1:T(8,128)(4,1)} %get-tuple-element.754) | copy-start | bytes 196612
  216.5 14.6 %copy-start.16 = (pred[256,256]{0,1:T(8,128)(4,1)S(1)}, pred[256,256]{0,1:T(8,128)(4,1)}, u32[]{:S(2)}) copy-start(pred[256,256]{0,1:T(8,128)(4,1)} %get-tuple-element.758) | copy-start | bytes 196612
  216.5 14.9 %copy-start.15 = (pred[256,256]{0,1:T(8,128)(4,1)S(1)}, pred[256,256]{0,1:T(8,128)(4,1)}, u32[]{:S(2)}) copy-start(pred[256,256]{0,1:T(8,128)(4,1)} %get-tuple-element.757) | copy-start | bytes 196612
  224.1 55.6 %collective-permute-start.2 = (bf16[4,2,256,4,128]{2,4,3,1,0:T(8,128)(2,1)S(1)}, bf16[4,2,256,4,128]{2,4,3,1,0:T(8,128)(2,1)S(1)}, u32[]{:S(2)}, u32[]{:S(2)}) collective-permute-start(bf16[4,2,256,4,128]{2,4,3,1,0:T(8,128)(2,1)S(1)} %pad_maximum_fusion.1), channel_id=1, source_target_pairs={{0,16},{4,20},{8,24},{12,28},{16,32},{20,36},{24,40},{28,44},{32,4... | collective-permute-start | bytes 6291464 | tf_op jit(solution)/shard_map/ppermute | solution.py:15
  232.3 1.2 copy-start.2
  232.3 1.5 copy-start.4
  279.7 2.6 copy-start
  282.2 135.4 %collective-permute-start.3 = (bf16[8,2,256,4,128]{2,4,3,1,0:T(8,128)(2,1)}, bf16[8,2,256,4,128]{2,4,3,1,0:T(8,128)(2,1)}, u32[]{:S(2)}, u32[]{:S(2)}) collective-permute-start(bf16[8,2,256,4,128]{2,4,3,1,0:T(8,128)(2,1)} %pad_maximum_fusion), channel_id=1, source_target_pairs={{0,32},{4,36},{8,40},{12,44},{16,48},{20,52},{24,56},{28,60},{32,6... | collective-permute-start | bytes 12582920 | tf_op jit(solution)/shard_map/ppermute | solution.py:15
  449.3 18.0 %all-to-all-start.3 = ((bf16[4,64,2048]{2,1,0:T(8,128)(2,1)}), bf16[4,64,2048]{2,1,0:T(8,128)(2,1)S(1)}, u32[]{:S(2)}, u32[]{:S(2)}) async-start(bf16[4,64,2048]{2,1,0:T(8,128)(2,1)} %bitcast.53), calls=%async_computation.3 | async-start | bytes 2097152 | tf_op jit(solution)/shard_map/all_to_all | solution.py:28
  470.1 18.0 %all-to-all-start.4 = ((bf16[4,64,2048]{2,1,0:T(8,128)(2,1)}), bf16[4,64,2048]{2,1,0:T(8,128)(2,1)S(1)}, u32[]{:S(2)}, u32[]{:S(2)}) async-start(bf16[4,64,2048]{2,1,0:T(8,128)(2,1)} %broadcast_in_dim.305), calls=%async_computation.4 | async-start | bytes 2097152 | tf_op jit(solution)/shard_map/all_to_all | solution.py:21
Sparse Core Ops, SparseCore 0:
  10.5 109.2 all-gather.2
  187.0 208.0 all-gather.4

commit v3 on v2

--- a/solution.py
+++ b/solution.py
@@ -77,35 +77,50 @@
 
     down_rows = w_down.shape[0]
     per_mp = down_rows // mp_size
-    down_shard = lax.all_to_all(
-        w_down.astype(half_type).reshape(mp_size, per_mp, narrow), mp, 0, 0, tiled=True
-    )
-    down_shard = jnp.transpose(down_shard, (1, 0, 2)).reshape(per_mp, mp_size * narrow)
     units_shard = w_gate.shape[1]
     blocks = units_shard // down_rows
 
-    def unit_columns(w):
+    def unit_pieces(w):
         pieces = w.astype(half_type).reshape(shard_rows, blocks, mp_size, per_mp)
-        pieces = jnp.transpose(pieces, (2, 0, 1, 3))
-        got = lax.all_to_all(pieces, mp, 0, 0, tiled=True)
-        return jnp.transpose(got, (1, 0, 2, 3)).reshape(shard_rows, mp_size * blocks * per_mp)
-
-    gate_shard = unit_columns(w_gate)
-    up_shard = unit_columns(w_up)
+        return jnp.transpose(pieces, (2, 0, 1, 3))
+
+    outgoing = [
+        unit_pieces(w_gate),
+        unit_pieces(w_up),
+        w_down.astype(half_type).reshape(mp_size, per_mp, narrow),
+        jnp.broadcast_to(w_out.astype(half_type)[None], (mp_size,) + w_out.shape),
+    ]
+    flat = jnp.concatenate([p.reshape(mp_size, -1) for p in outgoing], axis=1)
+    got = lax.all_to_all(flat, mp, 0, 0, tiled=True)
+    q_shard = w_query.astype(half_type)
+    kv_shard = jnp.concatenate([w.astype(half_type) for w in (w_key, w_value)], axis=1)
+    got, q_shard, kv_shard = lax.optimization_barrier((got, q_shard, kv_shard))
+    pieces = []
+    at = 0
+    for p in outgoing:
+        size = p[0].size
+        pieces.append(got[:, at : at + size].reshape(p.shape))
+        at += size
+    gate_got, up_got, down_got, out_got = pieces
+
+    def unit_columns(got_w):
+        return jnp.transpose(got_w, (1, 0, 2, 3)).reshape(shard_rows, mp_size * blocks * per_mp)
+
+    gate_shard = unit_columns(gate_got)
+    up_shard = unit_columns(up_got)
+    down_shard = jnp.transpose(down_got, (1, 0, 2)).reshape(per_mp, mp_size * narrow)
     units = gate_shard.shape[1]
     rest_shard = jnp.concatenate(
         [gate_shard, up_shard, down_shard.reshape(shard_rows, -1)], axis=1
     )
 
-    out_full_rows = gather_by_exchange(jnp.transpose(w_out.astype(half_type)), mp)
-    out_full_rows = jnp.transpose(out_full_rows)
+    out_full_rows = jnp.transpose(out_got, (1, 0, 2)).reshape(shard_rows, mp_size * narrow)
     swap = [(a * mp_size + b, b * mp_size + a) for a in range(y_size) for b in range(mp_size)]
     out_swapped = lax.ppermute(out_full_rows, ("y", mp), swap)
     server_out = gather_by_exchange(out_swapped, "r")
 
-    kv_shard = jnp.concatenate([w.astype(half_type) for w in (w_key, w_value)], axis=1)
     kv_full = gather_by_exchange(kv_shard, dp)
-    q_full = lax.all_gather(w_query.astype(half_type), dp, axis=0, tiled=True)
+    q_full = lax.all_gather(q_shard, dp, axis=0, tiled=True)
     rest_full = lax.all_gather(rest_shard, dp, axis=0, tiled=True)
 
     normed = layer_norm(tokens).astype(half_type)
@@ -114,8 +129,10 @@
     shaped = joined_kv.reshape(rows, 2, heads_dev, HEAD)
     keys = rotate(shaped[:, 0], q_offset).astype(half_type)
     values = shaped[:, 1].astype(half_type)
-    held = jnp.stack((keys, values))[None]
-    farthest = shifted(held, dp, reach)
+    own_pair = jnp.stack((keys, values))
+    plane = r_size
+    back_one = shifted(own_pair, dp, plane)
+    back_two = shifted(own_pair, dp, 2 * plane)
     joined_q = jnp.dot(normed, q_full, preferred_element_type=jnp.float32)
     query = rotate(joined_q.reshape(rows, heads_dev, HEAD), q_offset).astype(half_type)
     own_first = dp_index * rows
@@ -143,23 +160,22 @@
         jnp.zeros((heads_dev, rows, 1), jnp.float32),
         jnp.full((heads_dev, rows, 1), -jnp.inf, jnp.float32),
     )
-    state = online_step(state, held[0], own_first)
-    done = 1
-    span = 1
-    while span < reach:
-        arrived = shifted(held, dp, span)
-        if arrived.shape[0] < 4:
-            for slot in range(arrived.shape[0]):
-                state = online_step(state, arrived[slot], own_first - (done + slot) * rows)
-        else:
-            def slot_step(slot, state, arrived=arrived, done=done):
-                return online_step(state, arrived[slot], own_first - (done + slot) * rows)
-
-            state = lax.fori_loop(0, arrived.shape[0], slot_step, state)
-        done += arrived.shape[0]
-        held = jnp.concatenate([held, arrived], axis=0)
-        span *= 2
-    state = online_step(state, farthest[0], own_first - reach * rows)
+    r_index = lax.axis_index("r")
+    later = r_index < jnp.arange(plane)
+    nearer = jnp.where(later[:, None, None, None, None], own_pair[None], back_two[None])
+    payload = jnp.stack(
+        (nearer, jnp.broadcast_to(back_one[None], (plane,) + back_one.shape)), axis=1
+    )
+    received = lax.all_to_all(payload, "r", 0, 0, tiled=True)
+    state = online_step(state, own_pair, own_first)
+
+    def slot_step(back, state):
+        source = lax.rem(r_index - back + 2 * plane, plane)
+        middle = jnp.logical_and(back > r_index, back <= r_index + plane).astype(jnp.int32)
+        pair = received[source, middle]
+        return online_step(state, pair, own_first - back * rows)
+
+    state = lax.fori_loop(1, reach + 1, slot_step, state)
     accum, total, top = state
     context = (accum / jnp.transpose(total, (1, 0, 2))).astype(half_type).reshape(rows, narrow)
 

time: 531 us -> 489 us (0.921)
  waiting for transfers between devices: 305 us -> 268 us
  starting transfers between devices: 71.7 us -> 56 us
  local copies, waits for them, and re-layouts: 32.6 us -> 40.7 us
    ppermute x5 -> x2, waiting for transfers between devices: 177 us -> 12.8 us  [shifted(): lax.ppermute(value, axis, [(source, source + steps) for source in range(c...]
    all_to_all x3 -> x2, waiting for transfers between devices: 15.9 us -> 95.3 us  [the longest x1 85.9 us: on_device(): received = lax.all_to_all(payload, 'r', 0, 0, tiled=True)]
    all_gather x1, waiting for transfers between devices: 0.02 us -> 41.3 us  [on_device(): rest_full = lax.all_gather(rest_shard, dp, axis=0, tiled=True)]
    ppermute x5 -> x2, starting transfers between devices: 29.2 us -> 7.57 us  [shifted(): lax.ppermute(value, axis, [(source, source + steps) for source in range(c...]
    all_to_all x1, waiting for transfers between devices: 14.4 us -> 26.2 us  [scatter_sum(): got = lax.all_to_all(pieces, axis, 0, 0, tiled=True)]
    all_to_all x1, starting transfers between devices: 3.51 us -> 12.8 us  [scatter_sum(): got = lax.all_to_all(pieces, axis, 0, 0, tiled=True)]
    another operation x1 -> x3, other arithmetic: 0.78 us -> 7.3 us  [the longest x1 6.23 us: on_device(): jnp.stack((nearer, jnp.broadcast_to(back_one[None], (plane,) + back_one.s...]
    all_to_all x4 -> x3, waiting for transfers between devices: 6 us -> 0.01 us  [gather_by_exchange(): got = lax.all_to_all(copies, axis, 0, 0, tiled=True)]
  transfers between devices with their start and end apart: 16 -> 11, of which waited for: 10 -> 7; matrix products, arithmetic and copies ran while one was open for 19% -> 18% of each run, Pallas kernels for 0% -> 0%
where the time goes in v3:
time: 489 us; the launch traced here: 484 us
  waiting for transfers between devices  268 us (55%)
  matrix products  63.7 us (13%)
  starting transfers between devices  56 us (11%)
  local copies, waits for them, and re-layouts  40.7 us (8%)
  other arithmetic  22.5 us (5%)
  blocking collectives  17.6 us (4%)
  between operations  14 us (3%)
    all_gather x1, waiting for transfers between devices, on_device(): q_full = lax.all_gather(q_shard, dp, axis=0, tiled=True)  92.5 us
    all_to_all x1, waiting for transfers between devices, on_device(): received = lax.all_to_all(payload, 'r', 0, 0, tiled=True)  85.9 us
    all_gather x1, waiting for transfers between devices, on_device(): rest_full = lax.all_gather(rest_shard, dp, axis=0, tiled=True)  41.3 us
    all_to_all x1, waiting for transfers between devices, scatter_sum(): got = lax.all_to_all(pieces, axis, 0, 0, tiled=True)  26.2 us
    dot_general x17, matrix products, online_step(): jnp.einsum('hqk,khd->qhd', probs, pair[1], preferred_element_type=jnp.flo...  24 us
    dot_general x17, matrix products, online_step(): jnp.einsum('qhd,khd->hqk', query, pair[0], preferred_element_type=jnp.flo...  20.7 us
    all_to_all x3, starting transfers between devices, gather_by_exchange(): got = lax.all_to_all(copies, axis, 0, 0, tiled=True)  20.5 us
    all_to_all x1, blocking collectives, scatter_sum(): got = lax.all_to_all(pieces, axis, 0, 0, tiled=True)  17.6 us
  transfers between devices with their start and end apart: 11, of which 7 were waited for; matrix products, arithmetic and copies ran while one was open for 18% of the time, Pallas kernels for 0%

profile of v3, /device:TPU:4, one launch (start us, length us, event | category | flops | bytes accessed | tf_op | source)
XLA Modules:
  0.0 484.1 jit_solution(7430889361761597291)
XLA Ops:
  10.8 1.5 reduce
  12.3 1.5 reshape.428
  13.8 3.5 all-to-all-start
  18.1 9.4 %all-to-all-done = bf16[4,2,40960]{2,1,0:T(2,128)(2,1)S(1)} async-done(((bf16[4,2,40960]{2,1,0:T(2,128)(2,1)}), bf16[4,2,40960]{2,1,0:T(2,128)(2,1)S(1)}, u32[]{:S(2)}, u32[]{:S(2)}) %all-to-all-start) | async-done | bytes 655392 | tf_op jit(solution)/shard_map/all_to_all | solution.py:94
  28.2 1.7 copy.142
  29.9 2.5 broadcast_in_dim.183
  32.4 11.2 %all-to-all-start.1 = ((bf16[32,64,1024]{2,1,0:T(8,128)(2,1)}), bf16[32,64,1024]{2,1,0:T(8,128)(2,1)}, u32[]{:S(2)}, u32[]{:S(2)}) async-start(bf16[32,64,1024]{2,1,0:T(8,128)(2,1)} %broadcast_in_dim.183), calls=%async_computation.1 | async-start | bytes 8388608 | tf_op jit(solution)/shard_map/all_to_all | solution.py:21
  45.0 92.5 %all-gather.3.cloned.1.call-done = bf16[2048,512]{1,0:T(8,128)(2,1)} async-done(((bf16[64,512]{1,0:T(8,128)(2,1)}), bf16[2048,512]{1,0:T(8,128)(2,1)}) %all-gather.3.cloned.1.call-update) | async-done | bytes 2097168 | tf_op jit(solution)/shard_map/all_gather | solution.py:123
  137.5 2.6 fusion.53
  140.1 6.5 %copy.117 = bf16[1024,2048]{1,0:T(8,128)(2,1)} copy(bf16[1024,2048]{0,1:T(8,128)(2,1)} %bitcast.10) | data formatting | bytes 8388608 | tf_op jit(solution)/shard_map/dot_general | solution.py:127
  146.7 3.6 fusion.28
  151.4 4.2 collective-permute-start
  155.6 3.4 collective-permute-start.1
  159.3 7.9 %collective-permute-done = bf16[2,256,4,128]{1,3,2,0:T(8,128)(2,1)} collective-permute-done((bf16[2,256,4,128]{1,3,2,0:T(8,128)(2,1)S(1)}, bf16[2,256,4,128]{1,3,2,0:T(8,128)(2,1)}, u32[]{:S(2)}, u32[]{:S(2)}) %collective-permute-start) | collective-permute-done | bytes 524320 | tf_op jit(solution)/shard_map/ppermute | solution.py:15
  168.5 2.5 broadcast_select_fusion
  171.0 4.9 %collective-permute-done.1 = bf16[2,256,4,128]{1,3,2,0:T(8,128)(2,1)S(1)} collective-permute-done((bf16[2,256,4,128]{1,3,2,0:T(8,128)(2,1)S(1)}, bf16[2,256,4,128]{1,3,2,0:T(8,128)(2,1)S(1)}, u32[]{:S(2)}, u32[]{:S(2)}) %collective-permute-start.1) | collective-permute-done | bytes 524320 | tf_op jit(solution)/shard_map/ppermute | solution.py:15
  176.2 3.0 stack_broadcast_in_dim.2
  179.2 6.2 %pad_maximum_fusion = bf16[8,2,2,256,4,128]{5,3,4,2,1,0:T(8,128)(2,1)} fusion(bf16[8,1,2,256,4,128]{5,3,4,2,1,0:T(8,128)(2,1)} %stack_broadcast_in_dim.2, bf16[8,1,2,256,4,128]{5,3,4,2,1,0:T(8,128)(2,1)S(1)} %copy-done), kind=kLoop, calls=%fused_computation.23 | loop fusion | flops 4194304 | bytes 16777216 | tf_op jit(solution)/shard_map/stack | solution.py:166
  185.4 8.0 %all-to-all-start.2 = ((bf16[8,2,2,256,4,128]{5,3,4,2,1,0:T(8,128)(2,1)}), bf16[8,2,2,256,4,128]{5,3,4,2,1,0:T(8,128)(2,1)}, u32[]{:S(2)}, u32[]{:S(2)}) async-start(bf16[8,2,2,256,4,128]{5,3,4,2,1,0:T(8,128)(2,1)} %pad_maximum_fusion), calls=%async_computation.2 | async-start | bytes 16777216 | tf_op jit(solution)/shard_map/all_to_all | solution.py:169
  194.4 3.6 collective-permute-start.2
  203.1 85.9 %all-to-all-done.2 = bf16[8,2,2,256,4,128]{5,3,4,2,1,0:T(8,128)(2,1)} async-done(((bf16[8,2,2,256,4,128]{5,3,4,2,1,0:T(8,128)(2,1)}), bf16[8,2,2,256,4,128]{5,3,4,2,1,0:T(8,128)(2,1)}, u32[]{:S(2)}, u32[]{:S(2)}) %all-to-all-start.2) | async-done | bytes 8388640 | tf_op jit(solution)/shard_map/all_to_all | solution.py:169
  289.0 2.5 broadcast_in_dim.189
  291.5 5.5 %all-to-all-start.3 = ((bf16[8,64,2048]{2,1,0:T(8,128)(2,1)}), bf16[8,64,2048]{2,1,0:T(8,128)(2,1)}, u32[]{:S(2)}, u32[]{:S(2)}) async-start(bf16[8,64,2048]{2,1,0:T(8,128)(2,1)} %broadcast_in_dim.189), calls=%async_computation.3 | async-start | bytes 4194304 | tf_op jit(solution)/shard_map/all_to_all | solution.py:21
  297.1 51.3 %while.21 = (s32[]{:T(128)}, f32[256,4,128]{0,2,1:T(8,128)S(1)}, f32[4,256,1]{1,0,2:T(4,128)S(1)}, f32[4,256,1]{1,0,2:T(4,128)S(1)}, s32[256]{0:T(256)S(1)}, /*i...) while((s32[]{:T(128)}, f32[256,4,128]{0,2,1:T(8,128)S(1)}, ...), condition=%wide.region_11.12_spmd.clone.clone, body=%wide.region_7.11_spmd.clone.clone.sunk | while | flops 136518688 | bytes 5188022 | solution.py:178
  298.8 1.4 fusion.76
  302.0 1.4 fusion.76
  305.2 1.4 fusion.76
  308.4 1.4 fusion.76
  311.6 1.4 fusion.76
  314.8 1.4 fusion.76
  318.0 1.4 fusion.76
  321.2 1.4 fusion.76
  324.5 1.4 fusion.76
  327.7 1.4 fusion.76
  330.9 1.4 fusion.76
  334.1 1.4 fusion.76
  340.5 1.4 fusion.76
  346.9 1.4 fusion.76
  348.4 3.4 convolution_convert_fusion
  351.8 12.8 %all-to-all-start.4 = ((bf16[4,64,2048]{2,1,0:T(8,128)(2,1)}), bf16[4,64,2048]{2,1,0:T(8,128)(2,1)S(1)}, u32[]{:S(2)}, u32[]{:S(2)}) async-start(bf16[4,64,2048]{2,1,0:T(8,128)(2,1)} %bitcast.124), calls=%async_computation.4 | async-start | bytes 2097152 | tf_op jit(solution)/shard_map/all_to_all | solution.py:28
  364.6 26.2 %all-to-all-done.4 = bf16[4,64,2048]{2,1,0:T(8,128)(2,1)S(1)} async-done(((bf16[4,64,2048]{2,1,0:T(8,128)(2,1)}), bf16[4,64,2048]{2,1,0:T(8,128)(2,1)S(1)}, u32[]{:S(2)}, u32[]{:S(2)}) %all-to-all-start.4) | async-done | bytes 1048608 | tf_op jit(solution)/shard_map/all_to_all | solution.py:28
  392.6 3.7 all-to-all-start.5
  396.3 41.3 %all-gather.5.cloned.1.call-done = bf16[2048,3072]{1,0:T(8,128)(2,1)} async-done(((bf16[64,3072]{1,0:T(8,128)(2,1)}), bf16[2048,3072]{1,0:T(8,128)(2,1)}) %all-gather.5.cloned.1.call-update) | async-done | bytes 12582928 | tf_op jit(solution)/shard_map/all_gather | solution.py:124
  437.6 4.6 slice.84
  442.2 7.1 %reshape.424 = bf16[1024,2048]{1,0:T(8,128)(2,1)} reshape(bf16[2048,1024]{1,0:T(8,128)(2,1)} %slice.84) | data formatting | bytes 8388608 | tf_op jit(solution)/shard_map/reshape | solution.py:193
  449.3 3.4 fusion.14
  452.8 5.9 %convolution_convert_fusion.1 = bf16[256,2048]{1,0:T(8,128)(2,1)S(1)} fusion(bf16[1024,2048]{1,0:T(8,128)(2,1)} %reshape.424, bf16[256,2048]{1,0:T(8,128)(2,1)S(1)} %bitcast.134, bf16[2048,3072]{1,0:T(8,128)(2,1)} %all-gather.5.cloned.1.call-done, f32[256,1024]{1,0:T(8,128)S(1)} %fusion.14), kind=kOutput, calls=%fused_computation.32 | convolution fusion | flops 2149580800 | bytes 11534336 | tf_op jit(solution)/shard_map/dot_general | solution.py:194
  458.7 17.6 %all_to_all.42 = bf16[4,64,2048]{2,1,0:T(8,128)(2,1)S(1)} all-to-all(bf16[4,64,2048]{2,1,0:T(8,128)(2,1)S(1)} %bitcast.135), channel_id=1, replica_groups=mesh['y'=4,'r'=8,'mp'=4] {'mp'}, dimensions={0} | all-to-all | bytes 2097152 | tf_op jit(solution)/shard_map/all_to_all | solution.py:28
  (253 shorter events, 48.5 us)
Async XLA Ops:
  6.5 2.1 copy-start.11
  6.5 3.2 copy-start.12
  6.5 3.2 copy-start.10
  10.2 7.1 %copy-start.13 = (f32[64,512]{1,0:T(8,128)S(1)}, f32[64,512]{1,0:T(8,128)}, u32[]{:S(2)}) copy-start(f32[64,512]{1,0:T(8,128)} %param.14) | copy-start | bytes 393220
  10.3 7.1 %copy-start.14 = (f32[64,512]{1,0:T(8,128)S(1)}, f32[64,512]{1,0:T(8,128)}, u32[]{:S(2)}) copy-start(f32[64,512]{1,0:T(8,128)} %param.15) | copy-start | bytes 393220
  10.8 6.6 %copy-start.15 = (f32[64,512]{1,0:T(8,128)S(1)}, f32[64,512]{1,0:T(8,128)}, u32[]{:S(2)}) copy-start(f32[64,512]{1,0:T(8,128)} %param.13) | copy-start | bytes 393220
  13.8 13.7 %all-to-all-start = ((bf16[4,2,40960]{2,1,0:T(2,128)(2,1)}), bf16[4,2,40960]{2,1,0:T(2,128)(2,1)S(1)}, u32[]{:S(2)}, u32[]{:S(2)}) async-start(bf16[4,2,40960]{2,1,0:T(2,128)(2,1)} %reshape.428), calls=%async_computation | async-start | bytes 1310720 | tf_op jit(solution)/shard_map/all_to_all | solution.py:94
  17.3 120.1 %all-gather.3.cloned.1.call-start = ((), (), s32[]{:S(2)}) async-start(), calls=%async_computation.7 | async-start | bytes 2162688 | tf_op jit(solution)/shard_map/all_gather | solution.py:123
  32.4 11.3 %copy-start.16 = (s32[4]{0:T(128)S(1)}, s32[4]{0:T(128)}, u32[]{:S(2)}) copy-start(s32[4]{0:T(128)} %param.12) | copy-start | bytes 52
  32.4 11.6 %copy-start.1 = (bf16[256,2048]{1,0:T(8,128)(2,1)S(1)}, bf16[256,2048]{1,0:T(8,128)(2,1)}, u32[]{:S(2)}) copy-start(bf16[256,2048]{1,0:T(8,128)(2,1)} %param.11) | copy-start | bytes 3145732
  32.4 107.7 %all-to-all-start.1 = ((bf16[32,64,1024]{2,1,0:T(8,128)(2,1)}), bf16[32,64,1024]{2,1,0:T(8,128)(2,1)}, u32[]{:S(2)}, u32[]{:S(2)}) async-start(bf16[32,64,1024]{2,1,0:T(8,128)(2,1)} %broadcast_in_dim.183), calls=%async_computation.1 | async-start | bytes 8388608 | tf_op jit(solution)/shard_map/all_to_all | solution.py:21
  150.2 1.2 copy-start.3
  151.3 7.6 %copy-start.6 = (bf16[256,4,64]{0,2,1:T(8,128)(2,1)}, bf16[256,4,64]{0,2,1:T(8,128)(2,1)S(1)}, u32[]{:S(2)}) copy-start(bf16[256,4,64]{0,2,1:T(8,128)(2,1)S(1)} %get-tuple-element.432) | copy-start | bytes 393220
  151.3 7.6 %copy-start.8 = (bf16[256,4,64]{0,2,1:T(8,128)(2,1)}, bf16[256,4,64]{0,2,1:T(8,128)(2,1)S(1)}, u32[]{:S(2)}) copy-start(bf16[256,4,64]{0,2,1:T(8,128)(2,1)S(1)} %get-tuple-element.433) | copy-start | bytes 393220
  151.4 15.8 %collective-permute-start = (bf16[2,256,4,128]{1,3,2,0:T(8,128)(2,1)S(1)}, bf16[2,256,4,128]{1,3,2,0:T(8,128)(2,1)}, u32[]{:S(2)}, u32[]{:S(2)}) collective-permute-start(bf16[2,256,4,128]{1,3,2,0:T(8,128)(2,1)S(1)} %pad_maximum_fusion.2), channel_id=1, source_target_pairs={{0,64},{4,68},{8,72},{12,76},{16,80},{20,84},{24,88},{28,92},{32,9... | collective-permute-start | bytes 1572872 | tf_op jit(solution)/shard_map/ppermute | solution.py:15
  155.6 20.3 %collective-permute-start.1 = (bf16[2,256,4,128]{1,3,2,0:T(8,128)(2,1)S(1)}, bf16[2,256,4,128]{1,3,2,0:T(8,128)(2,1)S(1)}, u32[]{:S(2)}, u32[]{:S(2)}) collective-permute-start(bf16[2,256,4,128]{1,3,2,0:T(8,128)(2,1)S(1)} %pad_maximum_fusion.2), channel_id=1, source_target_pairs={{0,32},{4,36},{8,40},{12,44},{16,48},{20,52},{24,56},{28,60},{32,6... | collective-permute-start | bytes 1572872 | tf_op jit(solution)/shard_map/ppermute | solution.py:15
  176.2 3.0 copy-start
  185.4 8.2 %copy-start.2 = (bf16[4,1,81920]{2,0,1:T(4,128)(2,1)S(1)}, bf16[4,1,81920]{2,0,1:T(4,128)(2,1)}, u32[]{:S(2)}) copy-start(bf16[4,1,81920]{2,0,1:T(4,128)(2,1)} %copy.142) | copy-start | bytes 1966084
  185.4 103.6 %all-to-all-start.2 = ((bf16[8,2,2,256,4,128]{5,3,4,2,1,0:T(8,128)(2,1)}), bf16[8,2,2,256,4,128]{5,3,4,2,1,0:T(8,128)(2,1)}, u32[]{:S(2)}, u32[]{:S(2)}) async-start(bf16[8,2,2,256,4,128]{5,3,4,2,1,0:T(8,128)(2,1)} %pad_maximum_fusion), calls=%async_computation.2 | async-start | bytes 16777216 | tf_op jit(solution)/shard_map/all_to_all | solution.py:169
  193.4 244.2 %all-gather.5.cloned.1.call-start = ((), (), s32[]{:S(2)}) async-start(), calls=%async_computation.8 | async-start | bytes 12976128 | tf_op jit(solution)/shard_map/all_gather | solution.py:124
  194.4 8.7 %collective-permute-start.2 = (bf16[64,2048]{1,0:T(8,128)(2,1)}, bf16[64,2048]{1,0:T(8,128)(2,1)}, u32[]{:S(2)}, u32[]{:S(2)}) collective-permute-start(bf16[64,2048]{1,0:T(8,128)(2,1)} %bitcast.63), channel_id=1, source_target_pairs={{0,0},{1,32},{2,64},{3,96},{32,1},{33,33},{34,65},{35,97},{64,2},{... | collective-permute-start | bytes 786440 | tf_op jit(solution)/shard_map/ppermute | solution.py:119
  199.4 1.5 copy-start.4
  199.4 1.5 copy-start.5
  199.7 1.4 copy-start.7
  199.7 1.4 copy-start.9
  291.5 56.9 %all-to-all-start.3 = ((bf16[8,64,2048]{2,1,0:T(8,128)(2,1)}), bf16[8,64,2048]{2,1,0:T(8,128)(2,1)}, u32[]{:S(2)}, u32[]{:S(2)}) async-start(bf16[8,64,2048]{2,1,0:T(8,128)(2,1)} %broadcast_in_dim.189), calls=%async_computation.3 | async-start | bytes 4194304 | tf_op jit(solution)/shard_map/all_to_all | solution.py:21
  351.8 39.0 %all-to-all-start.4 = ((bf16[4,64,2048]{2,1,0:T(8,128)(2,1)}), bf16[4,64,2048]{2,1,0:T(8,128)(2,1)S(1)}, u32[]{:S(2)}, u32[]{:S(2)}) async-start(bf16[4,64,2048]{2,1,0:T(8,128)(2,1)} %bitcast.124), calls=%async_computation.4 | async-start | bytes 2097152 | tf_op jit(solution)/shard_map/all_to_all | solution.py:28
  392.6 56.8 %all-to-all-start.5 = ((bf16[4,64,2048]{2,1,0:T(8,128)(2,1)}), bf16[4,64,2048]{2,1,0:T(8,128)(2,1)S(1)}, u32[]{:S(2)}, u32[]{:S(2)}) async-start(bf16[4,64,2048]{2,1,0:T(8,128)(2,1)} %broadcast_in_dim.190), calls=%async_computation.5 | async-start | bytes 2097152 | tf_op jit(solution)/shard_map/all_to_all | solution.py:21
Sparse Core Ops, SparseCore 0:
  30.0 107.3 all-gather.2
  201.0 236.5 all-gather.4

commit v4 on v3

--- a/solution.py
+++ b/solution.py
@@ -92,9 +92,8 @@
     ]
     flat = jnp.concatenate([p.reshape(mp_size, -1) for p in outgoing], axis=1)
     got = lax.all_to_all(flat, mp, 0, 0, tiled=True)
-    q_shard = w_query.astype(half_type)
-    kv_shard = jnp.concatenate([w.astype(half_type) for w in (w_key, w_value)], axis=1)
-    got, q_shard, kv_shard = lax.optimization_barrier((got, q_shard, kv_shard))
+    qkv_shard = jnp.concatenate([w.astype(half_type) for w in (w_key, w_value, w_query)], axis=1)
+    got, qkv_shard = lax.optimization_barrier((got, qkv_shard))
     pieces = []
     at = 0
     for p in outgoing:
@@ -119,8 +118,9 @@
     out_swapped = lax.ppermute(out_full_rows, ("y", mp), swap)
     server_out = gather_by_exchange(out_swapped, "r")
 
-    kv_full = gather_by_exchange(kv_shard, dp)
-    q_full = lax.all_gather(q_shard, dp, axis=0, tiled=True)
+    qkv_full = gather_by_exchange(qkv_shard, dp)
+    kv_full = qkv_full[:, : 2 * narrow]
+    q_full = qkv_full[:, 2 * narrow :]
     rest_full = lax.all_gather(rest_shard, dp, axis=0, tiled=True)
 
     normed = layer_norm(tokens).astype(half_type)
@@ -167,6 +167,7 @@
         (nearer, jnp.broadcast_to(back_one[None], (plane,) + back_one.shape)), axis=1
     )
     received = lax.all_to_all(payload, "r", 0, 0, tiled=True)
+    received, rest_full = lax.optimization_barrier((received, rest_full))
     state = online_step(state, own_pair, own_first)
 
     def slot_step(back, state):

time: 489 us -> 463 us (0.947)
  waiting for transfers between devices: 268 us -> 229 us
  starting transfers between devices: 56 us -> 77.6 us
    all_gather x1 -> x0, waiting for transfers between devices: 92.5 us -> none  [on_device(): q_full = lax.all_gather(q_shard, dp, axis=0, tiled=True)]
    all_to_all x3, waiting for transfers between devices: 0.01 us -> 85.2 us  [gather_by_exchange(): got = lax.all_to_all(copies, axis, 0, 0, tiled=True)]
    all_gather x1, waiting for transfers between devices: 41.3 us -> 0.01 us  [on_device(): rest_full = lax.all_gather(rest_shard, dp, axis=0, tiled=True)]
    all_to_all x1, starting transfers between devices: 8 us -> 26.1 us  [on_device(): received = lax.all_to_all(payload, 'r', 0, 0, tiled=True)]
    all_to_all x1, waiting for transfers between devices: 85.9 us -> 99.5 us  [on_device(): received = lax.all_to_all(payload, 'r', 0, 0, tiled=True)]
    all_to_all x1, waiting for transfers between devices: 26.2 us -> 14.5 us  [scatter_sum(): got = lax.all_to_all(pieces, axis, 0, 0, tiled=True)]
    ppermute x2, waiting for transfers between devices: 12.8 us -> 20 us  [shifted(): lax.ppermute(value, axis, [(source, source + steps) for source in range(c...]
    dot_general x1 -> x0, local copies, waits for them, and re-layouts: 6.53 us -> none  [on_device(): joined_kv = jnp.dot(normed, kv_full, preferred_element_type=jnp.float32)]
  transfers between devices with their start and end apart: 11 -> 10, of which waited for: 7 -> 7; matrix products, arithmetic and copies ran while one was open for 18% -> 20% of each run, Pallas kernels for 0% -> 0%
where the time goes in v4:
time: 463 us; the launch traced here: 461 us
  waiting for transfers between devices  229 us (49%)
  starting transfers between devices  77.6 us (17%)
  matrix products  63.3 us (14%)
  local copies, waits for them, and re-layouts  36.1 us (8%)
  other arithmetic  22.5 us (5%)
  blocking collectives  16.9 us (4%)
  between operations  13.9 us (3%)
    all_to_all x1, waiting for transfers between devices, on_device(): received = lax.all_to_all(payload, 'r', 0, 0, tiled=True)  99.5 us
    all_to_all x3, waiting for transfers between devices, gather_by_exchange(): got = lax.all_to_all(copies, axis, 0, 0, tiled=True)  85.2 us
    all_to_all x1, starting transfers between devices, on_device(): received = lax.all_to_all(payload, 'r', 0, 0, tiled=True)  26.1 us
    all_to_all x3, starting transfers between devices, gather_by_exchange(): got = lax.all_to_all(copies, axis, 0, 0, tiled=True)  24.6 us
    dot_general x17, matrix products, online_step(): jnp.einsum('hqk,khd->qhd', probs, pair[1], preferred_element_type=jnp.flo...  23 us
    dot_general x17, matrix products, online_step(): jnp.einsum('qhd,khd->hqk', query, pair[0], preferred_element_type=jnp.flo...  20.7 us
    ppermute x2, waiting for transfers between devices, shifted(): lax.ppermute(value, axis, [(source, source + steps) for source in range(c...  20 us
    all_to_all x1, blocking collectives, scatter_sum(): got = lax.all_to_all(pieces, axis, 0, 0, tiled=True)  16.9 us
  transfers between devices with their start and end apart: 10, of which 7 were waited for; matrix products, arithmetic and copies ran while one was open for 20% of the time, Pallas kernels for 0%

profile of v4, /device:TPU:4, one launch (start us, length us, event | category | flops | bytes accessed | tf_op | source)
XLA Modules:
  0.0 461.0 jit_solution(3662721390959569930)
XLA Ops:
  10.8 1.5 reduce
  12.3 1.5 reshape.429
  13.8 3.5 all-to-all-start
  17.5 10.1 %all-to-all-done = bf16[4,2,40960]{2,1,0:T(2,128)(2,1)S(1)} async-done(((bf16[4,2,40960]{2,1,0:T(2,128)(2,1)}), bf16[4,2,40960]{2,1,0:T(2,128)(2,1)S(1)}, u32[]{:S(2)}, u32[]{:S(2)}) %all-to-all-start) | async-done | bytes 655392 | tf_op jit(solution)/shard_map/all_to_all | solution.py:94
  32.8 3.3 broadcast_in_dim.183
  36.1 11.3 %all-to-all-start.1 = ((bf16[32,64,1536]{2,1,0:T(8,128)(2,1)}), bf16[32,64,1536]{2,1,0:T(8,128)(2,1)}, u32[]{:S(2)}, u32[]{:S(2)}) async-start(bf16[32,64,1536]{2,1,0:T(8,128)(2,1)} %broadcast_in_dim.183), calls=%async_computation.1 | async-start | bytes 12582912 | tf_op jit(solution)/shard_map/all_to_all | solution.py:21
  49.6 82.7 %all-to-all-done.1 = bf16[32,64,1536]{2,1,0:T(8,128)(2,1)} async-done(((bf16[32,64,1536]{2,1,0:T(8,128)(2,1)}), bf16[32,64,1536]{2,1,0:T(8,128)(2,1)}, u32[]{:S(2)}, u32[]{:S(2)}) %all-to-all-start.1) | async-done | bytes 6291488 | tf_op jit(solution)/shard_map/all_to_all | solution.py:21
  132.3 4.5 fusion.12
  136.8 1.7 reshape.414
  138.8 2.4 fusion.22
  143.7 5.1 %collective-permute-start = (bf16[2,256,4,128]{3,1,2,0:T(8,128)(2,1)S(1)}, bf16[2,256,4,128]{3,1,2,0:T(8,128)(2,1)S(1)}, u32[]{:S(2)}, u32[]{:S(2)}) collective-permute-start(bf16[2,256,4,128]{3,1,2,0:T(8,128)(2,1)S(1)} %pad_maximum_fusion.2), channel_id=1, source_target_pairs={{0,64},{4,68},{8,72},{12,76},{16,80},{20,84},{24,88},{28,92},{32,9... | collective-permute-start | bytes 1572872 | tf_op jit(solution)/shard_map/ppermute | solution.py:15
  148.8 1.4 collective-permute-start.1
  150.2 10.9 %collective-permute-done = bf16[2,256,4,128]{3,1,2,0:T(8,128)(2,1)S(1)} collective-permute-done((bf16[2,256,4,128]{3,1,2,0:T(8,128)(2,1)S(1)}, bf16[2,256,4,128]{3,1,2,0:T(8,128)(2,1)S(1)}, u32[]{:S(2)}, u32[]{:S(2)}) %collective-permute-start) | collective-permute-done | bytes 524320 | tf_op jit(solution)/shard_map/ppermute | solution.py:15
  161.7 9.0 %collective-permute-done.1 = bf16[2,256,4,128]{3,1,2,0:T(8,128)(2,1)S(1)} collective-permute-done((bf16[2,256,4,128]{3,1,2,0:T(8,128)(2,1)S(1)}, bf16[2,256,4,128]{3,1,2,0:T(8,128)(2,1)S(1)}, u32[]{:S(2)}, u32[]{:S(2)}) %collective-permute-start.1) | collective-permute-done | bytes 524320 | tf_op jit(solution)/shard_map/ppermute | solution.py:15
  170.8 3.0 stack_broadcast_in_dim.2
  173.7 7.4 %pad_maximum_fusion = bf16[8,2,2,256,4,128]{5,3,4,2,1,0:T(8,128)(2,1)} fusion(bf16[8,1,2,256,4,128]{5,3,4,2,1,0:T(8,128)(2,1)} %stack_broadcast_in_dim.2, bf16[8,1,2,256,4,128]{5,3,4,2,1,0:T(8,128)(2,1)S(1)} %broadcast_select_fusion), kind=kLoop, calls=%fused_computation.23 | loop fusion | flops 4194304 | bytes 16777216 | tf_op jit(solution)/shard_map/stack | solution.py:166
  181.1 26.1 %all-to-all-start.2 = ((bf16[8,2,2,256,4,128]{5,3,4,2,1,0:T(8,128)(2,1)}), bf16[8,2,2,256,4,128]{5,3,4,2,1,0:T(8,128)(2,1)}, u32[]{:S(2)}, u32[]{:S(2)}) async-start(bf16[8,2,2,256,4,128]{5,3,4,2,1,0:T(8,128)(2,1)} %pad_maximum_fusion), calls=%async_computation.2 | async-start | bytes 16777216 | tf_op jit(solution)/shard_map/all_to_all | solution.py:169
  208.5 1.4 collective-permute-start.2
  210.9 99.5 %all-to-all-done.2 = bf16[8,2,2,256,4,128]{5,3,4,2,1,0:T(8,128)(2,1)} async-done(((bf16[8,2,2,256,4,128]{5,3,4,2,1,0:T(8,128)(2,1)}), bf16[8,2,2,256,4,128]{5,3,4,2,1,0:T(8,128)(2,1)}, u32[]{:S(2)}, u32[]{:S(2)}) %all-to-all-start.2) | async-done | bytes 8388640 | tf_op jit(solution)/shard_map/all_to_all | solution.py:169
  310.4 2.5 broadcast_in_dim.189
  312.9 9.6 %all-to-all-start.3 = ((bf16[8,64,2048]{2,1,0:T(8,128)(2,1)}), bf16[8,64,2048]{2,1,0:T(8,128)(2,1)}, u32[]{:S(2)}, u32[]{:S(2)}) async-start(bf16[8,64,2048]{2,1,0:T(8,128)(2,1)} %broadcast_in_dim.189), calls=%async_computation.3 | async-start | bytes 4194304 | tf_op jit(solution)/shard_map/all_to_all | solution.py:21
  322.5 51.2 %while.21 = (s32[]{:T(128)}, f32[256,4,128]{0,2,1:T(8,128)S(1)}, f32[4,256,1]{1,0,2:T(4,128)S(1)}, f32[4,256,1]{1,0,2:T(4,128)S(1)}, s32[256]{0:T(256)S(1)}, /*i...) while((s32[]{:T(128)}, f32[256,4,128]{0,2,1:T(8,128)S(1)}, ...), condition=%wide.region_11.12_spmd.clone.clone, body=%wide.region_7.11_spmd.clone.clone.sunk | while | flops 136518688 | bytes 5188022 | solution.py:179
  324.2 1.4 fusion.77
  327.4 1.4 fusion.77
  330.6 1.4 fusion.77
  333.8 1.4 fusion.77
  337.0 1.4 fusion.77
  340.2 1.4 fusion.77
  343.4 1.4 fusion.77
  346.6 1.4 fusion.77
  349.9 1.4 fusion.77
  353.1 1.4 fusion.77
  356.3 1.4 fusion.77
  359.5 1.4 fusion.77
  362.7 1.4 fusion.77
  365.9 1.4 fusion.77
  369.1 1.4 fusion.77
  372.3 1.4 fusion.77
  373.8 3.4 convolution_convert_fusion
  377.1 15.6 %all-to-all-start.4 = ((bf16[4,64,2048]{2,1,0:T(8,128)(2,1)}), bf16[4,64,2048]{2,1,0:T(8,128)(2,1)S(1)}, u32[]{:S(2)}, u32[]{:S(2)}) async-start(bf16[4,64,2048]{2,1,0:T(8,128)(2,1)} %bitcast.116), calls=%async_computation.4 | async-start | bytes 2097152 | tf_op jit(solution)/shard_map/all_to_all | solution.py:28
  392.7 14.5 %all-to-all-done.4 = bf16[4,64,2048]{2,1,0:T(8,128)(2,1)S(1)} async-done(((bf16[4,64,2048]{2,1,0:T(8,128)(2,1)}), bf16[4,64,2048]{2,1,0:T(8,128)(2,1)S(1)}, u32[]{:S(2)}, u32[]{:S(2)}) %all-to-all-start.4) | async-done | bytes 1048608 | tf_op jit(solution)/shard_map/all_to_all | solution.py:28
  409.0 3.7 all-to-all-start.5
  412.8 4.6 slice.79
  417.3 7.1 %reshape.426 = bf16[1024,2048]{1,0:T(8,128)(2,1)} reshape(bf16[2048,1024]{1,0:T(8,128)(2,1)} %slice.79) | data formatting | bytes 8388608 | tf_op jit(solution)/shard_map/reshape | solution.py:194
  424.5 2.5 all-to-all-done.5
  427.0 3.4 fusion.16
  430.4 5.9 %convolution_convert_fusion.1 = bf16[256,2048]{1,0:T(8,128)(2,1)S(1)} fusion(bf16[1024,2048]{1,0:T(8,128)(2,1)} %reshape.426, bf16[256,2048]{1,0:T(8,128)(2,1)S(1)} %bitcast.129, bf16[2048,3072]{1,0:T(8,128)(2,1)} %all-gather.2.cloned.1.call-done, f32[256,1024]{1,0:T(8,128)S(1)} %fusion.16), kind=kOutput, calls=%fused_computation.34 | convolution fusion | flops 2149580800 | bytes 11534336 | tf_op jit(solution)/shard_map/dot_general | solution.py:195
  436.3 16.9 %all_to_all.42 = bf16[4,64,2048]{2,1,0:T(8,128)(2,1)S(1)} all-to-all(bf16[4,64,2048]{2,1,0:T(8,128)(2,1)S(1)} %bitcast.130), channel_id=1, replica_groups=mesh['y'=4,'r'=8,'mp'=4] {'mp'}, dimensions={0} | all-to-all | bytes 2097152 | tf_op jit(solution)/shard_map/all_to_all | solution.py:28
  (245 shorter events, 47.1 us)
Async XLA Ops:
  6.5 2.1 copy-start.9
  6.5 3.2 copy-start.10
  6.5 3.2 copy-start.8
  10.2 7.1 %copy-start.11 = (f32[64,512]{1,0:T(8,128)S(1)}, f32[64,512]{1,0:T(8,128)}, u32[]{:S(2)}) copy-start(f32[64,512]{1,0:T(8,128)} %param.14) | copy-start | bytes 393220
  10.3 7.1 %copy-start.12 = (f32[64,512]{1,0:T(8,128)S(1)}, f32[64,512]{1,0:T(8,128)}, u32[]{:S(2)}) copy-start(f32[64,512]{1,0:T(8,128)} %param.15) | copy-start | bytes 393220
  10.8 6.6 %copy-start.13 = (f32[64,512]{1,0:T(8,128)S(1)}, f32[64,512]{1,0:T(8,128)}, u32[]{:S(2)}) copy-start(f32[64,512]{1,0:T(8,128)} %param.13) | copy-start | bytes 393220
  13.8 13.7 %all-to-all-start = ((bf16[4,2,40960]{2,1,0:T(2,128)(2,1)}), bf16[4,2,40960]{2,1,0:T(2,128)(2,1)S(1)}, u32[]{:S(2)}, u32[]{:S(2)}) async-start(bf16[4,2,40960]{2,1,0:T(2,128)(2,1)} %reshape.429), calls=%async_computation | async-start | bytes 1310720 | tf_op jit(solution)/shard_map/all_to_all | solution.py:94
  17.3 305.2 %all-gather.2.cloned.1.call-start = ((), (), s32[]{:S(2)}) async-start(), calls=%async_computation.7 | async-start | bytes 12976128 | tf_op jit(solution)/shard_map/all_gather | solution.py:124
  29.0 0.9 copy-start.1
  36.1 11.3 %copy-start.14 = (s32[4]{0:T(128)S(1)}, s32[4]{0:T(128)}, u32[]{:S(2)}) copy-start(s32[4]{0:T(128)} %param.12) | copy-start | bytes 52
  36.1 11.6 %copy-start = (bf16[256,2048]{1,0:T(8,128)(2,1)S(1)}, bf16[256,2048]{1,0:T(8,128)(2,1)}, u32[]{:S(2)}) copy-start(bf16[256,2048]{1,0:T(8,128)(2,1)} %param.11) | copy-start | bytes 3145732
  36.1 96.2 %all-to-all-start.1 = ((bf16[32,64,1536]{2,1,0:T(8,128)(2,1)}), bf16[32,64,1536]{2,1,0:T(8,128)(2,1)}, u32[]{:S(2)}, u32[]{:S(2)}) async-start(bf16[32,64,1536]{2,1,0:T(8,128)(2,1)} %broadcast_in_dim.183), calls=%async_computation.1 | async-start | bytes 12582912 | tf_op jit(solution)/shard_map/all_to_all | solution.py:21
  141.4 0.9 copy-start.6
  141.4 1.0 copy-start.7
  143.5 6.7 %copy-start.2 = (bf16[256,4,64]{2,0,1:T(8,128)(2,1)}, bf16[256,4,64]{2,0,1:T(8,128)(2,1)S(1)}, u32[]{:S(2)}) copy-start(bf16[256,4,64]{2,0,1:T(8,128)(2,1)S(1)} %get-tuple-element.371) | copy-start | bytes 393220
  143.7 17.5 %collective-permute-start = (bf16[2,256,4,128]{3,1,2,0:T(8,128)(2,1)S(1)}, bf16[2,256,4,128]{3,1,2,0:T(8,128)(2,1)S(1)}, u32[]{:S(2)}, u32[]{:S(2)}) collective-permute-start(bf16[2,256,4,128]{3,1,2,0:T(8,128)(2,1)S(1)} %pad_maximum_fusion.2), channel_id=1, source_target_pairs={{0,64},{4,68},{8,72},{12,76},{16,80},{20,84},{24,88},{28,92},{32,9... | collective-permute-start | bytes 1572872 | tf_op jit(solution)/shard_map/ppermute | solution.py:15
  148.8 21.9 %collective-permute-start.1 = (bf16[2,256,4,128]{3,1,2,0:T(8,128)(2,1)S(1)}, bf16[2,256,4,128]{3,1,2,0:T(8,128)(2,1)S(1)}, u32[]{:S(2)}, u32[]{:S(2)}) collective-permute-start(bf16[2,256,4,128]{3,1,2,0:T(8,128)(2,1)S(1)} %pad_maximum_fusion.2), channel_id=1, source_target_pairs={{0,32},{4,36},{8,40},{12,44},{16,48},{20,52},{24,56},{28,60},{32,6... | collective-permute-start | bytes 1572872 | tf_op jit(solution)/shard_map/ppermute | solution.py:15
  181.1 28.7 %copy-start.4 = (bf16[256,4,64]{2,0,1:T(8,128)(2,1)S(1)}, bf16[256,4,64]{2,0,1:T(8,128)(2,1)}, u32[]{:S(2)}) copy-start(bf16[256,4,64]{2,0,1:T(8,128)(2,1)} %get-tuple-element.361) | copy-start | bytes 393220
  181.1 28.7 %copy-start.5 = (bf16[256,4,64]{2,0,1:T(8,128)(2,1)S(1)}, bf16[256,4,64]{2,0,1:T(8,128)(2,1)}, u32[]{:S(2)}) copy-start(bf16[256,4,64]{2,0,1:T(8,128)(2,1)} %get-tuple-element.362) | copy-start | bytes 393220
  181.1 28.9 %copy-start.3 = (bf16[256,4,64]{2,0,1:T(8,128)(2,1)S(1)}, bf16[256,4,64]{2,0,1:T(8,128)(2,1)}, u32[]{:S(2)}) copy-start(bf16[256,4,64]{2,0,1:T(8,128)(2,1)} %copy-done.2) | copy-start | bytes 393220
  181.1 129.3 %all-to-all-start.2 = ((bf16[8,2,2,256,4,128]{5,3,4,2,1,0:T(8,128)(2,1)}), bf16[8,2,2,256,4,128]{5,3,4,2,1,0:T(8,128)(2,1)}, u32[]{:S(2)}, u32[]{:S(2)}) async-start(bf16[8,2,2,256,4,128]{5,3,4,2,1,0:T(8,128)(2,1)} %pad_maximum_fusion), calls=%async_computation.2 | async-start | bytes 16777216 | tf_op jit(solution)/shard_map/all_to_all | solution.py:169
  208.5 2.4 collective-permute-start.2
  312.9 60.9 %all-to-all-start.3 = ((bf16[8,64,2048]{2,1,0:T(8,128)(2,1)}), bf16[8,64,2048]{2,1,0:T(8,128)(2,1)}, u32[]{:S(2)}, u32[]{:S(2)}) async-start(bf16[8,64,2048]{2,1,0:T(8,128)(2,1)} %broadcast_in_dim.189), calls=%async_computation.3 | async-start | bytes 4194304 | tf_op jit(solution)/shard_map/all_to_all | solution.py:21
  377.1 30.0 %all-to-all-start.4 = ((bf16[4,64,2048]{2,1,0:T(8,128)(2,1)}), bf16[4,64,2048]{2,1,0:T(8,128)(2,1)S(1)}, u32[]{:S(2)}, u32[]{:S(2)}) async-start(bf16[4,64,2048]{2,1,0:T(8,128)(2,1)} %bitcast.116), calls=%async_computation.4 | async-start | bytes 2097152 | tf_op jit(solution)/shard_map/all_to_all | solution.py:28
  409.0 18.0 %all-to-all-start.5 = ((bf16[4,64,2048]{2,1,0:T(8,128)(2,1)}), bf16[4,64,2048]{2,1,0:T(8,128)(2,1)S(1)}, u32[]{:S(2)}, u32[]{:S(2)}) async-start(bf16[4,64,2048]{2,1,0:T(8,128)(2,1)} %broadcast_in_dim.190), calls=%async_computation.5 | async-start | bytes 2097152 | tf_op jit(solution)/shard_map/all_to_all | solution.py:21
Sparse Core Ops, SparseCore 0:
  32.9 273.0 all-gather.1

commit v5 on v4

--- a/solution.py
+++ b/solution.py
@@ -129,12 +129,13 @@
     shaped = joined_kv.reshape(rows, 2, heads_dev, HEAD)
     keys = rotate(shaped[:, 0], q_offset).astype(half_type)
     values = shaped[:, 1].astype(half_type)
-    own_pair = jnp.stack((keys, values))
+    own_pair = jnp.transpose(jnp.stack((keys, values)), (0, 2, 1, 3))
     plane = r_size
     back_one = shifted(own_pair, dp, plane)
     back_two = shifted(own_pair, dp, 2 * plane)
     joined_q = jnp.dot(normed, q_full, preferred_element_type=jnp.float32)
     query = rotate(joined_q.reshape(rows, heads_dev, HEAD), q_offset).astype(half_type)
+    query = jnp.transpose(query, (1, 0, 2))
     own_first = dp_index * rows
     scale = 1.0 / HEAD**0.5
 
@@ -142,7 +143,7 @@
         accum, total, top = state
         k_prompt, k_offset, k_where = prompt_coords(first, rows, lengths)
         scores = (
-            jnp.einsum("qhd,khd->hqk", query, pair[0], preferred_element_type=jnp.float32) * scale
+            jnp.einsum("hqd,hkd->hqk", query, pair[0], preferred_element_type=jnp.float32) * scale
         )
         allowed = (q_prompt[:, None] == k_prompt[None, :]) & (k_where[None, :] <= q_where[:, None])
         scores = jnp.where(allowed[None], scores, -jnp.inf)
@@ -150,13 +151,13 @@
         fade = jnp.exp(top - new_top)
         weights = jnp.exp(scores - new_top)
         probs = weights.astype(half_type)
-        product = jnp.einsum("hqk,khd->qhd", probs, pair[1], preferred_element_type=jnp.float32)
-        accum = accum * jnp.transpose(fade, (1, 0, 2)) + product
+        product = jnp.einsum("hqk,hkd->hqd", probs, pair[1], preferred_element_type=jnp.float32)
+        accum = accum * fade + product
         total = total * fade + jnp.sum(weights, axis=-1, keepdims=True)
         return (accum, total, new_top)
 
     state = (
-        jnp.zeros((rows, heads_dev, HEAD), jnp.float32),
+        jnp.zeros((heads_dev, rows, HEAD), jnp.float32),
         jnp.zeros((heads_dev, rows, 1), jnp.float32),
         jnp.full((heads_dev, rows, 1), -jnp.inf, jnp.float32),
     )
@@ -167,7 +168,12 @@
         (nearer, jnp.broadcast_to(back_one[None], (plane,) + back_one.shape)), axis=1
     )
     received = lax.all_to_all(payload, "r", 0, 0, tiled=True)
-    received, rest_full = lax.optimization_barrier((received, rest_full))
+    server_gate = rest_full[:, :units]
+    server_up = rest_full[:, units : 2 * units]
+    server_down = rest_full[:, 2 * units :].reshape(units, -1)
+    received, server_gate, server_up, server_down = lax.optimization_barrier(
+        (received, server_gate, server_up, server_down)
+    )
     state = online_step(state, own_pair, own_first)
 
     def slot_step(back, state):
@@ -178,7 +184,7 @@
 
     state = lax.fori_loop(1, reach + 1, slot_step, state)
     accum, total, top = state
-    context = (accum / jnp.transpose(total, (1, 0, 2))).astype(half_type).reshape(rows, narrow)
+    context = jnp.transpose((accum / total).astype(half_type), (1, 0, 2)).reshape(rows, narrow)
 
     partial_out = jnp.dot(context, server_out, preferred_element_type=jnp.float32)
     attended = scatter_sum(partial_out.astype(half_type), mp)
@@ -188,10 +194,9 @@
     normed_own = layer_norm(mixed).astype(half_type)
     normed_two = gather_by_exchange(normed_own, mp)
 
-    gate = jnp.dot(normed_two, rest_full[:, :units], preferred_element_type=jnp.float32)
-    upper = jnp.dot(normed_two, rest_full[:, units : 2 * units], preferred_element_type=jnp.float32)
+    gate = jnp.dot(normed_two, server_gate, preferred_element_type=jnp.float32)
+    upper = jnp.dot(normed_two, server_up, preferred_element_type=jnp.float32)
     hidden = (jax.nn.silu(gate) * upper).astype(half_type)
-    server_down = rest_full[:, 2 * units :].reshape(units, -1)
     partial_down = jnp.dot(hidden, server_down, preferred_element_type=jnp.float32)
     share = scatter_sum(partial_down.astype(half_type), mp)
     return (mixed.astype(jnp.float32) + share).astype(half_type)

time: 463 us -> 461 us (level)
  starting transfers between devices: 77.6 us -> 60.2 us
  blocking collectives: 16.9 us -> 34 us
    all_to_all x1, waiting for transfers between devices: 99.5 us -> 0.01 us  [on_device(): received = lax.all_to_all(payload, 'r', 0, 0, tiled=True)]
    all_gather x1, waiting for transfers between devices: 0.01 us -> 98.1 us  [on_device(): rest_full = lax.all_gather(rest_shard, dp, axis=0, tiled=True)]
    all_to_all x0 -> x1, blocking collectives: none -> 17.1 us  [gather_by_exchange(): got = lax.all_to_all(copies, axis, 0, 0, tiled=True)]
    all_to_all x1, starting transfers between devices: 15.6 us -> 4.26 us  [scatter_sum(): got = lax.all_to_all(pieces, axis, 0, 0, tiled=True)]
    all_to_all x3 -> x2, starting transfers between devices: 24.6 us -> 18.8 us  [gather_by_exchange(): got = lax.all_to_all(copies, axis, 0, 0, tiled=True)]
    all_to_all x3 -> x2, waiting for transfers between devices: 85.2 us -> 82.6 us  [gather_by_exchange(): got = lax.all_to_all(copies, axis, 0, 0, tiled=True)]
  transfers between devices with their start and end apart: 10 -> 9, of which waited for: 7 -> 6; matrix products, arithmetic and copies ran while one was open for 20% -> 21% of each run, Pallas kernels for 0% -> 0%
where the time goes in v5:
time: 461 us; the launch traced here: 457 us
  waiting for transfers between devices  225 us (49%)
  starting transfers between devices  60.2 us (13%)
  matrix products  59.5 us (13%)
  local copies, waits for them, and re-layouts  37.4 us (8%)
  blocking collectives  34 us (7%)
  other arithmetic  25.1 us (5%)
  between operations  13.9 us (3%)
    all_gather x1, waiting for transfers between devices, on_device(): rest_full = lax.all_gather(rest_shard, dp, axis=0, tiled=True)  98.1 us
    all_to_all x2, waiting for transfers between devices, gather_by_exchange(): got = lax.all_to_all(copies, axis, 0, 0, tiled=True)  82.6 us
    all_to_all x1, starting transfers between devices, on_device(): received = lax.all_to_all(payload, 'r', 0, 0, tiled=True)  26.4 us
    dot_general x17, matrix products, online_step(): jnp.einsum('hqk,hkd->hqd', probs, pair[1], preferred_element_type=jnp.flo...  23.1 us
    dot_general x17, matrix products, online_step(): jnp.einsum('hqd,hkd->hqk', query, pair[0], preferred_element_type=jnp.flo...  20.7 us
    ppermute x2, waiting for transfers between devices, shifted(): lax.ppermute(value, axis, [(source, source + steps) for source in range(c...  20 us
    all_to_all x2, starting transfers between devices, gather_by_exchange(): got = lax.all_to_all(copies, axis, 0, 0, tiled=True)  18.8 us
    all_to_all x1, blocking collectives, gather_by_exchange(): got = lax.all_to_all(copies, axis, 0, 0, tiled=True)  17.1 us
  transfers between devices with their start and end apart: 9, of which 6 were waited for; matrix products, arithmetic and copies ran while one was open for 21% of the time, Pallas kernels for 0%

profile of v5, /device:TPU:4, one launch (start us, length us, event | category | flops | bytes accessed | tf_op | source)
XLA Modules:
  0.0 456.9 jit_solution(204794781337081777)
XLA Ops:
  13.5 1.5 reduce
  15.0 1.5 reshape.430
  16.5 3.5 all-to-all-start
  20.1 10.1 %all-to-all-done = bf16[4,2,40960]{2,1,0:T(2,128)(2,1)S(1)} async-done(((bf16[4,2,40960]{2,1,0:T(2,128)(2,1)}), bf16[4,2,40960]{2,1,0:T(2,128)(2,1)S(1)}, u32[]{:S(2)}, u32[]{:S(2)}) %all-to-all-start) | async-done | bytes 655392 | tf_op jit(solution)/shard_map/all_to_all | solution.py:94
  34.6 3.3 broadcast_in_dim.187
  37.9 11.3 %all-to-all-start.1 = ((bf16[32,64,1536]{2,1,0:T(8,128)(2,1)}), bf16[32,64,1536]{2,1,0:T(8,128)(2,1)}, u32[]{:S(2)}, u32[]{:S(2)}) async-start(bf16[32,64,1536]{2,1,0:T(8,128)(2,1)} %broadcast_in_dim.187), calls=%async_computation.1 | async-start | bytes 12582912 | tf_op jit(solution)/shard_map/all_to_all | solution.py:21
  51.4 82.6 %all-to-all-done.1 = bf16[32,64,1536]{2,1,0:T(8,128)(2,1)} async-done(((bf16[32,64,1536]{2,1,0:T(8,128)(2,1)}), bf16[32,64,1536]{2,1,0:T(8,128)(2,1)}, u32[]{:S(2)}, u32[]{:S(2)}) %all-to-all-start.1) | async-done | bytes 6291488 | tf_op jit(solution)/shard_map/all_to_all | solution.py:21
  134.1 4.5 fusion.11
  138.5 1.7 reshape.415
  140.4 2.4 fusion.17
  143.5 1.4 subtract_convert_fusion.1
  145.0 5.2 %collective-permute-start = (bf16[2,4,256,128]{3,2,1,0:T(8,128)(2,1)S(1)}, bf16[2,4,256,128]{3,2,1,0:T(8,128)(2,1)S(1)}, u32[]{:S(2)}, u32[]{:S(2)}) collective-permute-start(bf16[2,4,256,128]{3,2,1,0:T(8,128)(2,1)S(1)} %maximum_bitcast_fusion.1), channel_id=1, source_target_pairs={{0,64},{4,68},{8,72},{12,76},{16,80},{20,84},{24,88},{28,92},{32,9... | collective-permute-start | bytes 1572872 | tf_op jit(solution)/shard_map/ppermute | solution.py:15
  150.2 1.3 collective-permute-start.1
  151.6 11.0 %collective-permute-done = bf16[2,4,256,128]{3,2,1,0:T(8,128)(2,1)S(1)} collective-permute-done((bf16[2,4,256,128]{3,2,1,0:T(8,128)(2,1)S(1)}, bf16[2,4,256,128]{3,2,1,0:T(8,128)(2,1)S(1)}, u32[]{:S(2)}, u32[]{:S(2)}) %collective-permute-start) | collective-permute-done | bytes 524320 | tf_op jit(solution)/shard_map/ppermute | solution.py:15
  163.2 9.0 %collective-permute-done.1 = bf16[2,4,256,128]{3,2,1,0:T(8,128)(2,1)S(1)} collective-permute-done((bf16[2,4,256,128]{3,2,1,0:T(8,128)(2,1)S(1)}, bf16[2,4,256,128]{3,2,1,0:T(8,128)(2,1)S(1)}, u32[]{:S(2)}, u32[]{:S(2)}) %collective-permute-start.1) | collective-permute-done | bytes 524320 | tf_op jit(solution)/shard_map/ppermute | solution.py:15
  172.2 3.0 stack_broadcast_in_dim.2
  175.1 6.9 %pad_maximum_fusion = bf16[8,2,2,4,256,128]{5,4,3,2,1,0:T(8,128)(2,1)} fusion(bf16[8,1,2,4,256,128]{5,4,3,2,1,0:T(8,128)(2,1)} %stack_broadcast_in_dim.2, bf16[8,1,2,4,256,128]{5,4,3,2,1,0:T(8,128)(2,1)S(1)} %broadcast_select_fusion), kind=kLoop, calls=%fused_computation.22 | loop fusion | flops 4194304 | bytes 16777216 | tf_op jit(solution)/shard_map/stack | solution.py:167
  182.1 26.4 %all-to-all-start.2 = ((bf16[8,2,2,4,256,128]{5,4,3,2,1,0:T(8,128)(2,1)}), bf16[8,2,2,4,256,128]{5,4,3,2,1,0:T(8,128)(2,1)}, u32[]{:S(2)}, u32[]{:S(2)}) async-start(bf16[8,2,2,4,256,128]{5,4,3,2,1,0:T(8,128)(2,1)} %pad_maximum_fusion), calls=%async_computation.2 | async-start | bytes 16777216 | tf_op jit(solution)/shard_map/all_to_all | solution.py:170
  210.5 98.1 %all-gather.2.cloned.1.call-done = bf16[2048,3072]{1,0:T(8,128)(2,1)} async-done(((bf16[64,3072]{1,0:T(8,128)(2,1)}), bf16[2048,3072]{1,0:T(8,128)(2,1)}) %all-gather.2.cloned.1.call-update) | async-done | bytes 12582928 | tf_op jit(solution)/shard_map/all_gather | solution.py:124
  308.7 9.1 %fusion.40 = (bf16[2048,1024]{1,0:T(8,128)(2,1)}, bf16[2048,1024]{1,0:T(8,128)(2,1)}, bf16[2048,1024]{1,0:T(8,128)(2,1)}) fusion(bf16[2048,3072]{1,0:T(8,128)(2,1)} %all-gather.2.cloned.1.call-done), kind=kLoop, calls=%fused_computation.96 | loop fusion | bytes 25165824 | tf_op jit(solution)/shard_map/slice | solution.py:173
  317.8 7.1 %reshape.421 = bf16[1024,2048]{1,0:T(8,128)(2,1)} reshape(bf16[2048,1024]{1,0:T(8,128)(2,1)} %get-tuple-element.365) | data formatting | bytes 8388608 | tf_op jit(solution)/shard_map/reshape | solution.py:173
  324.9 1.6 broadcast_in_dim.195
  326.5 7.5 %all-to-all-start.3 = ((bf16[8,64,2048]{2,1,0:T(8,128)(2,1)}), bf16[8,64,2048]{2,1,0:T(8,128)(2,1)S(1)}, u32[]{:S(2)}, u32[]{:S(2)}) async-start(bf16[8,64,2048]{2,1,0:T(8,128)(2,1)} %broadcast_in_dim.195), calls=%async_computation.3 | async-start | bytes 4194304 | tf_op jit(solution)/shard_map/all_to_all | solution.py:21
  334.0 51.2 %while.21 = (s32[]{:T(128)}, f32[4,256,128]{2,1,0:T(8,128)S(1)}, f32[4,256,1]{1,0,2:T(4,128)S(1)}, f32[4,256,1]{1,0,2:T(4,128)S(1)}, s32[256]{0:T(256)S(1)}, /*i...) while((s32[]{:T(128)}, f32[4,256,128]{2,1,0:T(8,128)S(1)}, ...), condition=%wide.region_11.12_spmd.clone.clone, body=%wide.region_7.11_spmd.clone.clone.sunk | while | flops 136518688 | bytes 5188022 | solution.py:185
  334.3 1.3 fusion.61
  335.7 1.4 convolution_add_fusion.3
  338.9 1.4 convolution_add_fusion.3
  342.1 1.4 convolution_add_fusion.3
  345.3 1.4 convolution_add_fusion.3
  348.5 1.4 convolution_add_fusion.3
  351.7 1.4 convolution_add_fusion.3
  354.9 1.4 convolution_add_fusion.3
  358.1 1.4 convolution_add_fusion.3
  361.3 1.4 convolution_add_fusion.3
  364.5 1.4 convolution_add_fusion.3
  367.7 1.4 convolution_add_fusion.3
  371.0 1.4 convolution_add_fusion.3
  374.2 1.4 convolution_add_fusion.3
  377.4 1.4 convolution_add_fusion.3
  380.6 1.4 convolution_add_fusion.3
  383.8 1.4 convolution_add_fusion.3
  385.5 1.7 convolution_convert_fusion
  387.2 4.3 all-to-all-start.4
  391.5 14.5 %all-to-all-done.4 = bf16[4,64,2048]{2,1,0:T(8,128)(2,1)S(1)} async-done(((bf16[4,64,2048]{2,1,0:T(8,128)(2,1)}), bf16[4,64,2048]{2,1,0:T(8,128)(2,1)S(1)}, u32[]{:S(2)}, u32[]{:S(2)}) %all-to-all-start.4) | async-done | bytes 1048608 | tf_op jit(solution)/shard_map/all_to_all | solution.py:28
  407.9 17.1 %all_to_all.42 = bf16[4,64,2048]{2,1,0:T(8,128)(2,1)S(1)} all-to-all(bf16[4,64,2048]{2,1,0:T(8,128)(2,1)S(1)} %broadcast_in_dim.196), channel_id=1, replica_groups=mesh['y'=4,'r'=8,'mp'=4] {'mp'}, dimensions={0} | all-to-all | bytes 2097152 | tf_op jit(solution)/shard_map/all_to_all | solution.py:21
  425.0 1.3 fusion.44
  426.3 5.9 %convolution_convert_fusion.1 = bf16[256,2048]{1,0:T(8,128)(2,1)S(1)} fusion(bf16[1024,2048]{1,0:T(8,128)(2,1)} %reshape.421, bf16[256,2048]{1,0:T(8,128)(2,1)S(1)} %bitcast.124, bf16[2048,1024]{1,0:T(8,128)(2,1)} %get-tuple-element.278, f32[256,1024]{1,0:T(8,128)S(1)} %fusion.44), kind=kOutput, calls=%fused_computation.29 | convolution fusion | flops 2149580800 | bytes 11534336 | tf_op jit(solution)/shard_map/dot_general | solution.py:200
  432.2 16.9 %all_to_all.43 = bf16[4,64,2048]{2,1,0:T(8,128)(2,1)S(1)} all-to-all(bf16[4,64,2048]{2,1,0:T(8,128)(2,1)S(1)} %bitcast.125), channel_id=1, replica_groups=mesh['y'=4,'r'=8,'mp'=4] {'mp'}, dimensions={0} | all-to-all | bytes 2097152 | tf_op jit(solution)/shard_map/all_to_all | solution.py:28
  (230 shorter events, 46.0 us)
Async XLA Ops:
  10.0 10.0 %copy-start.2 = (f32[64,512]{1,0:T(8,128)S(1)}, f32[64,512]{1,0:T(8,128)}, u32[]{:S(2)}) copy-start(f32[64,512]{1,0:T(8,128)} %param.13) | copy-start | bytes 393220
  10.0 10.1 %copy-start.3 = (f32[64,512]{1,0:T(8,128)S(1)}, f32[64,512]{1,0:T(8,128)}, u32[]{:S(2)}) copy-start(f32[64,512]{1,0:T(8,128)} %param.14) | copy-start | bytes 393220
  10.0 10.1 %copy-start.4 = (f32[64,512]{1,0:T(8,128)S(1)}, f32[64,512]{1,0:T(8,128)}, u32[]{:S(2)}) copy-start(f32[64,512]{1,0:T(8,128)} %param.15) | copy-start | bytes 393220
  16.5 13.7 %all-to-all-start = ((bf16[4,2,40960]{2,1,0:T(2,128)(2,1)}), bf16[4,2,40960]{2,1,0:T(2,128)(2,1)S(1)}, u32[]{:S(2)}, u32[]{:S(2)}) async-start(bf16[4,2,40960]{2,1,0:T(2,128)(2,1)} %reshape.430), calls=%async_computation | async-start | bytes 1310720 | tf_op jit(solution)/shard_map/all_to_all | solution.py:94
  20.0 288.7 %all-gather.2.cloned.1.call-start = ((), (), s32[]{:S(2)}) async-start(), calls=%async_computation.7 | async-start | bytes 12976128 | tf_op jit(solution)/shard_map/all_gather | solution.py:124
  37.9 11.3 %copy-start.6 = (s32[4]{0:T(128)S(1)}, s32[4]{0:T(128)}, u32[]{:S(2)}) copy-start(s32[4]{0:T(128)} %param.12) | copy-start | bytes 52
  37.9 11.6 %copy-start = (bf16[256,2048]{1,0:T(8,128)(2,1)S(1)}, bf16[256,2048]{1,0:T(8,128)(2,1)}, u32[]{:S(2)}) copy-start(bf16[256,2048]{1,0:T(8,128)(2,1)} %param.11) | copy-start | bytes 3145732
  37.9 96.1 %all-to-all-start.1 = ((bf16[32,64,1536]{2,1,0:T(8,128)(2,1)}), bf16[32,64,1536]{2,1,0:T(8,128)(2,1)}, u32[]{:S(2)}, u32[]{:S(2)}) async-start(bf16[32,64,1536]{2,1,0:T(8,128)(2,1)} %broadcast_in_dim.187), calls=%async_computation.1 | async-start | bytes 12582912 | tf_op jit(solution)/shard_map/all_to_all | solution.py:21
  50.2 88.4 %copy-start.5 = (f32[256]{0:T(256)}, f32[256]{0:T(256)S(1)}, u32[]{:S(2)}) copy-start(f32[256]{0:T(256)S(1)} %add_rsqrt_fusion) | copy-start | bytes 3076
  145.0 17.6 %collective-permute-start = (bf16[2,4,256,128]{3,2,1,0:T(8,128)(2,1)S(1)}, bf16[2,4,256,128]{3,2,1,0:T(8,128)(2,1)S(1)}, u32[]{:S(2)}, u32[]{:S(2)}) collective-permute-start(bf16[2,4,256,128]{3,2,1,0:T(8,128)(2,1)S(1)} %maximum_bitcast_fusion.1), channel_id=1, source_target_pairs={{0,64},{4,68},{8,72},{12,76},{16,80},{20,84},{24,88},{28,92},{32,9... | collective-permute-start | bytes 1572872 | tf_op jit(solution)/shard_map/ppermute | solution.py:15
  150.2 21.9 %collective-permute-start.1 = (bf16[2,4,256,128]{3,2,1,0:T(8,128)(2,1)S(1)}, bf16[2,4,256,128]{3,2,1,0:T(8,128)(2,1)S(1)}, u32[]{:S(2)}, u32[]{:S(2)}) collective-permute-start(bf16[2,4,256,128]{3,2,1,0:T(8,128)(2,1)S(1)} %maximum_bitcast_fusion.1), channel_id=1, source_target_pairs={{0,32},{4,36},{8,40},{12,44},{16,48},{20,52},{24,56},{28,60},{32,6... | collective-permute-start | bytes 1572872 | tf_op jit(solution)/shard_map/ppermute | solution.py:15
  182.1 142.8 %all-to-all-start.2 = ((bf16[8,2,2,4,256,128]{5,4,3,2,1,0:T(8,128)(2,1)}), bf16[8,2,2,4,256,128]{5,4,3,2,1,0:T(8,128)(2,1)}, u32[]{:S(2)}, u32[]{:S(2)}) async-start(bf16[8,2,2,4,256,128]{5,4,3,2,1,0:T(8,128)(2,1)} %pad_maximum_fusion), calls=%async_computation.2 | async-start | bytes 16777216 | tf_op jit(solution)/shard_map/all_to_all | solution.py:170
  208.8 116.1 %collective-permute-start.2 = (bf16[64,2048]{1,0:T(8,128)(2,1)S(1)}, bf16[64,2048]{1,0:T(8,128)(2,1)S(1)}, u32[]{:S(2)}, u32[]{:S(2)}) collective-permute-start(bf16[64,2048]{1,0:T(8,128)(2,1)S(1)} %bitcast.133), channel_id=1, source_target_pairs={{0,0},{1,32},{2,64},{3,96},{32,1},{33,33},{34,65},{35,97},{64,2},{... | collective-permute-start | bytes 786440 | tf_op jit(solution)/shard_map/ppermute | solution.py:118
  326.5 59.0 %all-to-all-start.3 = ((bf16[8,64,2048]{2,1,0:T(8,128)(2,1)}), bf16[8,64,2048]{2,1,0:T(8,128)(2,1)S(1)}, u32[]{:S(2)}, u32[]{:S(2)}) async-start(bf16[8,64,2048]{2,1,0:T(8,128)(2,1)} %broadcast_in_dim.195), calls=%async_computation.3 | async-start | bytes 4194304 | tf_op jit(solution)/shard_map/all_to_all | solution.py:21
  387.2 18.7 %all-to-all-start.4 = ((bf16[4,64,2048]{2,1,0:T(8,128)(2,1)}), bf16[4,64,2048]{2,1,0:T(8,128)(2,1)S(1)}, u32[]{:S(2)}, u32[]{:S(2)}) async-start(bf16[4,64,2048]{2,1,0:T(8,128)(2,1)} %bitcast.113), calls=%async_computation.4 | async-start | bytes 2097152 | tf_op jit(solution)/shard_map/all_to_all | solution.py:28
  405.9 19.1 %copy-start.1 = (bf16[2048,1024]{1,0:T(8,128)(2,1)S(1)}, bf16[2048,1024]{1,0:T(8,128)(2,1)}, u32[]{:S(2)}) copy-start(bf16[2048,1024]{1,0:T(8,128)(2,1)} %get-tuple-element.277) | copy-start | bytes 12582916
Sparse Core Ops, SparseCore 0:
  34.7 273.8 all-gather.1

commit v6 on v5

--- a/solution.py
+++ b/solution.py
@@ -92,8 +92,8 @@
     ]
     flat = jnp.concatenate([p.reshape(mp_size, -1) for p in outgoing], axis=1)
     got = lax.all_to_all(flat, mp, 0, 0, tiled=True)
-    qkv_shard = jnp.concatenate([w.astype(half_type) for w in (w_key, w_value, w_query)], axis=1)
-    got, qkv_shard = lax.optimization_barrier((got, qkv_shard))
+    kv_shard = jnp.concatenate([w.astype(half_type) for w in (w_key, w_value)], axis=1)
+    got, kv_shard = lax.optimization_barrier((got, kv_shard))
     pieces = []
     at = 0
     for p in outgoing:
@@ -110,7 +110,7 @@
     down_shard = jnp.transpose(down_got, (1, 0, 2)).reshape(per_mp, mp_size * narrow)
     units = gate_shard.shape[1]
     rest_shard = jnp.concatenate(
-        [gate_shard, up_shard, down_shard.reshape(shard_rows, -1)], axis=1
+        [w_query.astype(half_type), gate_shard, up_shard, down_shard.reshape(shard_rows, -1)], axis=1
     )
 
     out_full_rows = jnp.transpose(out_got, (1, 0, 2)).reshape(shard_rows, mp_size * narrow)
@@ -118,9 +118,7 @@
     out_swapped = lax.ppermute(out_full_rows, ("y", mp), swap)
     server_out = gather_by_exchange(out_swapped, "r")
 
-    qkv_full = gather_by_exchange(qkv_shard, dp)
-    kv_full = qkv_full[:, : 2 * narrow]
-    q_full = qkv_full[:, 2 * narrow :]
+    kv_full = gather_by_exchange(kv_shard, dp)
     rest_full = lax.all_gather(rest_shard, dp, axis=0, tiled=True)
 
     normed = layer_norm(tokens).astype(half_type)
@@ -133,9 +131,6 @@
     plane = r_size
     back_one = shifted(own_pair, dp, plane)
     back_two = shifted(own_pair, dp, 2 * plane)
-    joined_q = jnp.dot(normed, q_full, preferred_element_type=jnp.float32)
-    query = rotate(joined_q.reshape(rows, heads_dev, HEAD), q_offset).astype(half_type)
-    query = jnp.transpose(query, (1, 0, 2))
     own_first = dp_index * rows
     scale = 1.0 / HEAD**0.5
 
@@ -168,12 +163,16 @@
         (nearer, jnp.broadcast_to(back_one[None], (plane,) + back_one.shape)), axis=1
     )
     received = lax.all_to_all(payload, "r", 0, 0, tiled=True)
-    server_gate = rest_full[:, :units]
-    server_up = rest_full[:, units : 2 * units]
-    server_down = rest_full[:, 2 * units :].reshape(units, -1)
-    received, server_gate, server_up, server_down = lax.optimization_barrier(
-        (received, server_gate, server_up, server_down)
-    )
+    q_full = rest_full[:, :narrow]
+    server_gate = rest_full[:, narrow : narrow + units]
+    server_up = rest_full[:, narrow + units : narrow + 2 * units]
+    server_down = rest_full[:, narrow + 2 * units :].reshape(units, -1)
+    received, q_full, server_gate, server_up, server_down = lax.optimization_barrier(
+        (received, q_full, server_gate, server_up, server_down)
+    )
+    joined_q = jnp.dot(normed, q_full, preferred_element_type=jnp.float32)
+    query = rotate(joined_q.reshape(rows, heads_dev, HEAD), q_offset).astype(half_type)
+    query = jnp.transpose(query, (1, 0, 2))
     state = online_step(state, own_pair, own_first)
 
     def slot_step(back, state):

time: 461 us -> 449 us (0.974)
  starting transfers between devices: 60.2 us -> 41.8 us
  local copies, waits for them, and re-layouts: 37.4 us -> 44.3 us
    all_to_all x2, waiting for transfers between devices: 82.6 us -> 56.5 us  [gather_by_exchange(): got = lax.all_to_all(copies, axis, 0, 0, tiled=True)]
    all_gather x1, waiting for transfers between devices: 98.1 us -> 123 us  [on_device(): rest_full = lax.all_gather(rest_shard, dp, axis=0, tiled=True)]
    all_to_all x1, starting transfers between devices: 26.4 us -> 10.6 us  [on_device(): received = lax.all_to_all(payload, 'r', 0, 0, tiled=True)]
    dot_general x0 -> x1, local copies, waits for them, and re-layouts: none -> 6.52 us  [on_device(): joined_kv = jnp.dot(normed, kv_full, preferred_element_type=jnp.float32)]
    slice x4 -> x3, local copies, waits for them, and re-layouts: 9.61 us -> 9.07 us  [the longest x1 9.07 us: on_device(): server_down = rest_full[:, narrow + 2 * units:].reshape(units, -1)]
  transfers between devices with their start and end apart: 9 -> 9, of which waited for: 6 -> 6; matrix products, arithmetic and copies ran while one was open for 21% -> 23% of each run, Pallas kernels for 0% -> 0%
where the time goes in v6:
time: 449 us; the launch traced here: 446 us
  waiting for transfers between devices  227 us (51%)
  matrix products  60.8 us (14%)
  local copies, waits for them, and re-layouts  44.3 us (10%)
  starting transfers between devices  41.8 us (9%)
  blocking collectives  33.9 us (8%)
  other arithmetic  23.1 us (5%)
  between operations  13.9 us (3%)
    all_gather x1, waiting for transfers between devices, on_device(): rest_full = lax.all_gather(rest_shard, dp, axis=0, tiled=True)  123 us
    all_to_all x2, waiting for transfers between devices, gather_by_exchange(): got = lax.all_to_all(copies, axis, 0, 0, tiled=True)  56.5 us
    dot_general x17, matrix products, online_step(): jnp.einsum('hqk,hkd->hqd', probs, pair[1], preferred_element_type=jnp.flo...  24 us
    ppermute x2, waiting for transfers between devices, shifted(): lax.ppermute(value, axis, [(source, source + steps) for source in range(c...  23 us
    dot_general x17, matrix products, online_step(): jnp.einsum('hqd,hkd->hqk', query, pair[0], preferred_element_type=jnp.flo...  21.7 us
    all_to_all x2, starting transfers between devices, gather_by_exchange(): got = lax.all_to_all(copies, axis, 0, 0, tiled=True)  17.2 us
    all_to_all x1, blocking collectives, gather_by_exchange(): got = lax.all_to_all(copies, axis, 0, 0, tiled=True)  17 us
    all_to_all x1, blocking collectives, scatter_sum(): got = lax.all_to_all(pieces, axis, 0, 0, tiled=True)  16.9 us
  transfers between devices with their start and end apart: 9, of which 6 were waited for; matrix products, arithmetic and copies ran while one was open for 23% of the time, Pallas kernels for 0%

profile of v6, /device:TPU:4, one launch (start us, length us, event | category | flops | bytes accessed | tf_op | source)
XLA Modules:
  0.0 446.4 jit_solution(5128202686256242654)
XLA Ops:
  12.6 1.5 reduce
  14.1 1.5 reshape.429
  15.6 3.5 all-to-all-start
  19.4 9.9 %all-to-all-done = bf16[4,2,40960]{2,1,0:T(2,128)(2,1)S(1)} async-done(((bf16[4,2,40960]{2,1,0:T(2,128)(2,1)}), bf16[4,2,40960]{2,1,0:T(2,128)(2,1)S(1)}, u32[]{:S(2)}, u32[]{:S(2)}) %all-to-all-start) | async-done | bytes 655392 | tf_op jit(solution)/shard_map/all_to_all | solution.py:94
  33.8 2.6 broadcast_in_dim.188
  36.4 11.2 %all-to-all-start.1 = ((bf16[32,64,1024]{2,1,0:T(8,128)(2,1)}), bf16[32,64,1024]{2,1,0:T(8,128)(2,1)}, u32[]{:S(2)}, u32[]{:S(2)}) async-start(bf16[32,64,1024]{2,1,0:T(8,128)(2,1)} %broadcast_in_dim.188), calls=%async_computation.1 | async-start | bytes 8388608 | tf_op jit(solution)/shard_map/all_to_all | solution.py:21
  48.9 56.5 %all-to-all-done.1 = bf16[32,64,1024]{2,1,0:T(8,128)(2,1)} async-done(((bf16[32,64,1024]{2,1,0:T(8,128)(2,1)}), bf16[32,64,1024]{2,1,0:T(8,128)(2,1)}, u32[]{:S(2)}, u32[]{:S(2)}) %all-to-all-start.1) | async-done | bytes 4194336 | tf_op jit(solution)/shard_map/all_to_all | solution.py:21
  105.4 6.5 %copy.139 = bf16[1024,2048]{1,0:T(8,128)(2,1)} copy(bf16[1024,2048]{0,1:T(8,128)(2,1)} %bitcast.10) | data formatting | bytes 8388608 | tf_op jit(solution)/shard_map/dot_general | solution.py:125
  112.0 3.6 fusion.17
  115.7 3.5 collective-permute-start.1
  119.2 2.8 collective-permute-start
  123.1 14.5 %collective-permute-done.1 = bf16[2,4,256,128]{2,3,1,0:T(8,128)(2,1)} collective-permute-done((bf16[2,4,256,128]{2,3,1,0:T(8,128)(2,1)S(1)}, bf16[2,4,256,128]{2,3,1,0:T(8,128)(2,1)}, u32[]{:S(2)}, u32[]{:S(2)}) %collective-permute-start.1) | collective-permute-done | bytes 524320 | tf_op jit(solution)/shard_map/ppermute | solution.py:15
  137.6 2.1 copy.142
  139.6 8.5 %collective-permute-done = bf16[2,4,256,128]{2,3,1,0:T(8,128)(2,1)S(1)} collective-permute-done((bf16[2,4,256,128]{2,3,1,0:T(8,128)(2,1)S(1)}, bf16[2,4,256,128]{2,3,1,0:T(8,128)(2,1)S(1)}, u32[]{:S(2)}, u32[]{:S(2)}) %collective-permute-start) | collective-permute-done | bytes 524320 | tf_op jit(solution)/shard_map/ppermute | solution.py:15
  149.1 1.8 broadcast_select_fusion
  150.9 3.0 stack_broadcast_in_dim.2
  153.9 7.1 %pad_maximum_fusion = bf16[8,2,2,4,256,128]{5,4,3,2,1,0:T(8,128)(2,1)} fusion(bf16[8,1,2,4,256,128]{5,4,3,2,1,0:T(8,128)(2,1)} %stack_broadcast_in_dim.2, bf16[8,1,2,4,256,128]{5,4,3,2,1,0:T(8,128)(2,1)S(1)} %broadcast_select_fusion), kind=kLoop, calls=%fused_computation.22 | loop fusion | flops 4194304 | bytes 16777216 | tf_op jit(solution)/shard_map/stack | solution.py:162
  161.0 10.6 %all-to-all-start.2 = ((bf16[8,2,2,4,256,128]{5,4,3,2,1,0:T(8,128)(2,1)}), bf16[8,2,2,4,256,128]{5,4,3,2,1,0:T(8,128)(2,1)}, u32[]{:S(2)}, u32[]{:S(2)}) async-start(bf16[8,2,2,4,256,128]{5,4,3,2,1,0:T(8,128)(2,1)} %pad_maximum_fusion), calls=%async_computation.2 | async-start | bytes 16777216 | tf_op jit(solution)/shard_map/all_to_all | solution.py:165
  172.6 123.2 %all-gather.2.cloned.1.call-done = bf16[2048,3584]{1,0:T(8,128)(2,1)} async-done(((bf16[64,3584]{1,0:T(8,128)(2,1)}), bf16[2048,3584]{1,0:T(8,128)(2,1)}) %all-gather.2.cloned.1.call-update) | async-done | bytes 14680080 | tf_op jit(solution)/shard_map/all_gather | solution.py:122
  295.8 9.1 %fusion.39 = (bf16[2048,1024]{1,0:T(8,128)(2,1)}, bf16[2048,1024]{1,0:T(8,128)(2,1)}, bf16[2048,1024]{1,0:T(8,128)(2,1)}) fusion(bf16[2048,3584]{1,0:T(8,128)(2,1)} %all-gather.2.cloned.1.call-done), kind=kLoop, calls=%fused_computation.95 | loop fusion | bytes 25165824 | tf_op jit(solution)/shard_map/slice | solution.py:169
  304.8 7.1 %reshape.418 = bf16[1024,2048]{1,0:T(8,128)(2,1)} reshape(bf16[2048,1024]{1,0:T(8,128)(2,1)} %get-tuple-element.444) | data formatting | bytes 8388608 | tf_op jit(solution)/shard_map/reshape | solution.py:169
  312.0 1.7 broadcast_in_dim.195
  313.6 5.9 %all-to-all-start.3 = ((bf16[8,64,2048]{2,1,0:T(8,128)(2,1)}), bf16[8,64,2048]{2,1,0:T(8,128)(2,1)}, u32[]{:S(2)}, u32[]{:S(2)}) async-start(bf16[8,64,2048]{2,1,0:T(8,128)(2,1)} %broadcast_in_dim.195), calls=%async_computation.3 | async-start | bytes 4194304 | tf_op jit(solution)/shard_map/all_to_all | solution.py:21
  320.9 1.3 fusion.41
  322.4 1.3 convolution_add_fusion.1
  323.7 51.2 %while.21 = (s32[]{:T(128)}, f32[4,256,128]{2,1,0:T(8,128)S(1)}, f32[4,256,1]{1,0,2:T(4,128)S(1)}, f32[4,256,1]{1,0,2:T(4,128)S(1)}, s32[256]{0:T(256)S(1)}, /*i...) while((s32[]{:T(128)}, f32[4,256,128]{2,1,0:T(8,128)S(1)}, ...), condition=%wide.region_11.12_spmd.clone.clone, body=%wide.region_7.11_spmd.clone.clone.sunk | while | flops 136518688 | bytes 5188022 | solution.py:184
  325.5 1.4 convolution_add_fusion.3
  328.7 1.4 convolution_add_fusion.3
  331.9 1.4 convolution_add_fusion.3
  335.1 1.4 convolution_add_fusion.3
  338.3 1.4 convolution_add_fusion.3
  341.5 1.4 convolution_add_fusion.3
  344.7 1.4 convolution_add_fusion.3
  347.9 1.4 convolution_add_fusion.3
  351.1 1.4 convolution_add_fusion.3
  354.3 1.4 convolution_add_fusion.3
  357.5 1.4 convolution_add_fusion.3
  360.7 1.4 convolution_add_fusion.3
  363.9 1.4 convolution_add_fusion.3
  367.1 1.4 convolution_add_fusion.3
  370.3 1.4 convolution_add_fusion.3
  373.5 1.4 convolution_add_fusion.3
  375.3 3.4 convolution_convert_fusion
  378.7 3.5 all-to-all-start.4
  382.2 14.4 %all-to-all-done.4 = bf16[4,64,2048]{2,1,0:T(8,128)(2,1)S(1)} async-done(((bf16[4,64,2048]{2,1,0:T(8,128)(2,1)}), bf16[4,64,2048]{2,1,0:T(8,128)(2,1)S(1)}, u32[]{:S(2)}, u32[]{:S(2)}) %all-to-all-start.4) | async-done | bytes 1048608 | tf_op jit(solution)/shard_map/all_to_all | solution.py:28
  397.5 17.0 %all_to_all.42 = bf16[4,64,2048]{2,1,0:T(8,128)(2,1)S(1)} all-to-all(bf16[4,64,2048]{2,1,0:T(8,128)(2,1)S(1)} %broadcast_in_dim.196), channel_id=1, replica_groups=mesh['y'=4,'r'=8,'mp'=4] {'mp'}, dimensions={0} | all-to-all | bytes 2097152 | tf_op jit(solution)/shard_map/all_to_all | solution.py:21
  415.8 5.9 %convolution_convert_fusion.1 = bf16[256,2048]{1,0:T(8,128)(2,1)S(1)} fusion(bf16[1024,2048]{1,0:T(8,128)(2,1)} %reshape.418, bf16[256,2048]{1,0:T(8,128)(2,1)S(1)} %bitcast.134, bf16[2048,1024]{1,0:T(8,128)(2,1)} %get-tuple-element.280, f32[256,1024]{1,0:T(8,128)S(1)} %fusion.42), kind=kOutput, calls=%fused_computation.27 | convolution fusion | flops 2149580800 | bytes 11534336 | tf_op jit(solution)/shard_map/dot_general | solution.py:199
  421.7 16.9 %all_to_all.43 = bf16[4,64,2048]{2,1,0:T(8,128)(2,1)S(1)} all-to-all(bf16[4,64,2048]{2,1,0:T(8,128)(2,1)S(1)} %bitcast.135), channel_id=1, replica_groups=mesh['y'=4,'r'=8,'mp'=4] {'mp'}, dimensions={0} | all-to-all | bytes 2097152 | tf_op jit(solution)/shard_map/all_to_all | solution.py:28
  (238 shorter events, 47.0 us)
Async XLA Ops:
  6.5 4.1 copy-start.4
  12.1 7.1 %copy-start.5 = (f32[64,512]{1,0:T(8,128)S(1)}, f32[64,512]{1,0:T(8,128)}, u32[]{:S(2)}) copy-start(f32[64,512]{1,0:T(8,128)} %param.13) | copy-start | bytes 393220
  12.6 6.7 %copy-start.6 = (f32[64,512]{1,0:T(8,128)S(1)}, f32[64,512]{1,0:T(8,128)}, u32[]{:S(2)}) copy-start(f32[64,512]{1,0:T(8,128)} %param.14) | copy-start | bytes 393220
  12.6 6.8 %copy-start.7 = (f32[64,512]{1,0:T(8,128)S(1)}, f32[64,512]{1,0:T(8,128)}, u32[]{:S(2)}) copy-start(f32[64,512]{1,0:T(8,128)} %param.15) | copy-start | bytes 393220
  15.6 13.7 %all-to-all-start = ((bf16[4,2,40960]{2,1,0:T(2,128)(2,1)}), bf16[4,2,40960]{2,1,0:T(2,128)(2,1)S(1)}, u32[]{:S(2)}, u32[]{:S(2)}) async-start(bf16[4,2,40960]{2,1,0:T(2,128)(2,1)} %reshape.429), calls=%async_computation | async-start | bytes 1310720 | tf_op jit(solution)/shard_map/all_to_all | solution.py:94
  19.1 276.7 %all-gather.2.cloned.1.call-start = ((), (), s32[]{:S(2)}) async-start(), calls=%async_computation.7 | async-start | bytes 15138816 | tf_op jit(solution)/shard_map/all_gather | solution.py:122
  36.4 11.3 %copy-start.8 = (s32[4]{0:T(128)S(1)}, s32[4]{0:T(128)}, u32[]{:S(2)}) copy-start(s32[4]{0:T(128)} %param.12) | copy-start | bytes 52
  36.4 11.6 %copy-start = (bf16[256,2048]{1,0:T(8,128)(2,1)S(1)}, bf16[256,2048]{1,0:T(8,128)(2,1)}, u32[]{:S(2)}) copy-start(bf16[256,2048]{1,0:T(8,128)(2,1)} %param.11) | copy-start | bytes 3145732
  36.4 69.1 %all-to-all-start.1 = ((bf16[32,64,1024]{2,1,0:T(8,128)(2,1)}), bf16[32,64,1024]{2,1,0:T(8,128)(2,1)}, u32[]{:S(2)}, u32[]{:S(2)}) async-start(bf16[32,64,1024]{2,1,0:T(8,128)(2,1)} %broadcast_in_dim.188), calls=%async_computation.1 | async-start | bytes 8388608 | tf_op jit(solution)/shard_map/all_to_all | solution.py:21
  115.7 32.4 %copy-start.2 = (bf16[2,4,256,128]{2,3,1,0:T(8,128)(2,1)}, bf16[2,4,256,128]{2,3,1,0:T(8,128)(2,1)S(1)}, u32[]{:S(2)}) copy-start(bf16[2,4,256,128]{2,3,1,0:T(8,128)(2,1)S(1)} %maximum_bitcast_fusion.1) | copy-start | bytes 1572868
  115.7 21.9 %collective-permute-start.1 = (bf16[2,4,256,128]{2,3,1,0:T(8,128)(2,1)S(1)}, bf16[2,4,256,128]{2,3,1,0:T(8,128)(2,1)}, u32[]{:S(2)}, u32[]{:S(2)}) collective-permute-start(bf16[2,4,256,128]{2,3,1,0:T(8,128)(2,1)S(1)} %maximum_bitcast_fusion.1), channel_id=1, source_target_pairs={{0,32},{4,36},{8,40},{12,44},{16,48},{20,52},{24,56},{28,60},{32,6... | collective-permute-start | bytes 1572872 | tf_op jit(solution)/shard_map/ppermute | solution.py:15
  119.2 28.9 %collective-permute-start = (bf16[2,4,256,128]{2,3,1,0:T(8,128)(2,1)S(1)}, bf16[2,4,256,128]{2,3,1,0:T(8,128)(2,1)S(1)}, u32[]{:S(2)}, u32[]{:S(2)}) collective-permute-start(bf16[2,4,256,128]{2,3,1,0:T(8,128)(2,1)S(1)} %maximum_bitcast_fusion.1), channel_id=1, source_target_pairs={{0,64},{4,68},{8,72},{12,76},{16,80},{20,84},{24,88},{28,92},{32,9... | collective-permute-start | bytes 1572872 | tf_op jit(solution)/shard_map/ppermute | solution.py:15
  149.1 1.8 copy-start.3
  161.0 151.0 %all-to-all-start.2 = ((bf16[8,2,2,4,256,128]{5,4,3,2,1,0:T(8,128)(2,1)}), bf16[8,2,2,4,256,128]{5,4,3,2,1,0:T(8,128)(2,1)}, u32[]{:S(2)}, u32[]{:S(2)}) async-start(bf16[8,2,2,4,256,128]{5,4,3,2,1,0:T(8,128)(2,1)} %pad_maximum_fusion), calls=%async_computation.2 | async-start | bytes 16777216 | tf_op jit(solution)/shard_map/all_to_all | solution.py:165
  171.9 140.1 %collective-permute-start.2 = (bf16[64,2048]{1,0:T(8,128)(2,1)S(1)}, bf16[64,2048]{1,0:T(8,128)(2,1)S(1)}, u32[]{:S(2)}, u32[]{:S(2)}) collective-permute-start(bf16[64,2048]{1,0:T(8,128)(2,1)S(1)} %bitcast.142), channel_id=1, source_target_pairs={{0,0},{1,32},{2,64},{3,96},{32,1},{33,33},{34,65},{35,97},{64,2},{... | collective-permute-start | bytes 786440 | tf_op jit(solution)/shard_map/ppermute | solution.py:118
  313.6 5.9 %slice-start = ((bf16[2048,3584]{1,0:T(8,128)(2,1)}), bf16[2048,512]{1,0:T(8,128)(2,1)S(1)}, s32[]{:S(2)}) async-start(bf16[2048,3584]{1,0:T(8,128)(2,1)} %all-gather.2.cloned.1.call-done), calls=%async_computation.8 | async-start | bytes 4194304 | tf_op jit(solution)/shard_map/slice | solution.py:166
  313.6 61.6 %all-to-all-start.3 = ((bf16[8,64,2048]{2,1,0:T(8,128)(2,1)}), bf16[8,64,2048]{2,1,0:T(8,128)(2,1)}, u32[]{:S(2)}, u32[]{:S(2)}) async-start(bf16[8,64,2048]{2,1,0:T(8,128)(2,1)} %broadcast_in_dim.195), calls=%async_computation.3 | async-start | bytes 4194304 | tf_op jit(solution)/shard_map/all_to_all | solution.py:21
  378.7 18.0 %all-to-all-start.4 = ((bf16[4,64,2048]{2,1,0:T(8,128)(2,1)}), bf16[4,64,2048]{2,1,0:T(8,128)(2,1)S(1)}, u32[]{:S(2)}, u32[]{:S(2)}) async-start(bf16[4,64,2048]{2,1,0:T(8,128)(2,1)} %bitcast.35), calls=%async_computation.4 | async-start | bytes 2097152 | tf_op jit(solution)/shard_map/all_to_all | solution.py:28
  397.0 17.5 %copy-start.1 = (bf16[2048,1024]{1,0:T(8,128)(2,1)S(1)}, bf16[2048,1024]{1,0:T(8,128)(2,1)}, u32[]{:S(2)}) copy-start(bf16[2048,1024]{1,0:T(8,128)(2,1)} %get-tuple-element.279) | copy-start | bytes 12582916
Sparse Core Ops, SparseCore 0:
  33.9 261.7 all-gather.1

commit v7 on v6

--- a/solution.py
+++ b/solution.py
@@ -2,6 +2,8 @@
 import jax.numpy as jnp
 from jax import lax
 from jax.sharding import Mesh, PartitionSpec as P
+from jax.experimental import pallas as pl
+from jax.experimental.pallas import tpu as pltpu
 
 HEAD = 128
 
@@ -57,6 +59,79 @@
     return jnp.concatenate(
         [first_half * cosine - second_half * sine, second_half * cosine + first_half * sine],
         axis=-1,
+    )
+
+
+def attend_kernel(meta, query_ref, own_ref, received_ref, qp_ref, qw_ref, kp_ref, kw_ref, out_ref):
+    r_index = meta[0]
+    plane = received_ref.shape[0]
+    steps = kp_ref.shape[0]
+    heads = query_ref.shape[0]
+    scale = 1.0 / query_ref.shape[-1] ** 0.5
+    qp = qp_ref[...]
+    qw = qw_ref[...]
+
+    def one_step(head, keys, values, back, carry):
+        accum, total, top = carry
+        scores = lax.dot_general(
+            query_ref[head], keys, (((1,), (1,)), ((), ())), preferred_element_type=jnp.float32
+        ) * scale
+        allowed = (qp == kp_ref[back]) & (kw_ref[back] <= qw)
+        scores = jnp.where(allowed, scores, -jnp.inf)
+        new_top = jnp.maximum(top, jnp.max(scores, axis=1, keepdims=True))
+        fade = jnp.exp(top - new_top)
+        weights = jnp.exp(scores - new_top)
+        probs = weights.astype(jnp.bfloat16)
+        product = jnp.dot(probs, values, preferred_element_type=jnp.float32)
+        accum = accum * fade + product
+        total = total * fade + jnp.sum(weights, axis=1, keepdims=True)
+        return (accum, total, new_top)
+
+    for head in range(heads):
+        rows, width = query_ref.shape[1], query_ref.shape[2]
+        carry = (
+            jnp.zeros((rows, width), jnp.float32),
+            jnp.zeros((rows, 1), jnp.float32),
+            jnp.full((rows, 1), -jnp.inf, jnp.float32),
+        )
+        carry = one_step(head, own_ref[0, head], own_ref[1, head], 0, carry)
+
+        def body(back, carry, head=head):
+            source = lax.rem(r_index - back + 2 * plane, plane)
+            middle = jnp.logical_and(back > r_index, back <= r_index + plane).astype(jnp.int32)
+            keys = received_ref[source, middle, 0, head]
+            values = received_ref[source, middle, 1, head]
+            return one_step(head, keys, values, back, carry)
+
+        accum, total, top = lax.fori_loop(1, steps, body, carry)
+        out_ref[head] = (accum / total).astype(out_ref.dtype)
+
+
+def attend(r_index, query, own_pair, received, q_prompt, q_where, k_prompt, k_where):
+    heads, rows, width = query.shape
+    steps = k_prompt.shape[0]
+    flops = 4 * heads * rows * rows * width * steps
+    vmem = pl.BlockSpec(memory_space=pltpu.VMEM)
+    return pl.pallas_call(
+        attend_kernel,
+        out_shape=jax.ShapeDtypeStruct((heads, rows, width), jnp.bfloat16),
+        in_specs=[pl.BlockSpec(memory_space=pltpu.SMEM)] + [vmem] * 7,
+        out_specs=vmem,
+        compiler_params=pltpu.CompilerParams(vmem_limit_bytes=48 * 1024 * 1024),
+        cost_estimate=pl.CostEstimate(
+            flops=flops,
+            transcendentals=heads * rows * rows * steps,
+            bytes_accessed=received.size * 2 + own_pair.size * 2 + query.size * 4,
+        ),
+    )(
+        jnp.reshape(r_index, (1,)).astype(jnp.int32),
+        query,
+        own_pair,
+        received,
+        q_prompt.reshape(rows, 1).astype(jnp.int32),
+        q_where.reshape(rows, 1).astype(jnp.int32),
+        k_prompt.reshape(steps, 1, rows).astype(jnp.int32),
+        k_where.reshape(steps, 1, rows).astype(jnp.int32),
     )
 
 
@@ -132,30 +207,7 @@
     back_one = shifted(own_pair, dp, plane)
     back_two = shifted(own_pair, dp, 2 * plane)
     own_first = dp_index * rows
-    scale = 1.0 / HEAD**0.5
-
-    def online_step(state, pair, first):
-        accum, total, top = state
-        k_prompt, k_offset, k_where = prompt_coords(first, rows, lengths)
-        scores = (
-            jnp.einsum("hqd,hkd->hqk", query, pair[0], preferred_element_type=jnp.float32) * scale
-        )
-        allowed = (q_prompt[:, None] == k_prompt[None, :]) & (k_where[None, :] <= q_where[:, None])
-        scores = jnp.where(allowed[None], scores, -jnp.inf)
-        new_top = jnp.maximum(top, jnp.max(scores, axis=-1, keepdims=True))
-        fade = jnp.exp(top - new_top)
-        weights = jnp.exp(scores - new_top)
-        probs = weights.astype(half_type)
-        product = jnp.einsum("hqk,hkd->hqd", probs, pair[1], preferred_element_type=jnp.float32)
-        accum = accum * fade + product
-        total = total * fade + jnp.sum(weights, axis=-1, keepdims=True)
-        return (accum, total, new_top)
-
-    state = (
-        jnp.zeros((heads_dev, rows, HEAD), jnp.float32),
-        jnp.zeros((heads_dev, rows, 1), jnp.float32),
-        jnp.full((heads_dev, rows, 1), -jnp.inf, jnp.float32),
-    )
+
     r_index = lax.axis_index("r")
     later = r_index < jnp.arange(plane)
     nearer = jnp.where(later[:, None, None, None, None], own_pair[None], back_two[None])
@@ -173,17 +225,10 @@
     joined_q = jnp.dot(normed, q_full, preferred_element_type=jnp.float32)
     query = rotate(joined_q.reshape(rows, heads_dev, HEAD), q_offset).astype(half_type)
     query = jnp.transpose(query, (1, 0, 2))
-    state = online_step(state, own_pair, own_first)
-
-    def slot_step(back, state):
-        source = lax.rem(r_index - back + 2 * plane, plane)
-        middle = jnp.logical_and(back > r_index, back <= r_index + plane).astype(jnp.int32)
-        pair = received[source, middle]
-        return online_step(state, pair, own_first - back * rows)
-
-    state = lax.fori_loop(1, reach + 1, slot_step, state)
-    accum, total, top = state
-    context = jnp.transpose((accum / total).astype(half_type), (1, 0, 2)).reshape(rows, narrow)
+    firsts = own_first - rows * jnp.arange(reach + 1)
+    k_prompt, k_offset, k_where = jax.vmap(lambda first: prompt_coords(first, rows, lengths))(firsts)
+    context = attend(r_index, query, own_pair, received, q_prompt, q_where, k_prompt, k_where)
+    context = jnp.transpose(context, (1, 0, 2)).reshape(rows, narrow)
 
     partial_out = jnp.dot(context, server_out, preferred_element_type=jnp.float32)
     attended = scatter_sum(partial_out.astype(half_type), mp)

time: 449 us -> 443 us (0.987)
  matrix products: 60.8 us -> 13.5 us
  Pallas kernels: 0 us -> 34.2 us
  starting transfers between devices: 41.8 us -> 52 us
    all_to_all x1, waiting for transfers between devices: 0.01 us -> 126 us  [on_device(): received = lax.all_to_all(payload, 'r', 0, 0, tiled=True)]
    all_gather x1, waiting for transfers between devices: 123 us -> 0.01 us  [on_device(): rest_full = lax.all_gather(rest_shard, dp, axis=0, tiled=True)]
    dot_general x34 -> x0, matrix products: 45.7 us -> none  [the longest x17 24 us: online_step(): jnp.einsum('hqk,hkd->hqd', probs, pair[1], preferred_element_type=jnp.flo...]
    pallas_call x0 -> x1, Pallas kernels: none -> 34.2 us  [attend(): pl.pallas_call(attend_kernel, out_shape=jax.ShapeDtypeStruct((heads, rows...]
    all_to_all x1, starting transfers between devices: 3.51 us -> 10.2 us  [scatter_sum(): got = lax.all_to_all(pieces, axis, 0, 0, tiled=True)]
  transfers between devices with their start and end apart: 9 -> 9, of which waited for: 6 -> 6; matrix products, arithmetic and copies ran while one was open for 23% -> 12% of each run, Pallas kernels for 0% -> 8%
where the time goes in v7:
time: 443 us; the launch traced here: 442 us
  waiting for transfers between devices  228 us (51%)
  starting transfers between devices  52 us (12%)
  local copies, waits for them, and re-layouts  45.6 us (10%)
  Pallas kernels  34.2 us (8%)
  blocking collectives  33.9 us (8%)
  other arithmetic  20.4 us (5%)
  between operations  13.9 us (3%)
  matrix products  13.5 us (3%)
    all_to_all x1, waiting for transfers between devices, on_device(): received = lax.all_to_all(payload, 'r', 0, 0, tiled=True)  126 us
    all_to_all x2, waiting for transfers between devices, gather_by_exchange(): got = lax.all_to_all(copies, axis, 0, 0, tiled=True)  56.2 us
    pallas_call x1, Pallas kernels, attend(): pl.pallas_call(attend_kernel, out_shape=jax.ShapeDtypeStruct((heads, rows...  34.2 us
    ppermute x2, waiting for transfers between devices, shifted(): lax.ppermute(value, axis, [(source, source + steps) for source in range(c...  21.5 us
    all_to_all x2, starting transfers between devices, gather_by_exchange(): got = lax.all_to_all(copies, axis, 0, 0, tiled=True)  20.1 us
    all_to_all x1, blocking collectives, gather_by_exchange(): got = lax.all_to_all(copies, axis, 0, 0, tiled=True)  17 us
    all_to_all x1, blocking collectives, scatter_sum(): got = lax.all_to_all(pieces, axis, 0, 0, tiled=True)  16.9 us
    all_to_all x1, waiting for transfers between devices, scatter_sum(): got = lax.all_to_all(pieces, axis, 0, 0, tiled=True)  14.5 us
  transfers between devices with their start and end apart: 9, of which 6 were waited for; matrix products, arithmetic and copies ran while one was open for 12% of the time, Pallas kernels for 8%

profile of v7, /device:TPU:4, one launch (start us, length us, event | category | flops | bytes accessed | tf_op | source)
XLA Modules:
  0.0 442.0 jit_solution(16427458392572864356)
XLA Ops:
  6.5 1.0 convert_bitcast_fusion
  7.5 1.0 convert_element_type.97
  8.6 1.1 copy.105
  10.1 0.6 reshape.345
  11.1 0.6 reshape.347
  12.6 1.5 reduce
  14.1 1.5 reshape.367
  15.6 3.5 all-to-all-start
  19.4 9.9 %all-to-all-done = bf16[4,2,40960]{2,1,0:T(2,128)(2,1)S(1)} async-done(((bf16[4,2,40960]{2,1,0:T(2,128)(2,1)}), bf16[4,2,40960]{2,1,0:T(2,128)(2,1)S(1)}, u32[]{:S(2)}, u32[]{:S(2)}) %all-to-all-start) | async-done | bytes 655392 | tf_op jit(solution)/shard_map/all_to_all | solution.py:169
  29.3 0.6 reshape.368
  30.0 0.8 copy.134
  32.7 1.1 copy.118
  33.8 2.5 broadcast_in_dim.44
  36.4 11.2 %all-to-all-start.1 = ((bf16[32,64,1024]{2,1,0:T(8,128)(2,1)}), bf16[32,64,1024]{2,1,0:T(8,128)(2,1)}, u32[]{:S(2)}, u32[]{:S(2)}) async-start(bf16[32,64,1024]{2,1,0:T(8,128)(2,1)} %broadcast_in_dim.44), calls=%async_computation.1 | async-start | bytes 8388608 | tf_op jit(solution)/shard_map/all_to_all | solution.py:23
  48.6 0.5 multiply_cosine_fusion
  49.2 56.2 %all-to-all-done.1 = bf16[32,64,1024]{2,1,0:T(8,128)(2,1)} async-done(((bf16[32,64,1024]{2,1,0:T(8,128)(2,1)}), bf16[32,64,1024]{2,1,0:T(8,128)(2,1)}, u32[]{:S(2)}, u32[]{:S(2)}) %all-to-all-start.1) | async-done | bytes 4194336 | tf_op jit(solution)/shard_map/all_to_all | solution.py:23
  105.4 6.5 %copy.110 = bf16[1024,2048]{1,0:T(8,128)(2,1)} copy(bf16[1024,2048]{0,1:T(8,128)(2,1)} %bitcast.9) | data formatting | bytes 8388608 | tf_op jit(solution)/shard_map/dot_general | solution.py:200
  111.9 3.5 fusion.5
  115.9 4.5 %collective-permute-start = (bf16[2,4,256,128]{3,2,1,0:T(8,128)(2,1)S(1)}, bf16[2,4,256,128]{3,2,1,0:T(8,128)(2,1)S(1)}, u32[]{:S(2)}, u32[]{:S(2)}) collective-permute-start(bf16[2,4,256,128]{3,2,1,0:T(8,128)(2,1)S(1)} %maximum_bitcast_fusion.1.own_ref), channel_id=1, source_target_pairs={{0,64},{4,68},{8,72},{12,76},{16,80},{20,84},{24,88},{28,92},{32,9... | collective-permute-start | bytes 1572872 | tf_op jit(solution)/shard_map/ppermute | solution.py:17
  120.5 1.6 collective-permute-start.1
  122.1 14.6 %collective-permute-done = bf16[2,4,256,128]{3,2,1,0:T(8,128)(2,1)S(1)} collective-permute-done((bf16[2,4,256,128]{3,2,1,0:T(8,128)(2,1)S(1)}, bf16[2,4,256,128]{3,2,1,0:T(8,128)(2,1)S(1)}, u32[]{:S(2)}, u32[]{:S(2)}) %collective-permute-start) | collective-permute-done | bytes 524320 | tf_op jit(solution)/shard_map/ppermute | solution.py:17
  136.8 2.5 broadcast_select_fusion
  139.3 6.9 %collective-permute-done.1 = bf16[2,4,256,128]{3,2,1,0:T(8,128)(2,1)S(1)} collective-permute-done((bf16[2,4,256,128]{3,2,1,0:T(8,128)(2,1)S(1)}, bf16[2,4,256,128]{3,2,1,0:T(8,128)(2,1)S(1)}, u32[]{:S(2)}, u32[]{:S(2)}) %collective-permute-start.1) | collective-permute-done | bytes 524320 | tf_op jit(solution)/shard_map/ppermute | solution.py:17
  146.2 3.0 stack_broadcast_in_dim.2
  149.2 7.6 %pad_maximum_fusion = bf16[8,2,2,4,256,128]{5,4,3,2,1,0:T(8,128)(2,1)} fusion(bf16[8,1,2,4,256,128]{5,4,3,2,1,0:T(8,128)(2,1)} %stack_broadcast_in_dim.2, bf16[8,1,2,4,256,128]{5,4,3,2,1,0:T(8,128)(2,1)} %broadcast_select_fusion), kind=kLoop, calls=%fused_computation | loop fusion | flops 4194304 | bytes 16777216 | tf_op jit(solution)/shard_map/stack | solution.py:214
  156.7 11.3 %all-to-all-start.2 = ((bf16[8,2,2,4,256,128]{5,4,3,2,1,0:T(8,128)(2,1)}), bf16[8,2,2,4,256,128]{5,4,3,2,1,0:T(8,128)(2,1)}, u32[]{:S(2)}, u32[]{:S(2)}) async-start(bf16[8,2,2,4,256,128]{5,4,3,2,1,0:T(8,128)(2,1)} %pad_maximum_fusion), calls=%async_computation.2 | async-start | bytes 16777216 | tf_op jit(solution)/shard_map/all_to_all | solution.py:217
  168.4 0.7 collective-permute-start.2
  169.4 126.2 %all-to-all-done.2.received_ref = bf16[8,2,2,4,256,128]{5,4,3,2,1,0:T(8,128)(2,1)} async-done(((bf16[8,2,2,4,256,128]{5,4,3,2,1,0:T(8,128)(2,1)}), bf16[8,2,2,4,256,128]{5,4,3,2,1,0:T(8,128)(2,1)}, u32[]{:S(2)}, u32[]{:S(2)}) %all-to-all-start.2) | async-done | bytes 8388640 | tf_op jit(solution)/shard_map/all_to_all | solution.py:217
  295.6 1.6 broadcast_in_dim.49
  297.2 8.8 %all-to-all-start.3 = ((bf16[8,64,2048]{2,1,0:T(8,128)(2,1)}), bf16[8,64,2048]{2,1,0:T(8,128)(2,1)S(1)}, u32[]{:S(2)}, u32[]{:S(2)}) async-start(bf16[8,64,2048]{2,1,0:T(8,128)(2,1)} %broadcast_in_dim.49), calls=%async_computation.3 | async-start | bytes 4194304 | tf_op jit(solution)/shard_map/all_to_all | solution.py:23
  306.1 9.1 %fusion.22 = (bf16[2048,1024]{1,0:T(8,128)(2,1)}, bf16[2048,1024]{1,0:T(8,128)(2,1)}, bf16[2048,1024]{1,0:T(8,128)(2,1)}) fusion(bf16[2048,3584]{1,0:T(8,128)(2,1)} %all-gather.2.cloned.1.call-done), kind=kLoop, calls=%fused_computation.65 | loop fusion | bytes 25165824 | tf_op jit(solution)/shard_map/slice | solution.py:221
  315.1 7.1 %reshape.356 = bf16[1024,2048]{1,0:T(8,128)(2,1)} reshape(bf16[2048,1024]{1,0:T(8,128)(2,1)} %get-tuple-element.23) | data formatting | bytes 8388608 | tf_op jit(solution)/shard_map/reshape | solution.py:221
  322.2 1.6 slice-done
  324.1 1.1 fusion.19
  325.2 0.7 fusion.24
  326.0 2.0 copy.130
  328.0 1.0 copy.129
  329.0 1.3 subtract_convert_fusion
  330.5 34.2 %shard_map.91 = bf16[4,256,128]{2,1,0:T(8,128)(2,1)S(1)} custom-call(s32[1]{0:T(128)} %bitcast.meta, bf16[4,256,128]{2,1,0:T(8,128)(2,1)S(1)} %maximum_bitcast_fusion.2.query_ref, bf16[2,4,256,128]{3,2,1,0:T(8,128)(2,1)S(1)} %maximum_bitcast_fusion.1.own_ref, bf16[8,2,2,4,256,128]{5,4,3,2,1,0:T(8,128)(2,1)} %all-to-all-done.2.received_ref, ...), custom_call_target="tpu_custom_call" | custom-call | flops 2281701376 | bytes 9437184 | tf_op jit(solution)/shard_map/pallas_call | solution.py:115
  364.9 1.7 convolution_convert_fusion
  366.6 10.2 %all-to-all-start.4 = ((bf16[4,64,2048]{2,1,0:T(8,128)(2,1)}), bf16[4,64,2048]{2,1,0:T(8,128)(2,1)S(1)}, u32[]{:S(2)}, u32[]{:S(2)}) async-start(bf16[4,64,2048]{2,1,0:T(8,128)(2,1)} %bitcast.74), calls=%async_computation.4 | async-start | bytes 2097152 | tf_op jit(solution)/shard_map/all_to_all | solution.py:30
  376.8 14.5 %all-to-all-done.4 = bf16[4,64,2048]{2,1,0:T(8,128)(2,1)S(1)} async-done(((bf16[4,64,2048]{2,1,0:T(8,128)(2,1)}), bf16[4,64,2048]{2,1,0:T(8,128)(2,1)S(1)}, u32[]{:S(2)}, u32[]{:S(2)}) %all-to-all-start.4) | async-done | bytes 1048608 | tf_op jit(solution)/shard_map/all_to_all | solution.py:30
  391.4 1.1 convert_reduce_fusion.3
  393.1 17.0 %all_to_all.42 = bf16[4,64,2048]{2,1,0:T(8,128)(2,1)S(1)} all-to-all(bf16[4,64,2048]{2,1,0:T(8,128)(2,1)S(1)} %broadcast_in_dim.50), channel_id=1, replica_groups=mesh['y'=4,'r'=8,'mp'=4] {'mp'}, dimensions={0} | all-to-all | bytes 2097152 | tf_op jit(solution)/shard_map/all_to_all | solution.py:23
  410.1 1.3 fusion.25
  411.4 5.9 %convolution_convert_fusion.1 = bf16[256,2048]{1,0:T(8,128)(2,1)S(1)} fusion(bf16[1024,2048]{1,0:T(8,128)(2,1)} %reshape.356, bf16[256,2048]{1,0:T(8,128)(2,1)S(1)} %bitcast.84, bf16[2048,1024]{1,0:T(8,128)(2,1)} %get-tuple-element.17, f32[256,1024]{1,0:T(8,128)S(1)} %fusion.25), kind=kOutput, calls=%fused_computation.5 | convolution fusion | flops 2149580800 | bytes 11534336 | tf_op jit(solution)/shard_map/dot_general | solution.py:244
  417.3 16.9 %all_to_all.43 = bf16[4,64,2048]{2,1,0:T(8,128)(2,1)S(1)} all-to-all(bf16[4,64,2048]{2,1,0:T(8,128)(2,1)S(1)} %bitcast.85), channel_id=1, replica_groups=mesh['y'=4,'r'=8,'mp'=4] {'mp'}, dimensions={0} | all-to-all | bytes 2097152 | tf_op jit(solution)/shard_map/all_to_all | solution.py:30
  434.4 0.8 fusion.11
  (74 shorter events, 7.3 us)
Async XLA Ops:
  6.5 4.1 copy-start.3
  12.1 7.1 %copy-start.4 = (f32[64,512]{1,0:T(8,128)S(1)}, f32[64,512]{1,0:T(8,128)}, u32[]{:S(2)}) copy-start(f32[64,512]{1,0:T(8,128)} %param.11) | copy-start | bytes 393220
  12.6 6.7 %copy-start.5 = (f32[64,512]{1,0:T(8,128)S(1)}, f32[64,512]{1,0:T(8,128)}, u32[]{:S(2)}) copy-start(f32[64,512]{1,0:T(8,128)} %param.12) | copy-start | bytes 393220
  12.6 6.8 %copy-start.6 = (f32[64,512]{1,0:T(8,128)S(1)}, f32[64,512]{1,0:T(8,128)}, u32[]{:S(2)}) copy-start(f32[64,512]{1,0:T(8,128)} %param.13) | copy-start | bytes 393220
  15.6 13.7 %all-to-all-start = ((bf16[4,2,40960]{2,1,0:T(2,128)(2,1)}), bf16[4,2,40960]{2,1,0:T(2,128)(2,1)S(1)}, u32[]{:S(2)}, u32[]{:S(2)}) async-start(bf16[4,2,40960]{2,1,0:T(2,128)(2,1)} %reshape.367), calls=%async_computation | async-start | bytes 1310720 | tf_op jit(solution)/shard_map/all_to_all | solution.py:169
  19.1 286.9 %all-gather.2.cloned.1.call-start = ((), (), s32[]{:S(2)}) async-start(), calls=%async_computation.7 | async-start | bytes 15138816 | tf_op jit(solution)/shard_map/all_gather | solution.py:197
  36.4 11.3 %copy-start.7 = (s32[4]{0:T(128)S(1)}, s32[4]{0:T(128)}, u32[]{:S(2)}) copy-start(s32[4]{0:T(128)} %param.10) | copy-start | bytes 52
  36.4 11.6 %copy-start = (bf16[256,2048]{1,0:T(8,128)(2,1)S(1)}, bf16[256,2048]{1,0:T(8,128)(2,1)}, u32[]{:S(2)}) copy-start(bf16[256,2048]{1,0:T(8,128)(2,1)} %param.9) | copy-start | bytes 3145732
  36.4 69.0 %all-to-all-start.1 = ((bf16[32,64,1024]{2,1,0:T(8,128)(2,1)}), bf16[32,64,1024]{2,1,0:T(8,128)(2,1)}, u32[]{:S(2)}, u32[]{:S(2)}) async-start(bf16[32,64,1024]{2,1,0:T(8,128)(2,1)} %broadcast_in_dim.44), calls=%async_computation.1 | async-start | bytes 8388608 | tf_op jit(solution)/shard_map/all_to_all | solution.py:23
  115.9 20.8 %collective-permute-start = (bf16[2,4,256,128]{3,2,1,0:T(8,128)(2,1)S(1)}, bf16[2,4,256,128]{3,2,1,0:T(8,128)(2,1)S(1)}, u32[]{:S(2)}, u32[]{:S(2)}) collective-permute-start(bf16[2,4,256,128]{3,2,1,0:T(8,128)(2,1)S(1)} %maximum_bitcast_fusion.1.own_ref), channel_id=1, source_target_pairs={{0,64},{4,68},{8,72},{12,76},{16,80},{20,84},{24,88},{28,92},{32,9... | collective-permute-start | bytes 1572872 | tf_op jit(solution)/shard_map/ppermute | solution.py:17
  120.5 25.7 %collective-permute-start.1 = (bf16[2,4,256,128]{3,2,1,0:T(8,128)(2,1)S(1)}, bf16[2,4,256,128]{3,2,1,0:T(8,128)(2,1)S(1)}, u32[]{:S(2)}, u32[]{:S(2)}) collective-permute-start(bf16[2,4,256,128]{3,2,1,0:T(8,128)(2,1)S(1)} %maximum_bitcast_fusion.1.own_ref), channel_id=1, source_target_pairs={{0,32},{4,36},{8,40},{12,44},{16,48},{20,52},{24,56},{28,60},{32,6... | collective-permute-start | bytes 1572872 | tf_op jit(solution)/shard_map/ppermute | solution.py:17
  156.7 138.9 %all-to-all-start.2 = ((bf16[8,2,2,4,256,128]{5,4,3,2,1,0:T(8,128)(2,1)}), bf16[8,2,2,4,256,128]{5,4,3,2,1,0:T(8,128)(2,1)}, u32[]{:S(2)}, u32[]{:S(2)}) async-start(bf16[8,2,2,4,256,128]{5,4,3,2,1,0:T(8,128)(2,1)} %pad_maximum_fusion), calls=%async_computation.2 | async-start | bytes 16777216 | tf_op jit(solution)/shard_map/all_to_all | solution.py:217
  168.4 1.0 collective-permute-start.2
  297.2 67.6 %all-to-all-start.3 = ((bf16[8,64,2048]{2,1,0:T(8,128)(2,1)}), bf16[8,64,2048]{2,1,0:T(8,128)(2,1)S(1)}, u32[]{:S(2)}, u32[]{:S(2)}) async-start(bf16[8,64,2048]{2,1,0:T(8,128)(2,1)} %broadcast_in_dim.49), calls=%async_computation.3 | async-start | bytes 4194304 | tf_op jit(solution)/shard_map/all_to_all | solution.py:23
  322.2 1.6 slice-start
  322.2 1.9 copy-start.1
  366.6 24.7 %all-to-all-start.4 = ((bf16[4,64,2048]{2,1,0:T(8,128)(2,1)}), bf16[4,64,2048]{2,1,0:T(8,128)(2,1)S(1)}, u32[]{:S(2)}, u32[]{:S(2)}) async-start(bf16[4,64,2048]{2,1,0:T(8,128)(2,1)} %bitcast.74), calls=%async_computation.4 | async-start | bytes 2097152 | tf_op jit(solution)/shard_map/all_to_all | solution.py:30
  392.5 17.6 %copy-start.2 = (bf16[2048,1024]{1,0:T(8,128)(2,1)S(1)}, bf16[2048,1024]{1,0:T(8,128)(2,1)}, u32[]{:S(2)}) copy-start(bf16[2048,1024]{1,0:T(8,128)(2,1)} %get-tuple-element.16) | copy-start | bytes 12582916
Sparse Core Ops, SparseCore 0:
  34.0 255.2 all-gather.1

commit v8 on v7

--- a/solution.py
+++ b/solution.py
@@ -215,13 +215,11 @@
         (nearer, jnp.broadcast_to(back_one[None], (plane,) + back_one.shape)), axis=1
     )
     received = lax.all_to_all(payload, "r", 0, 0, tiled=True)
+    received, rest_full = lax.optimization_barrier((received, rest_full))
     q_full = rest_full[:, :narrow]
     server_gate = rest_full[:, narrow : narrow + units]
     server_up = rest_full[:, narrow + units : narrow + 2 * units]
     server_down = rest_full[:, narrow + 2 * units :].reshape(units, -1)
-    received, q_full, server_gate, server_up, server_down = lax.optimization_barrier(
-        (received, q_full, server_gate, server_up, server_down)
-    )
     joined_q = jnp.dot(normed, q_full, preferred_element_type=jnp.float32)
     query = rotate(joined_q.reshape(rows, heads_dev, HEAD), q_offset).astype(half_type)
     query = jnp.transpose(query, (1, 0, 2))

time: 443 us -> 433 us (0.977)
  blocking collectives: 33.9 us -> 16.9 us
  waiting for transfers between devices: 228 us -> 235 us
  local copies, waits for them, and re-layouts: 45.6 us -> 40.5 us
    all_to_all x1 -> x0, blocking collectives: 17 us -> none  [gather_by_exchange(): got = lax.all_to_all(copies, axis, 0, 0, tiled=True)]
    slice x1, local copies, waits for them, and re-layouts: 9.09 us -> 4.64 us  [on_device(): server_down = rest_full[:, narrow + 2 * units:].reshape(units, -1)]
    all_to_all x2 -> x3, starting transfers between devices: 20.1 us -> 23.9 us  [gather_by_exchange(): got = lax.all_to_all(copies, axis, 0, 0, tiled=True)]
    all_to_all x2 -> x3, waiting for transfers between devices: 56.2 us -> 58.8 us  [gather_by_exchange(): got = lax.all_to_all(copies, axis, 0, 0, tiled=True)]
  transfers between devices with their start and end apart: 9 -> 10, of which waited for: 6 -> 7; matrix products, arithmetic and copies ran while one was open for 12% -> 12% of each run, Pallas kernels for 8% -> 8%
where the time goes in v8:
time: 433 us; the launch traced here: 432 us
  waiting for transfers between devices  235 us (54%)
  starting transfers between devices  54.3 us (13%)
  local copies, waits for them, and re-layouts  40.5 us (9%)
  Pallas kernels  34.2 us (8%)
  other arithmetic  19.5 us (5%)
  matrix products  17.5 us (4%)
  blocking collectives  16.9 us (4%)
  between operations  13.9 us (3%)
    all_to_all x1, waiting for transfers between devices, on_device(): received = lax.all_to_all(payload, 'r', 0, 0, tiled=True)  128 us
    all_to_all x3, waiting for transfers between devices, gather_by_exchange(): got = lax.all_to_all(copies, axis, 0, 0, tiled=True)  58.8 us
    pallas_call x1, Pallas kernels, attend(): pl.pallas_call(attend_kernel, out_shape=jax.ShapeDtypeStruct((heads, rows...  34.2 us
    ppermute x2, waiting for transfers between devices, shifted(): lax.ppermute(value, axis, [(source, source + steps) for source in range(c...  23.9 us
    all_to_all x3, starting transfers between devices, gather_by_exchange(): got = lax.all_to_all(copies, axis, 0, 0, tiled=True)  23.9 us
    all_to_all x1, blocking collectives, scatter_sum(): got = lax.all_to_all(pieces, axis, 0, 0, tiled=True)  16.9 us
    all_to_all x1, waiting for transfers between devices, scatter_sum(): got = lax.all_to_all(pieces, axis, 0, 0, tiled=True)  14.5 us
    all_to_all x1, starting transfers between devices, on_device(): received = lax.all_to_all(payload, 'r', 0, 0, tiled=True)  10.4 us
  transfers between devices with their start and end apart: 10, of which 7 were waited for; matrix products, arithmetic and copies ran while one was open for 12% of the time, Pallas kernels for 8%

profile of v8, /device:TPU:4, one launch (start us, length us, event | category | flops | bytes accessed | tf_op | source)
XLA Modules:
  0.0 432.2 jit_solution(3428446530278415358)
XLA Ops:
  6.5 1.2 copy.105
  8.1 0.6 reshape.345
  9.1 0.6 reshape.347
  10.3 0.5 broadcast.240
  10.8 1.5 reduce
  12.3 1.5 reshape.367
  13.8 3.5 all-to-all-start
  17.6 9.9 %all-to-all-done = bf16[4,2,40960]{2,1,0:T(2,128)(2,1)S(1)} async-done(((bf16[4,2,40960]{2,1,0:T(2,128)(2,1)}), bf16[4,2,40960]{2,1,0:T(2,128)(2,1)S(1)}, u32[]{:S(2)}, u32[]{:S(2)}) %all-to-all-start) | async-done | bytes 655392 | tf_op jit(solution)/shard_map/all_to_all | solution.py:169
  27.5 0.6 reshape.368
  28.2 0.8 copy.134
  30.9 1.1 copy.118
  32.0 2.5 broadcast_in_dim.44
  34.6 11.3 %all-to-all-start.1 = ((bf16[32,64,1024]{2,1,0:T(8,128)(2,1)}), bf16[32,64,1024]{2,1,0:T(8,128)(2,1)}, u32[]{:S(2)}, u32[]{:S(2)}) async-start(bf16[32,64,1024]{2,1,0:T(8,128)(2,1)} %broadcast_in_dim.44), calls=%async_computation.1 | async-start | bytes 8388608 | tf_op jit(solution)/shard_map/all_to_all | solution.py:23
  46.8 0.5 multiply_cosine_fusion
  47.4 56.3 %all-to-all-done.1 = bf16[32,64,1024]{2,1,0:T(8,128)(2,1)} async-done(((bf16[32,64,1024]{2,1,0:T(8,128)(2,1)}), bf16[32,64,1024]{2,1,0:T(8,128)(2,1)}, u32[]{:S(2)}, u32[]{:S(2)}) %all-to-all-start.1) | async-done | bytes 4194336 | tf_op jit(solution)/shard_map/all_to_all | solution.py:23
  103.7 6.5 %copy.110 = bf16[1024,2048]{1,0:T(8,128)(2,1)} copy(bf16[1024,2048]{0,1:T(8,128)(2,1)} %bitcast.9) | data formatting | bytes 8388608 | tf_op jit(solution)/shard_map/dot_general | solution.py:200
  110.2 3.5 fusion.16
  114.2 3.9 collective-permute-start
  118.1 1.8 collective-permute-start.1
  120.0 16.6 %collective-permute-done = bf16[2,4,256,128]{3,2,1,0:T(8,128)(2,1)S(1)} collective-permute-done((bf16[2,4,256,128]{3,2,1,0:T(8,128)(2,1)S(1)}, bf16[2,4,256,128]{3,2,1,0:T(8,128)(2,1)S(1)}, u32[]{:S(2)}, u32[]{:S(2)}) %collective-permute-start) | collective-permute-done | bytes 524320 | tf_op jit(solution)/shard_map/ppermute | solution.py:17
  136.6 2.5 broadcast_select_fusion
  139.1 7.3 %collective-permute-done.1 = bf16[2,4,256,128]{3,2,1,0:T(8,128)(2,1)S(1)} collective-permute-done((bf16[2,4,256,128]{3,2,1,0:T(8,128)(2,1)S(1)}, bf16[2,4,256,128]{3,2,1,0:T(8,128)(2,1)S(1)}, u32[]{:S(2)}, u32[]{:S(2)}) %collective-permute-start.1) | collective-permute-done | bytes 524320 | tf_op jit(solution)/shard_map/ppermute | solution.py:17
  146.4 3.0 stack_broadcast_in_dim.2
  149.4 8.5 %pad_maximum_fusion = bf16[8,2,2,4,256,128]{5,4,3,2,1,0:T(8,128)(2,1)} fusion(bf16[8,1,2,4,256,128]{5,4,3,2,1,0:T(8,128)(2,1)} %stack_broadcast_in_dim.2, bf16[8,1,2,4,256,128]{5,4,3,2,1,0:T(8,128)(2,1)} %broadcast_select_fusion), kind=kLoop, calls=%fused_computation | loop fusion | flops 4194304 | bytes 16777216 | tf_op jit(solution)/shard_map/stack | solution.py:214
  158.0 10.4 %all-to-all-start.2 = ((bf16[8,2,2,4,256,128]{5,4,3,2,1,0:T(8,128)(2,1)}), bf16[8,2,2,4,256,128]{5,4,3,2,1,0:T(8,128)(2,1)}, u32[]{:S(2)}, u32[]{:S(2)}) async-start(bf16[8,2,2,4,256,128]{5,4,3,2,1,0:T(8,128)(2,1)} %pad_maximum_fusion), calls=%async_computation.2 | async-start | bytes 16777216 | tf_op jit(solution)/shard_map/all_to_all | solution.py:217
  168.5 0.7 collective-permute-start.2
  169.2 128.2 %all-to-all-done.2.received_ref = bf16[8,2,2,4,256,128]{5,4,3,2,1,0:T(8,128)(2,1)} async-done(((bf16[8,2,2,4,256,128]{5,4,3,2,1,0:T(8,128)(2,1)}), bf16[8,2,2,4,256,128]{5,4,3,2,1,0:T(8,128)(2,1)}, u32[]{:S(2)}, u32[]{:S(2)}) %all-to-all-start.2) | async-done | bytes 8388640 | tf_op jit(solution)/shard_map/all_to_all | solution.py:217
  297.4 1.6 broadcast_in_dim.49
  299.0 8.9 %all-to-all-start.3 = ((bf16[8,64,2048]{2,1,0:T(8,128)(2,1)}), bf16[8,64,2048]{2,1,0:T(8,128)(2,1)S(1)}, u32[]{:S(2)}, u32[]{:S(2)}) async-start(bf16[8,64,2048]{2,1,0:T(8,128)(2,1)} %broadcast_in_dim.49), calls=%async_computation.3 | async-start | bytes 4194304 | tf_op jit(solution)/shard_map/all_to_all | solution.py:23
  308.4 3.0 fusion.8
  311.4 0.7 fusion.35
  312.1 2.0 copy.129
  314.1 1.1 copy.130
  315.2 1.3 subtract_convert_fusion
  316.7 34.2 %shard_map.91 = bf16[4,256,128]{2,1,0:T(8,128)(2,1)S(1)} custom-call(s32[1]{0:T(128)} %bitcast.meta, bf16[4,256,128]{2,1,0:T(8,128)(2,1)S(1)} %maximum_bitcast_fusion.2.query_ref, bf16[2,4,256,128]{3,2,1,0:T(8,128)(2,1)S(1)} %maximum_bitcast_fusion.1.own_ref, bf16[8,2,2,4,256,128]{5,4,3,2,1,0:T(8,128)(2,1)} %all-to-all-done.2.received_ref, ...), custom_call_target="tpu_custom_call" | custom-call | flops 2281701376 | bytes 9437184 | tf_op jit(solution)/shard_map/pallas_call | solution.py:115
  351.1 1.7 convolution_convert_fusion
  352.8 10.1 %all-to-all-start.4 = ((bf16[4,64,2048]{2,1,0:T(8,128)(2,1)}), bf16[4,64,2048]{2,1,0:T(8,128)(2,1)S(1)}, u32[]{:S(2)}, u32[]{:S(2)}) async-start(bf16[4,64,2048]{2,1,0:T(8,128)(2,1)} %bitcast.71), calls=%async_computation.4 | async-start | bytes 2097152 | tf_op jit(solution)/shard_map/all_to_all | solution.py:30
  362.9 14.5 %all-to-all-done.4 = bf16[4,64,2048]{2,1,0:T(8,128)(2,1)S(1)} async-done(((bf16[4,64,2048]{2,1,0:T(8,128)(2,1)}), bf16[4,64,2048]{2,1,0:T(8,128)(2,1)S(1)}, u32[]{:S(2)}, u32[]{:S(2)}) %all-to-all-start.4) | async-done | bytes 1048608 | tf_op jit(solution)/shard_map/all_to_all | solution.py:30
  377.5 1.1 convert_reduce_fusion.3
  379.1 1.1 broadcast_in_dim.50
  380.2 3.7 all-to-all-start.5
  383.9 4.6 %slice.56 = bf16[2048,1024]{1,0:T(8,128)(2,1)} slice(bf16[2048,3584]{1,0:T(8,128)(2,1)} %all-gather.2.cloned.1.call-done), slice={[0:2048], [2560:3584]} | slice | bytes 8388608 | tf_op jit(solution)/shard_map/slice | solution.py:222
  388.6 7.1 %reshape.363 = bf16[1024,2048]{1,0:T(8,128)(2,1)} reshape(bf16[2048,1024]{1,0:T(8,128)(2,1)} %slice.56) | data formatting | bytes 8388608 | tf_op jit(solution)/shard_map/reshape | solution.py:222
  395.7 2.5 all-to-all-done.5
  398.1 3.4 fusion.2
  401.6 5.9 %convolution_convert_fusion.1 = bf16[256,2048]{1,0:T(8,128)(2,1)S(1)} fusion(bf16[1024,2048]{1,0:T(8,128)(2,1)} %reshape.363, bf16[256,2048]{1,0:T(8,128)(2,1)S(1)} %bitcast.81, bf16[2048,3584]{1,0:T(8,128)(2,1)} %all-gather.2.cloned.1.call-done, f32[256,1024]{1,0:T(8,128)S(1)} %fusion.2), kind=kOutput, calls=%fused_computation.9 | convolution fusion | flops 2149580800 | bytes 11534336 | tf_op jit(solution)/shard_map/dot_general | solution.py:242
  407.5 16.9 %all_to_all.42 = bf16[4,64,2048]{2,1,0:T(8,128)(2,1)S(1)} all-to-all(bf16[4,64,2048]{2,1,0:T(8,128)(2,1)S(1)} %bitcast.82), channel_id=1, replica_groups=mesh['y'=4,'r'=8,'mp'=4] {'mp'}, dimensions={0} | all-to-all | bytes 2097152 | tf_op jit(solution)/shard_map/all_to_all | solution.py:30
  424.6 0.8 fusion.24
  (73 shorter events, 6.5 us)
Async XLA Ops:
  6.5 2.1 copy-start.2
  6.5 3.2 copy-start.3
  6.5 3.2 copy-start.1
  10.2 7.1 %copy-start.4 = (f32[64,512]{1,0:T(8,128)S(1)}, f32[64,512]{1,0:T(8,128)}, u32[]{:S(2)}) copy-start(f32[64,512]{1,0:T(8,128)} %param.13) | copy-start | bytes 393220
  10.3 7.1 %copy-start.5 = (f32[64,512]{1,0:T(8,128)S(1)}, f32[64,512]{1,0:T(8,128)}, u32[]{:S(2)}) copy-start(f32[64,512]{1,0:T(8,128)} %param.12) | copy-start | bytes 393220
  10.8 6.6 %copy-start.6 = (f32[64,512]{1,0:T(8,128)S(1)}, f32[64,512]{1,0:T(8,128)}, u32[]{:S(2)}) copy-start(f32[64,512]{1,0:T(8,128)} %param.11) | copy-start | bytes 393220
  13.8 13.7 %all-to-all-start = ((bf16[4,2,40960]{2,1,0:T(2,128)(2,1)}), bf16[4,2,40960]{2,1,0:T(2,128)(2,1)S(1)}, u32[]{:S(2)}, u32[]{:S(2)}) async-start(bf16[4,2,40960]{2,1,0:T(2,128)(2,1)} %reshape.367), calls=%async_computation | async-start | bytes 1310720 | tf_op jit(solution)/shard_map/all_to_all | solution.py:169
  17.3 291.1 %all-gather.2.cloned.1.call-start = ((), (), s32[]{:S(2)}) async-start(), calls=%async_computation.7 | async-start | bytes 15138816 | tf_op jit(solution)/shard_map/all_gather | solution.py:197
  34.6 11.3 %copy-start.7 = (s32[4]{0:T(128)S(1)}, s32[4]{0:T(128)}, u32[]{:S(2)}) copy-start(s32[4]{0:T(128)} %param.10) | copy-start | bytes 52
  34.6 11.6 %copy-start = (bf16[256,2048]{1,0:T(8,128)(2,1)S(1)}, bf16[256,2048]{1,0:T(8,128)(2,1)}, u32[]{:S(2)}) copy-start(bf16[256,2048]{1,0:T(8,128)(2,1)} %param.9) | copy-start | bytes 3145732
  34.6 69.1 %all-to-all-start.1 = ((bf16[32,64,1024]{2,1,0:T(8,128)(2,1)}), bf16[32,64,1024]{2,1,0:T(8,128)(2,1)}, u32[]{:S(2)}, u32[]{:S(2)}) async-start(bf16[32,64,1024]{2,1,0:T(8,128)(2,1)} %broadcast_in_dim.44), calls=%async_computation.1 | async-start | bytes 8388608 | tf_op jit(solution)/shard_map/all_to_all | solution.py:23
  114.2 22.4 %collective-permute-start = (bf16[2,4,256,128]{3,2,1,0:T(8,128)(2,1)S(1)}, bf16[2,4,256,128]{3,2,1,0:T(8,128)(2,1)S(1)}, u32[]{:S(2)}, u32[]{:S(2)}) collective-permute-start(bf16[2,4,256,128]{3,2,1,0:T(8,128)(2,1)S(1)} %maximum_bitcast_fusion.1.own_ref), channel_id=1, source_target_pairs={{0,64},{4,68},{8,72},{12,76},{16,80},{20,84},{24,88},{28,92},{32,9... | collective-permute-start | bytes 1572872 | tf_op jit(solution)/shard_map/ppermute | solution.py:17
  118.1 28.3 %collective-permute-start.1 = (bf16[2,4,256,128]{3,2,1,0:T(8,128)(2,1)S(1)}, bf16[2,4,256,128]{3,2,1,0:T(8,128)(2,1)S(1)}, u32[]{:S(2)}, u32[]{:S(2)}) collective-permute-start(bf16[2,4,256,128]{3,2,1,0:T(8,128)(2,1)S(1)} %maximum_bitcast_fusion.1.own_ref), channel_id=1, source_target_pairs={{0,32},{4,36},{8,40},{12,44},{16,48},{20,52},{24,56},{28,60},{32,6... | collective-permute-start | bytes 1572872 | tf_op jit(solution)/shard_map/ppermute | solution.py:17
  158.0 139.4 %all-to-all-start.2 = ((bf16[8,2,2,4,256,128]{5,4,3,2,1,0:T(8,128)(2,1)}), bf16[8,2,2,4,256,128]{5,4,3,2,1,0:T(8,128)(2,1)}, u32[]{:S(2)}, u32[]{:S(2)}) async-start(bf16[8,2,2,4,256,128]{5,4,3,2,1,0:T(8,128)(2,1)} %pad_maximum_fusion), calls=%async_computation.2 | async-start | bytes 16777216 | tf_op jit(solution)/shard_map/all_to_all | solution.py:217
  168.5 0.7 collective-permute-start.2
  299.0 52.0 %all-to-all-start.3 = ((bf16[8,64,2048]{2,1,0:T(8,128)(2,1)}), bf16[8,64,2048]{2,1,0:T(8,128)(2,1)S(1)}, u32[]{:S(2)}, u32[]{:S(2)}) async-start(bf16[8,64,2048]{2,1,0:T(8,128)(2,1)} %broadcast_in_dim.49), calls=%async_computation.3 | async-start | bytes 4194304 | tf_op jit(solution)/shard_map/all_to_all | solution.py:23
  352.8 24.6 %all-to-all-start.4 = ((bf16[4,64,2048]{2,1,0:T(8,128)(2,1)}), bf16[4,64,2048]{2,1,0:T(8,128)(2,1)S(1)}, u32[]{:S(2)}, u32[]{:S(2)}) async-start(bf16[4,64,2048]{2,1,0:T(8,128)(2,1)} %bitcast.71), calls=%async_computation.4 | async-start | bytes 2097152 | tf_op jit(solution)/shard_map/all_to_all | solution.py:30
  380.2 18.0 %all-to-all-start.5 = ((bf16[4,64,2048]{2,1,0:T(8,128)(2,1)}), bf16[4,64,2048]{2,1,0:T(8,128)(2,1)S(1)}, u32[]{:S(2)}, u32[]{:S(2)}) async-start(bf16[4,64,2048]{2,1,0:T(8,128)(2,1)} %broadcast_in_dim.50), calls=%async_computation.5 | async-start | bytes 2097152 | tf_op jit(solution)/shard_map/all_to_all | solution.py:23
Sparse Core Ops, SparseCore 0:
  32.2 258.8 all-gather.1

commit v9 on v8

--- a/solution.py
+++ b/solution.py
@@ -71,13 +71,14 @@
     qp = qp_ref[...]
     qw = qw_ref[...]
 
-    def one_step(head, keys, values, back, carry):
+    def one_step(head, keys, values, back, carry, masked=True):
         accum, total, top = carry
         scores = lax.dot_general(
             query_ref[head], keys, (((1,), (1,)), ((), ())), preferred_element_type=jnp.float32
         ) * scale
-        allowed = (qp == kp_ref[back]) & (kw_ref[back] <= qw)
-        scores = jnp.where(allowed, scores, -jnp.inf)
+        if masked:
+            allowed = (qp == kp_ref[back]) & (kw_ref[back] <= qw)
+            scores = jnp.where(allowed, scores, -jnp.inf)
         new_top = jnp.maximum(top, jnp.max(scores, axis=1, keepdims=True))
         fade = jnp.exp(top - new_top)
         weights = jnp.exp(scores - new_top)
@@ -99,9 +100,21 @@
         def body(back, carry, head=head):
             source = lax.rem(r_index - back + 2 * plane, plane)
             middle = jnp.logical_and(back > r_index, back <= r_index + plane).astype(jnp.int32)
-            keys = received_ref[source, middle, 0, head]
-            values = received_ref[source, middle, 1, head]
-            return one_step(head, keys, values, back, carry)
+            mode = meta[1 + back]
+
+            def run(carry, masked):
+                keys = received_ref[source, middle, 0, head]
+                values = received_ref[source, middle, 1, head]
+                return one_step(head, keys, values, back, carry, masked)
+
+            return lax.cond(
+                mode == 0,
+                lambda carry: carry,
+                lambda carry: lax.cond(
+                    mode == 2, lambda c: run(c, False), lambda c: run(c, True), carry
+                ),
+                carry,
+            )
 
         accum, total, top = lax.fori_loop(1, steps, body, carry)
         out_ref[head] = (accum / total).astype(out_ref.dtype)
@@ -110,6 +123,10 @@
 def attend(r_index, query, own_pair, received, q_prompt, q_where, k_prompt, k_where):
     heads, rows, width = query.shape
     steps = k_prompt.shape[0]
+    empty = k_prompt[:, -1] < q_prompt[0]
+    full = (k_prompt[:, 0] == q_prompt[-1]) & (k_prompt[:, -1] == q_prompt[0])
+    full = full & (jnp.arange(steps) > 0)
+    mode = jnp.where(empty, 0, jnp.where(full, 2, 1)).astype(jnp.int32)
     flops = 4 * heads * rows * rows * width * steps
     vmem = pl.BlockSpec(memory_space=pltpu.VMEM)
     return pl.pallas_call(
@@ -124,7 +141,7 @@
             bytes_accessed=received.size * 2 + own_pair.size * 2 + query.size * 4,
         ),
     )(
-        jnp.reshape(r_index, (1,)).astype(jnp.int32),
+        jnp.concatenate([jnp.reshape(r_index, (1,)).astype(jnp.int32), mode]),
         query,
         own_pair,
         received,

time: 433 us -> 435 us (level)
  the two profiles are of different devices: /device:TPU:4 before, /device:TPU:108 now
where the time goes in v9:
time: 435 us; the launch traced here: 434 us
  waiting for transfers between devices  233 us (54%)
  starting transfers between devices  51.3 us (12%)
  local copies, waits for them, and re-layouts  41.2 us (9%)
  Pallas kernels  39.9 us (9%)
  other arithmetic  20.3 us (5%)
  matrix products  17.5 us (4%)
  blocking collectives  16.9 us (4%)
  between operations  13.9 us (3%)
    all_to_all x1, waiting for transfers between devices, on_device(): received = lax.all_to_all(payload, 'r', 0, 0, tiled=True)  120 us
    all_to_all x3, waiting for transfers between devices, gather_by_exchange(): got = lax.all_to_all(copies, axis, 0, 0, tiled=True)  57.5 us
    pallas_call x1, Pallas kernels, attend(): pl.pallas_call(attend_kernel, out_shape=jax.ShapeDtypeStruct((heads, rows...  39.9 us
    ppermute x2, waiting for transfers between devices, shifted(): lax.ppermute(value, axis, [(source, source + steps) for source in range(c...  27.5 us
    all_to_all x3, starting transfers between devices, gather_by_exchange(): got = lax.all_to_all(copies, axis, 0, 0, tiled=True)  22.1 us
    all_to_all x1, blocking collectives, scatter_sum(): got = lax.all_to_all(pieces, axis, 0, 0, tiled=True)  16.9 us
    all_to_all x1, waiting for transfers between devices, scatter_sum(): got = lax.all_to_all(pieces, axis, 0, 0, tiled=True)  14.5 us
    all_to_all x1, starting transfers between devices, on_device(): received = lax.all_to_all(payload, 'r', 0, 0, tiled=True)  11.1 us
  transfers between devices with their start and end apart: 10, of which 8 were waited for; matrix products, arithmetic and copies ran while one was open for 12% of the time, Pallas kernels for 9%

profile of v9, /device:TPU:108, one launch (start us, length us, event | category | flops | bytes accessed | tf_op | source)
XLA Modules:
  0.0 434.1 jit_solution(17931835465522869017)
XLA Ops:
  6.5 1.2 copy.105
  8.1 0.6 reshape.354
  10.8 1.5 reduce.4
  12.3 1.5 reshape.376
  13.8 3.5 all-to-all-start
  17.6 9.9 %all-to-all-done = bf16[4,2,40960]{2,1,0:T(2,128)(2,1)S(1)} async-done(((bf16[4,2,40960]{2,1,0:T(2,128)(2,1)}), bf16[4,2,40960]{2,1,0:T(2,128)(2,1)S(1)}, u32[]{:S(2)}, u32[]{:S(2)}) %all-to-all-start) | async-done | bytes 655392 | tf_op jit(solution)/shard_map/all_to_all | solution.py:186
  27.5 0.6 reshape.377
  28.2 0.8 copy.134
  30.9 1.1 copy.118
  32.0 2.6 broadcast_in_dim.66
  34.6 9.8 %all-to-all-start.1 = ((bf16[32,64,1024]{2,1,0:T(8,128)(2,1)}), bf16[32,64,1024]{2,1,0:T(8,128)(2,1)}, u32[]{:S(2)}, u32[]{:S(2)}) async-start(bf16[32,64,1024]{2,1,0:T(8,128)(2,1)} %broadcast_in_dim.66), calls=%async_computation.1 | async-start | bytes 8388608 | tf_op jit(solution)/shard_map/all_to_all | solution.py:23
  45.9 55.0 %all-to-all-done.1 = bf16[32,64,1024]{2,1,0:T(8,128)(2,1)} async-done(((bf16[32,64,1024]{2,1,0:T(8,128)(2,1)}), bf16[32,64,1024]{2,1,0:T(8,128)(2,1)}, u32[]{:S(2)}, u32[]{:S(2)}) %all-to-all-start.1) | async-done | bytes 4194336 | tf_op jit(solution)/shard_map/all_to_all | solution.py:23
  100.9 6.5 %copy.110 = bf16[1024,2048]{1,0:T(8,128)(2,1)} copy(bf16[1024,2048]{0,1:T(8,128)(2,1)} %bitcast.13) | data formatting | bytes 8388608 | tf_op jit(solution)/shard_map/dot_general | solution.py:217
  107.4 3.5 fusion.16
  111.4 2.5 collective-permute-start
  114.0 2.1 collective-permute-start.1
  116.1 17.4 %collective-permute-done = bf16[2,4,256,128]{3,2,1,0:T(8,128)(2,1)S(1)} collective-permute-done((bf16[2,4,256,128]{3,2,1,0:T(8,128)(2,1)S(1)}, bf16[2,4,256,128]{3,2,1,0:T(8,128)(2,1)S(1)}, u32[]{:S(2)}, u32[]{:S(2)}) %collective-permute-start) | collective-permute-done | bytes 524320 | tf_op jit(solution)/shard_map/ppermute | solution.py:17
  133.5 2.6 broadcast_select_fusion
  136.1 10.1 %collective-permute-done.1 = bf16[2,4,256,128]{3,2,1,0:T(8,128)(2,1)S(1)} collective-permute-done((bf16[2,4,256,128]{3,2,1,0:T(8,128)(2,1)S(1)}, bf16[2,4,256,128]{3,2,1,0:T(8,128)(2,1)S(1)}, u32[]{:S(2)}, u32[]{:S(2)}) %collective-permute-start.1) | collective-permute-done | bytes 524320 | tf_op jit(solution)/shard_map/ppermute | solution.py:17
  146.2 3.1 stack_broadcast_in_dim.2
  149.2 7.7 %pad_maximum_fusion = bf16[8,2,2,4,256,128]{5,4,3,2,1,0:T(8,128)(2,1)} fusion(bf16[8,1,2,4,256,128]{5,4,3,2,1,0:T(8,128)(2,1)} %stack_broadcast_in_dim.2, bf16[8,1,2,4,256,128]{5,4,3,2,1,0:T(8,128)(2,1)} %broadcast_select_fusion), kind=kLoop, calls=%fused_computation | loop fusion | flops 4194304 | bytes 16777216 | tf_op jit(solution)/shard_map/stack | solution.py:231
  156.9 11.1 %all-to-all-start.2 = ((bf16[8,2,2,4,256,128]{5,4,3,2,1,0:T(8,128)(2,1)}), bf16[8,2,2,4,256,128]{5,4,3,2,1,0:T(8,128)(2,1)}, u32[]{:S(2)}, u32[]{:S(2)}) async-start(bf16[8,2,2,4,256,128]{5,4,3,2,1,0:T(8,128)(2,1)} %pad_maximum_fusion), calls=%async_computation.2 | async-start | bytes 16777216 | tf_op jit(solution)/shard_map/all_to_all | solution.py:234
  168.3 1.9 collective-permute-start.2
  170.3 0.7 fusion.39
  171.0 1.5 fusion.30
  172.5 3.5 collective-permute-done.2
  176.0 120.0 %all-to-all-done.2.received_ref = bf16[8,2,2,4,256,128]{5,4,3,2,1,0:T(8,128)(2,1)} async-done(((bf16[8,2,2,4,256,128]{5,4,3,2,1,0:T(8,128)(2,1)}), bf16[8,2,2,4,256,128]{5,4,3,2,1,0:T(8,128)(2,1)}, u32[]{:S(2)}, u32[]{:S(2)}) %all-to-all-start.2) | async-done | bytes 8388640 | tf_op jit(solution)/shard_map/all_to_all | solution.py:234
  296.0 1.6 broadcast_in_dim.110
  297.6 8.6 %all-to-all-start.3 = ((bf16[8,64,2048]{2,1,0:T(8,128)(2,1)}), bf16[8,64,2048]{2,1,0:T(8,128)(2,1)S(1)}, u32[]{:S(2)}, u32[]{:S(2)}) async-start(bf16[8,64,2048]{2,1,0:T(8,128)(2,1)} %broadcast_in_dim.110), calls=%async_computation.3 | async-start | bytes 4194304 | tf_op jit(solution)/shard_map/all_to_all | solution.py:23
  306.6 3.0 fusion.8
  309.6 0.7 fusion.38
  310.3 2.0 copy.129
  312.3 1.1 copy.130
  313.4 1.4 subtract_convert_fusion
  314.9 39.9 %shard_map.91 = bf16[4,256,128]{2,1,0:T(8,128)(2,1)S(1)} custom-call(s32[18]{0:T(128)S(1)} %pad_add_fusion.meta, bf16[4,256,128]{2,1,0:T(8,128)(2,1)S(1)} %maximum_bitcast_fusion.2.query_ref, bf16[2,4,256,128]{3,2,1,0:T(8,128)(2,1)S(1)} %maximum_bitcast_fusion.1.own_ref, bf16[8,2,2,4,256,128]{5,4,3,2,1,0:T(8,128)(2,1)} %all-to-all-done.2.received_ref, ...), custom_call_target="tpu_custom_call" | custom-call | flops 2281701376 | bytes 9437184 | tf_op jit(solution)/shard_map/pallas_call | solution.py:132
  355.0 1.7 convolution_convert_fusion
  356.7 8.1 %all-to-all-start.4 = ((bf16[4,64,2048]{2,1,0:T(8,128)(2,1)}), bf16[4,64,2048]{2,1,0:T(8,128)(2,1)S(1)}, u32[]{:S(2)}, u32[]{:S(2)}) async-start(bf16[4,64,2048]{2,1,0:T(8,128)(2,1)} %bitcast.73), calls=%async_computation.4 | async-start | bytes 2097152 | tf_op jit(solution)/shard_map/all_to_all | solution.py:30
  364.8 14.5 %all-to-all-done.4 = bf16[4,64,2048]{2,1,0:T(8,128)(2,1)S(1)} async-done(((bf16[4,64,2048]{2,1,0:T(8,128)(2,1)}), bf16[4,64,2048]{2,1,0:T(8,128)(2,1)S(1)}, u32[]{:S(2)}, u32[]{:S(2)}) %all-to-all-start.4) | async-done | bytes 1048608 | tf_op jit(solution)/shard_map/all_to_all | solution.py:30
  379.4 1.1 convert_reduce_fusion.3
  381.0 1.1 broadcast_in_dim.111
  382.1 3.7 all-to-all-start.5
  385.8 4.7 %slice.74 = bf16[2048,1024]{1,0:T(8,128)(2,1)} slice(bf16[2048,3584]{1,0:T(8,128)(2,1)} %all-gather.2.cloned.1.call-done), slice={[0:2048], [2560:3584]} | slice | bytes 8388608 | tf_op jit(solution)/shard_map/slice | solution.py:239
  390.5 7.1 %reshape.370 = bf16[1024,2048]{1,0:T(8,128)(2,1)} reshape(bf16[2048,1024]{1,0:T(8,128)(2,1)} %slice.74) | data formatting | bytes 8388608 | tf_op jit(solution)/shard_map/reshape | solution.py:239
  397.6 2.4 all-to-all-done.5
  400.1 3.4 fusion.2
  403.5 5.9 %convolution_convert_fusion.1 = bf16[256,2048]{1,0:T(8,128)(2,1)S(1)} fusion(bf16[1024,2048]{1,0:T(8,128)(2,1)} %reshape.370, bf16[256,2048]{1,0:T(8,128)(2,1)S(1)} %bitcast.83, bf16[2048,3584]{1,0:T(8,128)(2,1)} %all-gather.2.cloned.1.call-done, f32[256,1024]{1,0:T(8,128)S(1)} %fusion.2), kind=kOutput, calls=%fused_computation.9 | convolution fusion | flops 2149580800 | bytes 11534336 | tf_op jit(solution)/shard_map/dot_general | solution.py:259
  409.4 16.9 %all_to_all.42 = bf16[4,64,2048]{2,1,0:T(8,128)(2,1)S(1)} all-to-all(bf16[4,64,2048]{2,1,0:T(8,128)(2,1)S(1)} %bitcast.84), channel_id=1, replica_groups=mesh['y'=4,'r'=8,'mp'=4] {'mp'}, dimensions={0} | all-to-all | bytes 2097152 | tf_op jit(solution)/shard_map/all_to_all | solution.py:30
  426.5 0.8 fusion.24
  (78 shorter events, 8.2 us)
Async XLA Ops:
  6.5 2.1 copy-start.2
  6.5 3.2 copy-start.3
  6.5 3.2 copy-start.1
  10.2 7.1 %copy-start.4 = (f32[64,512]{1,0:T(8,128)S(1)}, f32[64,512]{1,0:T(8,128)}, u32[]{:S(2)}) copy-start(f32[64,512]{1,0:T(8,128)} %param.12) | copy-start | bytes 393220
  10.3 7.1 %copy-start.5 = (f32[64,512]{1,0:T(8,128)S(1)}, f32[64,512]{1,0:T(8,128)}, u32[]{:S(2)}) copy-start(f32[64,512]{1,0:T(8,128)} %param.13) | copy-start | bytes 393220
  10.8 6.6 %copy-start.6 = (f32[64,512]{1,0:T(8,128)S(1)}, f32[64,512]{1,0:T(8,128)}, u32[]{:S(2)}) copy-start(f32[64,512]{1,0:T(8,128)} %param.11) | copy-start | bytes 393220
  13.8 13.7 %all-to-all-start = ((bf16[4,2,40960]{2,1,0:T(2,128)(2,1)}), bf16[4,2,40960]{2,1,0:T(2,128)(2,1)S(1)}, u32[]{:S(2)}, u32[]{:S(2)}) async-start(bf16[4,2,40960]{2,1,0:T(2,128)(2,1)} %reshape.376), calls=%async_computation | async-start | bytes 1310720 | tf_op jit(solution)/shard_map/all_to_all | solution.py:186
  17.3 289.3 %all-gather.2.cloned.1.call-start = ((), (), s32[]{:S(2)}) async-start(), calls=%async_computation.7 | async-start | bytes 15138816 | tf_op jit(solution)/shard_map/all_gather | solution.py:214
  34.6 9.8 %copy-start.7 = (s32[4]{0:T(128)S(1)}, s32[4]{0:T(128)}, u32[]{:S(2)}) copy-start(s32[4]{0:T(128)} %param.10) | copy-start | bytes 52
  34.6 10.1 %copy-start = (bf16[256,2048]{1,0:T(8,128)(2,1)S(1)}, bf16[256,2048]{1,0:T(8,128)(2,1)}, u32[]{:S(2)}) copy-start(bf16[256,2048]{1,0:T(8,128)(2,1)} %param.9) | copy-start | bytes 3145732
  34.6 66.3 %all-to-all-start.1 = ((bf16[32,64,1024]{2,1,0:T(8,128)(2,1)}), bf16[32,64,1024]{2,1,0:T(8,128)(2,1)}, u32[]{:S(2)}, u32[]{:S(2)}) async-start(bf16[32,64,1024]{2,1,0:T(8,128)(2,1)} %broadcast_in_dim.66), calls=%async_computation.1 | async-start | bytes 8388608 | tf_op jit(solution)/shard_map/all_to_all | solution.py:23
  111.4 22.1 %collective-permute-start = (bf16[2,4,256,128]{3,2,1,0:T(8,128)(2,1)S(1)}, bf16[2,4,256,128]{3,2,1,0:T(8,128)(2,1)S(1)}, u32[]{:S(2)}, u32[]{:S(2)}) collective-permute-start(bf16[2,4,256,128]{3,2,1,0:T(8,128)(2,1)S(1)} %maximum_bitcast_fusion.1.own_ref), channel_id=1, source_target_pairs={{0,64},{4,68},{8,72},{12,76},{16,80},{20,84},{24,88},{28,92},{32,9... | collective-permute-start | bytes 1572872 | tf_op jit(solution)/shard_map/ppermute | solution.py:17
  114.0 32.2 %collective-permute-start.1 = (bf16[2,4,256,128]{3,2,1,0:T(8,128)(2,1)S(1)}, bf16[2,4,256,128]{3,2,1,0:T(8,128)(2,1)S(1)}, u32[]{:S(2)}, u32[]{:S(2)}) collective-permute-start(bf16[2,4,256,128]{3,2,1,0:T(8,128)(2,1)S(1)} %maximum_bitcast_fusion.1.own_ref), channel_id=1, source_target_pairs={{0,32},{4,36},{8,40},{12,44},{16,48},{20,52},{24,56},{28,60},{32,6... | collective-permute-start | bytes 1572872 | tf_op jit(solution)/shard_map/ppermute | solution.py:17
  156.9 139.1 %all-to-all-start.2 = ((bf16[8,2,2,4,256,128]{5,4,3,2,1,0:T(8,128)(2,1)}), bf16[8,2,2,4,256,128]{5,4,3,2,1,0:T(8,128)(2,1)}, u32[]{:S(2)}, u32[]{:S(2)}) async-start(bf16[8,2,2,4,256,128]{5,4,3,2,1,0:T(8,128)(2,1)} %pad_maximum_fusion), calls=%async_computation.2 | async-start | bytes 16777216 | tf_op jit(solution)/shard_map/all_to_all | solution.py:234
  168.3 7.7 %collective-permute-start.2 = (bf16[64,2048]{1,0:T(8,128)(2,1)S(1)}, bf16[64,2048]{1,0:T(8,128)(2,1)S(1)}, u32[]{:S(2)}, u32[]{:S(2)}) collective-permute-start(bf16[64,2048]{1,0:T(8,128)(2,1)S(1)} %bitcast.90), channel_id=1, source_target_pairs={{0,0},{1,32},{2,64},{3,96},{32,1},{33,33},{34,65},{35,97},{64,2},{... | collective-permute-start | bytes 786440 | tf_op jit(solution)/shard_map/ppermute | solution.py:210
  297.6 57.4 %all-to-all-start.3 = ((bf16[8,64,2048]{2,1,0:T(8,128)(2,1)}), bf16[8,64,2048]{2,1,0:T(8,128)(2,1)S(1)}, u32[]{:S(2)}, u32[]{:S(2)}) async-start(bf16[8,64,2048]{2,1,0:T(8,128)(2,1)} %broadcast_in_dim.110), calls=%async_computation.3 | async-start | bytes 4194304 | tf_op jit(solution)/shard_map/all_to_all | solution.py:23
  356.7 22.5 %all-to-all-start.4 = ((bf16[4,64,2048]{2,1,0:T(8,128)(2,1)}), bf16[4,64,2048]{2,1,0:T(8,128)(2,1)S(1)}, u32[]{:S(2)}, u32[]{:S(2)}) async-start(bf16[4,64,2048]{2,1,0:T(8,128)(2,1)} %bitcast.73), calls=%async_computation.4 | async-start | bytes 2097152 | tf_op jit(solution)/shard_map/all_to_all | solution.py:30
  382.1 18.0 %all-to-all-start.5 = ((bf16[4,64,2048]{2,1,0:T(8,128)(2,1)}), bf16[4,64,2048]{2,1,0:T(8,128)(2,1)S(1)}, u32[]{:S(2)}, u32[]{:S(2)}) async-start(bf16[4,64,2048]{2,1,0:T(8,128)(2,1)} %broadcast_in_dim.111), calls=%async_computation.5 | async-start | bytes 2097152 | tf_op jit(solution)/shard_map/all_to_all | solution.py:23
Sparse Core Ops, SparseCore 0:
  32.1 255.3 all-gather.1

commit v10 on v8

--- a/solution.py
+++ b/solution.py
@@ -87,23 +87,33 @@
         total = total * fade + jnp.sum(weights, axis=1, keepdims=True)
         return (accum, total, new_top)
 
+    rows, width = query_ref.shape[1], query_ref.shape[2]
+    carries = []
     for head in range(heads):
-        rows, width = query_ref.shape[1], query_ref.shape[2]
         carry = (
             jnp.zeros((rows, width), jnp.float32),
             jnp.zeros((rows, 1), jnp.float32),
             jnp.full((rows, 1), -jnp.inf, jnp.float32),
         )
-        carry = one_step(head, own_ref[0, head], own_ref[1, head], 0, carry)
-
-        def body(back, carry, head=head):
-            source = lax.rem(r_index - back + 2 * plane, plane)
-            middle = jnp.logical_and(back > r_index, back <= r_index + plane).astype(jnp.int32)
-            keys = received_ref[source, middle, 0, head]
-            values = received_ref[source, middle, 1, head]
-            return one_step(head, keys, values, back, carry)
-
-        accum, total, top = lax.fori_loop(1, steps, body, carry)
+        carries.append(one_step(head, own_ref[0, head], own_ref[1, head], 0, carry))
+
+    def body(back, carries):
+        source = lax.rem(r_index - back + 2 * plane, plane)
+        middle = jnp.logical_and(back > r_index, back <= r_index + plane).astype(jnp.int32)
+        return tuple(
+            one_step(
+                head,
+                received_ref[source, middle, 0, head],
+                received_ref[source, middle, 1, head],
+                back,
+                carries[head],
+            )
+            for head in range(heads)
+        )
+
+    carries = lax.fori_loop(1, steps, body, tuple(carries))
+    for head in range(heads):
+        accum, total, top = carries[head]
         out_ref[head] = (accum / total).astype(out_ref.dtype)
 
 

time: 433 us -> 420 us (0.970)
  Pallas kernels: 34.2 us -> 21.3 us
    pallas_call x1, Pallas kernels: 34.2 us -> 21.3 us  [attend(): pl.pallas_call(attend_kernel, out_shape=jax.ShapeDtypeStruct((heads, rows...]
  transfers between devices with their start and end apart: 10 -> 10, of which waited for: 7 -> 7; matrix products, arithmetic and copies ran while one was open for 12% -> 12% of each run, Pallas kernels for 8% -> 5%
where the time goes in v10:
time: 420 us; the launch traced here: 419 us
  waiting for transfers between devices  236 us (56%)
  starting transfers between devices  54.1 us (13%)
  local copies, waits for them, and re-layouts  40.5 us (10%)
  Pallas kernels  21.3 us (5%)
  other arithmetic  19.5 us (5%)
  matrix products  17.5 us (4%)
  blocking collectives  16.9 us (4%)
  between operations  13.9 us (3%)
    all_to_all x1, waiting for transfers between devices, on_device(): received = lax.all_to_all(payload, 'r', 0, 0, tiled=True)  128 us
    all_to_all x3, waiting for transfers between devices, gather_by_exchange(): got = lax.all_to_all(copies, axis, 0, 0, tiled=True)  59 us
    ppermute x2, waiting for transfers between devices, shifted(): lax.ppermute(value, axis, [(source, source + steps) for source in range(c...  23.9 us
    all_to_all x3, starting transfers between devices, gather_by_exchange(): got = lax.all_to_all(copies, axis, 0, 0, tiled=True)  23.6 us
    pallas_call x1, Pallas kernels, attend(): pl.pallas_call(attend_kernel, out_shape=jax.ShapeDtypeStruct((heads, rows...  21.3 us
    all_to_all x1, blocking collectives, scatter_sum(): got = lax.all_to_all(pieces, axis, 0, 0, tiled=True)  16.9 us
    all_to_all x1, waiting for transfers between devices, scatter_sum(): got = lax.all_to_all(pieces, axis, 0, 0, tiled=True)  14.5 us
    all_to_all x1, starting transfers between devices, on_device(): received = lax.all_to_all(payload, 'r', 0, 0, tiled=True)  10.4 us
  transfers between devices with their start and end apart: 10, of which 7 were waited for; matrix products, arithmetic and copies ran while one was open for 12% of the time, Pallas kernels for 5%

profile of v10, /device:TPU:4, one launch (start us, length us, event | category | flops | bytes accessed | tf_op | source)
XLA Modules:
  0.0 419.2 jit_solution(12560709066256638433)
XLA Ops:
  6.5 1.2 copy.105
  8.1 0.6 reshape.345
  9.1 0.6 reshape.347
  10.3 0.5 broadcast.240
  10.8 1.5 reduce
  12.3 1.5 reshape.367
  13.8 3.5 all-to-all-start
  17.6 9.9 %all-to-all-done = bf16[4,2,40960]{2,1,0:T(2,128)(2,1)S(1)} async-done(((bf16[4,2,40960]{2,1,0:T(2,128)(2,1)}), bf16[4,2,40960]{2,1,0:T(2,128)(2,1)S(1)}, u32[]{:S(2)}, u32[]{:S(2)}) %all-to-all-start) | async-done | bytes 655392 | tf_op jit(solution)/shard_map/all_to_all | solution.py:179
  27.5 0.6 reshape.368
  28.2 0.8 copy.134
  30.9 1.1 copy.118
  32.0 2.5 broadcast_in_dim.44
  34.6 11.3 %all-to-all-start.1 = ((bf16[32,64,1024]{2,1,0:T(8,128)(2,1)}), bf16[32,64,1024]{2,1,0:T(8,128)(2,1)}, u32[]{:S(2)}, u32[]{:S(2)}) async-start(bf16[32,64,1024]{2,1,0:T(8,128)(2,1)} %broadcast_in_dim.44), calls=%async_computation.1 | async-start | bytes 8388608 | tf_op jit(solution)/shard_map/all_to_all | solution.py:23
  46.8 0.5 multiply_cosine_fusion
  47.4 56.3 %all-to-all-done.1 = bf16[32,64,1024]{2,1,0:T(8,128)(2,1)} async-done(((bf16[32,64,1024]{2,1,0:T(8,128)(2,1)}), bf16[32,64,1024]{2,1,0:T(8,128)(2,1)}, u32[]{:S(2)}, u32[]{:S(2)}) %all-to-all-start.1) | async-done | bytes 4194336 | tf_op jit(solution)/shard_map/all_to_all | solution.py:23
  103.7 6.5 %copy.110 = bf16[1024,2048]{1,0:T(8,128)(2,1)} copy(bf16[1024,2048]{0,1:T(8,128)(2,1)} %bitcast.9) | data formatting | bytes 8388608 | tf_op jit(solution)/shard_map/dot_general | solution.py:210
  110.2 3.5 fusion.16
  114.2 3.9 collective-permute-start
  118.1 1.8 collective-permute-start.1
  120.0 16.6 %collective-permute-done = bf16[2,4,256,128]{3,2,1,0:T(8,128)(2,1)S(1)} collective-permute-done((bf16[2,4,256,128]{3,2,1,0:T(8,128)(2,1)S(1)}, bf16[2,4,256,128]{3,2,1,0:T(8,128)(2,1)S(1)}, u32[]{:S(2)}, u32[]{:S(2)}) %collective-permute-start) | collective-permute-done | bytes 524320 | tf_op jit(solution)/shard_map/ppermute | solution.py:17
  136.6 2.5 broadcast_select_fusion
  139.1 7.3 %collective-permute-done.1 = bf16[2,4,256,128]{3,2,1,0:T(8,128)(2,1)S(1)} collective-permute-done((bf16[2,4,256,128]{3,2,1,0:T(8,128)(2,1)S(1)}, bf16[2,4,256,128]{3,2,1,0:T(8,128)(2,1)S(1)}, u32[]{:S(2)}, u32[]{:S(2)}) %collective-permute-start.1) | collective-permute-done | bytes 524320 | tf_op jit(solution)/shard_map/ppermute | solution.py:17
  146.4 3.0 stack_broadcast_in_dim.2
  149.4 8.5 %pad_maximum_fusion = bf16[8,2,2,4,256,128]{5,4,3,2,1,0:T(8,128)(2,1)} fusion(bf16[8,1,2,4,256,128]{5,4,3,2,1,0:T(8,128)(2,1)} %stack_broadcast_in_dim.2, bf16[8,1,2,4,256,128]{5,4,3,2,1,0:T(8,128)(2,1)} %broadcast_select_fusion), kind=kLoop, calls=%fused_computation | loop fusion | flops 4194304 | bytes 16777216 | tf_op jit(solution)/shard_map/stack | solution.py:224
  158.0 10.4 %all-to-all-start.2 = ((bf16[8,2,2,4,256,128]{5,4,3,2,1,0:T(8,128)(2,1)}), bf16[8,2,2,4,256,128]{5,4,3,2,1,0:T(8,128)(2,1)}, u32[]{:S(2)}, u32[]{:S(2)}) async-start(bf16[8,2,2,4,256,128]{5,4,3,2,1,0:T(8,128)(2,1)} %pad_maximum_fusion), calls=%async_computation.2 | async-start | bytes 16777216 | tf_op jit(solution)/shard_map/all_to_all | solution.py:227
  168.5 0.7 collective-permute-start.2
  169.2 128.2 %all-to-all-done.2.received_ref = bf16[8,2,2,4,256,128]{5,4,3,2,1,0:T(8,128)(2,1)} async-done(((bf16[8,2,2,4,256,128]{5,4,3,2,1,0:T(8,128)(2,1)}), bf16[8,2,2,4,256,128]{5,4,3,2,1,0:T(8,128)(2,1)}, u32[]{:S(2)}, u32[]{:S(2)}) %all-to-all-start.2) | async-done | bytes 8388640 | tf_op jit(solution)/shard_map/all_to_all | solution.py:227
  297.4 1.6 broadcast_in_dim.49
  299.0 8.9 %all-to-all-start.3 = ((bf16[8,64,2048]{2,1,0:T(8,128)(2,1)}), bf16[8,64,2048]{2,1,0:T(8,128)(2,1)S(1)}, u32[]{:S(2)}, u32[]{:S(2)}) async-start(bf16[8,64,2048]{2,1,0:T(8,128)(2,1)} %broadcast_in_dim.49), calls=%async_computation.3 | async-start | bytes 4194304 | tf_op jit(solution)/shard_map/all_to_all | solution.py:23
  308.4 3.0 fusion.8
  311.4 0.7 fusion.35
  312.1 2.0 copy.129
  314.1 1.1 copy.130
  315.2 1.3 subtract_convert_fusion
  316.7 21.3 %shard_map.91 = bf16[4,256,128]{2,1,0:T(8,128)(2,1)S(1)} custom-call(s32[1]{0:T(128)} %bitcast.meta, bf16[4,256,128]{2,1,0:T(8,128)(2,1)S(1)} %maximum_bitcast_fusion.2.query_ref, bf16[2,4,256,128]{3,2,1,0:T(8,128)(2,1)S(1)} %maximum_bitcast_fusion.1.own_ref, bf16[8,2,2,4,256,128]{5,4,3,2,1,0:T(8,128)(2,1)} %all-to-all-done.2.received_ref, ...), custom_call_target="tpu_custom_call" | custom-call | flops 2281701376 | bytes 9437184 | tf_op jit(solution)/shard_map/pallas_call | solution.py:125
  338.1 1.7 convolution_convert_fusion
  339.8 10.1 %all-to-all-start.4 = ((bf16[4,64,2048]{2,1,0:T(8,128)(2,1)}), bf16[4,64,2048]{2,1,0:T(8,128)(2,1)S(1)}, u32[]{:S(2)}, u32[]{:S(2)}) async-start(bf16[4,64,2048]{2,1,0:T(8,128)(2,1)} %bitcast.71), calls=%async_computation.4 | async-start | bytes 2097152 | tf_op jit(solution)/shard_map/all_to_all | solution.py:30
  349.9 14.5 %all-to-all-done.4 = bf16[4,64,2048]{2,1,0:T(8,128)(2,1)S(1)} async-done(((bf16[4,64,2048]{2,1,0:T(8,128)(2,1)}), bf16[4,64,2048]{2,1,0:T(8,128)(2,1)S(1)}, u32[]{:S(2)}, u32[]{:S(2)}) %all-to-all-start.4) | async-done | bytes 1048608 | tf_op jit(solution)/shard_map/all_to_all | solution.py:30
  364.5 1.1 convert_reduce_fusion.3
  366.1 1.1 broadcast_in_dim.50
  367.2 3.5 all-to-all-start.5
  370.7 4.6 %slice.56 = bf16[2048,1024]{1,0:T(8,128)(2,1)} slice(bf16[2048,3584]{1,0:T(8,128)(2,1)} %all-gather.2.cloned.1.call-done), slice={[0:2048], [2560:3584]} | slice | bytes 8388608 | tf_op jit(solution)/shard_map/slice | solution.py:232
  375.4 7.1 %reshape.363 = bf16[1024,2048]{1,0:T(8,128)(2,1)} reshape(bf16[2048,1024]{1,0:T(8,128)(2,1)} %slice.56) | data formatting | bytes 8388608 | tf_op jit(solution)/shard_map/reshape | solution.py:232
  382.5 2.7 all-to-all-done.5
  385.2 3.4 fusion.2
  388.6 5.9 %convolution_convert_fusion.1 = bf16[256,2048]{1,0:T(8,128)(2,1)S(1)} fusion(bf16[1024,2048]{1,0:T(8,128)(2,1)} %reshape.363, bf16[256,2048]{1,0:T(8,128)(2,1)S(1)} %bitcast.81, bf16[2048,3584]{1,0:T(8,128)(2,1)} %all-gather.2.cloned.1.call-done, f32[256,1024]{1,0:T(8,128)S(1)} %fusion.2), kind=kOutput, calls=%fused_computation.9 | convolution fusion | flops 2149580800 | bytes 11534336 | tf_op jit(solution)/shard_map/dot_general | solution.py:252
  394.5 16.9 %all_to_all.42 = bf16[4,64,2048]{2,1,0:T(8,128)(2,1)S(1)} all-to-all(bf16[4,64,2048]{2,1,0:T(8,128)(2,1)S(1)} %bitcast.82), channel_id=1, replica_groups=mesh['y'=4,'r'=8,'mp'=4] {'mp'}, dimensions={0} | all-to-all | bytes 2097152 | tf_op jit(solution)/shard_map/all_to_all | solution.py:30
  411.6 0.8 fusion.24
  (73 shorter events, 6.5 us)
Async XLA Ops:
  6.5 2.1 copy-start.2
  6.5 3.2 copy-start.3
  6.5 3.2 copy-start.1
  10.2 7.1 %copy-start.4 = (f32[64,512]{1,0:T(8,128)S(1)}, f32[64,512]{1,0:T(8,128)}, u32[]{:S(2)}) copy-start(f32[64,512]{1,0:T(8,128)} %param.13) | copy-start | bytes 393220
  10.3 7.1 %copy-start.5 = (f32[64,512]{1,0:T(8,128)S(1)}, f32[64,512]{1,0:T(8,128)}, u32[]{:S(2)}) copy-start(f32[64,512]{1,0:T(8,128)} %param.12) | copy-start | bytes 393220
  10.8 6.6 %copy-start.6 = (f32[64,512]{1,0:T(8,128)S(1)}, f32[64,512]{1,0:T(8,128)}, u32[]{:S(2)}) copy-start(f32[64,512]{1,0:T(8,128)} %param.11) | copy-start | bytes 393220
  13.8 13.7 %all-to-all-start = ((bf16[4,2,40960]{2,1,0:T(2,128)(2,1)}), bf16[4,2,40960]{2,1,0:T(2,128)(2,1)S(1)}, u32[]{:S(2)}, u32[]{:S(2)}) async-start(bf16[4,2,40960]{2,1,0:T(2,128)(2,1)} %reshape.367), calls=%async_computation | async-start | bytes 1310720 | tf_op jit(solution)/shard_map/all_to_all | solution.py:179
  17.3 291.1 %all-gather.2.cloned.1.call-start = ((), (), s32[]{:S(2)}) async-start(), calls=%async_computation.7 | async-start | bytes 15138816 | tf_op jit(solution)/shard_map/all_gather | solution.py:207
  34.6 11.3 %copy-start.7 = (s32[4]{0:T(128)S(1)}, s32[4]{0:T(128)}, u32[]{:S(2)}) copy-start(s32[4]{0:T(128)} %param.10) | copy-start | bytes 52
  34.6 11.6 %copy-start = (bf16[256,2048]{1,0:T(8,128)(2,1)S(1)}, bf16[256,2048]{1,0:T(8,128)(2,1)}, u32[]{:S(2)}) copy-start(bf16[256,2048]{1,0:T(8,128)(2,1)} %param.9) | copy-start | bytes 3145732
  34.6 69.1 %all-to-all-start.1 = ((bf16[32,64,1024]{2,1,0:T(8,128)(2,1)}), bf16[32,64,1024]{2,1,0:T(8,128)(2,1)}, u32[]{:S(2)}, u32[]{:S(2)}) async-start(bf16[32,64,1024]{2,1,0:T(8,128)(2,1)} %broadcast_in_dim.44), calls=%async_computation.1 | async-start | bytes 8388608 | tf_op jit(solution)/shard_map/all_to_all | solution.py:23
  114.2 22.4 %collective-permute-start = (bf16[2,4,256,128]{3,2,1,0:T(8,128)(2,1)S(1)}, bf16[2,4,256,128]{3,2,1,0:T(8,128)(2,1)S(1)}, u32[]{:S(2)}, u32[]{:S(2)}) collective-permute-start(bf16[2,4,256,128]{3,2,1,0:T(8,128)(2,1)S(1)} %maximum_bitcast_fusion.1.own_ref), channel_id=1, source_target_pairs={{0,64},{4,68},{8,72},{12,76},{16,80},{20,84},{24,88},{28,92},{32,9... | collective-permute-start | bytes 1572872 | tf_op jit(solution)/shard_map/ppermute | solution.py:17
  118.1 28.3 %collective-permute-start.1 = (bf16[2,4,256,128]{3,2,1,0:T(8,128)(2,1)S(1)}, bf16[2,4,256,128]{3,2,1,0:T(8,128)(2,1)S(1)}, u32[]{:S(2)}, u32[]{:S(2)}) collective-permute-start(bf16[2,4,256,128]{3,2,1,0:T(8,128)(2,1)S(1)} %maximum_bitcast_fusion.1.own_ref), channel_id=1, source_target_pairs={{0,32},{4,36},{8,40},{12,44},{16,48},{20,52},{24,56},{28,60},{32,6... | collective-permute-start | bytes 1572872 | tf_op jit(solution)/shard_map/ppermute | solution.py:17
  158.0 139.4 %all-to-all-start.2 = ((bf16[8,2,2,4,256,128]{5,4,3,2,1,0:T(8,128)(2,1)}), bf16[8,2,2,4,256,128]{5,4,3,2,1,0:T(8,128)(2,1)}, u32[]{:S(2)}, u32[]{:S(2)}) async-start(bf16[8,2,2,4,256,128]{5,4,3,2,1,0:T(8,128)(2,1)} %pad_maximum_fusion), calls=%async_computation.2 | async-start | bytes 16777216 | tf_op jit(solution)/shard_map/all_to_all | solution.py:227
  168.5 0.7 collective-permute-start.2
  299.0 39.1 %all-to-all-start.3 = ((bf16[8,64,2048]{2,1,0:T(8,128)(2,1)}), bf16[8,64,2048]{2,1,0:T(8,128)(2,1)S(1)}, u32[]{:S(2)}, u32[]{:S(2)}) async-start(bf16[8,64,2048]{2,1,0:T(8,128)(2,1)} %broadcast_in_dim.49), calls=%async_computation.3 | async-start | bytes 4194304 | tf_op jit(solution)/shard_map/all_to_all | solution.py:23
  339.8 24.6 %all-to-all-start.4 = ((bf16[4,64,2048]{2,1,0:T(8,128)(2,1)}), bf16[4,64,2048]{2,1,0:T(8,128)(2,1)S(1)}, u32[]{:S(2)}, u32[]{:S(2)}) async-start(bf16[4,64,2048]{2,1,0:T(8,128)(2,1)} %bitcast.71), calls=%async_computation.4 | async-start | bytes 2097152 | tf_op jit(solution)/shard_map/all_to_all | solution.py:30
  367.2 18.0 %all-to-all-start.5 = ((bf16[4,64,2048]{2,1,0:T(8,128)(2,1)}), bf16[4,64,2048]{2,1,0:T(8,128)(2,1)S(1)}, u32[]{:S(2)}, u32[]{:S(2)}) async-start(bf16[4,64,2048]{2,1,0:T(8,128)(2,1)} %broadcast_in_dim.50), calls=%async_computation.5 | async-start | bytes 2097152 | tf_op jit(solution)/shard_map/all_to_all | solution.py:23
Sparse Core Ops, SparseCore 0:
  32.2 258.8 all-gather.1

commit v11 on v10

--- a/solution.py
+++ b/solution.py
@@ -220,9 +220,11 @@
 
     r_index = lax.axis_index("r")
     later = r_index < jnp.arange(plane)
-    nearer = jnp.where(later[:, None, None, None, None], own_pair[None], back_two[None])
-    payload = jnp.stack(
-        (nearer, jnp.broadcast_to(back_one[None], (plane,) + back_one.shape)), axis=1
+    first_slot = (jnp.arange(2) == 0)[None, :]
+    pick_own = (later[:, None] & first_slot)[:, :, None, None, None, None]
+    pick_two = (jnp.logical_not(later)[:, None] & first_slot)[:, :, None, None, None, None]
+    payload = jnp.where(
+        pick_own, own_pair[None, None], jnp.where(pick_two, back_two[None, None], back_one[None, None])
     )
     received = lax.all_to_all(payload, "r", 0, 0, tiled=True)
     received, rest_full = lax.optimization_barrier((received, rest_full))

time: 420 us -> 420 us (level)
  waiting for transfers between devices: 236 us -> 243 us
  other arithmetic: 19.5 us -> 13.3 us
    another operation x3 -> x2, other arithmetic: 10.1 us -> 1.45 us  [the longest x1 8.54 us: on_device(): jnp.stack((nearer, jnp.broadcast_to(back_one[None], (plane,) + back_one.s...]
    all_to_all x1, waiting for transfers between devices: 128 us -> 133 us  [on_device(): received = lax.all_to_all(payload, 'r', 0, 0, tiled=True)]
  transfers between devices with their start and end apart: 10 -> 10, of which waited for: 7 -> 7; matrix products, arithmetic and copies ran while one was open for 12% -> 10% of each run, Pallas kernels for 5% -> 5%
where the time goes in v11:
time: 420 us; the launch traced here: 419 us
  waiting for transfers between devices  243 us (58%)
  starting transfers between devices  54.9 us (13%)
  local copies, waits for them, and re-layouts  37.7 us (9%)
  Pallas kernels  21.3 us (5%)
  matrix products  17.5 us (4%)
  blocking collectives  16.9 us (4%)
  between operations  14 us (3%)
  other arithmetic  13.3 us (3%)
    all_to_all x1, waiting for transfers between devices, on_device(): received = lax.all_to_all(payload, 'r', 0, 0, tiled=True)  133 us
    all_to_all x3, waiting for transfers between devices, gather_by_exchange(): got = lax.all_to_all(copies, axis, 0, 0, tiled=True)  59 us
    ppermute x2, waiting for transfers between devices, shifted(): lax.ppermute(value, axis, [(source, source + steps) for source in range(c...  26.4 us
    all_to_all x3, starting transfers between devices, gather_by_exchange(): got = lax.all_to_all(copies, axis, 0, 0, tiled=True)  23.6 us
    pallas_call x1, Pallas kernels, attend(): pl.pallas_call(attend_kernel, out_shape=jax.ShapeDtypeStruct((heads, rows...  21.3 us
    all_to_all x1, blocking collectives, scatter_sum(): got = lax.all_to_all(pieces, axis, 0, 0, tiled=True)  16.9 us
    all_to_all x1, waiting for transfers between devices, scatter_sum(): got = lax.all_to_all(pieces, axis, 0, 0, tiled=True)  14.5 us
    all_to_all x1, starting transfers between devices, on_device(): received = lax.all_to_all(payload, 'r', 0, 0, tiled=True)  11.6 us
  transfers between devices with their start and end apart: 10, of which 7 were waited for; matrix products, arithmetic and copies ran while one was open for 10% of the time, Pallas kernels for 5%

profile of v11, /device:TPU:4, one launch (start us, length us, event | category | flops | bytes accessed | tf_op | source)
XLA Modules:
  0.0 418.8 jit_solution(2595440295862156535)
XLA Ops:
  6.5 1.2 copy.105
  8.1 0.6 reshape.398
  9.1 0.6 reshape.400
  10.3 0.5 broadcast.265
  10.8 1.5 reduce
  12.3 1.5 reshape.420
  13.8 3.5 all-to-all-start
  17.6 9.9 %all-to-all-done = bf16[4,2,40960]{2,1,0:T(2,128)(2,1)S(1)} async-done(((bf16[4,2,40960]{2,1,0:T(2,128)(2,1)}), bf16[4,2,40960]{2,1,0:T(2,128)(2,1)S(1)}, u32[]{:S(2)}, u32[]{:S(2)}) %all-to-all-start) | async-done | bytes 655392 | tf_op jit(solution)/shard_map/all_to_all | solution.py:179
  27.5 0.6 reshape.421
  28.2 0.8 copy.134
  29.5 0.3 copy.113
  30.9 1.1 copy.118
  32.0 2.6 broadcast_in_dim.54
  34.6 11.3 %all-to-all-start.1 = ((bf16[32,64,1024]{2,1,0:T(8,128)(2,1)}), bf16[32,64,1024]{2,1,0:T(8,128)(2,1)}, u32[]{:S(2)}, u32[]{:S(2)}) async-start(bf16[32,64,1024]{2,1,0:T(8,128)(2,1)} %broadcast_in_dim.54), calls=%async_computation.1 | async-start | bytes 8388608 | tf_op jit(solution)/shard_map/all_to_all | solution.py:23
  46.4 0.4 fusion.6
  46.9 0.5 multiply_cosine_fusion
  47.4 56.3 %all-to-all-done.1 = bf16[32,64,1024]{2,1,0:T(8,128)(2,1)} async-done(((bf16[32,64,1024]{2,1,0:T(8,128)(2,1)}), bf16[32,64,1024]{2,1,0:T(8,128)(2,1)}, u32[]{:S(2)}, u32[]{:S(2)}) %all-to-all-start.1) | async-done | bytes 4194336 | tf_op jit(solution)/shard_map/all_to_all | solution.py:23
  103.7 6.5 %copy.110 = bf16[1024,2048]{1,0:T(8,128)(2,1)} copy(bf16[1024,2048]{0,1:T(8,128)(2,1)} %bitcast.9) | data formatting | bytes 8388608 | tf_op jit(solution)/shard_map/dot_general | solution.py:210
  110.2 3.5 fusion.16
  114.2 3.7 collective-permute-start
  117.9 1.9 collective-permute-start.1
  119.9 16.6 %collective-permute-done = bf16[2,4,256,128]{3,2,1,0:T(8,128)(2,1)S(1)} collective-permute-done((bf16[2,4,256,128]{3,2,1,0:T(8,128)(2,1)S(1)}, bf16[2,4,256,128]{3,2,1,0:T(8,128)(2,1)S(1)}, u32[]{:S(2)}, u32[]{:S(2)}) %collective-permute-start) | collective-permute-done | bytes 524320 | tf_op jit(solution)/shard_map/ppermute | solution.py:17
  136.5 9.8 %collective-permute-done.1 = bf16[2,4,256,128]{3,2,1,0:T(8,128)(2,1)S(1)} collective-permute-done((bf16[2,4,256,128]{3,2,1,0:T(8,128)(2,1)S(1)}, bf16[2,4,256,128]{3,2,1,0:T(8,128)(2,1)S(1)}, u32[]{:S(2)}, u32[]{:S(2)}) %collective-permute-start.1) | collective-permute-done | bytes 524320 | tf_op jit(solution)/shard_map/ppermute | solution.py:17
  146.3 4.9 %select_select_fusion = bf16[8,2,2,4,256,128]{5,4,3,2,1,0:T(8,128)(2,1)} fusion(pred[8,2]{1,0:T(8,128)(4,1)S(1)} %get-tuple-element.31, pred[8,2]{1,0:T(8,128)(4,1)S(1)} %get-tuple-element.30, bf16[2,4,256,128]{3,2,1,0:T(8,128)(2,1)S(1)} %collective-permute-done.1, bf16[2,4,256,128]{3,2,1,0:T(8,128)(2,1)S(1)} %collective-permute-done, ...), kind=kLoop, calls=%fused_computation | loop fusion | flops 8388608 | bytes 9961504 | tf_op jit(solution)/shard_map/jit(_where)/select_n | solution.py:226
  151.3 11.6 %all-to-all-start.2 = ((bf16[8,2,2,4,256,128]{5,4,3,2,1,0:T(8,128)(2,1)}), bf16[8,2,2,4,256,128]{5,4,3,2,1,0:T(8,128)(2,1)}, u32[]{:S(2)}, u32[]{:S(2)}) async-start(bf16[8,2,2,4,256,128]{5,4,3,2,1,0:T(8,128)(2,1)} %select_select_fusion), calls=%async_computation.2 | async-start | bytes 16777216 | tf_op jit(solution)/shard_map/all_to_all | solution.py:229
  163.1 0.7 collective-permute-start.2
  163.8 133.4 %all-to-all-done.2.received_ref = bf16[8,2,2,4,256,128]{5,4,3,2,1,0:T(8,128)(2,1)} async-done(((bf16[8,2,2,4,256,128]{5,4,3,2,1,0:T(8,128)(2,1)}), bf16[8,2,2,4,256,128]{5,4,3,2,1,0:T(8,128)(2,1)}, u32[]{:S(2)}, u32[]{:S(2)}) %all-to-all-start.2) | async-done | bytes 8388640 | tf_op jit(solution)/shard_map/all_to_all | solution.py:229
  297.2 1.6 broadcast_in_dim.67
  298.8 8.9 %all-to-all-start.3 = ((bf16[8,64,2048]{2,1,0:T(8,128)(2,1)}), bf16[8,64,2048]{2,1,0:T(8,128)(2,1)S(1)}, u32[]{:S(2)}, u32[]{:S(2)}) async-start(bf16[8,64,2048]{2,1,0:T(8,128)(2,1)} %broadcast_in_dim.67), calls=%async_computation.3 | async-start | bytes 4194304 | tf_op jit(solution)/shard_map/all_to_all | solution.py:23
  308.1 3.0 fusion.8
  311.1 0.9 fusion.36
  312.0 1.1 copy.129
  313.1 2.0 copy.130
  315.1 1.3 subtract_convert_fusion
  316.5 21.3 %shard_map.91 = bf16[4,256,128]{2,1,0:T(8,128)(2,1)S(1)} custom-call(s32[1]{0:T(128)} %bitcast.meta, bf16[4,256,128]{2,1,0:T(8,128)(2,1)S(1)} %maximum_bitcast_fusion.2.query_ref, bf16[2,4,256,128]{3,2,1,0:T(8,128)(2,1)S(1)} %maximum_bitcast_fusion.1.own_ref, bf16[8,2,2,4,256,128]{5,4,3,2,1,0:T(8,128)(2,1)} %all-to-all-done.2.received_ref, ...), custom_call_target="tpu_custom_call" | custom-call | flops 2281701376 | bytes 9437184 | tf_op jit(solution)/shard_map/pallas_call | solution.py:125
  338.0 1.7 convolution_convert_fusion
  339.7 9.9 %all-to-all-start.4 = ((bf16[4,64,2048]{2,1,0:T(8,128)(2,1)}), bf16[4,64,2048]{2,1,0:T(8,128)(2,1)S(1)}, u32[]{:S(2)}, u32[]{:S(2)}) async-start(bf16[4,64,2048]{2,1,0:T(8,128)(2,1)} %bitcast.71), calls=%async_computation.4 | async-start | bytes 2097152 | tf_op jit(solution)/shard_map/all_to_all | solution.py:30
  349.6 14.5 %all-to-all-done.4 = bf16[4,64,2048]{2,1,0:T(8,128)(2,1)S(1)} async-done(((bf16[4,64,2048]{2,1,0:T(8,128)(2,1)}), bf16[4,64,2048]{2,1,0:T(8,128)(2,1)S(1)}, u32[]{:S(2)}, u32[]{:S(2)}) %all-to-all-start.4) | async-done | bytes 1048608 | tf_op jit(solution)/shard_map/all_to_all | solution.py:30
  364.2 1.1 convert_reduce_fusion.3
  365.7 1.1 broadcast_in_dim.68
  366.9 3.5 all-to-all-start.5
  370.4 4.7 %slice.56 = bf16[2048,1024]{1,0:T(8,128)(2,1)} slice(bf16[2048,3584]{1,0:T(8,128)(2,1)} %all-gather.2.cloned.1.call-done), slice={[0:2048], [2560:3584]} | slice | bytes 8388608 | tf_op jit(solution)/shard_map/slice | solution.py:234
  375.0 7.1 %reshape.416 = bf16[1024,2048]{1,0:T(8,128)(2,1)} reshape(bf16[2048,1024]{1,0:T(8,128)(2,1)} %slice.56) | data formatting | bytes 8388608 | tf_op jit(solution)/shard_map/reshape | solution.py:234
  382.1 2.7 all-to-all-done.5
  384.8 3.4 fusion.2
  388.2 5.9 %convolution_convert_fusion.1 = bf16[256,2048]{1,0:T(8,128)(2,1)S(1)} fusion(bf16[1024,2048]{1,0:T(8,128)(2,1)} %reshape.416, bf16[256,2048]{1,0:T(8,128)(2,1)S(1)} %bitcast.81, bf16[2048,3584]{1,0:T(8,128)(2,1)} %all-gather.2.cloned.1.call-done, f32[256,1024]{1,0:T(8,128)S(1)} %fusion.2), kind=kOutput, calls=%fused_computation.8 | convolution fusion | flops 2149580800 | bytes 11534336 | tf_op jit(solution)/shard_map/dot_general | solution.py:254
  394.2 16.9 %all_to_all.42 = bf16[4,64,2048]{2,1,0:T(8,128)(2,1)S(1)} all-to-all(bf16[4,64,2048]{2,1,0:T(8,128)(2,1)S(1)} %bitcast.82), channel_id=1, replica_groups=mesh['y'=4,'r'=8,'mp'=4] {'mp'}, dimensions={0} | all-to-all | bytes 2097152 | tf_op jit(solution)/shard_map/all_to_all | solution.py:30
  411.2 0.8 fusion.24
  (77 shorter events, 5.8 us)
Async XLA Ops:
  6.5 2.1 copy-start.4
  6.5 3.2 copy-start.5
  6.5 3.2 copy-start.3
  10.2 7.1 %copy-start.6 = (f32[64,512]{1,0:T(8,128)S(1)}, f32[64,512]{1,0:T(8,128)}, u32[]{:S(2)}) copy-start(f32[64,512]{1,0:T(8,128)} %param.13) | copy-start | bytes 393220
  10.3 7.1 %copy-start.7 = (f32[64,512]{1,0:T(8,128)S(1)}, f32[64,512]{1,0:T(8,128)}, u32[]{:S(2)}) copy-start(f32[64,512]{1,0:T(8,128)} %param.12) | copy-start | bytes 393220
  10.8 6.6 %copy-start.8 = (f32[64,512]{1,0:T(8,128)S(1)}, f32[64,512]{1,0:T(8,128)}, u32[]{:S(2)}) copy-start(f32[64,512]{1,0:T(8,128)} %param.11) | copy-start | bytes 393220
  13.8 13.7 %all-to-all-start = ((bf16[4,2,40960]{2,1,0:T(2,128)(2,1)}), bf16[4,2,40960]{2,1,0:T(2,128)(2,1)S(1)}, u32[]{:S(2)}, u32[]{:S(2)}) async-start(bf16[4,2,40960]{2,1,0:T(2,128)(2,1)} %reshape.420), calls=%async_computation | async-start | bytes 1310720 | tf_op jit(solution)/shard_map/all_to_all | solution.py:179
  17.3 290.8 %all-gather.2.cloned.1.call-start = ((), (), s32[]{:S(2)}) async-start(), calls=%async_computation.7 | async-start | bytes 15138816 | tf_op jit(solution)/shard_map/all_gather | solution.py:207
  34.6 11.3 %copy-start.9 = (s32[4]{0:T(128)S(1)}, s32[4]{0:T(128)}, u32[]{:S(2)}) copy-start(s32[4]{0:T(128)} %param.10) | copy-start | bytes 52
  34.6 11.6 %copy-start = (bf16[256,2048]{1,0:T(8,128)(2,1)S(1)}, bf16[256,2048]{1,0:T(8,128)(2,1)}, u32[]{:S(2)}) copy-start(bf16[256,2048]{1,0:T(8,128)(2,1)} %param.9) | copy-start | bytes 3145732
  34.6 69.1 %all-to-all-start.1 = ((bf16[32,64,1024]{2,1,0:T(8,128)(2,1)}), bf16[32,64,1024]{2,1,0:T(8,128)(2,1)}, u32[]{:S(2)}, u32[]{:S(2)}) async-start(bf16[32,64,1024]{2,1,0:T(8,128)(2,1)} %broadcast_in_dim.54), calls=%async_computation.1 | async-start | bytes 8388608 | tf_op jit(solution)/shard_map/all_to_all | solution.py:23
  47.4 66.4 %copy-start.1 = (f32[256,64]{1,0:T(8,128)}, f32[256,64]{1,0:T(8,128)S(1)}, u32[]{:S(2)}) copy-start(f32[256,64]{1,0:T(8,128)S(1)} %get-tuple-element.26) | copy-start | bytes 196612
  47.4 66.4 %copy-start.2 = (f32[256,64]{1,0:T(8,128)}, f32[256,64]{1,0:T(8,128)S(1)}, u32[]{:S(2)}) copy-start(f32[256,64]{1,0:T(8,128)S(1)} %get-tuple-element.27) | copy-start | bytes 196612
  114.2 22.3 %collective-permute-start = (bf16[2,4,256,128]{3,2,1,0:T(8,128)(2,1)S(1)}, bf16[2,4,256,128]{3,2,1,0:T(8,128)(2,1)S(1)}, u32[]{:S(2)}, u32[]{:S(2)}) collective-permute-start(bf16[2,4,256,128]{3,2,1,0:T(8,128)(2,1)S(1)} %maximum_bitcast_fusion.1.own_ref), channel_id=1, source_target_pairs={{0,64},{4,68},{8,72},{12,76},{16,80},{20,84},{24,88},{28,92},{32,9... | collective-permute-start | bytes 1572872 | tf_op jit(solution)/shard_map/ppermute | solution.py:17
  117.9 28.5 %collective-permute-start.1 = (bf16[2,4,256,128]{3,2,1,0:T(8,128)(2,1)S(1)}, bf16[2,4,256,128]{3,2,1,0:T(8,128)(2,1)S(1)}, u32[]{:S(2)}, u32[]{:S(2)}) collective-permute-start(bf16[2,4,256,128]{3,2,1,0:T(8,128)(2,1)S(1)} %maximum_bitcast_fusion.1.own_ref), channel_id=1, source_target_pairs={{0,32},{4,36},{8,40},{12,44},{16,48},{20,52},{24,56},{28,60},{32,6... | collective-permute-start | bytes 1572872 | tf_op jit(solution)/shard_map/ppermute | solution.py:17
  151.3 145.9 %all-to-all-start.2 = ((bf16[8,2,2,4,256,128]{5,4,3,2,1,0:T(8,128)(2,1)}), bf16[8,2,2,4,256,128]{5,4,3,2,1,0:T(8,128)(2,1)}, u32[]{:S(2)}, u32[]{:S(2)}) async-start(bf16[8,2,2,4,256,128]{5,4,3,2,1,0:T(8,128)(2,1)} %select_select_fusion), calls=%async_computation.2 | async-start | bytes 16777216 | tf_op jit(solution)/shard_map/all_to_all | solution.py:229
  163.1 0.7 collective-permute-start.2
  298.8 39.2 %all-to-all-start.3 = ((bf16[8,64,2048]{2,1,0:T(8,128)(2,1)}), bf16[8,64,2048]{2,1,0:T(8,128)(2,1)S(1)}, u32[]{:S(2)}, u32[]{:S(2)}) async-start(bf16[8,64,2048]{2,1,0:T(8,128)(2,1)} %broadcast_in_dim.67), calls=%async_computation.3 | async-start | bytes 4194304 | tf_op jit(solution)/shard_map/all_to_all | solution.py:23
  339.7 24.3 %all-to-all-start.4 = ((bf16[4,64,2048]{2,1,0:T(8,128)(2,1)}), bf16[4,64,2048]{2,1,0:T(8,128)(2,1)S(1)}, u32[]{:S(2)}, u32[]{:S(2)}) async-start(bf16[4,64,2048]{2,1,0:T(8,128)(2,1)} %bitcast.71), calls=%async_computation.4 | async-start | bytes 2097152 | tf_op jit(solution)/shard_map/all_to_all | solution.py:30
  366.9 18.0 %all-to-all-start.5 = ((bf16[4,64,2048]{2,1,0:T(8,128)(2,1)}), bf16[4,64,2048]{2,1,0:T(8,128)(2,1)S(1)}, u32[]{:S(2)}, u32[]{:S(2)}) async-start(bf16[4,64,2048]{2,1,0:T(8,128)(2,1)} %broadcast_in_dim.68), calls=%async_computation.5 | async-start | bytes 2097152 | tf_op jit(solution)/shard_map/all_to_all | solution.py:23
Sparse Core Ops, SparseCore 0:
  32.2 258.7 all-gather.1

commit v12 on v11

--- a/solution.py
+++ b/solution.py
@@ -176,9 +176,14 @@
         jnp.broadcast_to(w_out.astype(half_type)[None], (mp_size,) + w_out.shape),
     ]
     flat = jnp.concatenate([p.reshape(mp_size, -1) for p in outgoing], axis=1)
-    got = lax.all_to_all(flat, mp, 0, 0, tiled=True)
+    arrived = [flat[mp_index]]
+    for step in range(1, mp_size):
+        slot = lax.dynamic_index_in_dim(flat, lax.rem(mp_index + step, mp_size), 0, keepdims=False)
+        arrived.append(
+            lax.ppermute(slot, mp, [(i, (i + step) % mp_size) for i in range(mp_size)])
+        )
+    got = jnp.stack(arrived)[lax.rem(mp_index - jnp.arange(mp_size) + mp_size, mp_size)]
     kv_shard = jnp.concatenate([w.astype(half_type) for w in (w_key, w_value)], axis=1)
-    got, kv_shard = lax.optimization_barrier((got, kv_shard))
     pieces = []
     at = 0
     for p in outgoing:

time: 420 us -> 419 us (level)
  starting transfers between devices: 54.9 us -> 48.8 us
    all_to_all x1 -> x0, waiting for transfers between devices: 9.94 us -> none  [on_device(): got = lax.all_to_all(flat, mp, 0, 0, tiled=True)]
    ppermute x0 -> x3, waiting for transfers between devices: none -> 8.1 us  [on_device(): lax.ppermute(slot, mp, [(i, (i + step) % mp_size) for i in range(mp_size)])]
    all_to_all x1, waiting for transfers between devices: 133 us -> 139 us  [on_device(): received = lax.all_to_all(payload, 'r', 0, 0, tiled=True)]
  transfers between devices with their start and end apart: 10 -> 12, of which waited for: 7 -> 8; matrix products, arithmetic and copies ran while one was open for 10% -> 10% of each run, Pallas kernels for 5% -> 5%
where the time goes in v12:
time: 419 us; the launch traced here: 418 us
  waiting for transfers between devices  246 us (59%)
  starting transfers between devices  48.8 us (12%)
  local copies, waits for them, and re-layouts  39.1 us (9%)
  Pallas kernels  21.3 us (5%)
  matrix products  17.5 us (4%)
  blocking collectives  16.9 us (4%)
  other arithmetic  14.3 us (3%)
  between operations  14 us (3%)
    all_to_all x1, waiting for transfers between devices, on_device(): received = lax.all_to_all(payload, 'r', 0, 0, tiled=True)  139 us
    all_to_all x3, waiting for transfers between devices, gather_by_exchange(): got = lax.all_to_all(copies, axis, 0, 0, tiled=True)  58 us
    ppermute x2, waiting for transfers between devices, shifted(): lax.ppermute(value, axis, [(source, source + steps) for source in range(c...  26.5 us
    all_to_all x3, starting transfers between devices, gather_by_exchange(): got = lax.all_to_all(copies, axis, 0, 0, tiled=True)  23.9 us
    pallas_call x1, Pallas kernels, attend(): pl.pallas_call(attend_kernel, out_shape=jax.ShapeDtypeStruct((heads, rows...  21.3 us
    all_to_all x1, blocking collectives, scatter_sum(): got = lax.all_to_all(pieces, axis, 0, 0, tiled=True)  16.9 us
    all_to_all x1, waiting for transfers between devices, scatter_sum(): got = lax.all_to_all(pieces, axis, 0, 0, tiled=True)  14.5 us
    all_to_all x1, starting transfers between devices, scatter_sum(): got = lax.all_to_all(pieces, axis, 0, 0, tiled=True)  9.19 us
  transfers between devices with their start and end apart: 12, of which 8 were waited for; matrix products, arithmetic and copies ran while one was open for 10% of the time, Pallas kernels for 5%

profile of v12, /device:TPU:4, one launch (start us, length us, event | category | flops | bytes accessed | tf_op | source)
XLA Modules:
  0.0 418.1 jit_solution(14930725864663122075)
XLA Ops:
  6.5 1.0 convert_element_type.102
  7.6 1.1 copy.95
  9.1 0.6 reshape.438
  10.2 0.6 reshape.436
  11.2 3.3 dynamic-slice_reduce_fusion.2
  14.5 0.7 collective-permute-start.4
  15.2 0.8 collective-permute-start.3
  16.2 3.5 collective-permute-done.4
  19.9 4.6 %collective-permute-done.3 = bf16[81920]{0:T(1024)(128)(2,1)S(1)} collective-permute-done((bf16[81920]{0:T(1024)(128)(2,1)S(1)}, bf16[81920]{0:T(1024)(128)(2,1)S(1)}, u32[]{:S(2)}, u32[]{:S(2)}) %collective-permute-start.3) | collective-permute-done | bytes 163872 | tf_op jit(solution)/shard_map/ppermute | solution.py:183
  24.8 1.5 pad_maximum_fusion.1
  26.4 1.2 gather_fusion
  29.5 1.1 copy.102
  30.7 2.6 broadcast_in_dim.52
  33.2 11.3 %all-to-all-start = ((bf16[32,64,1024]{2,1,0:T(8,128)(2,1)}), bf16[32,64,1024]{2,1,0:T(8,128)(2,1)}, u32[]{:S(2)}, u32[]{:S(2)}) async-start(bf16[32,64,1024]{2,1,0:T(8,128)(2,1)} %broadcast_in_dim.52), calls=%async_computation | async-start | bytes 8388608 | tf_op jit(solution)/shard_map/all_to_all | solution.py:23
  45.0 0.4 fusion.6
  45.5 0.5 multiply_cosine_fusion
  46.0 55.3 %all-to-all-done = bf16[32,64,1024]{2,1,0:T(8,128)(2,1)} async-done(((bf16[32,64,1024]{2,1,0:T(8,128)(2,1)}), bf16[32,64,1024]{2,1,0:T(8,128)(2,1)}, u32[]{:S(2)}, u32[]{:S(2)}) %all-to-all-start) | async-done | bytes 4194336 | tf_op jit(solution)/shard_map/all_to_all | solution.py:23
  101.4 6.5 %copy.90 = bf16[1024,2048]{1,0:T(8,128)(2,1)} copy(bf16[1024,2048]{0,1:T(8,128)(2,1)} %bitcast.4) | data formatting | bytes 8388608 | tf_op jit(solution)/shard_map/dot_general | solution.py:215
  107.9 3.5 fusion.16
  111.9 1.3 collective-permute-start.1
  113.2 3.5 collective-permute-start
  116.8 16.0 %collective-permute-done.1 = bf16[2,4,256,128]{3,2,1,0:T(8,128)(2,1)S(1)} collective-permute-done((bf16[2,4,256,128]{3,2,1,0:T(8,128)(2,1)S(1)}, bf16[2,4,256,128]{3,2,1,0:T(8,128)(2,1)S(1)}, u32[]{:S(2)}, u32[]{:S(2)}) %collective-permute-start.1) | collective-permute-done | bytes 524320 | tf_op jit(solution)/shard_map/ppermute | solution.py:17
  132.8 10.5 %collective-permute-done = bf16[2,4,256,128]{3,2,1,0:T(8,128)(2,1)S(1)} collective-permute-done((bf16[2,4,256,128]{3,2,1,0:T(8,128)(2,1)S(1)}, bf16[2,4,256,128]{3,2,1,0:T(8,128)(2,1)S(1)}, u32[]{:S(2)}, u32[]{:S(2)}) %collective-permute-start) | collective-permute-done | bytes 524320 | tf_op jit(solution)/shard_map/ppermute | solution.py:17
  143.3 4.9 %select_select_fusion = bf16[8,2,2,4,256,128]{5,4,3,2,1,0:T(8,128)(2,1)} fusion(pred[8,2]{1,0:T(8,128)(4,1)S(1)} %get-tuple-element.31, pred[8,2]{1,0:T(8,128)(4,1)S(1)} %get-tuple-element.30, bf16[2,4,256,128]{3,2,1,0:T(8,128)(2,1)S(1)} %collective-permute-done.1, bf16[2,4,256,128]{3,2,1,0:T(8,128)(2,1)S(1)} %collective-permute-done, ...), kind=kLoop, calls=%fused_computation.1 | loop fusion | flops 8388608 | bytes 9961504 | tf_op jit(solution)/shard_map/jit(_where)/select_n | solution.py:231
  148.2 8.7 %all-to-all-start.1 = ((bf16[8,2,2,4,256,128]{5,4,3,2,1,0:T(8,128)(2,1)}), bf16[8,2,2,4,256,128]{5,4,3,2,1,0:T(8,128)(2,1)}, u32[]{:S(2)}, u32[]{:S(2)}) async-start(bf16[8,2,2,4,256,128]{5,4,3,2,1,0:T(8,128)(2,1)} %select_select_fusion), calls=%async_computation.1 | async-start | bytes 16777216 | tf_op jit(solution)/shard_map/all_to_all | solution.py:234
  157.1 0.7 collective-permute-start.5
  157.8 139.0 %all-to-all-done.1.received_ref = bf16[8,2,2,4,256,128]{5,4,3,2,1,0:T(8,128)(2,1)} async-done(((bf16[8,2,2,4,256,128]{5,4,3,2,1,0:T(8,128)(2,1)}), bf16[8,2,2,4,256,128]{5,4,3,2,1,0:T(8,128)(2,1)}, u32[]{:S(2)}, u32[]{:S(2)}) %all-to-all-start.1) | async-done | bytes 8388640 | tf_op jit(solution)/shard_map/all_to_all | solution.py:234
  296.8 1.6 broadcast_in_dim.67
  298.4 9.1 %all-to-all-start.2 = ((bf16[8,64,2048]{2,1,0:T(8,128)(2,1)}), bf16[8,64,2048]{2,1,0:T(8,128)(2,1)S(1)}, u32[]{:S(2)}, u32[]{:S(2)}) async-start(bf16[8,64,2048]{2,1,0:T(8,128)(2,1)} %broadcast_in_dim.67), calls=%async_computation.2 | async-start | bytes 4194304 | tf_op jit(solution)/shard_map/all_to_all | solution.py:23
  308.0 3.0 fusion.8
  311.0 0.9 fusion.38
  311.9 1.1 copy.113
  313.0 2.0 copy.112
  315.0 1.3 subtract_convert_fusion
  316.5 21.3 %shard_map.91 = bf16[4,256,128]{2,1,0:T(8,128)(2,1)S(1)} custom-call(s32[1]{0:T(128)} %bitcast.meta, bf16[4,256,128]{2,1,0:T(8,128)(2,1)S(1)} %maximum_bitcast_fusion.1.query_ref, bf16[2,4,256,128]{3,2,1,0:T(8,128)(2,1)S(1)} %maximum_bitcast_fusion.own_ref, bf16[8,2,2,4,256,128]{5,4,3,2,1,0:T(8,128)(2,1)} %all-to-all-done.1.received_ref, ...), custom_call_target="tpu_custom_call" | custom-call | flops 2281701376 | bytes 9437184 | tf_op jit(solution)/shard_map/pallas_call | solution.py:125
  337.9 1.7 convolution_convert_fusion
  339.6 9.2 %all-to-all-start.3 = ((bf16[4,64,2048]{2,1,0:T(8,128)(2,1)}), bf16[4,64,2048]{2,1,0:T(8,128)(2,1)S(1)}, u32[]{:S(2)}, u32[]{:S(2)}) async-start(bf16[4,64,2048]{2,1,0:T(8,128)(2,1)} %bitcast.68), calls=%async_computation.3 | async-start | bytes 2097152 | tf_op jit(solution)/shard_map/all_to_all | solution.py:30
  348.8 14.5 %all-to-all-done.3 = bf16[4,64,2048]{2,1,0:T(8,128)(2,1)S(1)} async-done(((bf16[4,64,2048]{2,1,0:T(8,128)(2,1)}), bf16[4,64,2048]{2,1,0:T(8,128)(2,1)S(1)}, u32[]{:S(2)}, u32[]{:S(2)}) %all-to-all-start.3) | async-done | bytes 1048608 | tf_op jit(solution)/shard_map/all_to_all | solution.py:30
  363.4 1.1 convert_reduce_fusion.3
  365.0 1.1 broadcast_in_dim.68
  366.1 3.5 all-to-all-start.4
  369.6 4.6 %slice.56 = bf16[2048,1024]{1,0:T(8,128)(2,1)} slice(bf16[2048,3584]{1,0:T(8,128)(2,1)} %all-gather.2.cloned.1.call-done), slice={[0:2048], [2560:3584]} | slice | bytes 8388608 | tf_op jit(solution)/shard_map/slice | solution.py:239
  374.3 7.1 %reshape.451 = bf16[1024,2048]{1,0:T(8,128)(2,1)} reshape(bf16[2048,1024]{1,0:T(8,128)(2,1)} %slice.56) | data formatting | bytes 8388608 | tf_op jit(solution)/shard_map/reshape | solution.py:239
  381.3 2.7 all-to-all-done.4
  384.0 3.4 fusion.2
  387.5 5.9 %convolution_convert_fusion.1 = bf16[256,2048]{1,0:T(8,128)(2,1)S(1)} fusion(bf16[1024,2048]{1,0:T(8,128)(2,1)} %reshape.451, bf16[256,2048]{1,0:T(8,128)(2,1)S(1)} %bitcast.76, bf16[2048,3584]{1,0:T(8,128)(2,1)} %all-gather.2.cloned.1.call-done, f32[256,1024]{1,0:T(8,128)S(1)} %fusion.2), kind=kOutput, calls=%fused_computation.9 | convolution fusion | flops 2149580800 | bytes 11534336 | tf_op jit(solution)/shard_map/dot_general | solution.py:259
  393.4 16.9 %all_to_all.30 = bf16[4,64,2048]{2,1,0:T(8,128)(2,1)S(1)} all-to-all(bf16[4,64,2048]{2,1,0:T(8,128)(2,1)S(1)} %bitcast.77), channel_id=1, replica_groups=mesh['y'=4,'r'=8,'mp'=4] {'mp'}, dimensions={0} | all-to-all | bytes 2097152 | tf_op jit(solution)/shard_map/all_to_all | solution.py:30
  410.5 0.8 fusion.24
  (82 shorter events, 6.6 us)
Async XLA Ops:
  6.5 3.1 copy-start.3
  6.5 301.5 %all-gather.2.cloned.1.call-start = ((), (), s32[]{:S(2)}) async-start(), calls=%async_computation.6 | async-start | bytes 15138816 | tf_op jit(solution)/shard_map/all_gather | solution.py:212
  7.6 3.2 copy-start.4
  10.8 5.3 %copy-start.5 = (f32[64,512]{1,0:T(8,128)S(1)}, f32[64,512]{1,0:T(8,128)}, u32[]{:S(2)}) copy-start(f32[64,512]{1,0:T(8,128)} %param.11) | copy-start | bytes 393220
  14.5 5.2 %collective-permute-start.4 = (bf16[81920]{0:T(1024)(128)(2,1)S(1)}, bf16[81920]{0:T(1024)(128)(2,1)S(1)}, u32[]{:S(2)}, u32[]{:S(2)}) collective-permute-start(bf16[81920]{0:T(1024)(128)(2,1)S(1)} %get-tuple-element.10), channel_id=1, source_target_pairs={{0,3},{1,0},{2,1},{3,2},{4,7},{5,4},{6,5},{7,6},{8,11},{9,8},{10,9... | collective-permute-start | bytes 491528 | tf_op jit(solution)/shard_map/ppermute | solution.py:183
  15.2 9.3 %collective-permute-start.3 = (bf16[81920]{0:T(1024)(128)(2,1)S(1)}, bf16[81920]{0:T(1024)(128)(2,1)S(1)}, u32[]{:S(2)}, u32[]{:S(2)}) collective-permute-start(bf16[81920]{0:T(1024)(128)(2,1)S(1)} %get-tuple-element.11), channel_id=1, source_target_pairs={{0,2},{1,3},{2,0},{3,1},{4,6},{5,7},{6,4},{7,5},{8,10},{9,11},{10,... | collective-permute-start | bytes 491528 | tf_op jit(solution)/shard_map/ppermute | solution.py:183
  16.0 8.6 %collective-permute-start.2 = (bf16[81920]{0:T(1024)(128)(2,1)S(1)}, bf16[81920]{0:T(1024)(128)(2,1)S(1)}, u32[]{:S(2)}, u32[]{:S(2)}) collective-permute-start(bf16[81920]{0:T(1024)(128)(2,1)S(1)} %get-tuple-element.9), channel_id=1, source_target_pairs={{0,1},{1,2},{2,3},{3,0},{4,5},{5,6},{6,7},{7,4},{8,9},{9,10},{10,1... | collective-permute-start | bytes 491528 | tf_op jit(solution)/shard_map/ppermute | solution.py:183
  28.9 1.7 copy-start.6
  29.3 1.3 copy-start.7
  33.2 11.3 %copy-start.8 = (s32[4]{0:T(128)S(1)}, s32[4]{0:T(128)}, u32[]{:S(2)}) copy-start(s32[4]{0:T(128)} %param.10) | copy-start | bytes 52
  33.2 11.6 %copy-start = (bf16[256,2048]{1,0:T(8,128)(2,1)S(1)}, bf16[256,2048]{1,0:T(8,128)(2,1)}, u32[]{:S(2)}) copy-start(bf16[256,2048]{1,0:T(8,128)(2,1)} %param.9) | copy-start | bytes 3145732
  33.2 68.1 %all-to-all-start = ((bf16[32,64,1024]{2,1,0:T(8,128)(2,1)}), bf16[32,64,1024]{2,1,0:T(8,128)(2,1)}, u32[]{:S(2)}, u32[]{:S(2)}) async-start(bf16[32,64,1024]{2,1,0:T(8,128)(2,1)} %broadcast_in_dim.52), calls=%async_computation | async-start | bytes 8388608 | tf_op jit(solution)/shard_map/all_to_all | solution.py:23
  46.0 65.5 %copy-start.1 = (f32[256,64]{1,0:T(8,128)}, f32[256,64]{1,0:T(8,128)S(1)}, u32[]{:S(2)}) copy-start(f32[256,64]{1,0:T(8,128)S(1)} %get-tuple-element.26) | copy-start | bytes 196612
  46.0 65.5 %copy-start.2 = (f32[256,64]{1,0:T(8,128)}, f32[256,64]{1,0:T(8,128)S(1)}, u32[]{:S(2)}) copy-start(f32[256,64]{1,0:T(8,128)S(1)} %get-tuple-element.27) | copy-start | bytes 196612
  111.9 20.9 %collective-permute-start.1 = (bf16[2,4,256,128]{3,2,1,0:T(8,128)(2,1)S(1)}, bf16[2,4,256,128]{3,2,1,0:T(8,128)(2,1)S(1)}, u32[]{:S(2)}, u32[]{:S(2)}) collective-permute-start(bf16[2,4,256,128]{3,2,1,0:T(8,128)(2,1)S(1)} %maximum_bitcast_fusion.own_ref), channel_id=1, source_target_pairs={{0,32},{4,36},{8,40},{12,44},{16,48},{20,52},{24,56},{28,60},{32,6... | collective-permute-start | bytes 1572872 | tf_op jit(solution)/shard_map/ppermute | solution.py:17
  113.2 30.1 %collective-permute-start = (bf16[2,4,256,128]{3,2,1,0:T(8,128)(2,1)S(1)}, bf16[2,4,256,128]{3,2,1,0:T(8,128)(2,1)S(1)}, u32[]{:S(2)}, u32[]{:S(2)}) collective-permute-start(bf16[2,4,256,128]{3,2,1,0:T(8,128)(2,1)S(1)} %maximum_bitcast_fusion.own_ref), channel_id=1, source_target_pairs={{0,64},{4,68},{8,72},{12,76},{16,80},{20,84},{24,88},{28,92},{32,9... | collective-permute-start | bytes 1572872 | tf_op jit(solution)/shard_map/ppermute | solution.py:17
  148.2 148.6 %all-to-all-start.1 = ((bf16[8,2,2,4,256,128]{5,4,3,2,1,0:T(8,128)(2,1)}), bf16[8,2,2,4,256,128]{5,4,3,2,1,0:T(8,128)(2,1)}, u32[]{:S(2)}, u32[]{:S(2)}) async-start(bf16[8,2,2,4,256,128]{5,4,3,2,1,0:T(8,128)(2,1)} %select_select_fusion), calls=%async_computation.1 | async-start | bytes 16777216 | tf_op jit(solution)/shard_map/all_to_all | solution.py:234
  157.1 0.7 collective-permute-start.5
  298.4 39.5 %all-to-all-start.2 = ((bf16[8,64,2048]{2,1,0:T(8,128)(2,1)}), bf16[8,64,2048]{2,1,0:T(8,128)(2,1)S(1)}, u32[]{:S(2)}, u32[]{:S(2)}) async-start(bf16[8,64,2048]{2,1,0:T(8,128)(2,1)} %broadcast_in_dim.67), calls=%async_computation.2 | async-start | bytes 4194304 | tf_op jit(solution)/shard_map/all_to_all | solution.py:23
  339.6 23.7 %all-to-all-start.3 = ((bf16[4,64,2048]{2,1,0:T(8,128)(2,1)}), bf16[4,64,2048]{2,1,0:T(8,128)(2,1)S(1)}, u32[]{:S(2)}, u32[]{:S(2)}) async-start(bf16[4,64,2048]{2,1,0:T(8,128)(2,1)} %bitcast.68), calls=%async_computation.3 | async-start | bytes 2097152 | tf_op jit(solution)/shard_map/all_to_all | solution.py:30
  366.1 18.0 %all-to-all-start.4 = ((bf16[4,64,2048]{2,1,0:T(8,128)(2,1)}), bf16[4,64,2048]{2,1,0:T(8,128)(2,1)S(1)}, u32[]{:S(2)}, u32[]{:S(2)}) async-start(bf16[4,64,2048]{2,1,0:T(8,128)(2,1)} %broadcast_in_dim.68), calls=%async_computation.4 | async-start | bytes 2097152 | tf_op jit(solution)/shard_map/all_to_all | solution.py:23
Sparse Core Ops, SparseCore 0:
  30.7 260.1 all-gather.1

commit v13 on v11

--- a/solution.py
+++ b/solution.py
@@ -194,9 +194,8 @@
     up_shard = unit_columns(up_got)
     down_shard = jnp.transpose(down_got, (1, 0, 2)).reshape(per_mp, mp_size * narrow)
     units = gate_shard.shape[1]
-    rest_shard = jnp.concatenate(
-        [w_query.astype(half_type), gate_shard, up_shard, down_shard.reshape(shard_rows, -1)], axis=1
-    )
+    rest_shard = jnp.concatenate([w_query.astype(half_type), gate_shard, up_shard], axis=1)
+    down_part = down_shard.reshape(shard_rows, -1)
 
     out_full_rows = jnp.transpose(out_got, (1, 0, 2)).reshape(shard_rows, mp_size * narrow)
     swap = [(a * mp_size + b, b * mp_size + a) for a in range(y_size) for b in range(mp_size)]
@@ -205,6 +204,7 @@
 
     kv_full = gather_by_exchange(kv_shard, dp)
     rest_full = lax.all_gather(rest_shard, dp, axis=0, tiled=True)
+    down_full = lax.all_gather(down_part, dp, axis=0, tiled=True)
 
     normed = layer_norm(tokens).astype(half_type)
     joined_kv = jnp.dot(normed, kv_full, preferred_element_type=jnp.float32)
@@ -231,7 +231,7 @@
     q_full = rest_full[:, :narrow]
     server_gate = rest_full[:, narrow : narrow + units]
     server_up = rest_full[:, narrow + units : narrow + 2 * units]
-    server_down = rest_full[:, narrow + 2 * units :].reshape(units, -1)
+    server_down = down_full.reshape(units, -1)
     joined_q = jnp.dot(normed, q_full, preferred_element_type=jnp.float32)
     query = rotate(joined_q.reshape(rows, heads_dev, HEAD), q_offset).astype(half_type)
     query = jnp.transpose(query, (1, 0, 2))

time: 420 us -> 412 us (0.981)
  waiting for transfers between devices: 243 us -> 237 us
  local copies, waits for them, and re-layouts: 37.7 us -> 33.2 us
    all_to_all x1, waiting for transfers between devices: 133 us -> 116 us  [on_device(): received = lax.all_to_all(payload, 'r', 0, 0, tiled=True)]
    all_gather x0 -> x1, waiting for transfers between devices: none -> 11.4 us  [on_device(): down_full = lax.all_gather(down_part, dp, axis=0, tiled=True)]
    all_to_all x1, waiting for transfers between devices: 14.5 us -> 20.2 us  [scatter_sum(): got = lax.all_to_all(pieces, axis, 0, 0, tiled=True)]
    slice x1 -> x0, local copies, waits for them, and re-layouts: 4.66 us -> none  [on_device(): server_down = rest_full[:, narrow + 2 * units:].reshape(units, -1)]
  transfers between devices with their start and end apart: 10 -> 11, of which waited for: 7 -> 7; matrix products, arithmetic and copies ran while one was open for 10% -> 10% of each run, Pallas kernels for 5% -> 5%
where the time goes in v13:
time: 412 us; the launch traced here: 409 us
  waiting for transfers between devices  237 us (58%)
  starting transfers between devices  54.3 us (13%)
  local copies, waits for them, and re-layouts  33.2 us (8%)
  Pallas kernels  21.3 us (5%)
  blocking collectives  17.7 us (4%)
  matrix products  17.5 us (4%)
  between operations  14 us (3%)
  other arithmetic  13.3 us (3%)
    all_to_all x1, waiting for transfers between devices, on_device(): received = lax.all_to_all(payload, 'r', 0, 0, tiled=True)  116 us
    all_to_all x3, waiting for transfers between devices, gather_by_exchange(): got = lax.all_to_all(copies, axis, 0, 0, tiled=True)  55.3 us
    ppermute x2, waiting for transfers between devices, shifted(): lax.ppermute(value, axis, [(source, source + steps) for source in range(c...  24.1 us
    all_to_all x3, starting transfers between devices, gather_by_exchange(): got = lax.all_to_all(copies, axis, 0, 0, tiled=True)  23.6 us
    pallas_call x1, Pallas kernels, attend(): pl.pallas_call(attend_kernel, out_shape=jax.ShapeDtypeStruct((heads, rows...  21.3 us
    all_to_all x1, waiting for transfers between devices, scatter_sum(): got = lax.all_to_all(pieces, axis, 0, 0, tiled=True)  20.2 us
    all_to_all x1, blocking collectives, scatter_sum(): got = lax.all_to_all(pieces, axis, 0, 0, tiled=True)  17.7 us
    all_gather x1, waiting for transfers between devices, on_device(): down_full = lax.all_gather(down_part, dp, axis=0, tiled=True)  11.4 us
  transfers between devices with their start and end apart: 11, of which 7 were waited for; matrix products, arithmetic and copies ran while one was open for 10% of the time, Pallas kernels for 5%

profile of v13, /device:TPU:4, one launch (start us, length us, event | category | flops | bytes accessed | tf_op | source)
XLA Modules:
  0.0 408.7 jit_solution(17830654298403043783)
XLA Ops:
  6.5 1.2 copy.84
  8.1 0.6 reshape.398
  9.1 0.6 reshape.400
  10.3 0.5 broadcast.265
  10.8 1.5 reduce
  12.3 1.5 reshape.420
  13.8 3.5 all-to-all-start
  17.6 9.9 %all-to-all-done = bf16[4,2,40960]{2,1,0:T(2,128)(2,1)S(1)} async-done(((bf16[4,2,40960]{2,1,0:T(2,128)(2,1)}), bf16[4,2,40960]{2,1,0:T(2,128)(2,1)S(1)}, u32[]{:S(2)}, u32[]{:S(2)}) %all-to-all-start) | async-done | bytes 655392 | tf_op jit(solution)/shard_map/all_to_all | solution.py:179
  27.5 0.6 reshape.421
  28.2 0.8 copy.112
  29.5 0.3 copy.92
  30.6 1.0 copy.95
  31.6 2.5 broadcast_in_dim.54
  34.1 11.3 %all-to-all-start.1 = ((bf16[32,64,1024]{2,1,0:T(8,128)(2,1)}), bf16[32,64,1024]{2,1,0:T(8,128)(2,1)}, u32[]{:S(2)}, u32[]{:S(2)}) async-start(bf16[32,64,1024]{2,1,0:T(8,128)(2,1)} %broadcast_in_dim.54), calls=%async_computation.1 | async-start | bytes 8388608 | tf_op jit(solution)/shard_map/all_to_all | solution.py:23
  45.9 0.4 fusion.6
  46.3 0.5 multiply_cosine_fusion
  46.9 55.2 %all-to-all-done.1 = bf16[32,64,1024]{2,1,0:T(8,128)(2,1)} async-done(((bf16[32,64,1024]{2,1,0:T(8,128)(2,1)}), bf16[32,64,1024]{2,1,0:T(8,128)(2,1)}, u32[]{:S(2)}, u32[]{:S(2)}) %all-to-all-start.1) | async-done | bytes 4194336 | tf_op jit(solution)/shard_map/all_to_all | solution.py:23
  102.1 6.5 %copy.89 = bf16[1024,2048]{1,0:T(8,128)(2,1)} copy(bf16[1024,2048]{0,1:T(8,128)(2,1)} %bitcast.9) | data formatting | bytes 8388608 | tf_op jit(solution)/shard_map/dot_general | solution.py:210
  108.6 3.5 fusion.16
  112.6 3.7 collective-permute-start
  116.4 1.9 collective-permute-start.1
  118.4 14.9 %collective-permute-done = bf16[2,4,256,128]{3,2,1,0:T(8,128)(2,1)S(1)} collective-permute-done((bf16[2,4,256,128]{3,2,1,0:T(8,128)(2,1)S(1)}, bf16[2,4,256,128]{3,2,1,0:T(8,128)(2,1)S(1)}, u32[]{:S(2)}, u32[]{:S(2)}) %collective-permute-start) | collective-permute-done | bytes 524320 | tf_op jit(solution)/shard_map/ppermute | solution.py:17
  133.3 9.2 %collective-permute-done.1 = bf16[2,4,256,128]{3,2,1,0:T(8,128)(2,1)S(1)} collective-permute-done((bf16[2,4,256,128]{3,2,1,0:T(8,128)(2,1)S(1)}, bf16[2,4,256,128]{3,2,1,0:T(8,128)(2,1)S(1)}, u32[]{:S(2)}, u32[]{:S(2)}) %collective-permute-start.1) | collective-permute-done | bytes 524320 | tf_op jit(solution)/shard_map/ppermute | solution.py:17
  142.5 5.0 %select_select_fusion = bf16[8,2,2,4,256,128]{5,4,3,2,1,0:T(8,128)(2,1)} fusion(pred[8,2]{1,0:T(8,128)(4,1)S(1)} %get-tuple-element.31, pred[8,2]{1,0:T(8,128)(4,1)S(1)} %get-tuple-element.30, bf16[2,4,256,128]{3,2,1,0:T(8,128)(2,1)S(1)} %collective-permute-done.1, bf16[2,4,256,128]{3,2,1,0:T(8,128)(2,1)S(1)} %collective-permute-done, ...), kind=kLoop, calls=%fused_computation | loop fusion | flops 8388608 | bytes 9961504 | tf_op jit(solution)/shard_map/jit(_where)/select_n | solution.py:226
  147.5 10.9 %all-to-all-start.2 = ((bf16[8,2,2,4,256,128]{5,4,3,2,1,0:T(8,128)(2,1)}), bf16[8,2,2,4,256,128]{5,4,3,2,1,0:T(8,128)(2,1)}, u32[]{:S(2)}, u32[]{:S(2)}) async-start(bf16[8,2,2,4,256,128]{5,4,3,2,1,0:T(8,128)(2,1)} %select_select_fusion), calls=%async_computation.2 | async-start | bytes 16777216 | tf_op jit(solution)/shard_map/all_to_all | solution.py:229
  158.4 0.7 reshape_reshape.7
  159.3 0.7 collective-permute-start.2
  160.1 116.4 %all-to-all-done.2.received_ref = bf16[8,2,2,4,256,128]{5,4,3,2,1,0:T(8,128)(2,1)} async-done(((bf16[8,2,2,4,256,128]{5,4,3,2,1,0:T(8,128)(2,1)}), bf16[8,2,2,4,256,128]{5,4,3,2,1,0:T(8,128)(2,1)}, u32[]{:S(2)}, u32[]{:S(2)}) %all-to-all-start.2) | async-done | bytes 8388640 | tf_op jit(solution)/shard_map/all_to_all | solution.py:229
  276.4 1.6 broadcast_in_dim.67
  278.0 8.8 %all-to-all-start.3 = ((bf16[8,64,2048]{2,1,0:T(8,128)(2,1)}), bf16[8,64,2048]{2,1,0:T(8,128)(2,1)S(1)}, u32[]{:S(2)}, u32[]{:S(2)}) async-start(bf16[8,64,2048]{2,1,0:T(8,128)(2,1)} %broadcast_in_dim.67), calls=%async_computation.3 | async-start | bytes 4194304 | tf_op jit(solution)/shard_map/all_to_all | solution.py:23
  287.3 3.0 fusion.8
  290.3 0.8 fusion.36
  291.1 1.1 copy.107
  292.3 2.0 copy.108
  294.3 1.3 subtract_convert_fusion
  295.7 21.3 %shard_map.91 = bf16[4,256,128]{2,1,0:T(8,128)(2,1)S(1)} custom-call(s32[1]{0:T(128)} %bitcast.meta, bf16[4,256,128]{2,1,0:T(8,128)(2,1)S(1)} %maximum_bitcast_fusion.2.query_ref, bf16[2,4,256,128]{3,2,1,0:T(8,128)(2,1)S(1)} %maximum_bitcast_fusion.1.own_ref, bf16[8,2,2,4,256,128]{5,4,3,2,1,0:T(8,128)(2,1)} %all-to-all-done.2.received_ref, ...), custom_call_target="tpu_custom_call" | custom-call | flops 2281701376 | bytes 9437184 | tf_op jit(solution)/shard_map/pallas_call | solution.py:125
  317.1 1.7 convolution_convert_fusion
  318.8 9.9 %all-to-all-start.4 = ((bf16[4,64,2048]{2,1,0:T(8,128)(2,1)}), bf16[4,64,2048]{2,1,0:T(8,128)(2,1)S(1)}, u32[]{:S(2)}, u32[]{:S(2)}) async-start(bf16[4,64,2048]{2,1,0:T(8,128)(2,1)} %bitcast.71), calls=%async_computation.4 | async-start | bytes 2097152 | tf_op jit(solution)/shard_map/all_to_all | solution.py:30
  328.8 20.2 %all-to-all-done.4 = bf16[4,64,2048]{2,1,0:T(8,128)(2,1)S(1)} async-done(((bf16[4,64,2048]{2,1,0:T(8,128)(2,1)}), bf16[4,64,2048]{2,1,0:T(8,128)(2,1)S(1)}, u32[]{:S(2)}, u32[]{:S(2)}) %all-to-all-start.4) | async-done | bytes 1048608 | tf_op jit(solution)/shard_map/all_to_all | solution.py:30
  349.2 1.1 convert_reduce_fusion.3
  350.7 1.1 broadcast_in_dim.68
  351.8 3.5 all-to-all-start.5
  355.4 11.4 %all-gather.5.cloned.1.call-done = bf16[2048,1024]{1,0:T(8,128)(2,1)} async-done(((bf16[64,1024]{1,0:T(8,128)(2,1)}), bf16[2048,1024]{1,0:T(8,128)(2,1)}) %all-gather.5.cloned.1.call-update) | async-done | bytes 4194320 | tf_op jit(solution)/shard_map/all_gather | solution.py:207
  366.8 7.1 %reshape.416 = bf16[1024,2048]{1,0:T(8,128)(2,1)} reshape(bf16[2048,1024]{1,0:T(8,128)(2,1)} %all-gather.5.cloned.1.call-done) | data formatting | bytes 8388608 | tf_op jit(solution)/shard_map/reshape | solution.py:234
  373.9 3.4 fusion.2
  377.3 5.9 %convolution_convert_fusion.1 = bf16[256,2048]{1,0:T(8,128)(2,1)S(1)} fusion(bf16[1024,2048]{1,0:T(8,128)(2,1)} %reshape.416, bf16[256,2048]{1,0:T(8,128)(2,1)S(1)} %bitcast.81, bf16[2048,2560]{1,0:T(8,128)(2,1)} %all-gather.3.cloned.1.call-done, f32[256,1024]{1,0:T(8,128)S(1)} %fusion.2), kind=kOutput, calls=%fused_computation.8 | convolution fusion | flops 2149580800 | bytes 11534336 | tf_op jit(solution)/shard_map/dot_general | solution.py:254
  383.2 17.7 %all_to_all.42 = bf16[4,64,2048]{2,1,0:T(8,128)(2,1)S(1)} all-to-all(bf16[4,64,2048]{2,1,0:T(8,128)(2,1)S(1)} %bitcast.82), channel_id=1, replica_groups=mesh['y'=4,'r'=8,'mp'=4] {'mp'}, dimensions={0} | all-to-all | bytes 2097152 | tf_op jit(solution)/shard_map/all_to_all | solution.py:30
  401.1 0.8 fusion.24
  (78 shorter events, 5.5 us)
Async XLA Ops:
  6.5 2.1 copy-start.4
  6.5 3.2 copy-start.5
  6.5 3.2 copy-start.3
  10.2 7.1 %copy-start.6 = (f32[64,512]{1,0:T(8,128)S(1)}, f32[64,512]{1,0:T(8,128)}, u32[]{:S(2)}) copy-start(f32[64,512]{1,0:T(8,128)} %param.13) | copy-start | bytes 393220
  10.3 7.1 %copy-start.7 = (f32[64,512]{1,0:T(8,128)S(1)}, f32[64,512]{1,0:T(8,128)}, u32[]{:S(2)}) copy-start(f32[64,512]{1,0:T(8,128)} %param.12) | copy-start | bytes 393220
  10.8 6.6 %copy-start.8 = (f32[64,512]{1,0:T(8,128)S(1)}, f32[64,512]{1,0:T(8,128)}, u32[]{:S(2)}) copy-start(f32[64,512]{1,0:T(8,128)} %param.11) | copy-start | bytes 393220
  13.8 13.7 %all-to-all-start = ((bf16[4,2,40960]{2,1,0:T(2,128)(2,1)}), bf16[4,2,40960]{2,1,0:T(2,128)(2,1)S(1)}, u32[]{:S(2)}, u32[]{:S(2)}) async-start(bf16[4,2,40960]{2,1,0:T(2,128)(2,1)} %reshape.420), calls=%async_computation | async-start | bytes 1310720 | tf_op jit(solution)/shard_map/all_to_all | solution.py:179
  17.3 270.0 %all-gather.3.cloned.1.call-start = ((), (), s32[]{:S(2)}) async-start(), calls=%async_computation.7 | async-start | bytes 10813440 | tf_op jit(solution)/shard_map/all_gather | solution.py:206
  34.1 11.3 %copy-start.9 = (s32[4]{0:T(128)S(1)}, s32[4]{0:T(128)}, u32[]{:S(2)}) copy-start(s32[4]{0:T(128)} %param.10) | copy-start | bytes 52
  34.1 11.6 %copy-start = (bf16[256,2048]{1,0:T(8,128)(2,1)S(1)}, bf16[256,2048]{1,0:T(8,128)(2,1)}, u32[]{:S(2)}) copy-start(bf16[256,2048]{1,0:T(8,128)(2,1)} %param.9) | copy-start | bytes 3145732
  34.1 68.0 %all-to-all-start.1 = ((bf16[32,64,1024]{2,1,0:T(8,128)(2,1)}), bf16[32,64,1024]{2,1,0:T(8,128)(2,1)}, u32[]{:S(2)}, u32[]{:S(2)}) async-start(bf16[32,64,1024]{2,1,0:T(8,128)(2,1)} %broadcast_in_dim.54), calls=%async_computation.1 | async-start | bytes 8388608 | tf_op jit(solution)/shard_map/all_to_all | solution.py:23
  46.9 65.3 %copy-start.1 = (f32[256,64]{1,0:T(8,128)}, f32[256,64]{1,0:T(8,128)S(1)}, u32[]{:S(2)}) copy-start(f32[256,64]{1,0:T(8,128)S(1)} %get-tuple-element.26) | copy-start | bytes 196612
  46.9 65.3 %copy-start.2 = (f32[256,64]{1,0:T(8,128)}, f32[256,64]{1,0:T(8,128)S(1)}, u32[]{:S(2)}) copy-start(f32[256,64]{1,0:T(8,128)S(1)} %get-tuple-element.27) | copy-start | bytes 196612
  112.6 20.6 %collective-permute-start = (bf16[2,4,256,128]{3,2,1,0:T(8,128)(2,1)S(1)}, bf16[2,4,256,128]{3,2,1,0:T(8,128)(2,1)S(1)}, u32[]{:S(2)}, u32[]{:S(2)}) collective-permute-start(bf16[2,4,256,128]{3,2,1,0:T(8,128)(2,1)S(1)} %maximum_bitcast_fusion.1.own_ref), channel_id=1, source_target_pairs={{0,64},{4,68},{8,72},{12,76},{16,80},{20,84},{24,88},{28,92},{32,9... | collective-permute-start | bytes 1572872 | tf_op jit(solution)/shard_map/ppermute | solution.py:17
  116.4 26.2 %collective-permute-start.1 = (bf16[2,4,256,128]{3,2,1,0:T(8,128)(2,1)S(1)}, bf16[2,4,256,128]{3,2,1,0:T(8,128)(2,1)S(1)}, u32[]{:S(2)}, u32[]{:S(2)}) collective-permute-start(bf16[2,4,256,128]{3,2,1,0:T(8,128)(2,1)S(1)} %maximum_bitcast_fusion.1.own_ref), channel_id=1, source_target_pairs={{0,32},{4,36},{8,40},{12,44},{16,48},{20,52},{24,56},{28,60},{32,6... | collective-permute-start | bytes 1572872 | tf_op jit(solution)/shard_map/ppermute | solution.py:17
  147.5 128.9 %all-to-all-start.2 = ((bf16[8,2,2,4,256,128]{5,4,3,2,1,0:T(8,128)(2,1)}), bf16[8,2,2,4,256,128]{5,4,3,2,1,0:T(8,128)(2,1)}, u32[]{:S(2)}, u32[]{:S(2)}) async-start(bf16[8,2,2,4,256,128]{5,4,3,2,1,0:T(8,128)(2,1)} %select_select_fusion), calls=%async_computation.2 | async-start | bytes 16777216 | tf_op jit(solution)/shard_map/all_to_all | solution.py:229
  158.4 208.3 %all-gather.5.cloned.1.call-start = ((), (), s32[]{:S(2)}) async-start(), calls=%async_computation.8 | async-start | bytes 4325376 | tf_op jit(solution)/shard_map/all_gather | solution.py:207
  159.3 0.7 collective-permute-start.2
  278.0 39.1 %all-to-all-start.3 = ((bf16[8,64,2048]{2,1,0:T(8,128)(2,1)}), bf16[8,64,2048]{2,1,0:T(8,128)(2,1)S(1)}, u32[]{:S(2)}, u32[]{:S(2)}) async-start(bf16[8,64,2048]{2,1,0:T(8,128)(2,1)} %broadcast_in_dim.67), calls=%async_computation.3 | async-start | bytes 4194304 | tf_op jit(solution)/shard_map/all_to_all | solution.py:23
  318.8 30.2 %all-to-all-start.4 = ((bf16[4,64,2048]{2,1,0:T(8,128)(2,1)}), bf16[4,64,2048]{2,1,0:T(8,128)(2,1)S(1)}, u32[]{:S(2)}, u32[]{:S(2)}) async-start(bf16[4,64,2048]{2,1,0:T(8,128)(2,1)} %bitcast.71), calls=%async_computation.4 | async-start | bytes 2097152 | tf_op jit(solution)/shard_map/all_to_all | solution.py:30
  351.8 22.0 %all-to-all-start.5 = ((bf16[4,64,2048]{2,1,0:T(8,128)(2,1)}), bf16[4,64,2048]{2,1,0:T(8,128)(2,1)S(1)}, u32[]{:S(2)}, u32[]{:S(2)}) async-start(bf16[4,64,2048]{2,1,0:T(8,128)(2,1)} %broadcast_in_dim.68), calls=%async_computation.5 | async-start | bytes 2097152 | tf_op jit(solution)/shard_map/all_to_all | solution.py:23
Sparse Core Ops, SparseCore 0:
  31.7 238.4 all-gather.2
  273.2 93.4 all-gather.4

commit v14 on v13

--- a/solution.py
+++ b/solution.py
@@ -195,7 +195,6 @@
     down_shard = jnp.transpose(down_got, (1, 0, 2)).reshape(per_mp, mp_size * narrow)
     units = gate_shard.shape[1]
     rest_shard = jnp.concatenate([w_query.astype(half_type), gate_shard, up_shard], axis=1)
-    down_part = down_shard.reshape(shard_rows, -1)
 
     out_full_rows = jnp.transpose(out_got, (1, 0, 2)).reshape(shard_rows, mp_size * narrow)
     swap = [(a * mp_size + b, b * mp_size + a) for a in range(y_size) for b in range(mp_size)]
@@ -204,7 +203,7 @@
 
     kv_full = gather_by_exchange(kv_shard, dp)
     rest_full = lax.all_gather(rest_shard, dp, axis=0, tiled=True)
-    down_full = lax.all_gather(down_part, dp, axis=0, tiled=True)
+    down_full = lax.all_gather(down_shard, dp, axis=0, tiled=True)
 
     normed = layer_norm(tokens).astype(half_type)
     joined_kv = jnp.dot(normed, kv_full, preferred_element_type=jnp.float32)
@@ -231,7 +230,7 @@
     q_full = rest_full[:, :narrow]
     server_gate = rest_full[:, narrow : narrow + units]
     server_up = rest_full[:, narrow + units : narrow + 2 * units]
-    server_down = down_full.reshape(units, -1)
+    server_down = down_full
     joined_q = jnp.dot(normed, q_full, preferred_element_type=jnp.float32)
     query = rotate(joined_q.reshape(rows, heads_dev, HEAD), q_offset).astype(half_type)
     query = jnp.transpose(query, (1, 0, 2))

time: 412 us -> 406 us (0.985)
  blocking collectives: 17.7 us -> 35.5 us
  waiting for transfers between devices: 237 us -> 226 us
  local copies, waits for them, and re-layouts: 33.2 us -> 25 us
    all_to_all x0 -> x1, blocking collectives: none -> 18.6 us  [gather_by_exchange(): got = lax.all_to_all(copies, axis, 0, 0, tiled=True)]
    all_gather x1, waiting for transfers between devices: 11.4 us -> 0.01 us  [on_device(): down_full = lax.all_gather(down_shard, dp, axis=0, tiled=True)]
    reshape x1 -> x0, local copies, waits for them, and re-layouts: 7.09 us -> none  [on_device(): server_down = down_full.reshape(units, -1)]
    all_to_all x3 -> x2, starting transfers between devices: 23.6 us -> 20.1 us  [gather_by_exchange(): got = lax.all_to_all(copies, axis, 0, 0, tiled=True)]
    all_to_all x3 -> x2, waiting for transfers between devices: 55.3 us -> 55.3 us  [gather_by_exchange(): got = lax.all_to_all(copies, axis, 0, 0, tiled=True)]
  transfers between devices with their start and end apart: 11 -> 10, of which waited for: 7 -> 6; matrix products, arithmetic and copies ran while one was open for 10% -> 10% of each run, Pallas kernels for 5% -> 5%
where the time goes in v14:
time: 406 us; the launch traced here: 405 us
  waiting for transfers between devices  226 us (56%)
  starting transfers between devices  50.8 us (13%)
  blocking collectives  35.5 us (9%)
  local copies, waits for them, and re-layouts  25 us (6%)
  Pallas kernels  21.3 us (5%)
  matrix products  18.8 us (5%)
  between operations  14 us (3%)
  other arithmetic  13.3 us (3%)
    all_to_all x1, waiting for transfers between devices, on_device(): received = lax.all_to_all(payload, 'r', 0, 0, tiled=True)  116 us
    all_to_all x2, waiting for transfers between devices, gather_by_exchange(): got = lax.all_to_all(copies, axis, 0, 0, tiled=True)  55.3 us
    ppermute x2, waiting for transfers between devices, shifted(): lax.ppermute(value, axis, [(source, source + steps) for source in range(c...  24.2 us
    pallas_call x1, Pallas kernels, attend(): pl.pallas_call(attend_kernel, out_shape=jax.ShapeDtypeStruct((heads, rows...  21.3 us
    all_to_all x1, waiting for transfers between devices, scatter_sum(): got = lax.all_to_all(pieces, axis, 0, 0, tiled=True)  20.3 us
    all_to_all x2, starting transfers between devices, gather_by_exchange(): got = lax.all_to_all(copies, axis, 0, 0, tiled=True)  20.1 us
    all_to_all x1, blocking collectives, gather_by_exchange(): got = lax.all_to_all(copies, axis, 0, 0, tiled=True)  18.6 us
    all_to_all x1, blocking collectives, scatter_sum(): got = lax.all_to_all(pieces, axis, 0, 0, tiled=True)  16.9 us
  transfers between devices with their start and end apart: 10, of which 6 were waited for; matrix products, arithmetic and copies ran while one was open for 10% of the time, Pallas kernels for 5%

profile of v14, /device:TPU:4, one launch (start us, length us, event | category | flops | bytes accessed | tf_op | source)
XLA Modules:
  0.0 404.9 jit_solution(10731593956762795646)
XLA Ops:
  6.5 1.2 copy.84
  7.7 0.3 copy.85
  8.1 0.6 reshape.398
  8.8 0.3 copy.87
  9.2 0.6 reshape.400
  10.3 0.5 broadcast.265
  10.8 1.5 reduce
  12.3 1.5 reshape.420
  13.8 3.5 all-to-all-start
  17.6 9.9 %all-to-all-done = bf16[4,2,40960]{2,1,0:T(2,128)(2,1)S(1)} async-done(((bf16[4,2,40960]{2,1,0:T(2,128)(2,1)}), bf16[4,2,40960]{2,1,0:T(2,128)(2,1)S(1)}, u32[]{:S(2)}, u32[]{:S(2)}) %all-to-all-start) | async-done | bytes 655392 | tf_op jit(solution)/shard_map/all_to_all | solution.py:179
  27.5 0.6 reshape.421
  28.2 0.8 copy.113
  29.5 0.3 copy.92
  30.1 0.3 copy.93
  30.6 1.0 copy.95
  31.6 2.5 broadcast_in_dim.54
  34.1 11.3 %all-to-all-start.1 = ((bf16[32,64,1024]{2,1,0:T(8,128)(2,1)}), bf16[32,64,1024]{2,1,0:T(8,128)(2,1)}, u32[]{:S(2)}, u32[]{:S(2)}) async-start(bf16[32,64,1024]{2,1,0:T(8,128)(2,1)} %broadcast_in_dim.54), calls=%async_computation.1 | async-start | bytes 8388608 | tf_op jit(solution)/shard_map/all_to_all | solution.py:23
  45.9 0.4 fusion.6
  46.3 0.5 multiply_cosine_fusion
  46.9 55.3 %all-to-all-done.1 = bf16[32,64,1024]{2,1,0:T(8,128)(2,1)} async-done(((bf16[32,64,1024]{2,1,0:T(8,128)(2,1)}), bf16[32,64,1024]{2,1,0:T(8,128)(2,1)}, u32[]{:S(2)}, u32[]{:S(2)}) %all-to-all-start.1) | async-done | bytes 4194336 | tf_op jit(solution)/shard_map/all_to_all | solution.py:23
  102.2 6.5 %copy.89 = bf16[1024,2048]{1,0:T(8,128)(2,1)} copy(bf16[1024,2048]{0,1:T(8,128)(2,1)} %bitcast.9) | data formatting | bytes 8388608 | tf_op jit(solution)/shard_map/dot_general | solution.py:209
  108.6 3.5 fusion.16
  112.6 3.6 collective-permute-start
  116.3 2.0 collective-permute-start.1
  118.4 14.9 %collective-permute-done = bf16[2,4,256,128]{3,2,1,0:T(8,128)(2,1)S(1)} collective-permute-done((bf16[2,4,256,128]{3,2,1,0:T(8,128)(2,1)S(1)}, bf16[2,4,256,128]{3,2,1,0:T(8,128)(2,1)S(1)}, u32[]{:S(2)}, u32[]{:S(2)}) %collective-permute-start) | collective-permute-done | bytes 524320 | tf_op jit(solution)/shard_map/ppermute | solution.py:17
  133.3 9.3 %collective-permute-done.1 = bf16[2,4,256,128]{3,2,1,0:T(8,128)(2,1)S(1)} collective-permute-done((bf16[2,4,256,128]{3,2,1,0:T(8,128)(2,1)S(1)}, bf16[2,4,256,128]{3,2,1,0:T(8,128)(2,1)S(1)}, u32[]{:S(2)}, u32[]{:S(2)}) %collective-permute-start.1) | collective-permute-done | bytes 524320 | tf_op jit(solution)/shard_map/ppermute | solution.py:17
  142.5 4.9 %select_select_fusion = bf16[8,2,2,4,256,128]{5,4,3,2,1,0:T(8,128)(2,1)} fusion(pred[8,2]{1,0:T(8,128)(4,1)S(1)} %get-tuple-element.31, pred[8,2]{1,0:T(8,128)(4,1)S(1)} %get-tuple-element.30, bf16[2,4,256,128]{3,2,1,0:T(8,128)(2,1)S(1)} %collective-permute-done.1, bf16[2,4,256,128]{3,2,1,0:T(8,128)(2,1)S(1)} %collective-permute-done, ...), kind=kLoop, calls=%fused_computation | loop fusion | flops 8388608 | bytes 9961504 | tf_op jit(solution)/shard_map/jit(_where)/select_n | solution.py:225
  147.5 10.9 %all-to-all-start.2 = ((bf16[8,2,2,4,256,128]{5,4,3,2,1,0:T(8,128)(2,1)}), bf16[8,2,2,4,256,128]{5,4,3,2,1,0:T(8,128)(2,1)}, u32[]{:S(2)}, u32[]{:S(2)}) async-start(bf16[8,2,2,4,256,128]{5,4,3,2,1,0:T(8,128)(2,1)} %select_select_fusion), calls=%async_computation.2 | async-start | bytes 16777216 | tf_op jit(solution)/shard_map/all_to_all | solution.py:228
  158.4 0.7 copy.111
  159.3 0.7 collective-permute-start.2
  160.0 116.4 %all-to-all-done.2.received_ref = bf16[8,2,2,4,256,128]{5,4,3,2,1,0:T(8,128)(2,1)} async-done(((bf16[8,2,2,4,256,128]{5,4,3,2,1,0:T(8,128)(2,1)}), bf16[8,2,2,4,256,128]{5,4,3,2,1,0:T(8,128)(2,1)}, u32[]{:S(2)}, u32[]{:S(2)}) %all-to-all-start.2) | async-done | bytes 8388640 | tf_op jit(solution)/shard_map/all_to_all | solution.py:228
  276.4 1.6 broadcast_in_dim.67
  278.0 8.8 %all-to-all-start.3 = ((bf16[8,64,2048]{2,1,0:T(8,128)(2,1)}), bf16[8,64,2048]{2,1,0:T(8,128)(2,1)S(1)}, u32[]{:S(2)}, u32[]{:S(2)}) async-start(bf16[8,64,2048]{2,1,0:T(8,128)(2,1)} %broadcast_in_dim.67), calls=%async_computation.3 | async-start | bytes 4194304 | tf_op jit(solution)/shard_map/all_to_all | solution.py:23
  287.3 3.0 fusion.8
  290.3 0.8 fusion.36
  291.2 1.1 copy.107
  292.3 2.0 copy.108
  294.3 1.3 subtract_convert_fusion
  295.7 21.3 %shard_map.91 = bf16[4,256,128]{2,1,0:T(8,128)(2,1)S(1)} custom-call(s32[1]{0:T(128)} %bitcast.meta, bf16[4,256,128]{2,1,0:T(8,128)(2,1)S(1)} %maximum_bitcast_fusion.2.query_ref, bf16[2,4,256,128]{3,2,1,0:T(8,128)(2,1)S(1)} %maximum_bitcast_fusion.1.own_ref, bf16[8,2,2,4,256,128]{5,4,3,2,1,0:T(8,128)(2,1)} %all-to-all-done.2.received_ref, ...), custom_call_target="tpu_custom_call" | custom-call | flops 2281701376 | bytes 9437184 | tf_op jit(solution)/shard_map/pallas_call | solution.py:125
  317.1 1.7 convolution_convert_fusion
  318.9 10.0 %all-to-all-start.4 = ((bf16[4,64,2048]{2,1,0:T(8,128)(2,1)}), bf16[4,64,2048]{2,1,0:T(8,128)(2,1)S(1)}, u32[]{:S(2)}, u32[]{:S(2)}) async-start(bf16[4,64,2048]{2,1,0:T(8,128)(2,1)} %bitcast.73), calls=%async_computation.4 | async-start | bytes 2097152 | tf_op jit(solution)/shard_map/all_to_all | solution.py:30
  328.8 20.3 %all-to-all-done.4 = bf16[4,64,2048]{2,1,0:T(8,128)(2,1)S(1)} async-done(((bf16[4,64,2048]{2,1,0:T(8,128)(2,1)}), bf16[4,64,2048]{2,1,0:T(8,128)(2,1)S(1)}, u32[]{:S(2)}, u32[]{:S(2)}) %all-to-all-start.4) | async-done | bytes 1048608 | tf_op jit(solution)/shard_map/all_to_all | solution.py:30
  349.3 1.1 convert_reduce_fusion.3
  351.0 18.6 %all_to_all.42 = bf16[4,64,2048]{2,1,0:T(8,128)(2,1)S(1)} all-to-all(bf16[4,64,2048]{2,1,0:T(8,128)(2,1)S(1)} %broadcast_in_dim.68), channel_id=1, replica_groups=mesh['y'=4,'r'=8,'mp'=4] {'mp'}, dimensions={0} | all-to-all | bytes 2097152 | tf_op jit(solution)/shard_map/all_to_all | solution.py:23
  369.6 4.4 %fusion.2 = f32[256,1024]{1,0:T(8,128)} fusion(bf16[256,2048]{1,0:T(8,128)(2,1)S(1)} %bitcast.82, bf16[2048,2560]{1,0:T(8,128)(2,1)} %all-gather.3.cloned.1.call-done), kind=kOutput, calls=%fused_computation.3 | convolution fusion | flops 1073741824 | bytes 6291456 | tf_op jit(solution)/shard_map/dot_general | solution.py:250
  374.0 6.2 %convolution_convert_fusion.1 = bf16[256,2048]{1,0:T(8,128)(2,1)S(1)} fusion(bf16[1024,2048]{1,0:T(8,128)(2,1)} %all-gather.5.cloned.1.call-done, bf16[256,2048]{1,0:T(8,128)(2,1)S(1)} %bitcast.83, bf16[2048,2560]{1,0:T(8,128)(2,1)} %all-gather.3.cloned.1.call-done, f32[256,1024]{1,0:T(8,128)} %fusion.2), kind=kOutput, calls=%fused_computation.8 | convolution fusion | flops 2149580800 | bytes 11534336 | tf_op jit(solution)/shard_map/dot_general | solution.py:253
  380.3 16.9 %all_to_all.43 = bf16[4,64,2048]{2,1,0:T(8,128)(2,1)S(1)} all-to-all(bf16[4,64,2048]{2,1,0:T(8,128)(2,1)S(1)} %bitcast.84), channel_id=1, replica_groups=mesh['y'=4,'r'=8,'mp'=4] {'mp'}, dimensions={0} | all-to-all | bytes 2097152 | tf_op jit(solution)/shard_map/all_to_all | solution.py:30
  397.3 0.8 fusion.24
  (76 shorter events, 4.6 us)
Async XLA Ops:
  6.5 2.1 copy-start.4
  6.5 3.2 copy-start.5
  6.5 3.2 copy-start.3
  10.3 7.1 %copy-start.6 = (f32[64,512]{1,0:T(8,128)S(1)}, f32[64,512]{1,0:T(8,128)}, u32[]{:S(2)}) copy-start(f32[64,512]{1,0:T(8,128)} %param.13) | copy-start | bytes 393220
  10.3 7.1 %copy-start.7 = (f32[64,512]{1,0:T(8,128)S(1)}, f32[64,512]{1,0:T(8,128)}, u32[]{:S(2)}) copy-start(f32[64,512]{1,0:T(8,128)} %param.12) | copy-start | bytes 393220
  10.8 6.6 %copy-start.8 = (f32[64,512]{1,0:T(8,128)S(1)}, f32[64,512]{1,0:T(8,128)}, u32[]{:S(2)}) copy-start(f32[64,512]{1,0:T(8,128)} %param.11) | copy-start | bytes 393220
  13.8 13.7 %all-to-all-start = ((bf16[4,2,40960]{2,1,0:T(2,128)(2,1)}), bf16[4,2,40960]{2,1,0:T(2,128)(2,1)S(1)}, u32[]{:S(2)}, u32[]{:S(2)}) async-start(bf16[4,2,40960]{2,1,0:T(2,128)(2,1)} %reshape.420), calls=%async_computation | async-start | bytes 1310720 | tf_op jit(solution)/shard_map/all_to_all | solution.py:179
  17.3 270.0 %all-gather.3.cloned.1.call-start = ((), (), s32[]{:S(2)}) async-start(), calls=%async_computation.7 | async-start | bytes 10813440 | tf_op jit(solution)/shard_map/all_gather | solution.py:205
  34.1 11.3 %copy-start.9 = (s32[4]{0:T(128)S(1)}, s32[4]{0:T(128)}, u32[]{:S(2)}) copy-start(s32[4]{0:T(128)} %param.10) | copy-start | bytes 52
  34.1 11.6 %copy-start = (bf16[256,2048]{1,0:T(8,128)(2,1)S(1)}, bf16[256,2048]{1,0:T(8,128)(2,1)}, u32[]{:S(2)}) copy-start(bf16[256,2048]{1,0:T(8,128)(2,1)} %param.9) | copy-start | bytes 3145732
  34.1 68.1 %all-to-all-start.1 = ((bf16[32,64,1024]{2,1,0:T(8,128)(2,1)}), bf16[32,64,1024]{2,1,0:T(8,128)(2,1)}, u32[]{:S(2)}, u32[]{:S(2)}) async-start(bf16[32,64,1024]{2,1,0:T(8,128)(2,1)} %broadcast_in_dim.54), calls=%async_computation.1 | async-start | bytes 8388608 | tf_op jit(solution)/shard_map/all_to_all | solution.py:23
  46.9 65.3 %copy-start.1 = (f32[256,64]{1,0:T(8,128)}, f32[256,64]{1,0:T(8,128)S(1)}, u32[]{:S(2)}) copy-start(f32[256,64]{1,0:T(8,128)S(1)} %get-tuple-element.26) | copy-start | bytes 196612
  46.9 65.3 %copy-start.2 = (f32[256,64]{1,0:T(8,128)}, f32[256,64]{1,0:T(8,128)S(1)}, u32[]{:S(2)}) copy-start(f32[256,64]{1,0:T(8,128)S(1)} %get-tuple-element.27) | copy-start | bytes 196612
  112.6 20.7 %collective-permute-start = (bf16[2,4,256,128]{3,2,1,0:T(8,128)(2,1)S(1)}, bf16[2,4,256,128]{3,2,1,0:T(8,128)(2,1)S(1)}, u32[]{:S(2)}, u32[]{:S(2)}) collective-permute-start(bf16[2,4,256,128]{3,2,1,0:T(8,128)(2,1)S(1)} %maximum_bitcast_fusion.1.own_ref), channel_id=1, source_target_pairs={{0,64},{4,68},{8,72},{12,76},{16,80},{20,84},{24,88},{28,92},{32,9... | collective-permute-start | bytes 1572872 | tf_op jit(solution)/shard_map/ppermute | solution.py:17
  116.3 26.3 %collective-permute-start.1 = (bf16[2,4,256,128]{3,2,1,0:T(8,128)(2,1)S(1)}, bf16[2,4,256,128]{3,2,1,0:T(8,128)(2,1)S(1)}, u32[]{:S(2)}, u32[]{:S(2)}) collective-permute-start(bf16[2,4,256,128]{3,2,1,0:T(8,128)(2,1)S(1)} %maximum_bitcast_fusion.1.own_ref), channel_id=1, source_target_pairs={{0,32},{4,36},{8,40},{12,44},{16,48},{20,52},{24,56},{28,60},{32,6... | collective-permute-start | bytes 1572872 | tf_op jit(solution)/shard_map/ppermute | solution.py:17
  147.5 129.0 %all-to-all-start.2 = ((bf16[8,2,2,4,256,128]{5,4,3,2,1,0:T(8,128)(2,1)}), bf16[8,2,2,4,256,128]{5,4,3,2,1,0:T(8,128)(2,1)}, u32[]{:S(2)}, u32[]{:S(2)}) async-start(bf16[8,2,2,4,256,128]{5,4,3,2,1,0:T(8,128)(2,1)} %select_select_fusion), calls=%async_computation.2 | async-start | bytes 16777216 | tf_op jit(solution)/shard_map/all_to_all | solution.py:228
  158.4 215.6 %all-gather.5.cloned.1.call-start = ((), (), s32[]{:S(2)}) async-start(), calls=%async_computation.8 | async-start | bytes 4325376 | tf_op jit(solution)/shard_map/all_gather | solution.py:206
  159.3 0.7 collective-permute-start.2
  278.0 39.1 %all-to-all-start.3 = ((bf16[8,64,2048]{2,1,0:T(8,128)(2,1)}), bf16[8,64,2048]{2,1,0:T(8,128)(2,1)S(1)}, u32[]{:S(2)}, u32[]{:S(2)}) async-start(bf16[8,64,2048]{2,1,0:T(8,128)(2,1)} %broadcast_in_dim.67), calls=%async_computation.3 | async-start | bytes 4194304 | tf_op jit(solution)/shard_map/all_to_all | solution.py:23
  318.9 30.3 %all-to-all-start.4 = ((bf16[4,64,2048]{2,1,0:T(8,128)(2,1)}), bf16[4,64,2048]{2,1,0:T(8,128)(2,1)S(1)}, u32[]{:S(2)}, u32[]{:S(2)}) async-start(bf16[4,64,2048]{2,1,0:T(8,128)(2,1)} %bitcast.73), calls=%async_computation.4 | async-start | bytes 2097152 | tf_op jit(solution)/shard_map/all_to_all | solution.py:30
Sparse Core Ops, SparseCore 0:
  31.7 238.4 all-gather.2
  273.3 95.4 all-gather.4

commit v15 on v14

--- a/solution.py
+++ b/solution.py
@@ -194,7 +194,8 @@
     up_shard = unit_columns(up_got)
     down_shard = jnp.transpose(down_got, (1, 0, 2)).reshape(per_mp, mp_size * narrow)
     units = gate_shard.shape[1]
-    rest_shard = jnp.concatenate([w_query.astype(half_type), gate_shard, up_shard], axis=1)
+    rest_shard = jnp.concatenate([w_query.astype(half_type), gate_shard], axis=1)
+    late_shard = jnp.concatenate([up_shard, down_shard.reshape(shard_rows, -1)], axis=1)
 
     out_full_rows = jnp.transpose(out_got, (1, 0, 2)).reshape(shard_rows, mp_size * narrow)
     swap = [(a * mp_size + b, b * mp_size + a) for a in range(y_size) for b in range(mp_size)]
@@ -203,7 +204,7 @@
 
     kv_full = gather_by_exchange(kv_shard, dp)
     rest_full = lax.all_gather(rest_shard, dp, axis=0, tiled=True)
-    down_full = lax.all_gather(down_shard, dp, axis=0, tiled=True)
+    late_full = lax.all_gather(late_shard, dp, axis=0, tiled=True)
 
     normed = layer_norm(tokens).astype(half_type)
     joined_kv = jnp.dot(normed, kv_full, preferred_element_type=jnp.float32)
@@ -229,8 +230,8 @@
     received, rest_full = lax.optimization_barrier((received, rest_full))
     q_full = rest_full[:, :narrow]
     server_gate = rest_full[:, narrow : narrow + units]
-    server_up = rest_full[:, narrow + units : narrow + 2 * units]
-    server_down = down_full
+    server_up = late_full[:, :units]
+    server_down = late_full[:, units:].reshape(units, -1)
     joined_q = jnp.dot(normed, q_full, preferred_element_type=jnp.float32)
     query = rotate(joined_q.reshape(rows, heads_dev, HEAD), q_offset).astype(half_type)
     query = jnp.transpose(query, (1, 0, 2))

time: 406 us -> 422 us (1.039)
  waiting for transfers between devices: 226 us -> 209 us
  local copies, waits for them, and re-layouts: 25 us -> 37.1 us
  blocking collectives: 35.5 us -> 46.2 us
  starting transfers between devices: 50.8 us -> 60.9 us
    all_to_all x1, waiting for transfers between devices: 116 us -> 95.5 us  [on_device(): received = lax.all_to_all(payload, 'r', 0, 0, tiled=True)]
    all_gather x1, waiting for transfers between devices: 0.01 us -> 10.5 us  [on_device(): late_full = lax.all_gather(late_shard, dp, axis=0, tiled=True)]
    all_to_all x1, blocking collectives: 18.6 us -> 28.4 us  [gather_by_exchange(): got = lax.all_to_all(copies, axis, 0, 0, tiled=True)]
    all_to_all x1, starting transfers between devices: 10.9 us -> 19.8 us  [on_device(): received = lax.all_to_all(payload, 'r', 0, 0, tiled=True)]
    reshape x0 -> x1, local copies, waits for them, and re-layouts: none -> 7.12 us  [on_device(): server_down = late_full[:, units:].reshape(units, -1)]
    ppermute x2, waiting for transfers between devices: 24.2 us -> 19.2 us  [shifted(): lax.ppermute(value, axis, [(source, source + steps) for source in range(c...]
    slice x0 -> x1, local copies, waits for them, and re-layouts: none -> 4.56 us  [on_device(): server_down = late_full[:, units:].reshape(units, -1)]
  transfers between devices with their start and end apart: 10 -> 10, of which waited for: 6 -> 7; matrix products, arithmetic and copies ran while one was open for 10% -> 9% of each run, Pallas kernels for 5% -> 5%
where the time goes in v15:
time: 422 us; the launch traced here: 420 us
  waiting for transfers between devices  209 us (50%)
  starting transfers between devices  60.9 us (14%)
  blocking collectives  46.2 us (11%)
  local copies, waits for them, and re-layouts  37.1 us (9%)
  Pallas kernels  21.3 us (5%)
  matrix products  17.6 us (4%)
  between operations  14 us (3%)
  other arithmetic  13.3 us (3%)
    all_to_all x1, waiting for transfers between devices, on_device(): received = lax.all_to_all(payload, 'r', 0, 0, tiled=True)  95.5 us
    all_to_all x2, waiting for transfers between devices, gather_by_exchange(): got = lax.all_to_all(copies, axis, 0, 0, tiled=True)  51.7 us
    all_to_all x1, blocking collectives, gather_by_exchange(): got = lax.all_to_all(copies, axis, 0, 0, tiled=True)  28.4 us
    all_to_all x1, waiting for transfers between devices, scatter_sum(): got = lax.all_to_all(pieces, axis, 0, 0, tiled=True)  22.3 us
    pallas_call x1, Pallas kernels, attend(): pl.pallas_call(attend_kernel, out_shape=jax.ShapeDtypeStruct((heads, rows...  21.3 us
    all_to_all x1, starting transfers between devices, on_device(): received = lax.all_to_all(payload, 'r', 0, 0, tiled=True)  19.8 us
    ppermute x2, waiting for transfers between devices, shifted(): lax.ppermute(value, axis, [(source, source + steps) for source in range(c...  19.2 us
    all_to_all x1, blocking collectives, scatter_sum(): got = lax.all_to_all(pieces, axis, 0, 0, tiled=True)  17.8 us
  transfers between devices with their start and end apart: 10, of which 7 were waited for; matrix products, arithmetic and copies ran while one was open for 9% of the time, Pallas kernels for 5%

profile of v15, /device:TPU:4, one launch (start us, length us, event | category | flops | bytes accessed | tf_op | source)
XLA Modules:
  0.0 419.6 jit_solution(5230269203540969205)
XLA Ops:
  6.5 1.2 copy.110
  8.1 0.6 reshape.398
  9.1 0.6 reshape.400
  10.3 0.5 broadcast.265
  10.8 1.5 reduce
  12.3 1.5 reshape.420
  13.8 3.5 all-to-all-start
  17.6 9.9 %all-to-all-done = bf16[4,2,40960]{2,1,0:T(2,128)(2,1)S(1)} async-done(((bf16[4,2,40960]{2,1,0:T(2,128)(2,1)}), bf16[4,2,40960]{2,1,0:T(2,128)(2,1)S(1)}, u32[]{:S(2)}, u32[]{:S(2)}) %all-to-all-start) | async-done | bytes 655392 | tf_op jit(solution)/shard_map/all_to_all | solution.py:179
  27.5 0.6 reshape.421
  28.2 0.8 copy.140
  29.9 0.9 copy.120
  30.8 2.5 broadcast_in_dim.54
  33.3 11.2 %all-to-all-start.1 = ((bf16[32,64,1024]{2,1,0:T(8,128)(2,1)}), bf16[32,64,1024]{2,1,0:T(8,128)(2,1)}, u32[]{:S(2)}, u32[]{:S(2)}) async-start(bf16[32,64,1024]{2,1,0:T(8,128)(2,1)} %broadcast_in_dim.54), calls=%async_computation.1 | async-start | bytes 8388608 | tf_op jit(solution)/shard_map/all_to_all | solution.py:23
  45.1 0.4 fusion.6
  45.8 0.3 copy.127
  46.5 0.9 copy.130
  47.5 0.5 multiply_cosine_fusion
  48.1 51.7 %all-to-all-done.1 = bf16[32,64,1024]{2,1,0:T(8,128)(2,1)} async-done(((bf16[32,64,1024]{2,1,0:T(8,128)(2,1)}), bf16[32,64,1024]{2,1,0:T(8,128)(2,1)}, u32[]{:S(2)}, u32[]{:S(2)}) %all-to-all-start.1) | async-done | bytes 4194336 | tf_op jit(solution)/shard_map/all_to_all | solution.py:23
  99.8 6.5 %copy.115 = bf16[1024,2048]{1,0:T(8,128)(2,1)} copy(bf16[1024,2048]{0,1:T(8,128)(2,1)} %bitcast.9) | data formatting | bytes 8388608 | tf_op jit(solution)/shard_map/dot_general | solution.py:210
  106.3 3.5 fusion.16
  110.4 3.5 collective-permute-start
  113.9 2.7 collective-permute-start.1
  116.6 9.6 %collective-permute-done = bf16[2,4,256,128]{3,2,1,0:T(8,128)(2,1)S(1)} collective-permute-done((bf16[2,4,256,128]{3,2,1,0:T(8,128)(2,1)S(1)}, bf16[2,4,256,128]{3,2,1,0:T(8,128)(2,1)S(1)}, u32[]{:S(2)}, u32[]{:S(2)}) %collective-permute-start) | collective-permute-done | bytes 524320 | tf_op jit(solution)/shard_map/ppermute | solution.py:17
  126.2 9.6 %collective-permute-done.1 = bf16[2,4,256,128]{3,2,1,0:T(8,128)(2,1)S(1)} collective-permute-done((bf16[2,4,256,128]{3,2,1,0:T(8,128)(2,1)S(1)}, bf16[2,4,256,128]{3,2,1,0:T(8,128)(2,1)S(1)}, u32[]{:S(2)}, u32[]{:S(2)}) %collective-permute-start.1) | collective-permute-done | bytes 524320 | tf_op jit(solution)/shard_map/ppermute | solution.py:17
  135.8 4.9 %select_select_fusion = bf16[8,2,2,4,256,128]{5,4,3,2,1,0:T(8,128)(2,1)} fusion(pred[8,2]{1,0:T(8,128)(4,1)S(1)} %get-tuple-element.31, pred[8,2]{1,0:T(8,128)(4,1)S(1)} %get-tuple-element.30, bf16[2,4,256,128]{3,2,1,0:T(8,128)(2,1)S(1)} %collective-permute-done.1, bf16[2,4,256,128]{3,2,1,0:T(8,128)(2,1)S(1)} %collective-permute-done, ...), kind=kLoop, calls=%fused_computation | loop fusion | flops 8388608 | bytes 9961504 | tf_op jit(solution)/shard_map/jit(_where)/select_n | solution.py:226
  140.7 19.8 %all-to-all-start.2 = ((bf16[8,2,2,4,256,128]{5,4,3,2,1,0:T(8,128)(2,1)}), bf16[8,2,2,4,256,128]{5,4,3,2,1,0:T(8,128)(2,1)}, u32[]{:S(2)}, u32[]{:S(2)}) async-start(bf16[8,2,2,4,256,128]{5,4,3,2,1,0:T(8,128)(2,1)} %select_select_fusion), calls=%async_computation.2 | async-start | bytes 16777216 | tf_op jit(solution)/shard_map/all_to_all | solution.py:229
  160.7 0.7 collective-permute-start.2
  161.4 95.5 %all-to-all-done.2.received_ref = bf16[8,2,2,4,256,128]{5,4,3,2,1,0:T(8,128)(2,1)} async-done(((bf16[8,2,2,4,256,128]{5,4,3,2,1,0:T(8,128)(2,1)}), bf16[8,2,2,4,256,128]{5,4,3,2,1,0:T(8,128)(2,1)}, u32[]{:S(2)}, u32[]{:S(2)}) %all-to-all-start.2) | async-done | bytes 8388640 | tf_op jit(solution)/shard_map/all_to_all | solution.py:229
  256.9 1.6 broadcast_in_dim.67
  258.5 6.1 %all-to-all-start.3 = ((bf16[8,64,2048]{2,1,0:T(8,128)(2,1)}), bf16[8,64,2048]{2,1,0:T(8,128)(2,1)S(1)}, u32[]{:S(2)}, u32[]{:S(2)}) async-start(bf16[8,64,2048]{2,1,0:T(8,128)(2,1)} %broadcast_in_dim.67), calls=%async_computation.3 | async-start | bytes 4194304 | tf_op jit(solution)/shard_map/all_to_all | solution.py:23
  265.0 3.0 fusion.8
  268.0 0.8 fusion.36
  268.8 1.1 copy.135
  270.0 2.0 copy.136
  271.9 1.3 subtract_convert_fusion
  273.4 21.3 %shard_map.91 = bf16[4,256,128]{2,1,0:T(8,128)(2,1)S(1)} custom-call(s32[1]{0:T(128)} %bitcast.meta, bf16[4,256,128]{2,1,0:T(8,128)(2,1)S(1)} %maximum_bitcast_fusion.2.query_ref, bf16[2,4,256,128]{3,2,1,0:T(8,128)(2,1)S(1)} %maximum_bitcast_fusion.1.own_ref, bf16[8,2,2,4,256,128]{5,4,3,2,1,0:T(8,128)(2,1)} %all-to-all-done.2.received_ref, ...), custom_call_target="tpu_custom_call" | custom-call | flops 2281701376 | bytes 9437184 | tf_op jit(solution)/shard_map/pallas_call | solution.py:125
  294.8 1.8 convolution_convert_fusion
  296.6 13.4 %all-to-all-start.4 = ((bf16[4,64,2048]{2,1,0:T(8,128)(2,1)}), bf16[4,64,2048]{2,1,0:T(8,128)(2,1)S(1)}, u32[]{:S(2)}, u32[]{:S(2)}) async-start(bf16[4,64,2048]{2,1,0:T(8,128)(2,1)} %bitcast.71), calls=%async_computation.4 | async-start | bytes 2097152 | tf_op jit(solution)/shard_map/all_to_all | solution.py:30
  310.0 22.3 %all-to-all-done.4 = bf16[4,64,2048]{2,1,0:T(8,128)(2,1)S(1)} async-done(((bf16[4,64,2048]{2,1,0:T(8,128)(2,1)}), bf16[4,64,2048]{2,1,0:T(8,128)(2,1)S(1)}, u32[]{:S(2)}, u32[]{:S(2)}) %all-to-all-start.4) | async-done | bytes 1048608 | tf_op jit(solution)/shard_map/all_to_all | solution.py:30
  332.4 1.1 convert_reduce_fusion.3
  334.1 28.4 %all_to_all.42 = bf16[4,64,2048]{2,1,0:T(8,128)(2,1)S(1)} all-to-all(bf16[4,64,2048]{2,1,0:T(8,128)(2,1)S(1)} %broadcast_in_dim.68), channel_id=1, replica_groups=mesh['y'=4,'r'=8,'mp'=4] {'mp'}, dimensions={0} | all-to-all | bytes 2097152 | tf_op jit(solution)/shard_map/all_to_all | solution.py:23
  362.5 3.4 fusion.2
  365.9 10.5 %all-gather.5.cloned.1.call-done = bf16[2048,2048]{1,0:T(8,128)(2,1)} async-done(((bf16[64,2048]{1,0:T(8,128)(2,1)}), bf16[2048,2048]{1,0:T(8,128)(2,1)}) %all-gather.5.cloned.1.call-update) | async-done | bytes 8388624 | tf_op jit(solution)/shard_map/all_gather | solution.py:207
  376.5 4.6 %slice.64 = bf16[2048,1024]{1,0:T(8,128)(2,1)} slice(bf16[2048,2048]{1,0:T(8,128)(2,1)} %all-gather.5.cloned.1.call-done), slice={[0:2048], [1024:2048]} | slice | bytes 8388608 | tf_op jit(solution)/shard_map/slice | solution.py:234
  381.0 7.1 %reshape.416 = bf16[1024,2048]{1,0:T(8,128)(2,1)} reshape(bf16[2048,1024]{1,0:T(8,128)(2,1)} %slice.64) | data formatting | bytes 8388608 | tf_op jit(solution)/shard_map/reshape | solution.py:234
  388.2 5.9 %convolution_convert_fusion.1 = bf16[256,2048]{1,0:T(8,128)(2,1)S(1)} fusion(bf16[1024,2048]{1,0:T(8,128)(2,1)} %reshape.416, bf16[256,2048]{1,0:T(8,128)(2,1)S(1)} %bitcast.80, bf16[2048,2048]{1,0:T(8,128)(2,1)} %all-gather.5.cloned.1.call-done, f32[256,1024]{1,0:T(8,128)S(1)} %fusion.2), kind=kOutput, calls=%fused_computation.8 | convolution fusion | flops 2149580800 | bytes 11534336 | tf_op jit(solution)/shard_map/dot_general | solution.py:254
  394.1 17.8 %all_to_all.43 = bf16[4,64,2048]{2,1,0:T(8,128)(2,1)S(1)} all-to-all(bf16[4,64,2048]{2,1,0:T(8,128)(2,1)S(1)} %bitcast.81), channel_id=1, replica_groups=mesh['y'=4,'r'=8,'mp'=4] {'mp'}, dimensions={0} | all-to-all | bytes 2097152 | tf_op jit(solution)/shard_map/all_to_all | solution.py:30
  412.1 0.8 fusion.24
  (81 shorter events, 6.0 us)
Async XLA Ops:
  6.5 2.1 copy-start.4
  6.5 3.2 copy-start.5
  6.5 3.2 copy-start.3
  10.2 7.1 %copy-start.6 = (f32[64,512]{1,0:T(8,128)S(1)}, f32[64,512]{1,0:T(8,128)}, u32[]{:S(2)}) copy-start(f32[64,512]{1,0:T(8,128)} %param.13) | copy-start | bytes 393220
  10.3 7.1 %copy-start.7 = (f32[64,512]{1,0:T(8,128)S(1)}, f32[64,512]{1,0:T(8,128)}, u32[]{:S(2)}) copy-start(f32[64,512]{1,0:T(8,128)} %param.12) | copy-start | bytes 393220
  10.8 6.6 %copy-start.8 = (f32[64,512]{1,0:T(8,128)S(1)}, f32[64,512]{1,0:T(8,128)}, u32[]{:S(2)}) copy-start(f32[64,512]{1,0:T(8,128)} %param.11) | copy-start | bytes 393220
  13.8 13.7 %all-to-all-start = ((bf16[4,2,40960]{2,1,0:T(2,128)(2,1)}), bf16[4,2,40960]{2,1,0:T(2,128)(2,1)S(1)}, u32[]{:S(2)}, u32[]{:S(2)}) async-start(bf16[4,2,40960]{2,1,0:T(2,128)(2,1)} %reshape.420), calls=%async_computation | async-start | bytes 1310720 | tf_op jit(solution)/shard_map/all_to_all | solution.py:179
  17.3 247.7 %all-gather.3.cloned.1.call-start = ((), (), s32[]{:S(2)}) async-start(), calls=%async_computation.7 | async-start | bytes 6488064 | tf_op jit(solution)/shard_map/all_gather | solution.py:206
  33.2 11.3 %copy-start.9 = (s32[4]{0:T(128)S(1)}, s32[4]{0:T(128)}, u32[]{:S(2)}) copy-start(s32[4]{0:T(128)} %param.10) | copy-start | bytes 52
  33.3 11.6 %copy-start = (bf16[256,2048]{1,0:T(8,128)(2,1)S(1)}, bf16[256,2048]{1,0:T(8,128)(2,1)}, u32[]{:S(2)}) copy-start(bf16[256,2048]{1,0:T(8,128)(2,1)} %param.9) | copy-start | bytes 3145732
  33.3 66.5 %all-to-all-start.1 = ((bf16[32,64,1024]{2,1,0:T(8,128)(2,1)}), bf16[32,64,1024]{2,1,0:T(8,128)(2,1)}, u32[]{:S(2)}, u32[]{:S(2)}) async-start(bf16[32,64,1024]{2,1,0:T(8,128)(2,1)} %broadcast_in_dim.54), calls=%async_computation.1 | async-start | bytes 8388608 | tf_op jit(solution)/shard_map/all_to_all | solution.py:23
  44.5 332.0 %all-gather.5.cloned.1.call-start = ((), (), s32[]{:S(2)}) async-start(), calls=%async_computation.8 | async-start | bytes 8650752 | tf_op jit(solution)/shard_map/all_gather | solution.py:207
  48.0 61.9 %copy-start.1 = (f32[256,64]{1,0:T(8,128)}, f32[256,64]{1,0:T(8,128)S(1)}, u32[]{:S(2)}) copy-start(f32[256,64]{1,0:T(8,128)S(1)} %get-tuple-element.26) | copy-start | bytes 196612
  48.0 61.9 %copy-start.2 = (f32[256,64]{1,0:T(8,128)}, f32[256,64]{1,0:T(8,128)S(1)}, u32[]{:S(2)}) copy-start(f32[256,64]{1,0:T(8,128)S(1)} %get-tuple-element.27) | copy-start | bytes 196612
  110.4 15.9 %collective-permute-start = (bf16[2,4,256,128]{3,2,1,0:T(8,128)(2,1)S(1)}, bf16[2,4,256,128]{3,2,1,0:T(8,128)(2,1)S(1)}, u32[]{:S(2)}, u32[]{:S(2)}) collective-permute-start(bf16[2,4,256,128]{3,2,1,0:T(8,128)(2,1)S(1)} %maximum_bitcast_fusion.1.own_ref), channel_id=1, source_target_pairs={{0,64},{4,68},{8,72},{12,76},{16,80},{20,84},{24,88},{28,92},{32,9... | collective-permute-start | bytes 1572872 | tf_op jit(solution)/shard_map/ppermute | solution.py:17
  113.9 22.0 %collective-permute-start.1 = (bf16[2,4,256,128]{3,2,1,0:T(8,128)(2,1)S(1)}, bf16[2,4,256,128]{3,2,1,0:T(8,128)(2,1)S(1)}, u32[]{:S(2)}, u32[]{:S(2)}) collective-permute-start(bf16[2,4,256,128]{3,2,1,0:T(8,128)(2,1)S(1)} %maximum_bitcast_fusion.1.own_ref), channel_id=1, source_target_pairs={{0,32},{4,36},{8,40},{12,44},{16,48},{20,52},{24,56},{28,60},{32,6... | collective-permute-start | bytes 1572872 | tf_op jit(solution)/shard_map/ppermute | solution.py:17
  140.7 116.2 %all-to-all-start.2 = ((bf16[8,2,2,4,256,128]{5,4,3,2,1,0:T(8,128)(2,1)}), bf16[8,2,2,4,256,128]{5,4,3,2,1,0:T(8,128)(2,1)}, u32[]{:S(2)}, u32[]{:S(2)}) async-start(bf16[8,2,2,4,256,128]{5,4,3,2,1,0:T(8,128)(2,1)} %select_select_fusion), calls=%async_computation.2 | async-start | bytes 16777216 | tf_op jit(solution)/shard_map/all_to_all | solution.py:229
  160.7 0.7 collective-permute-start.2
  258.5 36.3 %all-to-all-start.3 = ((bf16[8,64,2048]{2,1,0:T(8,128)(2,1)}), bf16[8,64,2048]{2,1,0:T(8,128)(2,1)S(1)}, u32[]{:S(2)}, u32[]{:S(2)}) async-start(bf16[8,64,2048]{2,1,0:T(8,128)(2,1)} %broadcast_in_dim.67), calls=%async_computation.3 | async-start | bytes 4194304 | tf_op jit(solution)/shard_map/all_to_all | solution.py:23
  296.6 35.7 %all-to-all-start.4 = ((bf16[4,64,2048]{2,1,0:T(8,128)(2,1)}), bf16[4,64,2048]{2,1,0:T(8,128)(2,1)S(1)}, u32[]{:S(2)}, u32[]{:S(2)}) async-start(bf16[4,64,2048]{2,1,0:T(8,128)(2,1)} %bitcast.71), calls=%async_computation.4 | async-start | bytes 2097152 | tf_op jit(solution)/shard_map/all_to_all | solution.py:30
Sparse Core Ops, SparseCore 0:
  30.9 164.4 all-gather.2
  198.6 177.8 all-gather.4

commit v16 on v14

--- a/solution.py
+++ b/solution.py
@@ -225,6 +225,7 @@
     payload = jnp.where(
         pick_own, own_pair[None, None], jnp.where(pick_two, back_two[None, None], back_one[None, None])
     )
+    payload, server_out = lax.optimization_barrier((payload, server_out))
     received = lax.all_to_all(payload, "r", 0, 0, tiled=True)
     received, rest_full = lax.optimization_barrier((received, rest_full))
     q_full = rest_full[:, :narrow]

time: 406 us -> 411 us (1.012); the launches traced: 405 us -> 404 us
  blocking collectives: 35.5 us -> 44.4 us
  waiting for transfers between devices: 226 us -> 219 us
    all_to_all x1, blocking collectives: 18.6 us -> 26.3 us  [gather_by_exchange(): got = lax.all_to_all(copies, axis, 0, 0, tiled=True)]
    all_to_all x1, starting transfers between devices: 9.97 us -> 3.52 us  [scatter_sum(): got = lax.all_to_all(pieces, axis, 0, 0, tiled=True)]
    all_to_all x1, waiting for transfers between devices: 20.3 us -> 14.4 us  [scatter_sum(): got = lax.all_to_all(pieces, axis, 0, 0, tiled=True)]
    all_to_all x2, starting transfers between devices: 20.1 us -> 24.9 us  [gather_by_exchange(): got = lax.all_to_all(copies, axis, 0, 0, tiled=True)]
    ppermute x2, waiting for transfers between devices: 24.2 us -> 19.7 us  [shifted(): lax.ppermute(value, axis, [(source, source + steps) for source in range(c...]
  transfers between devices with their start and end apart: 10 -> 10, of which waited for: 6 -> 7; matrix products, arithmetic and copies ran while one was open for 10% -> 9% of each run, Pallas kernels for 5% -> 5%
where the time goes in v16:
time: 411 us; the launch traced here: 404 us
  waiting for transfers between devices  219 us (53%)
  starting transfers between devices  49.6 us (12%)
  blocking collectives  44.4 us (11%)
  local copies, waits for them, and re-layouts  25 us (6%)
  Pallas kernels  21.3 us (5%)
  matrix products  17.5 us (4%)
  between operations  14 us (3%)
  other arithmetic  13.4 us (3%)
    all_to_all x1, waiting for transfers between devices, on_device(): received = lax.all_to_all(payload, 'r', 0, 0, tiled=True)  120 us
    all_to_all x2, waiting for transfers between devices, gather_by_exchange(): got = lax.all_to_all(copies, axis, 0, 0, tiled=True)  54.4 us
    all_to_all x1, blocking collectives, gather_by_exchange(): got = lax.all_to_all(copies, axis, 0, 0, tiled=True)  26.3 us
    all_to_all x2, starting transfers between devices, gather_by_exchange(): got = lax.all_to_all(copies, axis, 0, 0, tiled=True)  24.9 us
    pallas_call x1, Pallas kernels, attend(): pl.pallas_call(attend_kernel, out_shape=jax.ShapeDtypeStruct((heads, rows...  21.3 us
    ppermute x2, waiting for transfers between devices, shifted(): lax.ppermute(value, axis, [(source, source + steps) for source in range(c...  19.7 us
    all_to_all x1, blocking collectives, scatter_sum(): got = lax.all_to_all(pieces, axis, 0, 0, tiled=True)  18.1 us
    all_to_all x1, waiting for transfers between devices, scatter_sum(): got = lax.all_to_all(pieces, axis, 0, 0, tiled=True)  14.4 us
  transfers between devices with their start and end apart: 10, of which 7 were waited for; matrix products, arithmetic and copies ran while one was open for 9% of the time, Pallas kernels for 5%

profile of v16, /device:TPU:4, one launch (start us, length us, event | category | flops | bytes accessed | tf_op | source)
XLA Modules:
  0.0 404.4 jit_solution(11249751272872455774)
XLA Ops:
  6.5 1.2 copy.85
  7.7 0.3 copy.86
  8.1 0.6 reshape.398
  9.1 0.6 reshape.400
  10.3 0.5 broadcast.265
  10.8 1.5 reduce
  12.3 1.5 reshape.420
  13.8 3.5 all-to-all-start
  17.6 9.9 %all-to-all-done = bf16[4,2,40960]{2,1,0:T(2,128)(2,1)S(1)} async-done(((bf16[4,2,40960]{2,1,0:T(2,128)(2,1)}), bf16[4,2,40960]{2,1,0:T(2,128)(2,1)S(1)}, u32[]{:S(2)}, u32[]{:S(2)}) %all-to-all-start) | async-done | bytes 655392 | tf_op jit(solution)/shard_map/all_to_all | solution.py:179
  27.5 0.6 reshape.421
  28.2 0.8 copy.114
  29.5 0.3 copy.94
  30.1 0.3 copy.95
  30.6 1.0 copy.97
  31.6 2.5 broadcast_in_dim.54
  34.1 11.3 %all-to-all-start.1 = ((bf16[32,64,1024]{2,1,0:T(8,128)(2,1)}), bf16[32,64,1024]{2,1,0:T(8,128)(2,1)}, u32[]{:S(2)}, u32[]{:S(2)}) async-start(bf16[32,64,1024]{2,1,0:T(8,128)(2,1)} %broadcast_in_dim.54), calls=%async_computation.1 | async-start | bytes 8388608 | tf_op jit(solution)/shard_map/all_to_all | solution.py:23
  45.9 0.4 fusion.6
  46.5 0.7 collective-permute-start.2
  47.2 0.5 multiply_cosine_fusion
  47.7 54.4 %all-to-all-done.1 = bf16[32,64,1024]{2,1,0:T(8,128)(2,1)} async-done(((bf16[32,64,1024]{2,1,0:T(8,128)(2,1)}), bf16[32,64,1024]{2,1,0:T(8,128)(2,1)}, u32[]{:S(2)}, u32[]{:S(2)}) %all-to-all-start.1) | async-done | bytes 4194336 | tf_op jit(solution)/shard_map/all_to_all | solution.py:23
  102.1 1.6 broadcast_in_dim.65
  103.7 13.7 %all-to-all-start.2 = ((bf16[8,64,2048]{2,1,0:T(8,128)(2,1)}), bf16[8,64,2048]{2,1,0:T(8,128)(2,1)S(1)}, u32[]{:S(2)}, u32[]{:S(2)}) async-start(bf16[8,64,2048]{2,1,0:T(8,128)(2,1)} %broadcast_in_dim.65), calls=%async_computation.2 | async-start | bytes 4194304 | tf_op jit(solution)/shard_map/all_to_all | solution.py:23
  117.4 6.5 %copy.90 = bf16[1024,2048]{1,0:T(8,128)(2,1)} copy(bf16[1024,2048]{0,1:T(8,128)(2,1)} %bitcast.9) | data formatting | bytes 8388608 | tf_op jit(solution)/shard_map/dot_general | solution.py:209
  123.9 3.5 fusion.16
  127.9 8.2 %collective-permute-start = (bf16[2,4,256,128]{3,2,1,0:T(8,128)(2,1)S(1)}, bf16[2,4,256,128]{3,2,1,0:T(8,128)(2,1)S(1)}, u32[]{:S(2)}, u32[]{:S(2)}) collective-permute-start(bf16[2,4,256,128]{3,2,1,0:T(8,128)(2,1)S(1)} %maximum_bitcast_fusion.1.own_ref), channel_id=1, source_target_pairs={{0,64},{4,68},{8,72},{12,76},{16,80},{20,84},{24,88},{28,92},{32,9... | collective-permute-start | bytes 1572872 | tf_op jit(solution)/shard_map/ppermute | solution.py:17
  136.1 1.5 collective-permute-start.1
  137.7 10.7 %collective-permute-done = bf16[2,4,256,128]{3,2,1,0:T(8,128)(2,1)S(1)} collective-permute-done((bf16[2,4,256,128]{3,2,1,0:T(8,128)(2,1)S(1)}, bf16[2,4,256,128]{3,2,1,0:T(8,128)(2,1)S(1)}, u32[]{:S(2)}, u32[]{:S(2)}) %collective-permute-start) | collective-permute-done | bytes 524320 | tf_op jit(solution)/shard_map/ppermute | solution.py:17
  148.4 9.0 %collective-permute-done.1 = bf16[2,4,256,128]{3,2,1,0:T(8,128)(2,1)S(1)} collective-permute-done((bf16[2,4,256,128]{3,2,1,0:T(8,128)(2,1)S(1)}, bf16[2,4,256,128]{3,2,1,0:T(8,128)(2,1)S(1)}, u32[]{:S(2)}, u32[]{:S(2)}) %collective-permute-start.1) | collective-permute-done | bytes 524320 | tf_op jit(solution)/shard_map/ppermute | solution.py:17
  157.4 5.0 %select_select_fusion = bf16[8,2,2,4,256,128]{5,4,3,2,1,0:T(8,128)(2,1)} fusion(pred[8,2]{1,0:T(8,128)(4,1)S(1)} %get-tuple-element.35, pred[8,2]{1,0:T(8,128)(4,1)S(1)} %get-tuple-element.34, bf16[2,4,256,128]{3,2,1,0:T(8,128)(2,1)S(1)} %collective-permute-done.1, bf16[2,4,256,128]{3,2,1,0:T(8,128)(2,1)S(1)} %collective-permute-done, ...), kind=kLoop, calls=%fused_computation | loop fusion | flops 8388608 | bytes 9961504 | tf_op jit(solution)/shard_map/jit(_where)/select_n | solution.py:225
  162.3 7.3 %all-to-all-start.3 = ((bf16[8,2,2,4,256,128]{5,4,3,2,1,0:T(8,128)(2,1)}), bf16[8,2,2,4,256,128]{5,4,3,2,1,0:T(8,128)(2,1)}, u32[]{:S(2)}, u32[]{:S(2)}) async-start(bf16[8,2,2,4,256,128]{5,4,3,2,1,0:T(8,128)(2,1)} %select_select_fusion), calls=%async_computation.3 | async-start | bytes 16777216 | tf_op jit(solution)/shard_map/all_to_all | solution.py:229
  169.6 0.7 copy.112
  170.8 119.8 %all-to-all-done.3.received_ref = bf16[8,2,2,4,256,128]{5,4,3,2,1,0:T(8,128)(2,1)} async-done(((bf16[8,2,2,4,256,128]{5,4,3,2,1,0:T(8,128)(2,1)}), bf16[8,2,2,4,256,128]{5,4,3,2,1,0:T(8,128)(2,1)}, u32[]{:S(2)}, u32[]{:S(2)}) %all-to-all-start.3) | async-done | bytes 8388640 | tf_op jit(solution)/shard_map/all_to_all | solution.py:229
  290.6 3.0 fusion.8
  293.6 0.8 fusion.36
  294.4 1.1 copy.108
  295.6 2.0 copy.109
  297.5 1.3 subtract_convert_fusion
  299.0 21.3 %shard_map.91 = bf16[4,256,128]{2,1,0:T(8,128)(2,1)S(1)} custom-call(s32[1]{0:T(128)} %bitcast.meta, bf16[4,256,128]{2,1,0:T(8,128)(2,1)S(1)} %maximum_bitcast_fusion.2.query_ref, bf16[2,4,256,128]{3,2,1,0:T(8,128)(2,1)S(1)} %maximum_bitcast_fusion.1.own_ref, bf16[8,2,2,4,256,128]{5,4,3,2,1,0:T(8,128)(2,1)} %all-to-all-done.3.received_ref, ...), custom_call_target="tpu_custom_call" | custom-call | flops 2281701376 | bytes 9437184 | tf_op jit(solution)/shard_map/pallas_call | solution.py:125
  320.4 1.7 convolution_convert_fusion
  322.1 3.5 all-to-all-start.4
  325.6 14.4 %all-to-all-done.4 = bf16[4,64,2048]{2,1,0:T(8,128)(2,1)S(1)} async-done(((bf16[4,64,2048]{2,1,0:T(8,128)(2,1)}), bf16[4,64,2048]{2,1,0:T(8,128)(2,1)S(1)}, u32[]{:S(2)}, u32[]{:S(2)}) %all-to-all-start.4) | async-done | bytes 1048608 | tf_op jit(solution)/shard_map/all_to_all | solution.py:30
  340.2 1.2 convert_reduce_fusion.3
  342.0 26.3 %all_to_all.42 = bf16[4,64,2048]{2,1,0:T(8,128)(2,1)S(1)} all-to-all(bf16[4,64,2048]{2,1,0:T(8,128)(2,1)S(1)} %broadcast_in_dim.68), channel_id=1, replica_groups=mesh['y'=4,'r'=8,'mp'=4] {'mp'}, dimensions={0} | all-to-all | bytes 2097152 | tf_op jit(solution)/shard_map/all_to_all | solution.py:23
  368.3 3.4 fusion.2
  371.7 0.9 all-gather.5.cloned.1.call-done
  372.6 5.9 %convolution_convert_fusion.1 = bf16[256,2048]{1,0:T(8,128)(2,1)S(1)} fusion(bf16[1024,2048]{1,0:T(8,128)(2,1)} %all-gather.5.cloned.1.call-done, bf16[256,2048]{1,0:T(8,128)(2,1)S(1)} %bitcast.82, bf16[2048,2560]{1,0:T(8,128)(2,1)} %all-gather.3.cloned.1.call-done, f32[256,1024]{1,0:T(8,128)S(1)} %fusion.2), kind=kOutput, calls=%fused_computation.8 | convolution fusion | flops 2149580800 | bytes 11534336 | tf_op jit(solution)/shard_map/dot_general | solution.py:254
  378.5 18.1 %all_to_all.43 = bf16[4,64,2048]{2,1,0:T(8,128)(2,1)S(1)} all-to-all(bf16[4,64,2048]{2,1,0:T(8,128)(2,1)S(1)} %bitcast.83), channel_id=1, replica_groups=mesh['y'=4,'r'=8,'mp'=4] {'mp'}, dimensions={0} | all-to-all | bytes 2097152 | tf_op jit(solution)/shard_map/all_to_all | solution.py:30
  396.8 0.8 fusion.24
  (76 shorter events, 5.0 us)
Async XLA Ops:
  6.5 2.1 copy-start.4
  6.5 3.2 copy-start.5
  6.5 3.2 copy-start.3
  10.2 7.1 %copy-start.6 = (f32[64,512]{1,0:T(8,128)S(1)}, f32[64,512]{1,0:T(8,128)}, u32[]{:S(2)}) copy-start(f32[64,512]{1,0:T(8,128)} %param.13) | copy-start | bytes 393220
  10.3 7.1 %copy-start.7 = (f32[64,512]{1,0:T(8,128)S(1)}, f32[64,512]{1,0:T(8,128)}, u32[]{:S(2)}) copy-start(f32[64,512]{1,0:T(8,128)} %param.12) | copy-start | bytes 393220
  10.8 6.6 %copy-start.8 = (f32[64,512]{1,0:T(8,128)S(1)}, f32[64,512]{1,0:T(8,128)}, u32[]{:S(2)}) copy-start(f32[64,512]{1,0:T(8,128)} %param.11) | copy-start | bytes 393220
  13.8 13.7 %all-to-all-start = ((bf16[4,2,40960]{2,1,0:T(2,128)(2,1)}), bf16[4,2,40960]{2,1,0:T(2,128)(2,1)S(1)}, u32[]{:S(2)}, u32[]{:S(2)}) async-start(bf16[4,2,40960]{2,1,0:T(2,128)(2,1)} %reshape.420), calls=%async_computation | async-start | bytes 1310720 | tf_op jit(solution)/shard_map/all_to_all | solution.py:179
  17.3 273.3 %all-gather.3.cloned.1.call-start = ((), (), s32[]{:S(2)}) async-start(), calls=%async_computation.7 | async-start | bytes 10813440 | tf_op jit(solution)/shard_map/all_gather | solution.py:205
  34.1 11.3 %copy-start.9 = (s32[4]{0:T(128)S(1)}, s32[4]{0:T(128)}, u32[]{:S(2)}) copy-start(s32[4]{0:T(128)} %param.10) | copy-start | bytes 52
  34.1 11.6 %copy-start = (bf16[256,2048]{1,0:T(8,128)(2,1)S(1)}, bf16[256,2048]{1,0:T(8,128)(2,1)}, u32[]{:S(2)}) copy-start(bf16[256,2048]{1,0:T(8,128)(2,1)} %param.9) | copy-start | bytes 3145732
  34.1 68.1 %all-to-all-start.1 = ((bf16[32,64,1024]{2,1,0:T(8,128)(2,1)}), bf16[32,64,1024]{2,1,0:T(8,128)(2,1)}, u32[]{:S(2)}, u32[]{:S(2)}) async-start(bf16[32,64,1024]{2,1,0:T(8,128)(2,1)} %broadcast_in_dim.54), calls=%async_computation.1 | async-start | bytes 8388608 | tf_op jit(solution)/shard_map/all_to_all | solution.py:23
  46.5 1.3 collective-permute-start.2
  47.7 79.7 %copy-start.1 = (f32[256,64]{1,0:T(8,128)}, f32[256,64]{1,0:T(8,128)S(1)}, u32[]{:S(2)}) copy-start(f32[256,64]{1,0:T(8,128)S(1)} %get-tuple-element.30) | copy-start | bytes 196612
  47.7 79.7 %copy-start.2 = (f32[256,64]{1,0:T(8,128)}, f32[256,64]{1,0:T(8,128)S(1)}, u32[]{:S(2)}) copy-start(f32[256,64]{1,0:T(8,128)S(1)} %get-tuple-element.31) | copy-start | bytes 196612
  103.7 58.6 %all-to-all-start.2 = ((bf16[8,64,2048]{2,1,0:T(8,128)(2,1)}), bf16[8,64,2048]{2,1,0:T(8,128)(2,1)S(1)}, u32[]{:S(2)}, u32[]{:S(2)}) async-start(bf16[8,64,2048]{2,1,0:T(8,128)(2,1)} %broadcast_in_dim.65), calls=%async_computation.2 | async-start | bytes 4194304 | tf_op jit(solution)/shard_map/all_to_all | solution.py:23
  127.9 20.5 %collective-permute-start = (bf16[2,4,256,128]{3,2,1,0:T(8,128)(2,1)S(1)}, bf16[2,4,256,128]{3,2,1,0:T(8,128)(2,1)S(1)}, u32[]{:S(2)}, u32[]{:S(2)}) collective-permute-start(bf16[2,4,256,128]{3,2,1,0:T(8,128)(2,1)S(1)} %maximum_bitcast_fusion.1.own_ref), channel_id=1, source_target_pairs={{0,64},{4,68},{8,72},{12,76},{16,80},{20,84},{24,88},{28,92},{32,9... | collective-permute-start | bytes 1572872 | tf_op jit(solution)/shard_map/ppermute | solution.py:17
  136.1 21.3 %collective-permute-start.1 = (bf16[2,4,256,128]{3,2,1,0:T(8,128)(2,1)S(1)}, bf16[2,4,256,128]{3,2,1,0:T(8,128)(2,1)S(1)}, u32[]{:S(2)}, u32[]{:S(2)}) collective-permute-start(bf16[2,4,256,128]{3,2,1,0:T(8,128)(2,1)S(1)} %maximum_bitcast_fusion.1.own_ref), channel_id=1, source_target_pairs={{0,32},{4,36},{8,40},{12,44},{16,48},{20,52},{24,56},{28,60},{32,6... | collective-permute-start | bytes 1572872 | tf_op jit(solution)/shard_map/ppermute | solution.py:17
  162.3 128.3 %all-to-all-start.3 = ((bf16[8,2,2,4,256,128]{5,4,3,2,1,0:T(8,128)(2,1)}), bf16[8,2,2,4,256,128]{5,4,3,2,1,0:T(8,128)(2,1)}, u32[]{:S(2)}, u32[]{:S(2)}) async-start(bf16[8,2,2,4,256,128]{5,4,3,2,1,0:T(8,128)(2,1)} %select_select_fusion), calls=%async_computation.3 | async-start | bytes 16777216 | tf_op jit(solution)/shard_map/all_to_all | solution.py:229
  169.6 203.0 %all-gather.5.cloned.1.call-start = ((), (), s32[]{:S(2)}) async-start(), calls=%async_computation.8 | async-start | bytes 4325376 | tf_op jit(solution)/shard_map/all_gather | solution.py:206
  322.1 18.0 %all-to-all-start.4 = ((bf16[4,64,2048]{2,1,0:T(8,128)(2,1)}), bf16[4,64,2048]{2,1,0:T(8,128)(2,1)S(1)}, u32[]{:S(2)}, u32[]{:S(2)}) async-start(bf16[4,64,2048]{2,1,0:T(8,128)(2,1)} %bitcast.30), calls=%async_computation.4 | async-start | bytes 2097152 | tf_op jit(solution)/shard_map/all_to_all | solution.py:30
Sparse Core Ops, SparseCore 0:
  31.7 252.6 all-gather.2
  287.4 85.1 all-gather.4
